TPU v7x, 32 devices: a whole 2x2x4 slice. The times are simulated.
32 devices in a mesh: groups: 2 (over y), seq: 4 (over z), wloop: 2 (over x), heads: 2 (over core).
Axes of the slice: x: 2, y: 2, z: 4, core: 2. Of those that a mesh axis runs over, the one named last changes fastest.
Arguments:
- activations: bfloat16 [4, 2048, 2048], P(('groups', 'wloop'), 'seq'), parts along dimension 0, may hold values from -6 to 6
- norm_gain: float32 [2048], replicated, may hold values from 0.1 to 1.9
- w_query: bfloat16 [2048, 2048], P('wloop', 'heads'), may hold values from -0.125 to 0.125
- w_keyvalue: bfloat16 [2048, 2, 2048], P('wloop', None, 'heads'), may hold values from -0.125 to 0.125
- w_output: bfloat16 [2048, 2048], P('heads', 'wloop'), may hold values from -0.125 to 0.125
- log_retain: float32 [4, 16, 2048], P(('groups', 'wloop'), 'heads', 'seq'), parts along dimension 0, may hold values from -3 to 0, as said below
- resets: int32 [4, 4], P(('groups', 'wloop'), 'seq'), parts along dimension 0, may hold values 0 or 1
Outputs:
- layer_out: bfloat16 [4, 2048, 2048], P(('groups', 'wloop'), 'seq', 'heads'), parts along dimension 0
There are 2 independent parts, one for each index of `groups`. A program takes and returns all parts, laid end to end along the dimension named above; an argument that names none is the same for every part. Nothing has to cross between parts.
Inputs may be any that keep to these rules, and one draw needn't show every extreme that they name: `log_retain`: log retention per token and head, never above zero.
All inputs are finite; a program needn't handle non-finite values. No bound on the sum of `resets` on one device may be relied on, other than what follows from the above.
Results may differ from a plain program's by a relative error of at most 0.02.
Values may be sent and summed in bfloat16 or wider, within the bound.
No kernel may reach another device: no remote copies, remote signals or barrier semaphores. Data moves between devices by JAX's collectives and lax.ppermute only.
A program may use at most 128 MiB of HBM per device.

v0:
```python
import math

import jax
import jax.numpy as jnp
from jax import lax
from jax.sharding import PartitionSpec as P

SCORE_SCALE = 2.0


def shifted(value, axis, steps):
    count = lax.axis_size(axis)
    initial, last = (max(0, -steps), min(count, count - steps))
    return lax.ppermute(value, axis, [(source, source + steps) for source in range(initial, last)])


def rms_rows(values, eps):
    return values * lax.rsqrt(jnp.mean(values * values, axis=-1, keepdims=True) + eps)


def window_mix(queries, lookup_vectors, values, prior_keys, prior_values, allow, scale):
    own = (
        jnp.einsum("bihd,bjhd->bhij", queries, lookup_vectors, preferred_element_type=jnp.float32)
        * scale
    )
    prior = (
        jnp.einsum("bihd,bjhd->bhij", queries, prior_keys, preferred_element_type=jnp.float32)
        * scale
    )
    span = queries.shape[1]
    row_pos = lax.broadcasted_iota(jnp.int32, (span, span), 0)
    column_pos = lax.broadcasted_iota(jnp.int32, (span, span), 1)
    own_w = jnp.where(column_pos <= row_pos, jnp.exp(own), 0.0)
    prior_w = jnp.where((column_pos > row_pos) & allow[:, None, None, None], jnp.exp(prior), 0.0)
    total = jnp.sum(own_w, axis=-1, keepdims=True) + jnp.sum(prior_w, axis=-1, keepdims=True)
    own_p = (own_w / total).astype(jnp.bfloat16)
    prior_p = (prior_w / total).astype(jnp.bfloat16)
    return jnp.einsum(
        "bhij,bjhd->bihd", own_p, values, preferred_element_type=jnp.float32
    ) + jnp.einsum("bhij,bjhd->bihd", prior_p, prior_values, preferred_element_type=jnp.float32)


def shards(activations, norm_gain, w_query, w_keyvalue, w_output, log_retain, resets):
    trajs, span, width = activations.shape
    heads_here = log_retain.shape[1]
    inner_here = w_query.shape[1]
    head_dim = inner_here // heads_here
    scale = SCORE_SCALE / math.sqrt(head_dim)
    count = trajs * span
    normed = (rms_rows(activations.astype(jnp.float32), 1e-05) * norm_gain).astype(jnp.bfloat16)
    normed = normed.reshape(count, width)
    columns = normed
    query_raw = jnp.dot(
        columns,
        lax.all_gather(w_query, "wloop", axis=0, tiled=True),
        preferred_element_type=jnp.float32,
    )
    columns = normed
    pair_raw = jnp.einsum(
        "td,dje->jte",
        columns,
        lax.all_gather(w_keyvalue, "wloop", axis=0, tiled=True),
        preferred_element_type=jnp.float32,
    )
    lookup_vectors = rms_rows(pair_raw[0].reshape(trajs, span, heads_here, head_dim), 1e-06).astype(
        jnp.bfloat16
    )
    values = pair_raw[1].reshape(trajs, span, heads_here, head_dim).astype(jnp.bfloat16)
    prior_keys, prior_values = shifted(
        (lookup_vectors.reshape(trajs, span, inner_here), values.reshape(trajs, span, inner_here)),
        "seq",
        1,
    )
    queries = rms_rows(query_raw.reshape(trajs, span, heads_here, head_dim), 1e-06).astype(
        jnp.bfloat16
    )
    keep = (1 - resets[:, 0]).astype(jnp.float32)
    climb = jnp.cumsum(log_retain, axis=-1)
    whole = climb[:, :, -1]
    factor = jnp.exp(whole) * keep[:, None]
    weight = jnp.exp(whole[:, :, None] - climb)
    local_state = jnp.einsum(
        "bht,bthd,bthe->bhde",
        weight,
        lookup_vectors.astype(jnp.float32),
        values.astype(jnp.float32),
        precision=lax.Precision.HIGHEST,
    )
    local_mass = jnp.sum(weight * weight, axis=-1)

    def relay_turn(turn, carry):
        state, mass = carry
        return (
            shifted(
                (factor[:, :, None, None] * state + local_state).astype(jnp.bfloat16), "seq", 1
            ).astype(jnp.float32),
            shifted((factor * factor * mass + local_mass).astype(jnp.bfloat16), "seq", 1).astype(
                jnp.float32
            ),
        )

    entering, entering_mass = lax.fori_loop(
        0,
        lax.axis_size("seq") - 1,
        relay_turn,
        (jnp.zeros_like(local_state), jnp.zeros_like(local_mass)),
    )
    entering = entering * keep[:, None, None, None]
    entering_mass = entering_mass * keep[:, None]
    read = jnp.einsum(
        "bthd,bhde->bthe", queries.astype(jnp.float32), entering, precision=lax.Precision.HIGHEST
    )
    read = read * jnp.exp(climb).transpose(0, 2, 1)[..., None]
    read = read / jnp.sqrt(head_dim * (1.0 + entering_mass))[:, None, :, None]
    allow = (keep > 0.5) & (lax.axis_index("seq") > 0)
    window = window_mix(
        queries,
        lookup_vectors,
        values,
        prior_keys.reshape(trajs, span, heads_here, head_dim),
        prior_values.reshape(trajs, span, heads_here, head_dim),
        allow,
        scale,
    )
    attended = (window + read).astype(jnp.bfloat16).reshape(count, inner_here)
    partial_out = jnp.dot(
        attended,
        lax.all_gather(w_output, "wloop", axis=1, tiled=True),
        preferred_element_type=jnp.float32,
    )
    summed = lax.psum_scatter(
        partial_out.astype(jnp.bfloat16), "heads", scatter_dimension=1, tiled=True
    ).astype(jnp.float32)
    share = summed.shape[1]
    residual = lax.dynamic_slice_in_dim(
        activations.reshape(count, width), lax.axis_index("heads") * share, share, 1
    )
    return (residual.astype(jnp.float32) + summed).astype(jnp.bfloat16).reshape(trajs, span, share)


def solution(mesh):
    placed = (
        P(("groups", "wloop"), "seq", None),
        P(),
        P("wloop", "heads"),
        P("wloop", None, "heads"),
        P("heads", "wloop"),
        P(("groups", "wloop"), "heads", "seq"),
        P(("groups", "wloop"), "seq"),
    )
    return jax.shard_map(
        shards,
        mesh=mesh,
        in_specs=placed,
        out_specs=P(("groups", "wloop"), "seq", "heads"),
        check_vma=False,
    )
```

profile of v0, /device:TPU:0, one launch (start us, length us, event | category | flops | bytes accessed | tf_op | source)
XLA Modules:
  0.0 322.7 jit_solution(7021560980977442523)
XLA Ops:
  7.3 5.5 %copy.60 = bf16[1024,2,1024]{2,0,1:T(8,128)(2,1)} copy(bf16[1024,2,1024]{2,1,0:T(2,128)(2,1)} %param.12) | data formatting | bytes 8388608 | tf_op args[3]
  18.3 50.1 %all-gather.6.cloned.1.call-done = bf16[2048,1024]{1,0:T(8,128)(2,1)} async-done(((bf16[1024,1024]{1,0:T(8,128)(2,1)}), bf16[2048,1024]{1,0:T(8,128)(2,1)}) %all-gather.6.cloned.1.call-update) | async-done | bytes 4194320 | tf_op jit(solution)/shard_map/all_gather | solution.py:55
  68.4 4.6 %fusion.18 = f32[512,1024]{1,0:T(8,128)S(1)} fusion(bf16[2048,1024]{1,0:T(8,128)(2,1)} %all-gather.6.cloned.1.call-done, bf16[1,512,2048]{2,1,0:T(8,128)(2,1)S(1)} %copy-done.2, f32[2048]{0:T(1024)S(1)} %copy-done.12, f32[512]{0:T(512)S(1)} %add_rsqrt_fusion.2), kind=kOutput, calls=%fused_computation.32 | convolution fusion | flops 2151677952 | bytes 8398848 | tf_op jit(solution)/shard_map/dot_general | solution.py:53
  75.5 3.2 fusion.12
  78.7 95.3 %all-gather.4.cloned.1.call-done = bf16[2048,2,1024]{2,0,1:T(8,128)(2,1)} async-done(((bf16[1024,2,1024]{2,0,1:T(8,128)(2,1)}), bf16[2048,2,1024]{2,0,1:T(8,128)(2,1)}) %all-gather.4.cloned.1.call-update) | async-done | bytes 8388624 | tf_op jit(solution)/shard_map/all_gather | solution.py:62
  173.9 6.9 %convolution_bitcast_fusion = f32[2,512,1024]{2,1,0:T(8,128)S(1)} fusion(bf16[2048,2,1024]{2,0,1:T(8,128)(2,1)} %all-gather.4.cloned.1.call-done, bf16[1,512,2048]{2,1,0:T(8,128)(2,1)S(1)} %copy-done.3, f32[2048]{0:T(1024)S(1)} %copy-done.12, f32[512]{0:T(512)S(1)} %add_rsqrt_fusion.2), kind=kOutput, calls=%fused_computation.21 | convolution fusion | flops 4299161600 | bytes 14690304 | tf_op jit(solution)/shard_map/td,dje->jte/dot_general | solution.py:59
  181.2 1.5 slice_bitcast_fusion.1
  185.7 1.6 mul.196
  187.3 2.1 copy.79
  189.4 3.9 %multiply_convert_fusion = (bf16[1,512,1024]{2,1,0:T(8,128)(2,1)}, f32[1,512,1024]{2,1,0:T(8,128)}) fusion(f32[1,512,1024]{2,1,0:T(8,128)S(1)} %copy.79, f32[2,512,1024]{2,1,0:T(8,128)} %copy-done), kind=kLoop, calls=%fused_computation.37 | loop fusion | flops 1048576 | bytes 7340032 | tf_op jit(solution)/shard_map/convert_element_type | solution.py:65
  193.2 1.9 copy.78
  196.7 4.4 %collective-permute-start.2 = (bf16[1,512,1024]{2,1,0:T(8,128)(2,1)}, bf16[1,512,1024]{2,1,0:T(8,128)(2,1)}, u32[]{:S(2)}, u32[]{:S(2)}) collective-permute-start(bf16[1,512,1024]{2,1,0:T(8,128)(2,1)} %get-tuple-element.111), channel_id=1, source_target_pairs={{0,4},{4,8},{8,12},{1,5},{5,9},{9,13},{2,6},{6,10},{10,14},{3,7},{... | collective-permute-start | bytes 3145736 | tf_op jit(solution)/shard_map/ppermute | solution.py:14
  201.0 3.5 %collective-permute-start.3 = (bf16[1,512,1024]{2,1,0:T(8,128)(2,1)}, bf16[1,512,1024]{2,1,0:T(8,128)(2,1)}, u32[]{:S(2)}, u32[]{:S(2)}) collective-permute-start(bf16[1,512,1024]{2,1,0:T(8,128)(2,1)} %slice.31), channel_id=1, source_target_pairs={{0,4},{4,8},{8,12},{1,5},{5,9},{9,13},{2,6},{6,10},{10,14},{3,7},{... | collective-permute-start | bytes 3145736 | tf_op jit(solution)/shard_map/ppermute | solution.py:14
  205.9 64.6 %while.14 = (s32[]{:T(128)}, f32[1,8,128,128]{3,2,1,0:T(8,128)S(1)}, f32[1,8]{1,0:T(1,128)S(1)}, f32[1,8]{1,0:T(1,128)S(1)}, f32[1,8,128,128]{3,2,1,0:T(8,128)S(...) while((s32[]{:T(128)}, f32[1,8,128,128]{3,2,1,0:T(8,128)S(1)}, ...), condition=%wide.region_9.10_spmd.clone, body=%wide.region_8.9_spmd.clone.sunk | while | flops 655403 | bytes 3146168 | solution.py:102
  206.9 2.3 collective-permute-start
  209.3 1.9 collective-permute-start.1
  211.2 39.4 %collective-permute-done.1 = bf16[1,8]{1,0:T(2,128)(2,1)S(1)} collective-permute-done((bf16[1,8]{1,0:T(2,128)(2,1)S(1)}, bf16[1,8]{1,0:T(2,128)(2,1)S(1)}, u32[]{:S(2)}, u32[]{:S(2)}) %collective-permute-start.1) | collective-permute-done | bytes 48 | tf_op jit(solution)/shard_map/while/body/eval_jaxpr/ppermute | solution.py:14
  251.5 4.4 %collective-permute-start = (bf16[1,8,128,128]{3,2,1,0:T(8,128)(2,1)}, bf16[1,8,128,128]{3,2,1,0:T(8,128)(2,1)S(1)}, u32[]{:S(2)}, u32[]{:S(2)}) collective-permute-start(bf16[1,8,128,128]{3,2,1,0:T(8,128)(2,1)} %fusion.58), channel_id=1, source_target_pairs={{0,4},{4,8},{8,12},{1,5},{5,9},{9,13},{2,6},{6,10},{10,14},{3,7},{... | collective-permute-start | bytes 786440 | tf_op jit(solution)/shard_map/while/body/eval_jaxpr/ppermute | solution.py:14
  255.9 3.4 %collective-permute-start.1 = (bf16[1,8]{1,0:T(2,128)(2,1)S(1)}, bf16[1,8]{1,0:T(2,128)(2,1)S(1)}, u32[]{:S(2)}, u32[]{:S(2)}) collective-permute-start(bf16[1,8]{1,0:T(2,128)(2,1)S(1)} %fusion.59), channel_id=1, source_target_pairs={{0,4},{4,8},{8,12},{1,5},{5,9},{9,13},{2,6},{6,10},{10,14},{3,7},{... | collective-permute-start | bytes 56 | tf_op jit(solution)/shard_map/while/body/eval_jaxpr/ppermute | solution.py:14
  261.4 4.3 %collective-permute-start = (bf16[1,8,128,128]{3,2,1,0:T(8,128)(2,1)}, bf16[1,8,128,128]{3,2,1,0:T(8,128)(2,1)S(1)}, u32[]{:S(2)}, u32[]{:S(2)}) collective-permute-start(bf16[1,8,128,128]{3,2,1,0:T(8,128)(2,1)} %fusion.58), channel_id=1, source_target_pairs={{0,4},{4,8},{8,12},{1,5},{5,9},{9,13},{2,6},{6,10},{10,14},{3,7},{... | collective-permute-start | bytes 786440 | tf_op jit(solution)/shard_map/while/body/eval_jaxpr/ppermute | solution.py:14
  265.8 3.4 %collective-permute-start.1 = (bf16[1,8]{1,0:T(2,128)(2,1)S(1)}, bf16[1,8]{1,0:T(2,128)(2,1)S(1)}, u32[]{:S(2)}, u32[]{:S(2)}) collective-permute-start(bf16[1,8]{1,0:T(2,128)(2,1)S(1)} %fusion.59), channel_id=1, source_target_pairs={{0,4},{4,8},{8,12},{1,5},{5,9},{9,13},{2,6},{6,10},{10,14},{3,7},{... | collective-permute-start | bytes 56 | tf_op jit(solution)/shard_map/while/body/eval_jaxpr/ppermute | solution.py:14
  270.5 3.7 %fusion.35 = f32[8,128,512]{2,1,0:T(8,128)} fusion(bf16[512,8,128]{2,0,1:T(8,128)(2,1)} %fusion.12, f32[1,8,128,128]{3,2,1,0:T(8,128)S(1)} %get-tuple-element.67, f32[]{:T(128)} %bitcast.16), kind=kOutput, calls=%fused_computation.51 | convolution fusion | flops 805437440 | bytes 3670020 | tf_op jit(solution)/shard_map/bthd,bhde->bthe/dot_general | solution.py:110
  274.2 5.5 %fusion.5 = (f32[8,512]{1,0:T(8,128)S(1)}, f32[8,512,512]{1,2,0:T(8,128)}) fusion(pred[512,512]{0,1:T(8,128)(4,1)S(1)} %copy-done.9, bf16[512,8,128]{2,0,1:T(8,128)(2,1)S(1)} %copy-done.7, f32[512,8,128]{0,2,1:T(8,128)S(1)} %bitcast.104, f32[512,8]{0,1:T(8,128)S(1)} %add_rsqrt_fusion), kind=kOutput, calls=%fused_computation.11 | convolution fusion | flops 544206848 | bytes 11829248 | tf_op jit(solution)/shard_map/bihd,bjhd->bhij/dot_general | solution.py:23
  279.7 1.5 copy.85
  281.2 5.2 %fusion.6 = (f32[8,512]{1,0:T(8,128)S(1)}, f32[8,512,512]{1,2,0:T(8,128)}) fusion(pred[512,512]{0,1:T(8,128)(4,1)S(1)} %copy-done.10, bf16[512,8,128]{2,0,1:T(8,128)(2,1)S(1)} %copy-done.7, bf16[512,8,128]{2,1,0:T(8,128)(2,1)S(1)} %bitcast.111), kind=kOutput, calls=%fused_computation.12 | convolution fusion | flops 543158272 | bytes 10764288 | tf_op jit(solution)/shard_map/bihd,bjhd->bhij/dot_general | solution.py:27
  286.5 1.6 copy.80
  288.1 4.8 %fusion.10 = f32[8,128,512]{2,1,0:T(8,128)S(1)} fusion(f32[8,512,512]{1,2,0:T(8,128)} %get-tuple-element.114, f32[8,512]{1,0:T(8,128)S(1)} %add.75, pred[512,512]{0,1:T(8,128)(4,1)S(1)} %copy-done.9, bf16[512,8,128]{2,1,0:T(8,128)(2,1)S(1)} %bitcast.109), kind=kOutput, calls=%fused_computation.18 | convolution fusion | flops 545259520 | bytes 11812864 | tf_op jit(solution)/shard_map/bhij,bjhd->bihd/dot_general | solution.py:38
  293.0 1.6 copy-done.13
  294.6 2.5 fusion.15
  297.1 5.9 %convolution_convert_fusion = bf16[512,2048]{1,0:T(8,128)(2,1)} fusion(bf16[512,1024]{0,1:T(8,128)(2,1)S(1)} %bitcast.117, bf16[1024,2048]{1,0:T(8,128)(2,1)} %all-gather.8.cloned.1.call-done), kind=kOutput, calls=%fused_computation.20 | convolution fusion | flops 2148532224 | bytes 7340032 | tf_op jit(solution)/shard_map/dot_general | solution.py:126
  303.1 10.5 %reduce-scatter.2.cloned.1.call-done = bf16[512,1024]{1,0:T(8,128)(2,1)} async-done(((bf16[512,2048]{1,0:T(8,128)(2,1)}), bf16[512,1024]{1,0:T(8,128)(2,1)}) %reduce-scatter.2.cloned.1.call-update) | async-done | bytes 1048592 | tf_op jit(solution)/shard_map/reduce_scatter | solution.py:131
  313.5 2.6 fusion.26
  (85 shorter events, 19.4 us)
Async XLA Ops:
  6.5 61.8 %all-gather.6.cloned.1.call-start = ((), (), s32[]{:S(2)}) async-start(), calls=%async_computation.2 | async-start | bytes 6291456 | tf_op jit(solution)/shard_map/all_gather | solution.py:55
  7.3 166.7 %all-gather.4.cloned.1.call-start = ((), (), s32[]{:S(2)}) async-start(), calls=%async_computation.1 | async-start | bytes 12582912 | tf_op jit(solution)/shard_map/all_gather | solution.py:62
  12.8 0.8 copy-start.11
  12.8 4.2 %copy-start.2 = (bf16[1,512,2048]{2,1,0:T(8,128)(2,1)S(1)}, bf16[1,512,2048]{2,1,0:T(8,128)(2,1)}, u32[]{:S(2)}) copy-start(bf16[1,512,2048]{2,1,0:T(8,128)(2,1)} %param.9) | copy-start | bytes 6291460
  12.8 55.5 %copy-start.12 = (f32[2048]{0:T(1024)S(1)}, f32[2048]{0:T(1024)}, u32[]{:S(2)}) copy-start(f32[2048]{0:T(1024)} %param.10) | copy-start | bytes 24580
  12.8 284.3 %all-gather.8.cloned.1.call-start = ((), (), s32[]{:S(2)}) async-start(), calls=%async_computation.3 | async-start | bytes 6291456 | tf_op jit(solution)/shard_map/all_gather | solution.py:128
  13.6 300.0 %reduce-scatter.2.cloned.1.call-start = ((), (), s32[]{:S(2)}) async-start(), calls=%async_computation.4 | async-start | bytes 3145728 | tf_op jit(solution)/shard_map/reduce_scatter | solution.py:131
  72.9 1.3 copy-start.1
  75.3 98.6 %copy-start.3 = (bf16[1,512,2048]{2,1,0:T(8,128)(2,1)S(1)}, bf16[1,512,2048]{2,1,0:T(8,128)(2,1)}, u32[]{:S(2)}) copy-start(bf16[1,512,2048]{2,1,0:T(8,128)(2,1)} %param.9) | copy-start | bytes 6291460
  180.9 2.5 copy-start
  196.6 7.9 %copy-start.5 = (bf16[64,8,8,128]{3,2,1,0:T(8,128)(2,1)}, bf16[64,8,8,128]{3,2,1,0:T(8,128)(2,1)S(1)}, u32[]{:S(2)}) copy-start(bf16[64,8,8,128]{3,2,1,0:T(8,128)(2,1)S(1)} %copy.82) | copy-start | bytes 3145732
  196.7 83.0 %collective-permute-start.2 = (bf16[1,512,1024]{2,1,0:T(8,128)(2,1)}, bf16[1,512,1024]{2,1,0:T(8,128)(2,1)}, u32[]{:S(2)}, u32[]{:S(2)}) collective-permute-start(bf16[1,512,1024]{2,1,0:T(8,128)(2,1)} %get-tuple-element.111), channel_id=1, source_target_pairs={{0,4},{4,8},{8,12},{1,5},{5,9},{9,13},{2,6},{6,10},{10,14},{3,7},{... | collective-permute-start | bytes 3145736 | tf_op jit(solution)/shard_map/ppermute | solution.py:14
  201.0 85.5 %collective-permute-start.3 = (bf16[1,512,1024]{2,1,0:T(8,128)(2,1)}, bf16[1,512,1024]{2,1,0:T(8,128)(2,1)}, u32[]{:S(2)}, u32[]{:S(2)}) collective-permute-start(bf16[1,512,1024]{2,1,0:T(8,128)(2,1)} %slice.31), channel_id=1, source_target_pairs={{0,4},{4,8},{8,12},{1,5},{5,9},{9,13},{2,6},{6,10},{10,14},{3,7},{... | collective-permute-start | bytes 3145736 | tf_op jit(solution)/shard_map/ppermute | solution.py:14
  206.9 43.7 %collective-permute-start = (bf16[1,8,128,128]{3,2,1,0:T(8,128)(2,1)}, bf16[1,8,128,128]{3,2,1,0:T(8,128)(2,1)S(1)}, u32[]{:S(2)}, u32[]{:S(2)}) collective-permute-start(bf16[1,8,128,128]{3,2,1,0:T(8,128)(2,1)} %fusion.58), channel_id=1, source_target_pairs={{0,4},{4,8},{8,12},{1,5},{5,9},{9,13},{2,6},{6,10},{10,14},{3,7},{... | collective-permute-start | bytes 786440 | tf_op jit(solution)/shard_map/while/body/eval_jaxpr/ppermute | solution.py:14
  209.3 41.3 %collective-permute-start.1 = (bf16[1,8]{1,0:T(2,128)(2,1)S(1)}, bf16[1,8]{1,0:T(2,128)(2,1)S(1)}, u32[]{:S(2)}, u32[]{:S(2)}) collective-permute-start(bf16[1,8]{1,0:T(2,128)(2,1)S(1)} %fusion.59), channel_id=1, source_target_pairs={{0,4},{4,8},{8,12},{1,5},{5,9},{9,13},{2,6},{6,10},{10,14},{3,7},{... | collective-permute-start | bytes 56 | tf_op jit(solution)/shard_map/while/body/eval_jaxpr/ppermute | solution.py:14
  251.5 9.1 %collective-permute-start = (bf16[1,8,128,128]{3,2,1,0:T(8,128)(2,1)}, bf16[1,8,128,128]{3,2,1,0:T(8,128)(2,1)S(1)}, u32[]{:S(2)}, u32[]{:S(2)}) collective-permute-start(bf16[1,8,128,128]{3,2,1,0:T(8,128)(2,1)} %fusion.58), channel_id=1, source_target_pairs={{0,4},{4,8},{8,12},{1,5},{5,9},{9,13},{2,6},{6,10},{10,14},{3,7},{... | collective-permute-start | bytes 786440 | tf_op jit(solution)/shard_map/while/body/eval_jaxpr/ppermute | solution.py:14
  255.9 4.7 %collective-permute-start.1 = (bf16[1,8]{1,0:T(2,128)(2,1)S(1)}, bf16[1,8]{1,0:T(2,128)(2,1)S(1)}, u32[]{:S(2)}, u32[]{:S(2)}) collective-permute-start(bf16[1,8]{1,0:T(2,128)(2,1)S(1)} %fusion.59), channel_id=1, source_target_pairs={{0,4},{4,8},{8,12},{1,5},{5,9},{9,13},{2,6},{6,10},{10,14},{3,7},{... | collective-permute-start | bytes 56 | tf_op jit(solution)/shard_map/while/body/eval_jaxpr/ppermute | solution.py:14
  261.4 9.0 %collective-permute-start = (bf16[1,8,128,128]{3,2,1,0:T(8,128)(2,1)}, bf16[1,8,128,128]{3,2,1,0:T(8,128)(2,1)S(1)}, u32[]{:S(2)}, u32[]{:S(2)}) collective-permute-start(bf16[1,8,128,128]{3,2,1,0:T(8,128)(2,1)} %fusion.58), channel_id=1, source_target_pairs={{0,4},{4,8},{8,12},{1,5},{5,9},{9,13},{2,6},{6,10},{10,14},{3,7},{... | collective-permute-start | bytes 786440 | tf_op jit(solution)/shard_map/while/body/eval_jaxpr/ppermute | solution.py:14
  265.8 4.7 %collective-permute-start.1 = (bf16[1,8]{1,0:T(2,128)(2,1)S(1)}, bf16[1,8]{1,0:T(2,128)(2,1)S(1)}, u32[]{:S(2)}, u32[]{:S(2)}) collective-permute-start(bf16[1,8]{1,0:T(2,128)(2,1)S(1)} %fusion.59), channel_id=1, source_target_pairs={{0,4},{4,8},{8,12},{1,5},{5,9},{9,13},{2,6},{6,10},{10,14},{3,7},{... | collective-permute-start | bytes 56 | tf_op jit(solution)/shard_map/while/body/eval_jaxpr/ppermute | solution.py:14
  270.5 3.7 %copy-start.7 = (bf16[512,8,128]{2,0,1:T(8,128)(2,1)S(1)}, bf16[512,8,128]{2,0,1:T(8,128)(2,1)}, u32[]{:S(2)}) copy-start(bf16[512,8,128]{2,0,1:T(8,128)(2,1)} %fusion.12) | copy-start | bytes 3145732
  270.5 3.7 %copy-start.9 = (pred[512,512]{0,1:T(8,128)(4,1)S(1)}, pred[512,512]{0,1:T(8,128)(4,1)}, u32[]{:S(2)}) copy-start(pred[512,512]{0,1:T(8,128)(4,1)} %iota_compare_fusion.1) | copy-start | bytes 786436
  279.7 1.5 copy-start.10
  286.5 1.6 copy-start.6
  288.1 4.9 %copy-start.8 = (f32[8,128,512]{2,1,0:T(8,128)S(1)}, f32[8,128,512]{2,1,0:T(8,128)}, u32[]{:S(2)}) copy-start(f32[8,128,512]{2,1,0:T(8,128)} %fusion.35) | copy-start | bytes 6291460
  288.1 6.5 %copy-start.13 = (f32[8,512,512]{1,2,0:T(8,128)S(1)}, f32[8,512,512]{1,2,0:T(8,128)}, u32[]{:S(2)}) copy-start(f32[8,512,512]{1,2,0:T(8,128)} %get-tuple-element.116) | copy-start | bytes 25165828
  303.0 10.5 %copy-start.4 = (bf16[1,512,2048]{2,1,0:T(8,128)(2,1)S(1)}, bf16[1,512,2048]{2,1,0:T(8,128)(2,1)}, u32[]{:S(2)}) copy-start(bf16[1,512,2048]{2,1,0:T(8,128)(2,1)} %param.9) | copy-start | bytes 6291460
Sparse Core Ops, SparseCore 0:
  8.9 59.4 all-gather.5
  69.9 103.9 all-gather.3
  175.5 56.7 all-gather.7
  303.2 10.3 reduce-scatter.1
where the time goes:
time: 323 us
  waiting for transfers between devices  199 us (62%)
  matrix products  40.5 us (13%)
  starting transfers between devices  27.7 us (9%)
  local copies, waits for them, and re-layouts  23 us (7%)
  other arithmetic  17.9 us (6%)
  between operations  14.1 us (4%)
    all_gather x1, waiting for transfers between devices, shards(): lax.all_gather(w_keyvalue, 'wloop', axis=0, tiled=True)  95.3 us
    all_gather x1, waiting for transfers between devices, shards(): lax.all_gather(w_query, 'wloop', axis=0, tiled=True)  50.1 us
    ppermute x8, waiting for transfers between devices, shifted(): lax.ppermute(value, axis, [(source, source + steps) for source in range(i...  42 us
    ppermute x8, starting transfers between devices, shifted(): lax.ppermute(value, axis, [(source, source + steps) for source in range(i...  27.6 us
    unnamed x34, local copies, waits for them, and re-layouts  14.3 us
    reduce_scatter x1, waiting for transfers between devices, shards(): lax.psum_scatter(partial_out.astype(jnp.bfloat16), 'heads', scatter_dimen...  10.5 us
    dot_general x1, matrix products, shards(): jnp.einsum('td,dje->jte', columns, lax.all_gather(w_keyvalue, 'wloop', ax...  6.94 us
  transfers between devices with their start and end apart: 12, of which 6 were waited for; matrix products, arithmetic and copies ran while one was open for 22% of the time, Pallas kernels for 0%

commit v1 on v0

--- a/solution.py
+++ b/solution.py
@@ -49,18 +49,41 @@
     count = trajs * span
     normed = (rms_rows(activations.astype(jnp.float32), 1e-05) * norm_gain).astype(jnp.bfloat16)
     normed = normed.reshape(count, width)
-    columns = normed
-    query_raw = jnp.dot(
-        columns,
-        lax.all_gather(w_query, "wloop", axis=0, tiled=True),
-        preferred_element_type=jnp.float32,
+    ways = lax.axis_size("wloop")
+    me = lax.axis_index("wloop")
+    block = width // ways
+
+    def feature_block(index):
+        return lax.dynamic_slice_in_dim(normed, index * block, block, 1)
+
+    stacked = [feature_block(me)]
+    for step in range(1, ways):
+        stacked.append(
+            lax.ppermute(
+                feature_block((me + step) % ways),
+                "wloop",
+                [(source, (source + step) % ways) for source in range(ways)],
+            )
+        )
+
+    def gathered_sum(partials):
+        total = partials[0]
+        for step in range(1, ways):
+            total = total + lax.ppermute(
+                partials[step].astype(jnp.bfloat16),
+                "wloop",
+                [(source, (source - step) % ways) for source in range(ways)],
+            ).astype(jnp.float32)
+        return total
+
+    pair_raw = gathered_sum(
+        [
+            jnp.einsum("td,dje->jte", rows, w_keyvalue, preferred_element_type=jnp.float32)
+            for rows in stacked
+        ]
     )
-    columns = normed
-    pair_raw = jnp.einsum(
-        "td,dje->jte",
-        columns,
-        lax.all_gather(w_keyvalue, "wloop", axis=0, tiled=True),
-        preferred_element_type=jnp.float32,
+    query_raw = gathered_sum(
+        [jnp.dot(rows, w_query, preferred_element_type=jnp.float32) for rows in stacked]
     )
     lookup_vectors = rms_rows(pair_raw[0].reshape(trajs, span, heads_here, head_dim), 1e-06).astype(
         jnp.bfloat16

time: 323 us -> 304 us (0.941)
  waiting for transfers between devices: 199 us -> 165 us
  matrix products: 40.5 us -> 47.8 us
  starting transfers between devices: 27.7 us -> 34.2 us
  other arithmetic: 17.9 us -> 23.4 us
  local copies, waits for them, and re-layouts: 23 us -> 18.5 us
    all_gather x2 -> x0, waiting for transfers between devices: 145 us -> none  [the longest x1 95.3 us: shards(): lax.all_gather(w_keyvalue, 'wloop', axis=0, tiled=True)]
    ppermute x0 -> x3, waiting for transfers between devices: none -> 113 us  [the longest x2 79.4 us: gathered_sum(): lax.ppermute(partials[step].astype(jnp.bfloat16), 'wloop', [(source, (sou...]
    unnamed x34 -> x27, local copies, waits for them, and re-layouts: 14.3 us -> 8.09 us
    ppermute x0 -> x3, starting transfers between devices: none -> 5.63 us  [the longest x1 3.03 us: shards(): lax.ppermute(feature_block((me + step) % ways), 'wloop', [(source, (sourc...]
    dot_general x2 -> x4, matrix products: 11.5 us -> 16.7 us  [the longest x2 10.7 us: shards(): jnp.einsum('td,dje->jte', rows, w_keyvalue, preferred_element_type=jnp.fl...]
    add x0 -> x1, other arithmetic: none -> 3.55 us  [gathered_sum(): total + lax.ppermute(partials[step].astype(jnp.bfloat16), 'wloop', [(sour...]
    reduce_sum x3, other arithmetic: 1.7 us -> 5.06 us  [rms_rows(): jnp.mean(values * values, axis=-1, keepdims=True) + eps]
  transfers between devices with their start and end apart: 12 -> 13, of which waited for: 6 -> 6; matrix products, arithmetic and copies ran while one was open for 22% -> 24% of each run, Pallas kernels for 0% -> 0%
where the time goes in v1:
time: 304 us; the launch traced here: 303 us
  waiting for transfers between devices  165 us (54%)
  matrix products  47.8 us (16%)
  starting transfers between devices  34.2 us (11%)
  other arithmetic  23.4 us (8%)
  local copies, waits for them, and re-layouts  18.5 us (6%)
  between operations  14.4 us (5%)
    ppermute x2, waiting for transfers between devices, gathered_sum(): lax.ppermute(partials[step].astype(jnp.bfloat16), 'wloop', [(source, (sou...  79.4 us
    ppermute x8, waiting for transfers between devices, shifted(): lax.ppermute(value, axis, [(source, source + steps) for source in range(i...  41.7 us
    ppermute x1, waiting for transfers between devices, shards(): lax.ppermute(feature_block((me + step) % ways), 'wloop', [(source, (sourc...  33.5 us
    ppermute x8, starting transfers between devices, shifted(): lax.ppermute(value, axis, [(source, source + steps) for source in range(i...  28.5 us
    dot_general x2, matrix products, shards(): jnp.einsum('td,dje->jte', rows, w_keyvalue, preferred_element_type=jnp.fl...  10.7 us
    reduce_scatter x1, waiting for transfers between devices, shards(): lax.psum_scatter(partial_out.astype(jnp.bfloat16), 'heads', scatter_dimen...  10.4 us
    unnamed x27, local copies, waits for them, and re-layouts  8.09 us
    dot_general x1, matrix products, window_mix(): jnp.einsum('bihd,bjhd->bhij', queries, lookup_vectors, preferred_element_...  7.38 us
  transfers between devices with their start and end apart: 13, of which 6 were waited for; matrix products, arithmetic and copies ran while one was open for 24% of the time, Pallas kernels for 0%

profile of v1, /device:TPU:0, one launch (start us, length us, event | category | flops | bytes accessed | tf_op | source)
XLA Modules:
  0.0 303.4 jit_solution(10530522084903715507)
XLA Ops:
  6.5 2.2 fusion.7
  8.8 2.1 fusion.9
  12.4 3.0 collective-permute-start.2
  18.0 33.5 %collective-permute-done.2 = bf16[512,1024]{1,0:T(8,128)(2,1)} collective-permute-done((bf16[512,1024]{1,0:T(8,128)(2,1)S(1)}, bf16[512,1024]{1,0:T(8,128)(2,1)}, u32[]{:S(2)}, u32[]{:S(2)}) %collective-permute-start.2) | collective-permute-done | bytes 1048608 | tf_op jit(solution)/shard_map/ppermute | solution.py:62
  51.5 6.3 %convert_bitcast_fusion = bf16[2,512,1024]{2,1,0:T(8,128)(2,1)} fusion(bf16[1024,2,1024]{2,1,0:T(2,128)(2,1)} %param.12, bf16[512,1024]{1,0:T(8,128)(2,1)} %collective-permute-done.2), kind=kOutput, calls=%fused_computation.43 | convolution fusion | flops 2148532224 | bytes 7340032 | tf_op jit(solution)/shard_map/td,dje->jte/dot_general | solution.py:81
  57.8 2.6 collective-permute-start.3
  60.4 3.4 %convolution_convert_fusion.1 = bf16[512,1024]{1,0:T(8,128)(2,1)} fusion(bf16[512,1024]{1,0:T(8,128)(2,1)} %collective-permute-done.2, bf16[1024,1024]{1,0:T(8,128)(2,1)S(1)} %copy-done), kind=kOutput, calls=%fused_computation.44 | convolution fusion | flops 1074266112 | bytes 4194304 | tf_op jit(solution)/shard_map/dot_general | solution.py:86
  64.1 2.6 fusion.33
  67.3 4.4 %fusion.14 = f32[512,2,1024]{2,0,1:T(8,128)} fusion(bf16[1024,2,1024]{2,1,0:T(2,128)(2,1)S(1)} %copy-done.10, bf16[1,512,2048]{2,1,0:T(8,128)(2,1)S(1)} %copy-done.5, s32[]{:T(128)S(6)} %select_n.27), kind=kOutput, calls=%fused_computation.23 | convolution fusion | flops 2147483648 | bytes 9437188 | tf_op jit(solution)/shard_map/td,dje->jte/dot_general | solution.py:81
  71.6 79.4 %collective-permute-done.4 = bf16[512,1024]{1,0:T(8,128)(2,1)} collective-permute-done((bf16[512,1024]{1,0:T(8,128)(2,1)}, bf16[512,1024]{1,0:T(8,128)(2,1)}, u32[]{:S(2)}, u32[]{:S(2)}) %collective-permute-start.4) | collective-permute-done | bytes 1048608 | tf_op jit(solution)/shard_map/ppermute | solution.py:72
  154.6 2.2 reduce_sum.57
  158.4 3.6 %bitcast_add_fusion = f32[2,512,1024]{2,1,0:T(8,128)S(1)} fusion(f32[512,2,1024]{2,0,1:T(8,128)} %fusion.14, bf16[2,512,1024]{2,1,0:T(8,128)(2,1)} %collective-permute-done.3), kind=kLoop, calls=%fused_computation.18 | loop fusion | flops 2097152 | bytes 10485760 | tf_op jit(solution)/shard_map/add | solution.py:72
  168.2 1.9 copy.84
  170.1 3.9 %multiply_convert_fusion = (bf16[1,512,1024]{2,1,0:T(8,128)(2,1)}, f32[1,512,1024]{2,1,0:T(8,128)}) fusion(f32[1,512,1024]{2,1,0:T(8,128)S(1)} %copy.84, f32[2,512,1024]{2,1,0:T(8,128)} %copy-done.2), kind=kLoop, calls=%fused_computation.38 | loop fusion | flops 1048576 | bytes 7340032 | tf_op jit(solution)/shard_map/convert_element_type | solution.py:88
  174.0 3.0 %copy.83 = f32[1,512,1024]{1,2,0:T(8,128)} copy(f32[1,512,1024]{2,1,0:T(8,128)} %get-tuple-element.112) | data formatting | bytes 4194304 | tf_op jit(solution)/shard_map/reshape;squeeze | solution.py:88
  177.3 4.8 %collective-permute-start.5 = (bf16[1,512,1024]{2,1,0:T(8,128)(2,1)}, bf16[1,512,1024]{2,1,0:T(8,128)(2,1)}, u32[]{:S(2)}, u32[]{:S(2)}) collective-permute-start(bf16[1,512,1024]{2,1,0:T(8,128)(2,1)} %get-tuple-element.111), channel_id=1, source_target_pairs={{0,4},{4,8},{8,12},{1,5},{5,9},{9,13},{2,6},{6,10},{10,14},{3,7},{... | collective-permute-start | bytes 3145736 | tf_op jit(solution)/shard_map/ppermute | solution.py:14
  182.2 3.5 %collective-permute-start.6 = (bf16[1,512,1024]{2,1,0:T(8,128)(2,1)}, bf16[1,512,1024]{2,1,0:T(8,128)(2,1)}, u32[]{:S(2)}, u32[]{:S(2)}) collective-permute-start(bf16[1,512,1024]{2,1,0:T(8,128)(2,1)} %slice.31), channel_id=1, source_target_pairs={{0,4},{4,8},{8,12},{1,5},{5,9},{9,13},{2,6},{6,10},{10,14},{3,7},{... | collective-permute-start | bytes 3145736 | tf_op jit(solution)/shard_map/ppermute | solution.py:14
  187.1 62.5 %while.14 = (s32[]{:T(128)}, f32[1,8,128,128]{3,2,1,0:T(8,128)S(1)}, f32[1,8]{1,0:T(1,128)S(1)}, f32[1,8]{1,0:T(1,128)S(1)}, f32[1,8,128,128]{3,2,1,0:T(8,128)S(...) while((s32[]{:T(128)}, f32[1,8,128,128]{3,2,1,0:T(8,128)S(1)}, ...), condition=%wide.region_9.10_spmd.clone, body=%wide.region_8.9_spmd.clone.sunk | while | flops 655403 | bytes 3146168 | solution.py:125
  187.2 2.7 collective-permute-start
  191.9 39.1 %collective-permute-done.1 = bf16[1,8]{1,0:T(2,128)(2,1)S(1)} collective-permute-done((bf16[1,8]{1,0:T(2,128)(2,1)S(1)}, bf16[1,8]{1,0:T(2,128)(2,1)S(1)}, u32[]{:S(2)}, u32[]{:S(2)}) %collective-permute-start.1) | collective-permute-done | bytes 48 | tf_op jit(solution)/shard_map/while/body/eval_jaxpr/ppermute | solution.py:14
  231.1 4.5 %collective-permute-start = (bf16[1,8,128,128]{3,2,1,0:T(8,128)(2,1)S(1)}, bf16[1,8,128,128]{3,2,1,0:T(8,128)(2,1)S(1)}, u32[]{:S(2)}, u32[]{:S(2)}) collective-permute-start(bf16[1,8,128,128]{3,2,1,0:T(8,128)(2,1)S(1)} %fusion.67), channel_id=1, source_target_pairs={{0,4},{4,8},{8,12},{1,5},{5,9},{9,13},{2,6},{6,10},{10,14},{3,7},{... | collective-permute-start | bytes 786440 | tf_op jit(solution)/shard_map/while/body/eval_jaxpr/ppermute | solution.py:14
  235.6 3.5 %collective-permute-start.1 = (bf16[1,8]{1,0:T(2,128)(2,1)S(1)}, bf16[1,8]{1,0:T(2,128)(2,1)S(1)}, u32[]{:S(2)}, u32[]{:S(2)}) collective-permute-start(bf16[1,8]{1,0:T(2,128)(2,1)S(1)} %fusion.68), channel_id=1, source_target_pairs={{0,4},{4,8},{8,12},{1,5},{5,9},{9,13},{2,6},{6,10},{10,14},{3,7},{... | collective-permute-start | bytes 56 | tf_op jit(solution)/shard_map/while/body/eval_jaxpr/ppermute | solution.py:14
  240.6 4.2 %collective-permute-start = (bf16[1,8,128,128]{3,2,1,0:T(8,128)(2,1)S(1)}, bf16[1,8,128,128]{3,2,1,0:T(8,128)(2,1)S(1)}, u32[]{:S(2)}, u32[]{:S(2)}) collective-permute-start(bf16[1,8,128,128]{3,2,1,0:T(8,128)(2,1)S(1)} %fusion.67), channel_id=1, source_target_pairs={{0,4},{4,8},{8,12},{1,5},{5,9},{9,13},{2,6},{6,10},{10,14},{3,7},{... | collective-permute-start | bytes 786440 | tf_op jit(solution)/shard_map/while/body/eval_jaxpr/ppermute | solution.py:14
  244.8 3.5 %collective-permute-start.1 = (bf16[1,8]{1,0:T(2,128)(2,1)S(1)}, bf16[1,8]{1,0:T(2,128)(2,1)S(1)}, u32[]{:S(2)}, u32[]{:S(2)}) collective-permute-start(bf16[1,8]{1,0:T(2,128)(2,1)S(1)} %fusion.68), channel_id=1, source_target_pairs={{0,4},{4,8},{8,12},{1,5},{5,9},{9,13},{2,6},{6,10},{10,14},{3,7},{... | collective-permute-start | bytes 56 | tf_op jit(solution)/shard_map/while/body/eval_jaxpr/ppermute | solution.py:14
  249.6 7.4 %fusion.5 = (f32[8,512]{1,0:T(8,128)S(1)}, f32[8,512,512]{1,2,0:T(8,128)}) fusion(pred[512,512]{0,1:T(8,128)(4,1)S(1)} %iota_compare_fusion.1, bf16[512,8,128]{2,0,1:T(8,128)(2,1)} %fusion.16, f32[512,8,128]{0,2,1:T(8,128)} %bitcast.110, f32[512,8]{0,1:T(8,128)S(1)} %add_rsqrt_fusion), kind=kOutput, calls=%fused_computation.11 | convolution fusion | flops 544206848 | bytes 11829248 | tf_op jit(solution)/shard_map/bihd,bjhd->bhij/dot_general | solution.py:23
  258.6 5.2 %fusion.6 = (f32[8,512]{1,0:T(8,128)S(1)}, f32[8,512,512]{1,2,0:T(8,128)}) fusion(pred[512,512]{0,1:T(8,128)(4,1)S(1)} %fusion.38, bf16[512,8,128]{2,0,1:T(8,128)(2,1)S(1)} %copy-done.7, bf16[512,8,128]{2,1,0:T(8,128)(2,1)S(1)} %bitcast.118), kind=kOutput, calls=%fused_computation.12 | convolution fusion | flops 543158272 | bytes 10764288 | tf_op jit(solution)/shard_map/bihd,bjhd->bhij/dot_general | solution.py:27
  263.8 2.3 copy.85
  266.1 4.9 %fusion.11 = f32[8,128,512]{2,1,0:T(8,128)S(1)} fusion(bf16[512,8,128]{0,2,1:T(8,128)(2,1)} %bitcast.117, f32[8,512,512]{1,2,0:T(8,128)} %get-tuple-element.118, f32[8,512]{1,0:T(8,128)S(1)} %add.100, pred[512,512]{0,1:T(8,128)(4,1)S(1)} %fusion.38), kind=kOutput, calls=%fused_computation.20 | convolution fusion | flops 545259520 | bytes 11812864 | tf_op jit(solution)/shard_map/bhij,bjhd->bihd/dot_general | solution.py:40
  271.1 4.7 %fusion.10 = f32[8,128,512]{2,1,0:T(8,128)S(1)} fusion(f32[8,512,512]{1,2,0:T(8,128)} %get-tuple-element.116, f32[8,512]{1,0:T(8,128)S(1)} %add.100, pred[512,512]{0,1:T(8,128)(4,1)S(1)} %iota_compare_fusion.1, bf16[512,8,128]{2,1,0:T(8,128)(2,1)S(1)} %bitcast.116), kind=kOutput, calls=%fused_computation.19 | convolution fusion | flops 545259520 | bytes 11812864 | tf_op jit(solution)/shard_map/bhij,bjhd->bihd/dot_general | solution.py:38
  277.3 5.9 %convolution_convert_fusion = bf16[512,2048]{1,0:T(8,128)(2,1)} fusion(bf16[512,1024]{0,1:T(8,128)(2,1)S(1)} %bitcast.124, bf16[1024,2048]{1,0:T(8,128)(2,1)} %all-gather.2.cloned.1.call-done), kind=kOutput, calls=%fused_computation.25 | convolution fusion | flops 2148532224 | bytes 7340032 | tf_op jit(solution)/shard_map/dot_general | solution.py:149
  283.3 10.4 %reduce-scatter.2.cloned.1.call-done = bf16[512,1024]{1,0:T(8,128)(2,1)} async-done(((bf16[512,2048]{1,0:T(8,128)(2,1)}), bf16[512,1024]{1,0:T(8,128)(2,1)}) %reduce-scatter.2.cloned.1.call-update) | async-done | bytes 1048592 | tf_op jit(solution)/shard_map/reduce_scatter | solution.py:154
  293.6 2.9 fusion.30
  (83 shorter events, 25.1 us)
Async XLA Ops:
  6.5 53.8 %copy-start = (bf16[1024,1024]{1,0:T(8,128)(2,1)S(1)}, bf16[1024,1024]{1,0:T(8,128)(2,1)}, u32[]{:S(2)}) copy-start(bf16[1024,1024]{1,0:T(8,128)(2,1)} %param.11) | copy-start | bytes 6291460
  6.5 2.3 copy-start.9
  6.5 270.8 %all-gather.2.cloned.1.call-start = ((), (), s32[]{:S(2)}) async-start(), calls=%async_computation.1 | async-start | bytes 6291456 | tf_op jit(solution)/shard_map/all_gather | solution.py:151
  10.9 1.4 copy-start.4
  12.3 3.2 %copy-start.8 = (f32[1,8,512]{2,1,0:T(8,128)S(1)}, f32[1,8,512]{2,1,0:T(8,128)}, u32[]{:S(2)}) copy-start(f32[1,8,512]{2,1,0:T(8,128)} %param.14) | copy-start | bytes 49156
  12.4 39.1 %collective-permute-start.2 = (bf16[512,1024]{1,0:T(8,128)(2,1)S(1)}, bf16[512,1024]{1,0:T(8,128)(2,1)}, u32[]{:S(2)}, u32[]{:S(2)}) collective-permute-start(bf16[512,1024]{1,0:T(8,128)(2,1)S(1)} %dynamic-slice_bitcast_fusion), channel_id=1, source_target_pairs={{0,2},{2,0},{1,3},{3,1},{4,6},{6,4},{5,7},{7,5},{8,10},{10,8},{9,1... | collective-permute-start | bytes 3145736 | tf_op jit(solution)/shard_map/ppermute | solution.py:62
  15.4 278.2 %reduce-scatter.2.cloned.1.call-start = ((), (), s32[]{:S(2)}) async-start(), calls=%async_computation.2 | async-start | bytes 3145728 | tf_op jit(solution)/shard_map/reduce_scatter | solution.py:154
  57.8 100.7 %collective-permute-start.3 = (bf16[2,512,1024]{2,1,0:T(8,128)(2,1)}, bf16[2,512,1024]{2,1,0:T(8,128)(2,1)}, u32[]{:S(2)}, u32[]{:S(2)}) collective-permute-start(bf16[2,512,1024]{2,1,0:T(8,128)(2,1)} %convert_bitcast_fusion), channel_id=1, source_target_pairs={{0,2},{2,0},{1,3},{3,1},{4,6},{6,4},{5,7},{7,5},{8,10},{10,8},{9,1... | collective-permute-start | bytes 6291464 | tf_op jit(solution)/shard_map/ppermute | solution.py:72
  63.8 87.2 %collective-permute-start.4 = (bf16[512,1024]{1,0:T(8,128)(2,1)}, bf16[512,1024]{1,0:T(8,128)(2,1)}, u32[]{:S(2)}, u32[]{:S(2)}) collective-permute-start(bf16[512,1024]{1,0:T(8,128)(2,1)} %convolution_convert_fusion.1), channel_id=1, source_target_pairs={{0,2},{2,0},{1,3},{3,1},{4,6},{6,4},{5,7},{7,5},{8,10},{10,8},{9,1... | collective-permute-start | bytes 3145736 | tf_op jit(solution)/shard_map/ppermute | solution.py:72
  64.1 2.7 copy-start.5
  64.1 3.1 %copy-start.10 = (bf16[1024,2,1024]{2,1,0:T(2,128)(2,1)S(1)}, bf16[1024,2,1024]{2,1,0:T(2,128)(2,1)}, u32[]{:S(2)}) copy-start(bf16[1024,2,1024]{2,1,0:T(2,128)(2,1)} %param.12) | copy-start | bytes 12582916
  162.0 2.3 copy-start.2
  174.0 3.0 %copy-start.6 = (bf16[64,8,8,128]{3,1,2,0:T(8,128)(2,1)S(1)}, bf16[64,8,8,128]{3,1,2,0:T(8,128)(2,1)}, u32[]{:S(2)}) copy-start(bf16[64,8,8,128]{3,1,2,0:T(8,128)(2,1)} %slice_bitcast_fusion.1) | copy-start | bytes 3145732
  177.1 8.7 %copy-start.3 = (f32[1,512,1024]{1,2,0:T(8,128)S(1)}, f32[1,512,1024]{1,2,0:T(8,128)}, u32[]{:S(2)}) copy-start(f32[1,512,1024]{1,2,0:T(8,128)} %copy.83) | copy-start | bytes 6291460
  177.3 79.7 %collective-permute-start.5 = (bf16[1,512,1024]{2,1,0:T(8,128)(2,1)}, bf16[1,512,1024]{2,1,0:T(8,128)(2,1)}, u32[]{:S(2)}, u32[]{:S(2)}) collective-permute-start(bf16[1,512,1024]{2,1,0:T(8,128)(2,1)} %get-tuple-element.111), channel_id=1, source_target_pairs={{0,4},{4,8},{8,12},{1,5},{5,9},{9,13},{2,6},{6,10},{10,14},{3,7},{... | collective-permute-start | bytes 3145736 | tf_op jit(solution)/shard_map/ppermute | solution.py:14
  182.2 81.7 %collective-permute-start.6 = (bf16[1,512,1024]{2,1,0:T(8,128)(2,1)}, bf16[1,512,1024]{2,1,0:T(8,128)(2,1)}, u32[]{:S(2)}, u32[]{:S(2)}) collective-permute-start(bf16[1,512,1024]{2,1,0:T(8,128)(2,1)} %slice.31), channel_id=1, source_target_pairs={{0,4},{4,8},{8,12},{1,5},{5,9},{9,13},{2,6},{6,10},{10,14},{3,7},{... | collective-permute-start | bytes 3145736 | tf_op jit(solution)/shard_map/ppermute | solution.py:14
  187.2 43.7 %collective-permute-start = (bf16[1,8,128,128]{3,2,1,0:T(8,128)(2,1)S(1)}, bf16[1,8,128,128]{3,2,1,0:T(8,128)(2,1)S(1)}, u32[]{:S(2)}, u32[]{:S(2)}) collective-permute-start(bf16[1,8,128,128]{3,2,1,0:T(8,128)(2,1)S(1)} %fusion.67), channel_id=1, source_target_pairs={{0,4},{4,8},{8,12},{1,5},{5,9},{9,13},{2,6},{6,10},{10,14},{3,7},{... | collective-permute-start | bytes 786440 | tf_op jit(solution)/shard_map/while/body/eval_jaxpr/ppermute | solution.py:14
  189.9 41.0 %collective-permute-start.1 = (bf16[1,8]{1,0:T(2,128)(2,1)S(1)}, bf16[1,8]{1,0:T(2,128)(2,1)S(1)}, u32[]{:S(2)}, u32[]{:S(2)}) collective-permute-start(bf16[1,8]{1,0:T(2,128)(2,1)S(1)} %fusion.68), channel_id=1, source_target_pairs={{0,4},{4,8},{8,12},{1,5},{5,9},{9,13},{2,6},{6,10},{10,14},{3,7},{... | collective-permute-start | bytes 56 | tf_op jit(solution)/shard_map/while/body/eval_jaxpr/ppermute | solution.py:14
  231.1 9.2 %collective-permute-start = (bf16[1,8,128,128]{3,2,1,0:T(8,128)(2,1)S(1)}, bf16[1,8,128,128]{3,2,1,0:T(8,128)(2,1)S(1)}, u32[]{:S(2)}, u32[]{:S(2)}) collective-permute-start(bf16[1,8,128,128]{3,2,1,0:T(8,128)(2,1)S(1)} %fusion.67), channel_id=1, source_target_pairs={{0,4},{4,8},{8,12},{1,5},{5,9},{9,13},{2,6},{6,10},{10,14},{3,7},{... | collective-permute-start | bytes 786440 | tf_op jit(solution)/shard_map/while/body/eval_jaxpr/ppermute | solution.py:14
  235.6 4.8 %collective-permute-start.1 = (bf16[1,8]{1,0:T(2,128)(2,1)S(1)}, bf16[1,8]{1,0:T(2,128)(2,1)S(1)}, u32[]{:S(2)}, u32[]{:S(2)}) collective-permute-start(bf16[1,8]{1,0:T(2,128)(2,1)S(1)} %fusion.68), channel_id=1, source_target_pairs={{0,4},{4,8},{8,12},{1,5},{5,9},{9,13},{2,6},{6,10},{10,14},{3,7},{... | collective-permute-start | bytes 56 | tf_op jit(solution)/shard_map/while/body/eval_jaxpr/ppermute | solution.py:14
  240.6 9.0 %collective-permute-start = (bf16[1,8,128,128]{3,2,1,0:T(8,128)(2,1)S(1)}, bf16[1,8,128,128]{3,2,1,0:T(8,128)(2,1)S(1)}, u32[]{:S(2)}, u32[]{:S(2)}) collective-permute-start(bf16[1,8,128,128]{3,2,1,0:T(8,128)(2,1)S(1)} %fusion.67), channel_id=1, source_target_pairs={{0,4},{4,8},{8,12},{1,5},{5,9},{9,13},{2,6},{6,10},{10,14},{3,7},{... | collective-permute-start | bytes 786440 | tf_op jit(solution)/shard_map/while/body/eval_jaxpr/ppermute | solution.py:14
  244.8 4.8 %collective-permute-start.1 = (bf16[1,8]{1,0:T(2,128)(2,1)S(1)}, bf16[1,8]{1,0:T(2,128)(2,1)S(1)}, u32[]{:S(2)}, u32[]{:S(2)}) collective-permute-start(bf16[1,8]{1,0:T(2,128)(2,1)S(1)} %fusion.68), channel_id=1, source_target_pairs={{0,4},{4,8},{8,12},{1,5},{5,9},{9,13},{2,6},{6,10},{10,14},{3,7},{... | collective-permute-start | bytes 56 | tf_op jit(solution)/shard_map/while/body/eval_jaxpr/ppermute | solution.py:14
  257.0 1.6 copy-start.7
  283.3 13.3 %copy-start.1 = (bf16[1024,1024]{1,0:T(8,128)(2,1)S(1)}, bf16[1024,1024]{1,0:T(8,128)(2,1)}, u32[]{:S(2)}) copy-start(bf16[1024,1024]{1,0:T(8,128)(2,1)} %param.11) | copy-start | bytes 6291460
Sparse Core Ops, SparseCore 0:
  15.6 92.1 all-gather.1
  283.4 10.2 reduce-scatter.1

commit v2 on v1

--- a/solution.py
+++ b/solution.py
@@ -56,13 +56,29 @@
     def feature_block(index):
         return lax.dynamic_slice_in_dim(normed, index * block, block, 1)
 
+    cores = lax.axis_size("heads")
+    core = lax.axis_index("heads")
+    share_rows = count // cores
+
+    def from_cores(part):
+        pieces = [part]
+        for step in range(1, cores):
+            pieces.append(
+                lax.ppermute(part, "heads", [(source, (source + step) % cores) for source in range(cores)])
+            )
+        order = (core - jnp.arange(cores)) % cores
+        return jnp.take(jnp.stack(pieces), order, axis=0).reshape(count, block)
+
     stacked = [feature_block(me)]
     for step in range(1, ways):
+        part = lax.dynamic_slice_in_dim(feature_block((me + step) % ways), core * share_rows, share_rows, 0)
         stacked.append(
-            lax.ppermute(
-                feature_block((me + step) % ways),
-                "wloop",
-                [(source, (source + step) % ways) for source in range(ways)],
+            from_cores(
+                lax.ppermute(
+                    part,
+                    "wloop",
+                    [(source, (source + step) % ways) for source in range(ways)],
+                )
             )
         )
 
@@ -146,6 +162,7 @@
         scale,
     )
     attended = (window + read).astype(jnp.bfloat16).reshape(count, inner_here)
+    w_output = lax.optimization_barrier((w_output, query_raw))[0]
     partial_out = jnp.dot(
         attended,
         lax.all_gather(w_output, "wloop", axis=1, tiled=True),

time: 304 us -> 269 us (0.88)
  waiting for transfers between devices: 165 us -> 135 us
  other arithmetic: 23.4 us -> 18.9 us
    ppermute x1 -> x2, waiting for transfers between devices: 33.5 us -> 11.6 us  [the longest x1 9.81 us: shards(): lax.ppermute(part, 'wloop', [(source, (source + step) % ways) for source...]
    ppermute x8, waiting for transfers between devices: 41.7 us -> 29.3 us  [shifted(): lax.ppermute(value, axis, [(source, source + steps) for source in range(i...]
    add x1 -> x0, other arithmetic: 3.55 us -> none  [gathered_sum(): total + lax.ppermute(partials[step].astype(jnp.bfloat16), 'wloop', [(sour...]
    unnamed x27 -> x29, local copies, waits for them, and re-layouts: 8.09 us -> 6.92 us
  transfers between devices with their start and end apart: 13 -> 14, of which waited for: 6 -> 8; matrix products, arithmetic and copies ran while one was open for 24% -> 23% of each run, Pallas kernels for 0% -> 0%
where the time goes in v2:
time: 269 us; the launch traced here: 268 us
  waiting for transfers between devices  135 us (50%)
  matrix products  48.3 us (18%)
  starting transfers between devices  33.6 us (12%)
  other arithmetic  18.9 us (7%)
  local copies, waits for them, and re-layouts  18.1 us (7%)
  between operations  14.4 us (5%)
    ppermute x2, waiting for transfers between devices, gathered_sum(): lax.ppermute(partials[step].astype(jnp.bfloat16), 'wloop', [(source, (sou...  82.2 us
    ppermute x8, waiting for transfers between devices, shifted(): lax.ppermute(value, axis, [(source, source + steps) for source in range(i...  29.3 us
    ppermute x8, starting transfers between devices, shifted(): lax.ppermute(value, axis, [(source, source + steps) for source in range(i...  28.5 us
    reduce_scatter x1, waiting for transfers between devices, shards(): lax.psum_scatter(partial_out.astype(jnp.bfloat16), 'heads', scatter_dimen...  11.4 us
    ppermute x1, waiting for transfers between devices, shards(): lax.ppermute(part, 'wloop', [(source, (source + step) % ways) for source...  9.81 us
    dot_general x2, matrix products, shards(): jnp.einsum('td,dje->jte', rows, w_keyvalue, preferred_element_type=jnp.fl...  9.11 us
    dot_general x1, matrix products, window_mix(): jnp.einsum('bihd,bjhd->bhij', queries, lookup_vectors, preferred_element_...  7.05 us
    unnamed x29, local copies, waits for them, and re-layouts  6.92 us
  transfers between devices with their start and end apart: 14, of which 8 were waited for; matrix products, arithmetic and copies ran while one was open for 23% of the time, Pallas kernels for 0%

profile of v2, /device:TPU:0, one launch (start us, length us, event | category | flops | bytes accessed | tf_op | source)
XLA Modules:
  0.0 268.0 jit_solution(1861057485975101954)
XLA Ops:
  6.5 2.2 fusion.7
  11.1 3.0 %collective-permute-start.2 = (bf16[256,1024]{1,0:T(8,128)(2,1)S(1)}, bf16[256,1024]{1,0:T(8,128)(2,1)S(1)}, u32[]{:S(2)}, u32[]{:S(2)}) collective-permute-start(bf16[256,1024]{1,0:T(8,128)(2,1)S(1)} %dynamic-slice_bitcast_fusion), channel_id=1, source_target_pairs={{0,2},{2,0},{1,3},{3,1},{4,6},{6,4},{5,7},{7,5},{8,10},{10,8},{9,1... | collective-permute-start | bytes 1572872 | tf_op jit(solution)/shard_map/ppermute | solution.py:77
  16.3 9.8 %collective-permute-done.2 = bf16[256,1024]{1,0:T(8,128)(2,1)S(1)} collective-permute-done((bf16[256,1024]{1,0:T(8,128)(2,1)S(1)}, bf16[256,1024]{1,0:T(8,128)(2,1)S(1)}, u32[]{:S(2)}, u32[]{:S(2)}) %collective-permute-start.2) | collective-permute-done | bytes 524320 | tf_op jit(solution)/shard_map/ppermute | solution.py:77
  29.0 2.8 %gather_fusion = bf16[2,256,1024]{2,1,0:T(8,128)(2,1)} fusion(bf16[2,256,1024]{2,1,0:T(8,128)(2,1)} %pad_maximum_fusion, s32[1024]{0:T(1024)S(1)} %pad_clamp_fusion), kind=kCustom, calls=%fused_computation | custom fusion | bytes 2097160 | tf_op jit(solution)/shard_map/jit(_take)/gather | solution.py:70
  33.3 2.2 convolution_convert_fusion.1
  37.3 3.8 %convert_bitcast_fusion = bf16[2,512,1024]{2,1,0:T(8,128)(2,1)} fusion(bf16[1024,2,1024]{2,1,0:T(2,128)(2,1)S(1)} %copy-done.11, bf16[512,1024]{1,0:T(8,128)(2,1)S(1)} %bitcast_select_fusion), kind=kOutput, calls=%fused_computation.44 | convolution fusion | flops 2148532224 | bytes 7340032 | tf_op jit(solution)/shard_map/td,dje->jte/dot_general | solution.py:97
  42.0 19.9 %collective-permute-done.5 = bf16[512,1024]{1,0:T(8,128)(2,1)} collective-permute-done((bf16[512,1024]{1,0:T(8,128)(2,1)}, bf16[512,1024]{1,0:T(8,128)(2,1)}, u32[]{:S(2)}, u32[]{:S(2)}) %collective-permute-start.5) | collective-permute-done | bytes 1048608 | tf_op jit(solution)/shard_map/ppermute | solution.py:88
  61.9 4.1 %convert_add_fusion.1 = f32[512,1024]{1,0:T(8,128)} fusion(bf16[512,1024]{1,0:T(8,128)(2,1)} %collective-permute-done.5, bf16[1024,1024]{1,0:T(8,128)(2,1)S(1)} %copy-done, bf16[1,512,2048]{2,1,0:T(8,128)(2,1)} %copy-done.6, s32[]{:T(128)S(6)} %select_n.72), kind=kOutput, calls=%fused_computation.43 | convolution fusion | flops 1074790400 | bytes 6291460 | tf_op jit(solution)/shard_map/dot_general | solution.py:102
  69.0 2.8 %fusion.16 = bf16[512,8,128]{2,0,1:T(8,128)(2,1)} fusion(f32[512,8]{0,1:T(8,128)S(1)} %add_rsqrt_fusion.1, f32[512,1024]{1,0:T(8,128)} %convert_add_fusion.1), kind=kLoop, calls=%fused_computation.28 | loop fusion | flops 1048576 | bytes 3162112 | tf_op jit(solution)/shard_map/convert_element_type | solution.py:113
  71.8 62.3 %collective-permute-done.4 = bf16[2,512,1024]{2,1,0:T(8,128)(2,1)} collective-permute-done((bf16[2,512,1024]{2,1,0:T(8,128)(2,1)}, bf16[2,512,1024]{2,1,0:T(8,128)(2,1)}, u32[]{:S(2)}, u32[]{:S(2)}) %collective-permute-start.4) | collective-permute-done | bytes 2097184 | tf_op jit(solution)/shard_map/ppermute | solution.py:88
  134.1 5.3 %bitcast_add_fusion = f32[2,512,1024]{2,1,0:T(8,128)S(1)} fusion(bf16[2,512,1024]{2,1,0:T(8,128)(2,1)} %collective-permute-done.4, bf16[1024,2,1024]{2,1,0:T(2,128)(2,1)} %param.12, bf16[1,512,2048]{2,1,0:T(8,128)(2,1)S(1)} %copy-done.7, s32[]{:T(128)S(6)} %select_n.72), kind=kOutput, calls=%fused_computation.19 | convolution fusion | flops 2149580800 | bytes 11534340 | tf_op jit(solution)/shard_map/td,dje->jte/dot_general | solution.py:97
  142.6 4.4 %collective-permute-start.7 = (bf16[1,512,1024]{2,1,0:T(8,128)(2,1)}, bf16[1,512,1024]{2,1,0:T(8,128)(2,1)}, u32[]{:S(2)}, u32[]{:S(2)}) collective-permute-start(bf16[1,512,1024]{2,1,0:T(8,128)(2,1)} %slice.33), channel_id=1, source_target_pairs={{0,4},{4,8},{8,12},{1,5},{5,9},{9,13},{2,6},{6,10},{10,14},{3,7},{... | collective-permute-start | bytes 3145736 | tf_op jit(solution)/shard_map/ppermute | solution.py:14
  150.3 3.8 %multiply_convert_fusion = (bf16[1,512,1024]{2,1,0:T(8,128)(2,1)}, f32[1,512,1024]{2,1,0:T(8,128)S(1)}) fusion(f32[1,512,1024]{2,1,0:T(8,128)} %copy.84, f32[2,512,1024]{2,1,0:T(8,128)} %copy-done.3), kind=kLoop, calls=%fused_computation.39 | loop fusion | flops 1048576 | bytes 7340032 | tf_op jit(solution)/shard_map/convert_element_type | solution.py:104
  154.1 3.7 %collective-permute-start.6 = (bf16[1,512,1024]{2,1,0:T(8,128)(2,1)}, bf16[1,512,1024]{2,1,0:T(8,128)(2,1)}, u32[]{:S(2)}, u32[]{:S(2)}) collective-permute-start(bf16[1,512,1024]{2,1,0:T(8,128)(2,1)} %get-tuple-element.113), channel_id=1, source_target_pairs={{0,4},{4,8},{8,12},{1,5},{5,9},{9,13},{2,6},{6,10},{10,14},{3,7},{... | collective-permute-start | bytes 3145736 | tf_op jit(solution)/shard_map/ppermute | solution.py:14
  157.8 1.9 copy.83
  159.7 3.2 %fusion.28 = f32[1,8,128,128]{3,2,1,0:T(8,128)S(1)} fusion(f32[512,8]{0,1:T(8,128)S(1)} %fusion.52, bf16[512,8,128]{2,1,0:T(8,128)(2,1)} %bitcast.124, f32[512,8,128]{0,2,1:T(8,128)} %bitcast.119, f32[512,8]{0,1:T(8,128)S(1)} %add_rsqrt_fusion), kind=kOutput, calls=%fused_computation.46 | convolution fusion | flops 807403520 | bytes 3702784 | tf_op jit(solution)/shard_map/bht,bthd,bthe->bhde/dot_general | solution.py:121
  162.9 50.4 %while.14 = (s32[]{:T(128)}, f32[1,8,128,128]{3,2,1,0:T(8,128)S(1)}, f32[1,8]{1,0:T(1,128)S(1)}, f32[1,8]{1,0:T(1,128)S(1)}, f32[1,8,128,128]{3,2,1,0:T(8,128)S(...) while((s32[]{:T(128)}, f32[1,8,128,128]{3,2,1,0:T(8,128)S(1)}, ...), condition=%wide.region_9.10_spmd.clone, body=%wide.region_8.9_spmd.clone.sunk | while | flops 655403 | bytes 3146168 | solution.py:141
  163.1 2.8 %collective-permute-start = (bf16[1,8,128,128]{3,2,1,0:T(8,128)(2,1)S(1)}, bf16[1,8,128,128]{3,2,1,0:T(8,128)(2,1)S(1)}, u32[]{:S(2)}, u32[]{:S(2)}) collective-permute-start(bf16[1,8,128,128]{3,2,1,0:T(8,128)(2,1)S(1)} %fusion.74), channel_id=1, source_target_pairs={{0,4},{4,8},{8,12},{1,5},{5,9},{9,13},{2,6},{6,10},{10,14},{3,7},{... | collective-permute-start | bytes 786440 | tf_op jit(solution)/shard_map/while/body/eval_jaxpr/ppermute | solution.py:14
  165.8 1.9 collective-permute-start.1
  167.8 26.7 %collective-permute-done.1 = bf16[1,8]{1,0:T(2,128)(2,1)S(1)} collective-permute-done((bf16[1,8]{1,0:T(2,128)(2,1)S(1)}, bf16[1,8]{1,0:T(2,128)(2,1)S(1)}, u32[]{:S(2)}, u32[]{:S(2)}) %collective-permute-start.1) | collective-permute-done | bytes 48 | tf_op jit(solution)/shard_map/while/body/eval_jaxpr/ppermute | solution.py:14
  194.7 4.5 %collective-permute-start = (bf16[1,8,128,128]{3,2,1,0:T(8,128)(2,1)S(1)}, bf16[1,8,128,128]{3,2,1,0:T(8,128)(2,1)S(1)}, u32[]{:S(2)}, u32[]{:S(2)}) collective-permute-start(bf16[1,8,128,128]{3,2,1,0:T(8,128)(2,1)S(1)} %fusion.74), channel_id=1, source_target_pairs={{0,4},{4,8},{8,12},{1,5},{5,9},{9,13},{2,6},{6,10},{10,14},{3,7},{... | collective-permute-start | bytes 786440 | tf_op jit(solution)/shard_map/while/body/eval_jaxpr/ppermute | solution.py:14
  199.1 3.6 %collective-permute-start.1 = (bf16[1,8]{1,0:T(2,128)(2,1)S(1)}, bf16[1,8]{1,0:T(2,128)(2,1)S(1)}, u32[]{:S(2)}, u32[]{:S(2)}) collective-permute-start(bf16[1,8]{1,0:T(2,128)(2,1)S(1)} %fusion.75), channel_id=1, source_target_pairs={{0,4},{4,8},{8,12},{1,5},{5,9},{9,13},{2,6},{6,10},{10,14},{3,7},{... | collective-permute-start | bytes 56 | tf_op jit(solution)/shard_map/while/body/eval_jaxpr/ppermute | solution.py:14
  204.2 4.2 %collective-permute-start = (bf16[1,8,128,128]{3,2,1,0:T(8,128)(2,1)S(1)}, bf16[1,8,128,128]{3,2,1,0:T(8,128)(2,1)S(1)}, u32[]{:S(2)}, u32[]{:S(2)}) collective-permute-start(bf16[1,8,128,128]{3,2,1,0:T(8,128)(2,1)S(1)} %fusion.74), channel_id=1, source_target_pairs={{0,4},{4,8},{8,12},{1,5},{5,9},{9,13},{2,6},{6,10},{10,14},{3,7},{... | collective-permute-start | bytes 786440 | tf_op jit(solution)/shard_map/while/body/eval_jaxpr/ppermute | solution.py:14
  208.4 3.6 %collective-permute-start.1 = (bf16[1,8]{1,0:T(2,128)(2,1)S(1)}, bf16[1,8]{1,0:T(2,128)(2,1)S(1)}, u32[]{:S(2)}, u32[]{:S(2)}) collective-permute-start(bf16[1,8]{1,0:T(2,128)(2,1)S(1)} %fusion.75), channel_id=1, source_target_pairs={{0,4},{4,8},{8,12},{1,5},{5,9},{9,13},{2,6},{6,10},{10,14},{3,7},{... | collective-permute-start | bytes 56 | tf_op jit(solution)/shard_map/while/body/eval_jaxpr/ppermute | solution.py:14
  213.3 7.1 %fusion.5 = (f32[8,512]{1,0:T(8,128)S(1)}, f32[8,512,512]{1,2,0:T(8,128)}) fusion(pred[512,512]{0,1:T(8,128)(4,1)S(1)} %iota_compare_fusion.1, bf16[512,8,128]{2,0,1:T(8,128)(2,1)S(1)} %copy-done.8, f32[512,8,128]{0,2,1:T(8,128)} %bitcast.120, f32[512,8]{0,1:T(8,128)S(1)} %add_rsqrt_fusion), kind=kOutput, calls=%fused_computation.12 | convolution fusion | flops 544206848 | bytes 11829248 | tf_op jit(solution)/shard_map/bihd,bjhd->bhij/dot_general | solution.py:23
  221.9 5.2 %fusion.6 = (f32[8,512]{1,0:T(8,128)S(1)}, f32[8,512,512]{1,2,0:T(8,128)}) fusion(pred[512,512]{0,1:T(8,128)(4,1)S(1)} %fusion.41, bf16[512,8,128]{2,0,1:T(8,128)(2,1)S(1)} %copy-done.8, bf16[512,8,128]{2,1,0:T(8,128)(2,1)S(1)} %bitcast.127), kind=kOutput, calls=%fused_computation.13 | convolution fusion | flops 543158272 | bytes 10764288 | tf_op jit(solution)/shard_map/bihd,bjhd->bhij/dot_general | solution.py:27
  227.1 2.3 copy.85
  229.4 5.0 %fusion.11 = f32[8,128,512]{2,1,0:T(8,128)S(1)} fusion(bf16[512,8,128]{0,2,1:T(8,128)(2,1)} %bitcast.126, f32[8,512,512]{1,2,0:T(8,128)} %get-tuple-element.118, f32[8,512]{1,0:T(8,128)S(1)} %add.143, pred[512,512]{0,1:T(8,128)(4,1)S(1)} %fusion.41), kind=kOutput, calls=%fused_computation.21 | convolution fusion | flops 545259520 | bytes 11812864 | tf_op jit(solution)/shard_map/bhij,bjhd->bihd/dot_general | solution.py:40
  234.4 4.9 %fusion.10 = f32[8,128,512]{2,1,0:T(8,128)S(1)} fusion(f32[8,512,512]{1,2,0:T(8,128)} %get-tuple-element.116, f32[8,512]{1,0:T(8,128)S(1)} %add.143, pred[512,512]{0,1:T(8,128)(4,1)S(1)} %iota_compare_fusion.1, bf16[512,8,128]{2,1,0:T(8,128)(2,1)S(1)} %bitcast.125), kind=kOutput, calls=%fused_computation.20 | convolution fusion | flops 545259520 | bytes 11812864 | tf_op jit(solution)/shard_map/bhij,bjhd->bihd/dot_general | solution.py:38
  240.9 5.9 %convolution_convert_fusion = bf16[512,2048]{1,0:T(8,128)(2,1)} fusion(bf16[512,1024]{0,1:T(8,128)(2,1)S(1)} %bitcast.135, bf16[1024,2048]{1,0:T(8,128)(2,1)} %all-gather.2.cloned.1.call-done), kind=kOutput, calls=%fused_computation.26 | convolution fusion | flops 2148532224 | bytes 7340032 | tf_op jit(solution)/shard_map/dot_general | solution.py:166
  246.8 11.4 %reduce-scatter.2.cloned.1.call-done = bf16[512,1024]{1,0:T(8,128)(2,1)} async-done(((bf16[512,2048]{1,0:T(8,128)(2,1)}), bf16[512,1024]{1,0:T(8,128)(2,1)}) %reduce-scatter.2.cloned.1.call-update) | async-done | bytes 1048592 | tf_op jit(solution)/shard_map/reduce_scatter | solution.py:171
  258.3 2.9 %fusion.31 = bf16[1,512,1024]{2,1,0:T(8,128)(2,1)} fusion(bf16[512,1024]{1,0:T(8,128)(2,1)} %reduce-scatter.2.cloned.1.call-done, bf16[1,512,2048]{2,1,0:T(8,128)(2,1)} %param.9, s32[]{:T(128)S(6)} %select_n.71), kind=kLoop, calls=%fused_computation.47 | loop fusion | flops 2097152 | bytes 3145732 | tf_op jit(solution)/shard_map/reshape | solution.py:178
  (94 shorter events, 26.2 us)
Async XLA Ops:
  6.5 26.7 %copy-start = (bf16[1024,1024]{1,0:T(8,128)(2,1)S(1)}, bf16[1024,1024]{1,0:T(8,128)(2,1)}, u32[]{:S(2)}) copy-start(bf16[1024,1024]{1,0:T(8,128)(2,1)} %param.11) | copy-start | bytes 6291460
  6.5 2.2 copy-start.10
  6.5 234.3 %all-gather.2.cloned.1.call-start = ((), (), s32[]{:S(2)}) async-start(), calls=%async_computation.1 | async-start | bytes 6291456 | tf_op jit(solution)/shard_map/all_gather | solution.py:168
  6.5 2.4 copy-start.2
  8.9 6.0 %copy-start.9 = (f32[1,8,512]{2,1,0:T(8,128)S(1)}, f32[1,8,512]{2,1,0:T(8,128)}, u32[]{:S(2)}) copy-start(f32[1,8,512]{2,1,0:T(8,128)} %param.14) | copy-start | bytes 49156
  9.5 1.4 copy-start.6
  11.1 15.0 %collective-permute-start.2 = (bf16[256,1024]{1,0:T(8,128)(2,1)S(1)}, bf16[256,1024]{1,0:T(8,128)(2,1)S(1)}, u32[]{:S(2)}, u32[]{:S(2)}) collective-permute-start(bf16[256,1024]{1,0:T(8,128)(2,1)S(1)} %dynamic-slice_bitcast_fusion), channel_id=1, source_target_pairs={{0,2},{2,0},{1,3},{3,1},{4,6},{6,4},{5,7},{7,5},{8,10},{10,8},{9,1... | collective-permute-start | bytes 1572872 | tf_op jit(solution)/shard_map/ppermute | solution.py:77
  26.1 1.9 collective-permute-start.3
  33.3 4.0 %copy-start.11 = (bf16[1024,2,1024]{2,1,0:T(2,128)(2,1)S(1)}, bf16[1024,2,1024]{2,1,0:T(2,128)(2,1)}, u32[]{:S(2)}) copy-start(bf16[1024,2,1024]{2,1,0:T(2,128)(2,1)} %param.12) | copy-start | bytes 12582916
  35.5 26.3 %collective-permute-start.5 = (bf16[512,1024]{1,0:T(8,128)(2,1)}, bf16[512,1024]{1,0:T(8,128)(2,1)}, u32[]{:S(2)}, u32[]{:S(2)}) collective-permute-start(bf16[512,1024]{1,0:T(8,128)(2,1)} %convolution_convert_fusion.1), channel_id=1, source_target_pairs={{0,2},{2,0},{1,3},{3,1},{4,6},{6,4},{5,7},{7,5},{8,10},{10,8},{9,1... | collective-permute-start | bytes 3145736 | tf_op jit(solution)/shard_map/ppermute | solution.py:88
  41.0 93.1 %collective-permute-start.4 = (bf16[2,512,1024]{2,1,0:T(8,128)(2,1)}, bf16[2,512,1024]{2,1,0:T(8,128)(2,1)}, u32[]{:S(2)}, u32[]{:S(2)}) collective-permute-start(bf16[2,512,1024]{2,1,0:T(8,128)(2,1)} %convert_bitcast_fusion), channel_id=1, source_target_pairs={{0,2},{2,0},{1,3},{3,1},{4,6},{6,4},{5,7},{7,5},{8,10},{10,8},{9,1... | collective-permute-start | bytes 6291464 | tf_op jit(solution)/shard_map/ppermute | solution.py:88
  66.0 1.6 copy-start.4
  66.0 192.3 %reduce-scatter.2.cloned.1.call-start = ((), (), s32[]{:S(2)}) async-start(), calls=%async_computation.2 | async-start | bytes 3145728 | tf_op jit(solution)/shard_map/reduce_scatter | solution.py:171
  68.8 65.3 %copy-start.7 = (bf16[1,512,2048]{2,1,0:T(8,128)(2,1)S(1)}, bf16[1,512,2048]{2,1,0:T(8,128)(2,1)}, u32[]{:S(2)}) copy-start(bf16[1,512,2048]{2,1,0:T(8,128)(2,1)} %copy-done.6) | copy-start | bytes 6291460
  139.5 8.0 %copy-start.3 = (f32[2,512,1024]{2,1,0:T(8,128)}, f32[2,512,1024]{2,1,0:T(8,128)S(1)}, u32[]{:S(2)}) copy-start(f32[2,512,1024]{2,1,0:T(8,128)S(1)} %bitcast_add_fusion) | copy-start | bytes 12582916
  142.6 84.6 %collective-permute-start.7 = (bf16[1,512,1024]{2,1,0:T(8,128)(2,1)}, bf16[1,512,1024]{2,1,0:T(8,128)(2,1)}, u32[]{:S(2)}, u32[]{:S(2)}) collective-permute-start(bf16[1,512,1024]{2,1,0:T(8,128)(2,1)} %slice.33), channel_id=1, source_target_pairs={{0,4},{4,8},{8,12},{1,5},{5,9},{9,13},{2,6},{6,10},{10,14},{3,7},{... | collective-permute-start | bytes 3145736 | tf_op jit(solution)/shard_map/ppermute | solution.py:14
  154.1 66.3 %collective-permute-start.6 = (bf16[1,512,1024]{2,1,0:T(8,128)(2,1)}, bf16[1,512,1024]{2,1,0:T(8,128)(2,1)}, u32[]{:S(2)}, u32[]{:S(2)}) collective-permute-start(bf16[1,512,1024]{2,1,0:T(8,128)(2,1)} %get-tuple-element.113), channel_id=1, source_target_pairs={{0,4},{4,8},{8,12},{1,5},{5,9},{9,13},{2,6},{6,10},{10,14},{3,7},{... | collective-permute-start | bytes 3145736 | tf_op jit(solution)/shard_map/ppermute | solution.py:14
  162.9 50.4 %copy-start.8 = (bf16[512,8,128]{2,0,1:T(8,128)(2,1)S(1)}, bf16[512,8,128]{2,0,1:T(8,128)(2,1)}, u32[]{:S(2)}) copy-start(bf16[512,8,128]{2,0,1:T(8,128)(2,1)} %fusion.16) | copy-start | bytes 3145732
  163.1 31.4 %collective-permute-start = (bf16[1,8,128,128]{3,2,1,0:T(8,128)(2,1)S(1)}, bf16[1,8,128,128]{3,2,1,0:T(8,128)(2,1)S(1)}, u32[]{:S(2)}, u32[]{:S(2)}) collective-permute-start(bf16[1,8,128,128]{3,2,1,0:T(8,128)(2,1)S(1)} %fusion.74), channel_id=1, source_target_pairs={{0,4},{4,8},{8,12},{1,5},{5,9},{9,13},{2,6},{6,10},{10,14},{3,7},{... | collective-permute-start | bytes 786440 | tf_op jit(solution)/shard_map/while/body/eval_jaxpr/ppermute | solution.py:14
  165.8 28.6 %collective-permute-start.1 = (bf16[1,8]{1,0:T(2,128)(2,1)S(1)}, bf16[1,8]{1,0:T(2,128)(2,1)S(1)}, u32[]{:S(2)}, u32[]{:S(2)}) collective-permute-start(bf16[1,8]{1,0:T(2,128)(2,1)S(1)} %fusion.75), channel_id=1, source_target_pairs={{0,4},{4,8},{8,12},{1,5},{5,9},{9,13},{2,6},{6,10},{10,14},{3,7},{... | collective-permute-start | bytes 56 | tf_op jit(solution)/shard_map/while/body/eval_jaxpr/ppermute | solution.py:14
  194.7 9.3 %collective-permute-start = (bf16[1,8,128,128]{3,2,1,0:T(8,128)(2,1)S(1)}, bf16[1,8,128,128]{3,2,1,0:T(8,128)(2,1)S(1)}, u32[]{:S(2)}, u32[]{:S(2)}) collective-permute-start(bf16[1,8,128,128]{3,2,1,0:T(8,128)(2,1)S(1)} %fusion.74), channel_id=1, source_target_pairs={{0,4},{4,8},{8,12},{1,5},{5,9},{9,13},{2,6},{6,10},{10,14},{3,7},{... | collective-permute-start | bytes 786440 | tf_op jit(solution)/shard_map/while/body/eval_jaxpr/ppermute | solution.py:14
  199.1 4.8 %collective-permute-start.1 = (bf16[1,8]{1,0:T(2,128)(2,1)S(1)}, bf16[1,8]{1,0:T(2,128)(2,1)S(1)}, u32[]{:S(2)}, u32[]{:S(2)}) collective-permute-start(bf16[1,8]{1,0:T(2,128)(2,1)S(1)} %fusion.75), channel_id=1, source_target_pairs={{0,4},{4,8},{8,12},{1,5},{5,9},{9,13},{2,6},{6,10},{10,14},{3,7},{... | collective-permute-start | bytes 56 | tf_op jit(solution)/shard_map/while/body/eval_jaxpr/ppermute | solution.py:14
  204.2 9.1 %collective-permute-start = (bf16[1,8,128,128]{3,2,1,0:T(8,128)(2,1)S(1)}, bf16[1,8,128,128]{3,2,1,0:T(8,128)(2,1)S(1)}, u32[]{:S(2)}, u32[]{:S(2)}) collective-permute-start(bf16[1,8,128,128]{3,2,1,0:T(8,128)(2,1)S(1)} %fusion.74), channel_id=1, source_target_pairs={{0,4},{4,8},{8,12},{1,5},{5,9},{9,13},{2,6},{6,10},{10,14},{3,7},{... | collective-permute-start | bytes 786440 | tf_op jit(solution)/shard_map/while/body/eval_jaxpr/ppermute | solution.py:14
  208.4 4.8 %collective-permute-start.1 = (bf16[1,8]{1,0:T(2,128)(2,1)S(1)}, bf16[1,8]{1,0:T(2,128)(2,1)S(1)}, u32[]{:S(2)}, u32[]{:S(2)}) collective-permute-start(bf16[1,8]{1,0:T(2,128)(2,1)S(1)} %fusion.75), channel_id=1, source_target_pairs={{0,4},{4,8},{8,12},{1,5},{5,9},{9,13},{2,6},{6,10},{10,14},{3,7},{... | collective-permute-start | bytes 56 | tf_op jit(solution)/shard_map/while/body/eval_jaxpr/ppermute | solution.py:14
  229.4 5.0 %copy-start.5 = (bf16[64,8,8,128]{3,2,1,0:T(8,128)(2,1)S(1)}, bf16[64,8,8,128]{3,2,1,0:T(8,128)(2,1)}, u32[]{:S(2)}) copy-start(bf16[64,8,8,128]{3,2,1,0:T(8,128)(2,1)} %copy.87) | copy-start | bytes 3145732
  246.8 14.4 %copy-start.1 = (bf16[1024,1024]{1,0:T(8,128)(2,1)S(1)}, bf16[1024,1024]{1,0:T(8,128)(2,1)}, u32[]{:S(2)}) copy-start(bf16[1024,1024]{1,0:T(8,128)(2,1)} %param.11) | copy-start | bytes 6291460
Sparse Core Ops, SparseCore 0:
  66.1 84.8 all-gather.1
  246.9 11.2 reduce-scatter.1

commit v3 on v2

--- a/solution.py
+++ b/solution.py
@@ -82,11 +82,14 @@
             )
         )
 
-    def gathered_sum(partials):
+    def gathered_sum(partials, after=None):
         total = partials[0]
         for step in range(1, ways):
+            outgoing = partials[step].astype(jnp.bfloat16)
+            if after is not None:
+                outgoing = lax.optimization_barrier((outgoing, after))[0]
             total = total + lax.ppermute(
-                partials[step].astype(jnp.bfloat16),
+                outgoing,
                 "wloop",
                 [(source, (source - step) % ways) for source in range(ways)],
             ).astype(jnp.float32)
@@ -99,7 +102,8 @@
         ]
     )
     query_raw = gathered_sum(
-        [jnp.dot(rows, w_query, preferred_element_type=jnp.float32) for rows in stacked]
+        [jnp.dot(rows, w_query, preferred_element_type=jnp.float32) for rows in stacked],
+        after=pair_raw,
     )
     lookup_vectors = rms_rows(pair_raw[0].reshape(trajs, span, heads_here, head_dim), 1e-06).astype(
         jnp.bfloat16
@@ -127,23 +131,28 @@
     )
     local_mass = jnp.sum(weight * weight, axis=-1)
 
+    local_both = jnp.concatenate(
+        [local_state, jnp.broadcast_to(local_mass[:, :, None, None], local_state.shape[:2] + (1, head_dim))],
+        axis=2,
+    )
+    factor_both = jnp.concatenate(
+        [
+            jnp.broadcast_to(factor[:, :, None, None], local_state.shape),
+            jnp.broadcast_to((factor * factor)[:, :, None, None], local_state.shape[:2] + (1, head_dim)),
+        ],
+        axis=2,
+    )
+
     def relay_turn(turn, carry):
-        state, mass = carry
-        return (
-            shifted(
-                (factor[:, :, None, None] * state + local_state).astype(jnp.bfloat16), "seq", 1
-            ).astype(jnp.float32),
-            shifted((factor * factor * mass + local_mass).astype(jnp.bfloat16), "seq", 1).astype(
-                jnp.float32
-            ),
-        )
-
-    entering, entering_mass = lax.fori_loop(
-        0,
-        lax.axis_size("seq") - 1,
-        relay_turn,
-        (jnp.zeros_like(local_state), jnp.zeros_like(local_mass)),
-    )
+        return shifted((factor_both * carry + local_both).astype(jnp.bfloat16), "seq", 1).astype(
+            jnp.float32
+        )
+
+    entering_both = lax.fori_loop(
+        0, lax.axis_size("seq") - 1, relay_turn, jnp.zeros_like(local_both)
+    )
+    entering = entering_both[:, :, :head_dim, :]
+    entering_mass = entering_both[:, :, head_dim, 0]
     entering = entering * keep[:, None, None, None]
     entering_mass = entering_mass * keep[:, None]
     read = jnp.einsum(
@@ -163,17 +172,31 @@
     )
     attended = (window + read).astype(jnp.bfloat16).reshape(count, inner_here)
     w_output = lax.optimization_barrier((w_output, query_raw))[0]
-    partial_out = jnp.dot(
-        attended,
-        lax.all_gather(w_output, "wloop", axis=1, tiled=True),
-        preferred_element_type=jnp.float32,
-    )
-    summed = lax.psum_scatter(
-        partial_out.astype(jnp.bfloat16), "heads", scatter_dimension=1, tiled=True
-    ).astype(jnp.float32)
-    share = summed.shape[1]
+    w_output_rows = lax.all_gather(w_output, "wloop", axis=1, tiled=True)
+    cores = lax.axis_size("heads")
+    core = lax.axis_index("heads")
+    share = width // cores
+
+    def output_share(index):
+        return jnp.dot(
+            attended,
+            lax.dynamic_slice_in_dim(w_output_rows, index * share, share, 1),
+            preferred_element_type=jnp.float32,
+        )
+
+    received = [
+        lax.ppermute(
+            output_share((core + step) % cores).astype(jnp.bfloat16),
+            "heads",
+            [(source, (source + step) % cores) for source in range(cores)],
+        )
+        for step in range(1, cores)
+    ]
+    summed = output_share(core)
+    for piece in received:
+        summed = summed + piece.astype(jnp.float32)
     residual = lax.dynamic_slice_in_dim(
-        activations.reshape(count, width), lax.axis_index("heads") * share, share, 1
+        activations.reshape(count, width), core * share, share, 1
     )
     return (residual.astype(jnp.float32) + summed).astype(jnp.bfloat16).reshape(trajs, span, share)
 

time: 269 us -> 244 us (0.907)
  waiting for transfers between devices: 135 us -> 95.8 us
  local copies, waits for them, and re-layouts: 18.1 us -> 31.9 us
  starting transfers between devices: 33.6 us -> 27.4 us
  other arithmetic: 18.9 us -> 24.7 us
    ppermute x2 -> x3, waiting for transfers between devices: 82.2 us -> 41.1 us  [the longest x2 38.2 us: gathered_sum(): lax.ppermute(outgoing, 'wloop', [(source, (source - step) % ways) for sou...]
    ppermute x8 -> x5, waiting for transfers between devices: 29.3 us -> 40.9 us  [shifted(): lax.ppermute(value, axis, [(source, source + steps) for source in range(i...]
    reduce_scatter x1 -> x0, waiting for transfers between devices: 11.4 us -> none  [shards(): lax.psum_scatter(partial_out.astype(jnp.bfloat16), 'heads', scatter_dimen...]
    ppermute x8 -> x5, starting transfers between devices: 28.5 us -> 20.9 us  [shifted(): lax.ppermute(value, axis, [(source, source + steps) for source in range(i...]
    while x0 -> x2, local copies, waits for them, and re-layouts: none -> 6.1 us  [shards(): lax.fori_loop(0, lax.axis_size('seq') - 1, relay_turn, jnp.zeros_like(loc...]
    convert_element_type x12 -> x6, other arithmetic: 0.53 us -> 5.65 us  [the longest x3 5.54 us: relay_turn(): (factor_both * carry + local_both).astype(jnp.bfloat16)]
    unnamed x29 -> x41, local copies, waits for them, and re-layouts: 6.92 us -> 11.2 us
    reshape x1 -> x0, other arithmetic: 2.91 us -> none  [shards(): (residual.astype(jnp.float32) + summed).astype(jnp.bfloat16)]
  transfers between devices with their start and end apart: 14 -> 11, of which waited for: 8 -> 8; matrix products, arithmetic and copies ran while one was open for 23% -> 30% of each run, Pallas kernels for 0% -> 0%
where the time goes in v3:
time: 244 us
  waiting for transfers between devices  95.8 us (39%)
  matrix products  49.3 us (20%)
  local copies, waits for them, and re-layouts  31.9 us (13%)
  starting transfers between devices  27.4 us (11%)
  other arithmetic  24.7 us (10%)
  between operations  14.4 us (6%)
    ppermute x5, waiting for transfers between devices, shifted(): lax.ppermute(value, axis, [(source, source + steps) for source in range(i...  40.9 us
    ppermute x2, waiting for transfers between devices, gathered_sum(): lax.ppermute(outgoing, 'wloop', [(source, (source - step) % ways) for sou...  38.2 us
    ppermute x5, starting transfers between devices, shifted(): lax.ppermute(value, axis, [(source, source + steps) for source in range(i...  20.9 us
    ppermute x1, waiting for transfers between devices, shards(): lax.ppermute(part, 'wloop', [(source, (source + step) % ways) for source...  11.9 us
    unnamed x41, local copies, waits for them, and re-layouts  11.2 us
    dot_general x2, matrix products, shards(): jnp.einsum('td,dje->jte', rows, w_keyvalue, preferred_element_type=jnp.fl...  10.4 us
    dot_general x2, matrix products, output_share(): jnp.dot(attended, lax.dynamic_slice_in_dim(w_output_rows, index * share,...  8.69 us
    dot_general x2, matrix products, shards(): jnp.dot(rows, w_query, preferred_element_type=jnp.float32)  7.81 us
  transfers between devices with their start and end apart: 11, of which 8 were waited for; matrix products, arithmetic and copies ran while one was open for 30% of the time, Pallas kernels for 0%

profile of v3, /device:TPU:0, one launch (start us, length us, event | category | flops | bytes accessed | tf_op | source)
XLA Modules:
  0.0 243.7 jit_solution(3719203059028084426)
XLA Ops:
  6.5 2.2 fusion.4
  11.1 3.0 %collective-permute-start.1 = (bf16[256,1024]{1,0:T(8,128)(2,1)S(1)}, bf16[256,1024]{1,0:T(8,128)(2,1)S(1)}, u32[]{:S(2)}, u32[]{:S(2)}) collective-permute-start(bf16[256,1024]{1,0:T(8,128)(2,1)S(1)} %dynamic-slice_bitcast_fusion), channel_id=1, source_target_pairs={{0,2},{2,0},{1,3},{3,1},{4,6},{6,4},{5,7},{7,5},{8,10},{10,8},{9,1... | collective-permute-start | bytes 1572872 | tf_op jit(solution)/shard_map/ppermute | solution.py:77
  14.2 11.9 %collective-permute-done.1 = bf16[256,1024]{1,0:T(8,128)(2,1)S(1)} collective-permute-done((bf16[256,1024]{1,0:T(8,128)(2,1)S(1)}, bf16[256,1024]{1,0:T(8,128)(2,1)S(1)}, u32[]{:S(2)}, u32[]{:S(2)}) %collective-permute-start.1) | collective-permute-done | bytes 524320 | tf_op jit(solution)/shard_map/ppermute | solution.py:77
  31.1 6.4 %convert_bitcast_fusion = bf16[2,512,1024]{2,1,0:T(8,128)(2,1)} fusion(bf16[1024,2,1024]{2,1,0:T(2,128)(2,1)} %param.12, bf16[512,1024]{1,0:T(8,128)(2,1)S(1)} %bitcast_select_fusion), kind=kOutput, calls=%fused_computation.43 | convolution fusion | flops 2148532224 | bytes 7340032 | tf_op jit(solution)/shard_map/td,dje->jte/dot_general | solution.py:100
  43.6 3.7 %convolution_convert_fusion = bf16[512,1024]{1,0:T(8,128)(2,1)} fusion(bf16[512,1024]{1,0:T(8,128)(2,1)} %copy-done.9, bf16[1024,1024]{1,0:T(8,128)(2,1)S(1)} %copy-done), kind=kOutput, calls=%fused_computation.45 | convolution fusion | flops 1074266112 | bytes 4194304 | tf_op jit(solution)/shard_map/dot_general | solution.py:105
  47.3 38.2 %collective-permute-done.3 = bf16[2,512,1024]{2,1,0:T(8,128)(2,1)} collective-permute-done((bf16[2,512,1024]{2,1,0:T(8,128)(2,1)}, bf16[2,512,1024]{2,1,0:T(8,128)(2,1)}, u32[]{:S(2)}, u32[]{:S(2)}) %collective-permute-start.3) | collective-permute-done | bytes 2097184 | tf_op jit(solution)/shard_map/ppermute | solution.py:91
  85.5 4.1 %bitcast_add_fusion = f32[2,512,1024]{2,1,0:T(8,128)S(1)} fusion(bf16[2,512,1024]{2,1,0:T(8,128)(2,1)} %collective-permute-done.3, bf16[1024,2,1024]{2,1,0:T(2,128)(2,1)S(1)} %copy-done.16, bf16[1,512,2048]{2,1,0:T(8,128)(2,1)S(1)} %copy-done.8, s32[]{:T(128)S(6)} %select_n.80), kind=kOutput, calls=%fused_computation.15 | convolution fusion | flops 2149580800 | bytes 11534340 | tf_op jit(solution)/shard_map/td,dje->jte/dot_general | solution.py:100
  100.2 2.9 %copy.84 = f32[1,512,1024]{2,1,0:T(8,128)} copy(f32[1,512,1024]{1,2,0:T(8,128)} %bitcast.117) | data formatting | bytes 4194304 | tf_op jit(solution)/shard_map/mul | solution.py:18
  103.1 4.5 %multiply_convert_fusion = (bf16[1,512,1024]{2,1,0:T(8,128)(2,1)}, f32[1,512,1024]{2,1,0:T(8,128)}) fusion(f32[1,512,1024]{2,1,0:T(8,128)} %copy.84, f32[2,512,1024]{2,1,0:T(8,128)} %copy-done.3), kind=kLoop, calls=%fused_computation.38 | loop fusion | flops 1048576 | bytes 7340032 | tf_op jit(solution)/shard_map/convert_element_type | solution.py:108
  107.6 2.9 %copy.83 = f32[1,512,1024]{1,2,0:T(8,128)} copy(f32[1,512,1024]{2,1,0:T(8,128)} %get-tuple-element.60) | data formatting | bytes 4194304 | tf_op jit(solution)/shard_map/reshape;squeeze | solution.py:108
  110.5 3.2 %fusion.37 = f32[1,8,128,128]{3,2,1,0:T(8,128)S(1)} fusion(f32[512,8]{0,1:T(8,128)S(1)} %fusion.60, bf16[512,8,128]{2,1,0:T(8,128)(2,1)} %bitcast.118, f32[512,8,128]{0,2,1:T(8,128)} %bitcast.113, f32[512,8]{0,1:T(8,128)S(1)} %add_rsqrt_fusion), kind=kOutput, calls=%fused_computation.47 | convolution fusion | flops 807403520 | bytes 3702784 | tf_op jit(solution)/shard_map/bht,bthd,bthe->bhde/dot_general | solution.py:125
  114.9 2.8 %slice.55 = bf16[1,512,1024]{2,1,0:T(8,128)(2,1)} slice(f32[2,512,1024]{2,1,0:T(8,128)} %copy-done.3), slice={[1:2], [0:512], [0:1024]} | slice | bytes 2097152 | tf_op jit(solution)/shard_map/slice | solution.py:111
  117.7 32.0 %while.11 = (s32[]{:T(128)}, f32[1,8,129,128]{3,2,1,0:T(8,128)S(1)}, f32[1,8,129,128]{3,2,1,0:T(8,128)S(1)}, f32[1,8,129,128]{3,2,1,0:T(8,128)}, s32[]{:T(128)}, /*index=5*/s32[]{:T(128)}) while((s32[]{:T(128)}, f32[1,8,129,128]{3,2,1,0:T(8,128)S(1)}, f32[1,8,129,128]{3,2,1,0:T(8,128)S(1)}, f32[1,8,129,128]{3,2,1,0:T(8,128)}, ...), condition=%wide.region_9.10_spmd.clone, body=%wide.region_8.9_spmd.clone.sunk | while | flops 660483 | bytes 3698807 | solution.py:151
  119.5 3.5 %collective-permute-start = (bf16[1,8,129,128]{3,2,1,0:T(8,128)(2,1)}, bf16[1,8,129,128]{3,2,1,0:T(8,128)(2,1)S(1)}, u32[]{:S(2)}, u32[]{:S(2)}) collective-permute-start(bf16[1,8,129,128]{3,2,1,0:T(8,128)(2,1)} %fusion.88), channel_id=1, source_target_pairs={{0,4},{4,8},{8,12},{1,5},{5,9},{9,13},{2,6},{6,10},{10,14},{3,7},{... | collective-permute-start | bytes 792584 | tf_op jit(solution)/shard_map/while/body/eval_jaxpr/ppermute | solution.py:14
  123.0 5.4 %collective-permute-done = bf16[1,8,129,128]{3,2,1,0:T(8,128)(2,1)S(1)} collective-permute-done((bf16[1,8,129,128]{3,2,1,0:T(8,128)(2,1)}, bf16[1,8,129,128]{3,2,1,0:T(8,128)(2,1)S(1)}, u32[]{:S(2)}, u32[]{:S(2)}) %collective-permute-start) | collective-permute-done | bytes 264224 | tf_op jit(solution)/shard_map/while/body/eval_jaxpr/ppermute | solution.py:14
  130.3 4.3 %collective-permute-start = (bf16[1,8,129,128]{3,2,1,0:T(8,128)(2,1)}, bf16[1,8,129,128]{3,2,1,0:T(8,128)(2,1)S(1)}, u32[]{:S(2)}, u32[]{:S(2)}) collective-permute-start(bf16[1,8,129,128]{3,2,1,0:T(8,128)(2,1)} %fusion.88), channel_id=1, source_target_pairs={{0,4},{4,8},{8,12},{1,5},{5,9},{9,13},{2,6},{6,10},{10,14},{3,7},{... | collective-permute-start | bytes 792584 | tf_op jit(solution)/shard_map/while/body/eval_jaxpr/ppermute | solution.py:14
  134.6 4.5 %collective-permute-done = bf16[1,8,129,128]{3,2,1,0:T(8,128)(2,1)S(1)} collective-permute-done((bf16[1,8,129,128]{3,2,1,0:T(8,128)(2,1)}, bf16[1,8,129,128]{3,2,1,0:T(8,128)(2,1)S(1)}, u32[]{:S(2)}, u32[]{:S(2)}) %collective-permute-start) | collective-permute-done | bytes 264224 | tf_op jit(solution)/shard_map/while/body/eval_jaxpr/ppermute | solution.py:14
  141.0 4.3 %collective-permute-start = (bf16[1,8,129,128]{3,2,1,0:T(8,128)(2,1)}, bf16[1,8,129,128]{3,2,1,0:T(8,128)(2,1)S(1)}, u32[]{:S(2)}, u32[]{:S(2)}) collective-permute-start(bf16[1,8,129,128]{3,2,1,0:T(8,128)(2,1)} %fusion.88), channel_id=1, source_target_pairs={{0,4},{4,8},{8,12},{1,5},{5,9},{9,13},{2,6},{6,10},{10,14},{3,7},{... | collective-permute-start | bytes 792584 | tf_op jit(solution)/shard_map/while/body/eval_jaxpr/ppermute | solution.py:14
  145.3 4.3 %collective-permute-done = bf16[1,8,129,128]{3,2,1,0:T(8,128)(2,1)S(1)} collective-permute-done((bf16[1,8,129,128]{3,2,1,0:T(8,128)(2,1)}, bf16[1,8,129,128]{3,2,1,0:T(8,128)(2,1)S(1)}, u32[]{:S(2)}, u32[]{:S(2)}) %collective-permute-start) | collective-permute-done | bytes 264224 | tf_op jit(solution)/shard_map/while/body/eval_jaxpr/ppermute | solution.py:14
  151.0 4.8 %copy.79 = f32[1,8,129,128]{1,3,2,0:T(8,128)} copy(f32[1,8,129,128]{3,2,1,0:T(8,128)S(1)} %get-tuple-element.30) | data formatting | bytes 1056768 | tf_op jit(solution)/shard_map/while | solution.py:151
  155.8 5.3 %collective-permute-start.6 = (bf16[1,512,1024]{2,1,0:T(8,128)(2,1)}, bf16[1,512,1024]{2,1,0:T(8,128)(2,1)}, u32[]{:S(2)}, u32[]{:S(2)}) collective-permute-start(bf16[1,512,1024]{2,1,0:T(8,128)(2,1)} %slice.55), channel_id=1, source_target_pairs={{0,4},{4,8},{8,12},{1,5},{5,9},{9,13},{2,6},{6,10},{10,14},{3,7},{... | collective-permute-start | bytes 3145736 | tf_op jit(solution)/shard_map/ppermute | solution.py:14
  161.1 3.6 %collective-permute-start.5 = (bf16[1,512,1024]{2,1,0:T(8,128)(2,1)}, bf16[1,512,1024]{2,1,0:T(8,128)(2,1)}, u32[]{:S(2)}, u32[]{:S(2)}) collective-permute-start(bf16[1,512,1024]{2,1,0:T(8,128)(2,1)} %get-tuple-element.59), channel_id=1, source_target_pairs={{0,4},{4,8},{8,12},{1,5},{5,9},{9,13},{2,6},{6,10},{10,14},{3,7},{... | collective-permute-start | bytes 3145736 | tf_op jit(solution)/shard_map/ppermute | solution.py:14
  165.3 4.1 %convert_add_fusion.1 = f32[512,1024]{1,0:T(8,128)} fusion(bf16[512,1024]{1,0:T(8,128)(2,1)} %collective-permute-done.4, bf16[1024,1024]{1,0:T(8,128)(2,1)S(1)} %copy-done, bf16[1,512,2048]{2,1,0:T(8,128)(2,1)} %copy-done.7, s32[]{:T(128)S(6)} %select_n.80), kind=kOutput, calls=%fused_computation.42 | convolution fusion | flops 1074790400 | bytes 6291460 | tf_op jit(solution)/shard_map/dot_general | solution.py:105
  172.4 2.4 fusion.13
  174.8 26.7 %collective-permute-done.5 = bf16[1,512,1024]{2,1,0:T(8,128)(2,1)} collective-permute-done((bf16[1,512,1024]{2,1,0:T(8,128)(2,1)}, bf16[1,512,1024]{2,1,0:T(8,128)(2,1)}, u32[]{:S(2)}, u32[]{:S(2)}) %collective-permute-start.5) | collective-permute-done | bytes 1048608 | tf_op jit(solution)/shard_map/ppermute | solution.py:14
  203.1 5.3 %fusion.3 = (f32[8,512]{1,0:T(8,128)S(1)}, f32[8,512,512]{1,2,0:T(8,128)}) fusion(pred[512,512]{0,1:T(8,128)(4,1)S(1)} %copy-done.13, bf16[512,8,128]{2,0,1:T(8,128)(2,1)S(1)} %fusion.13, bf16[512,8,128]{2,1,0:T(8,128)(2,1)S(1)} %bitcast.121), kind=kOutput, calls=%fused_computation.9 | convolution fusion | flops 543158272 | bytes 10764288 | tf_op jit(solution)/shard_map/bihd,bjhd->bhij/dot_general | solution.py:27
  208.3 5.5 %fusion.2 = (f32[8,512]{1,0:T(8,128)S(1)}, f32[8,512,512]{1,2,0:T(8,128)}) fusion(pred[512,512]{0,1:T(8,128)(4,1)S(1)} %copy-done.12, bf16[512,8,128]{2,0,1:T(8,128)(2,1)S(1)} %fusion.13, f32[512,8,128]{0,2,1:T(8,128)S(1)} %bitcast.114, f32[512,8]{0,1:T(8,128)S(1)} %add_rsqrt_fusion), kind=kOutput, calls=%fused_computation.8 | convolution fusion | flops 544206848 | bytes 11829248 | tf_op jit(solution)/shard_map/bihd,bjhd->bhij/dot_general | solution.py:23
  215.4 4.8 %fusion.8 = f32[8,128,512]{2,1,0:T(8,128)S(1)} fusion(bf16[512,8,128]{0,2,1:T(8,128)(2,1)S(1)} %bitcast.120, f32[8,512,512]{1,2,0:T(8,128)} %get-tuple-element.64, f32[8,512]{1,0:T(8,128)S(1)} %add.155, pred[512,512]{0,1:T(8,128)(4,1)} %fusion.49), kind=kOutput, calls=%fused_computation.17 | convolution fusion | flops 545259520 | bytes 11812864 | tf_op jit(solution)/shard_map/bhij,bjhd->bihd/dot_general | solution.py:40
  221.6 2.3 fusion.7
  225.3 4.2 %fusion.29 = bf16[512,1024]{1,0:T(8,128)(2,1)} fusion(bf16[512,1024]{0,1:T(8,128)(2,1)S(1)} %bitcast.122, bf16[1024,2048]{1,0:T(8,128)(2,1)} %all-gather.2.cloned.1.call-done, s32[]{:T(128)S(6)} %select_n.94), kind=kOutput, calls=%fused_computation.44 | convolution fusion | flops 1074266112 | bytes 4194308 | tf_op jit(solution)/shard_map/dot_general | solution.py:181
  229.4 2.9 %collective-permute-done.7 = bf16[512,1024]{1,0:T(8,128)(2,1)S(1)} collective-permute-done((bf16[512,1024]{1,0:T(8,128)(2,1)}, bf16[512,1024]{1,0:T(8,128)(2,1)S(1)}, u32[]{:S(2)}, u32[]{:S(2)}) %collective-permute-start.7) | collective-permute-done | bytes 1048608 | tf_op jit(solution)/shard_map/ppermute | solution.py:188
  232.3 4.5 %fusion.34 = bf16[1,512,1024]{2,1,0:T(8,128)(2,1)} fusion(bf16[512,1024]{1,0:T(8,128)(2,1)S(1)} %collective-permute-done.7, bf16[512,1024]{0,1:T(8,128)(2,1)} %bitcast.123, bf16[1024,2048]{1,0:T(8,128)(2,1)} %all-gather.2.cloned.1.call-done, s32[]{:T(128)S(6)} %select_n.79, bf16[1,512,2048]{2,1,0:T(8,128)(2,1)} %param.9), kind=kOutput, calls=%fused_computation.46 | convolution fusion | flops 1076363264 | bytes 6292480 | tf_op jit(solution)/shard_map/dot_general | solution.py:181
  (98 shorter events, 40.8 us)
Async XLA Ops:
  6.5 37.0 %copy-start = (bf16[1024,1024]{1,0:T(8,128)(2,1)S(1)}, bf16[1024,1024]{1,0:T(8,128)(2,1)}, u32[]{:S(2)}) copy-start(bf16[1024,1024]{1,0:T(8,128)(2,1)} %param.11) | copy-start | bytes 6291460
  6.5 2.2 copy-start.15
  6.5 218.7 %all-gather.2.cloned.1.call-start = ((), (), s32[]{:S(2)}) async-start(), calls=%async_computation | async-start | bytes 6291456 | tf_op jit(solution)/shard_map/all_gather | solution.py:175
  6.5 2.4 copy-start.2
  9.5 1.4 copy-start.7
  11.1 15.0 %collective-permute-start.1 = (bf16[256,1024]{1,0:T(8,128)(2,1)S(1)}, bf16[256,1024]{1,0:T(8,128)(2,1)S(1)}, u32[]{:S(2)}, u32[]{:S(2)}) collective-permute-start(bf16[256,1024]{1,0:T(8,128)(2,1)S(1)} %dynamic-slice_bitcast_fusion), channel_id=1, source_target_pairs={{0,2},{2,0},{1,3},{3,1},{4,6},{6,4},{5,7},{7,5},{8,10},{10,8},{9,1... | collective-permute-start | bytes 1572872 | tf_op jit(solution)/shard_map/ppermute | solution.py:77
  26.1 1.9 collective-permute-start.2
  31.1 6.4 %copy-start.9 = (bf16[512,1024]{1,0:T(8,128)(2,1)}, bf16[512,1024]{1,0:T(8,128)(2,1)S(1)}, u32[]{:S(2)}) copy-start(bf16[512,1024]{1,0:T(8,128)(2,1)S(1)} %bitcast_select_fusion) | copy-start | bytes 3145732
  31.1 8.8 %copy-start.14 = (f32[1,8,512]{2,1,0:T(8,128)S(1)}, f32[1,8,512]{2,1,0:T(8,128)}, u32[]{:S(2)}) copy-start(f32[1,8,512]{2,1,0:T(8,128)} %param.14) | copy-start | bytes 49156
  37.5 48.0 %collective-permute-start.3 = (bf16[2,512,1024]{2,1,0:T(8,128)(2,1)}, bf16[2,512,1024]{2,1,0:T(8,128)(2,1)}, u32[]{:S(2)}, u32[]{:S(2)}) collective-permute-start(bf16[2,512,1024]{2,1,0:T(8,128)(2,1)} %convert_bitcast_fusion), channel_id=1, source_target_pairs={{0,2},{2,0},{1,3},{3,1},{4,6},{6,4},{5,7},{7,5},{8,10},{10,8},{9,1... | collective-permute-start | bytes 6291464 | tf_op jit(solution)/shard_map/ppermute | solution.py:91
  43.6 41.9 %copy-start.8 = (bf16[1,512,2048]{2,1,0:T(8,128)(2,1)S(1)}, bf16[1,512,2048]{2,1,0:T(8,128)(2,1)}, u32[]{:S(2)}) copy-start(bf16[1,512,2048]{2,1,0:T(8,128)(2,1)} %copy-done.7) | copy-start | bytes 6291460
  43.6 41.9 %copy-start.16 = (bf16[1024,2,1024]{2,1,0:T(2,128)(2,1)S(1)}, bf16[1024,2,1024]{2,1,0:T(2,128)(2,1)}, u32[]{:S(2)}) copy-start(bf16[1024,2,1024]{2,1,0:T(2,128)(2,1)} %param.12) | copy-start | bytes 12582916
  89.6 1.9 copy-start.3
  92.8 72.5 %collective-permute-start.4 = (bf16[512,1024]{1,0:T(8,128)(2,1)}, bf16[512,1024]{1,0:T(8,128)(2,1)}, u32[]{:S(2)}, u32[]{:S(2)}) collective-permute-start(bf16[512,1024]{1,0:T(8,128)(2,1)} %convolution_convert_fusion), channel_id=1, source_target_pairs={{0,2},{2,0},{1,3},{3,1},{4,6},{6,4},{5,7},{7,5},{8,10},{10,8},{9,1... | collective-permute-start | bytes 3145736 | tf_op jit(solution)/shard_map/ppermute | solution.py:91
  119.5 8.9 %collective-permute-start = (bf16[1,8,129,128]{3,2,1,0:T(8,128)(2,1)}, bf16[1,8,129,128]{3,2,1,0:T(8,128)(2,1)S(1)}, u32[]{:S(2)}, u32[]{:S(2)}) collective-permute-start(bf16[1,8,129,128]{3,2,1,0:T(8,128)(2,1)} %fusion.88), channel_id=1, source_target_pairs={{0,4},{4,8},{8,12},{1,5},{5,9},{9,13},{2,6},{6,10},{10,14},{3,7},{... | collective-permute-start | bytes 792584 | tf_op jit(solution)/shard_map/while/body/eval_jaxpr/ppermute | solution.py:14
  130.3 8.8 %collective-permute-start = (bf16[1,8,129,128]{3,2,1,0:T(8,128)(2,1)}, bf16[1,8,129,128]{3,2,1,0:T(8,128)(2,1)S(1)}, u32[]{:S(2)}, u32[]{:S(2)}) collective-permute-start(bf16[1,8,129,128]{3,2,1,0:T(8,128)(2,1)} %fusion.88), channel_id=1, source_target_pairs={{0,4},{4,8},{8,12},{1,5},{5,9},{9,13},{2,6},{6,10},{10,14},{3,7},{... | collective-permute-start | bytes 792584 | tf_op jit(solution)/shard_map/while/body/eval_jaxpr/ppermute | solution.py:14
  141.0 8.6 %collective-permute-start = (bf16[1,8,129,128]{3,2,1,0:T(8,128)(2,1)}, bf16[1,8,129,128]{3,2,1,0:T(8,128)(2,1)S(1)}, u32[]{:S(2)}, u32[]{:S(2)}) collective-permute-start(bf16[1,8,129,128]{3,2,1,0:T(8,128)(2,1)} %fusion.88), channel_id=1, source_target_pairs={{0,4},{4,8},{8,12},{1,5},{5,9},{9,13},{2,6},{6,10},{10,14},{3,7},{... | collective-permute-start | bytes 792584 | tf_op jit(solution)/shard_map/while/body/eval_jaxpr/ppermute | solution.py:14
  155.8 58.1 %collective-permute-start.6 = (bf16[1,512,1024]{2,1,0:T(8,128)(2,1)}, bf16[1,512,1024]{2,1,0:T(8,128)(2,1)}, u32[]{:S(2)}, u32[]{:S(2)}) collective-permute-start(bf16[1,512,1024]{2,1,0:T(8,128)(2,1)} %slice.55), channel_id=1, source_target_pairs={{0,4},{4,8},{8,12},{1,5},{5,9},{9,13},{2,6},{6,10},{10,14},{3,7},{... | collective-permute-start | bytes 3145736 | tf_op jit(solution)/shard_map/ppermute | solution.py:14
  161.1 40.5 %collective-permute-start.5 = (bf16[1,512,1024]{2,1,0:T(8,128)(2,1)}, bf16[1,512,1024]{2,1,0:T(8,128)(2,1)}, u32[]{:S(2)}, u32[]{:S(2)}) collective-permute-start(bf16[1,512,1024]{2,1,0:T(8,128)(2,1)} %get-tuple-element.59), channel_id=1, source_target_pairs={{0,4},{4,8},{8,12},{1,5},{5,9},{9,13},{2,6},{6,10},{10,14},{3,7},{... | collective-permute-start | bytes 3145736 | tf_op jit(solution)/shard_map/ppermute | solution.py:14
  169.4 1.6 copy-start.5
  172.4 30.6 %copy-start.13 = (pred[512,512]{0,1:T(8,128)(4,1)S(1)}, pred[512,512]{0,1:T(8,128)(4,1)}, u32[]{:S(2)}) copy-start(pred[512,512]{0,1:T(8,128)(4,1)} %fusion.49) | copy-start | bytes 786436
  203.0 5.3 %copy-start.4 = (f32[1,512,1024]{1,2,0:T(8,128)S(1)}, f32[1,512,1024]{1,2,0:T(8,128)}, u32[]{:S(2)}) copy-start(f32[1,512,1024]{1,2,0:T(8,128)} %copy.83) | copy-start | bytes 6291460
  203.1 5.3 %copy-start.12 = (pred[512,512]{0,1:T(8,128)(4,1)S(1)}, pred[512,512]{0,1:T(8,128)(4,1)}, u32[]{:S(2)}) copy-start(pred[512,512]{0,1:T(8,128)(4,1)} %iota_compare_fusion.1) | copy-start | bytes 786436
  215.3 4.9 %copy-start.6 = (bf16[64,8,8,128]{3,2,1,0:T(8,128)(2,1)S(1)}, bf16[64,8,8,128]{3,2,1,0:T(8,128)(2,1)}, u32[]{:S(2)}) copy-start(bf16[64,8,8,128]{3,2,1,0:T(8,128)(2,1)} %copy.87) | copy-start | bytes 3145732
  215.3 6.2 %copy-start.17 = (f32[8,512,512]{1,2,0:T(8,128)S(1)}, f32[8,512,512]{1,2,0:T(8,128)}, u32[]{:S(2)}) copy-start(f32[8,512,512]{1,2,0:T(8,128)} %get-tuple-element.62) | copy-start | bytes 25165828
  221.6 2.3 copy-start.10
  225.2 4.2 %copy-start.11 = (bf16[1,512,8,128]{1,3,2,0:T(8,128)(2,1)}, bf16[1,512,8,128]{1,3,2,0:T(8,128)(2,1)S(1)}, u32[]{:S(2)}) copy-start(bf16[1,512,8,128]{1,3,2,0:T(8,128)(2,1)S(1)} %fusion.16) | copy-start | bytes 3145732
  229.4 2.9 %collective-permute-start.7 = (bf16[512,1024]{1,0:T(8,128)(2,1)}, bf16[512,1024]{1,0:T(8,128)(2,1)S(1)}, u32[]{:S(2)}, u32[]{:S(2)}) collective-permute-start(bf16[512,1024]{1,0:T(8,128)(2,1)} %fusion.29), channel_id=1, source_target_pairs={{0,1},{1,0},{2,3},{3,2},{4,5},{5,4},{6,7},{7,6},{8,9},{9,8},{10,11... | collective-permute-start | bytes 3145736 | tf_op jit(solution)/shard_map/ppermute | solution.py:188
  229.4 7.4 %copy-start.1 = (bf16[1024,1024]{1,0:T(8,128)(2,1)S(1)}, bf16[1024,1024]{1,0:T(8,128)(2,1)}, u32[]{:S(2)}) copy-start(bf16[1024,1024]{1,0:T(8,128)(2,1)} %param.11) | copy-start | bytes 6291460
Sparse Core Ops, SparseCore 0:
  169.6 53.9 all-gather.1

commit v4 on v3

--- a/solution.py
+++ b/solution.py
@@ -148,6 +148,7 @@
             jnp.float32
         )
 
+    local_both, prior_keys, prior_values = lax.optimization_barrier((local_both, prior_keys, prior_values))
     entering_both = lax.fori_loop(
         0, lax.axis_size("seq") - 1, relay_turn, jnp.zeros_like(local_both)
     )
@@ -171,7 +172,7 @@
         scale,
     )
     attended = (window + read).astype(jnp.bfloat16).reshape(count, inner_here)
-    w_output = lax.optimization_barrier((w_output, query_raw))[0]
+    w_output = lax.optimization_barrier((w_output, pair_raw))[0]
     w_output_rows = lax.all_gather(w_output, "wloop", axis=1, tiled=True)
     cores = lax.axis_size("heads")
     core = lax.axis_index("heads")

time: 244 us -> 236 us (0.967)
  matrix products: 49.3 us -> 40.5 us
  waiting for transfers between devices: 95.8 us -> 98.7 us
  local copies, waits for them, and re-layouts: 31.9 us -> 29 us
    unnamed x41 -> x37, local copies, waits for them, and re-layouts: 11.2 us -> 7.49 us
    ppermute x2, waiting for transfers between devices: 38.2 us -> 41.6 us  [gathered_sum(): lax.ppermute(outgoing, 'wloop', [(source, (source - step) % ways) for sou...]
    dot_general x1, matrix products: 5.26 us -> 2.33 us  [window_mix(): jnp.einsum('bihd,bjhd->bhij', queries, prior_keys, preferred_element_type...]
    dot_general x1, matrix products: 5.5 us -> 2.58 us  [window_mix(): jnp.einsum('bihd,bjhd->bhij', queries, lookup_vectors, preferred_element_...]
  transfers between devices with their start and end apart: 11 -> 11, of which waited for: 8 -> 9; matrix products, arithmetic and copies ran while one was open for 30% -> 21% of each run, Pallas kernels for 0% -> 0%
where the time goes in v4:
time: 236 us; the launch traced here: 235 us
  waiting for transfers between devices  98.7 us (42%)
  matrix products  40.5 us (17%)
  local copies, waits for them, and re-layouts  29 us (12%)
  starting transfers between devices  27.4 us (12%)
  other arithmetic  25 us (11%)
  between operations  14.5 us (6%)
    ppermute x2, waiting for transfers between devices, gathered_sum(): lax.ppermute(outgoing, 'wloop', [(source, (source - step) % ways) for sou...  41.6 us
    ppermute x5, waiting for transfers between devices, shifted(): lax.ppermute(value, axis, [(source, source + steps) for source in range(i...  40.5 us
    ppermute x5, starting transfers between devices, shifted(): lax.ppermute(value, axis, [(source, source + steps) for source in range(i...  21.1 us
    ppermute x1, waiting for transfers between devices, shards(): lax.ppermute(part, 'wloop', [(source, (source + step) % ways) for source...  11.9 us
    dot_general x2, matrix products, shards(): jnp.einsum('td,dje->jte', rows, w_keyvalue, preferred_element_type=jnp.fl...  11.7 us
    dot_general x2, matrix products, output_share(): jnp.dot(attended, lax.dynamic_slice_in_dim(w_output_rows, index * share,...  8.32 us
    unnamed x37, local copies, waits for them, and re-layouts  7.49 us
    dot_general x2, matrix products, shards(): jnp.dot(rows, w_query, preferred_element_type=jnp.float32)  6.38 us
  transfers between devices with their start and end apart: 11, of which 9 were waited for; matrix products, arithmetic and copies ran while one was open for 21% of the time, Pallas kernels for 0%

profile of v4, /device:TPU:0, one launch (start us, length us, event | category | flops | bytes accessed | tf_op | source)
XLA Modules:
  0.0 235.2 jit_solution(1215804035298828218)
XLA Ops:
  12.6 3.0 %collective-permute-start.1 = (bf16[256,1024]{1,0:T(8,128)(2,1)S(1)}, bf16[256,1024]{1,0:T(8,128)(2,1)S(1)}, u32[]{:S(2)}, u32[]{:S(2)}) collective-permute-start(bf16[256,1024]{1,0:T(8,128)(2,1)S(1)} %dynamic-slice_bitcast_fusion), channel_id=1, source_target_pairs={{0,2},{2,0},{1,3},{3,1},{4,6},{6,4},{5,7},{7,5},{8,10},{10,8},{9,1... | collective-permute-start | bytes 1572872 | tf_op jit(solution)/shard_map/ppermute | solution.py:77
  15.6 11.9 %collective-permute-done.1 = bf16[256,1024]{1,0:T(8,128)(2,1)S(1)} collective-permute-done((bf16[256,1024]{1,0:T(8,128)(2,1)S(1)}, bf16[256,1024]{1,0:T(8,128)(2,1)S(1)}, u32[]{:S(2)}, u32[]{:S(2)}) %collective-permute-start.1) | collective-permute-done | bytes 524320 | tf_op jit(solution)/shard_map/ppermute | solution.py:77
  32.6 6.3 %convert_bitcast_fusion = bf16[2,512,1024]{2,1,0:T(8,128)(2,1)} fusion(bf16[1024,2,1024]{2,1,0:T(2,128)(2,1)} %param.12, bf16[512,1024]{1,0:T(8,128)(2,1)S(1)} %bitcast_select_fusion), kind=kOutput, calls=%fused_computation.43 | convolution fusion | flops 2148532224 | bytes 7340032 | tf_op jit(solution)/shard_map/td,dje->jte/dot_general | solution.py:100
  45.4 41.6 %collective-permute-done.3 = bf16[2,512,1024]{2,1,0:T(8,128)(2,1)} collective-permute-done((bf16[2,512,1024]{2,1,0:T(8,128)(2,1)}, bf16[2,512,1024]{2,1,0:T(8,128)(2,1)}, u32[]{:S(2)}, u32[]{:S(2)}) %collective-permute-start.3) | collective-permute-done | bytes 2097184 | tf_op jit(solution)/shard_map/ppermute | solution.py:91
  86.9 5.3 %bitcast_add_fusion = f32[2,512,1024]{2,1,0:T(8,128)S(1)} fusion(bf16[2,512,1024]{2,1,0:T(8,128)(2,1)} %collective-permute-done.3, bf16[1024,2,1024]{2,1,0:T(2,128)(2,1)} %param.12, bf16[1,512,2048]{2,1,0:T(8,128)(2,1)S(1)} %copy-done.6, s32[]{:T(128)S(6)} %select_n.80), kind=kOutput, calls=%fused_computation.15 | convolution fusion | flops 2149580800 | bytes 11534340 | tf_op jit(solution)/shard_map/td,dje->jte/dot_general | solution.py:100
  100.2 2.9 %copy.84 = f32[1,512,1024]{2,1,0:T(8,128)} copy(f32[1,512,1024]{1,2,0:T(8,128)} %bitcast.115) | data formatting | bytes 4194304 | tf_op jit(solution)/shard_map/mul | solution.py:18
  103.2 4.6 %multiply_convert_fusion = (bf16[1,512,1024]{2,1,0:T(8,128)(2,1)}, f32[1,512,1024]{2,1,0:T(8,128)}) fusion(f32[1,512,1024]{2,1,0:T(8,128)} %copy.84, f32[2,512,1024]{2,1,0:T(8,128)} %copy-done.3), kind=kLoop, calls=%fused_computation.35 | loop fusion | flops 1048576 | bytes 7340032 | tf_op jit(solution)/shard_map/convert_element_type | solution.py:108
  107.8 4.7 %collective-permute-start.5 = (bf16[1,512,1024]{2,1,0:T(8,128)(2,1)}, bf16[1,512,1024]{2,1,0:T(8,128)(2,1)}, u32[]{:S(2)}, u32[]{:S(2)}) collective-permute-start(bf16[1,512,1024]{2,1,0:T(8,128)(2,1)} %get-tuple-element.65), channel_id=1, source_target_pairs={{0,4},{4,8},{8,12},{1,5},{5,9},{9,13},{2,6},{6,10},{10,14},{3,7},{... | collective-permute-start | bytes 3145736 | tf_op jit(solution)/shard_map/ppermute | solution.py:14
  112.5 3.5 %collective-permute-start.6 = (bf16[1,512,1024]{2,1,0:T(8,128)(2,1)}, bf16[1,512,1024]{2,1,0:T(8,128)(2,1)}, u32[]{:S(2)}, u32[]{:S(2)}) collective-permute-start(bf16[1,512,1024]{2,1,0:T(8,128)(2,1)} %slice.55), channel_id=1, source_target_pairs={{0,4},{4,8},{8,12},{1,5},{5,9},{9,13},{2,6},{6,10},{10,14},{3,7},{... | collective-permute-start | bytes 3145736 | tf_op jit(solution)/shard_map/ppermute | solution.py:14
  116.3 2.2 convolution_convert_fusion
  118.5 2.3 copy.86
  122.3 2.9 %copy.83 = f32[1,512,1024]{1,2,0:T(8,128)} copy(f32[1,512,1024]{2,1,0:T(8,128)} %get-tuple-element.66) | data formatting | bytes 4194304 | tf_op jit(solution)/shard_map/reshape;squeeze | solution.py:108
  125.2 3.0 %fusion.38 = f32[1,8,128,128]{3,2,1,0:T(8,128)S(1)} fusion(bf16[512,8,128]{0,2,1:T(8,128)(2,1)} %bitcast.116, f32[512,8]{0,1:T(8,128)S(1)} %fusion.57, f32[512,8,128]{0,2,1:T(8,128)} %bitcast.111, f32[512,8]{0,1:T(8,128)S(1)} %add_rsqrt_fusion), kind=kOutput, calls=%fused_computation.48 | convolution fusion | flops 807403520 | bytes 3702784 | tf_op jit(solution)/shard_map/bht,bthd,bthe->bhde/dot_general | solution.py:125
  129.2 6.2 %collective-permute-done.5 = bf16[1,512,1024]{2,1,0:T(8,128)(2,1)} collective-permute-done((bf16[1,512,1024]{2,1,0:T(8,128)(2,1)}, bf16[1,512,1024]{2,1,0:T(8,128)(2,1)}, u32[]{:S(2)}, u32[]{:S(2)}) %collective-permute-start.5) | collective-permute-done | bytes 1048608 | tf_op jit(solution)/shard_map/ppermute | solution.py:14
  135.3 20.8 %collective-permute-done.6 = bf16[1,512,1024]{2,1,0:T(8,128)(2,1)} collective-permute-done((bf16[1,512,1024]{2,1,0:T(8,128)(2,1)}, bf16[1,512,1024]{2,1,0:T(8,128)(2,1)}, u32[]{:S(2)}, u32[]{:S(2)}) %collective-permute-start.6) | collective-permute-done | bytes 1048608 | tf_op jit(solution)/shard_map/ppermute | solution.py:14
  156.1 32.1 %while.11 = (s32[]{:T(128)}, f32[1,8,129,128]{3,2,1,0:T(8,128)S(1)}, f32[1,8,129,128]{3,2,1,0:T(8,128)S(1)}, f32[1,8,129,128]{3,2,1,0:T(8,128)}, s32[]{:T(128)}, /*index=5*/s32[]{:T(128)}) while((s32[]{:T(128)}, f32[1,8,129,128]{3,2,1,0:T(8,128)S(1)}, f32[1,8,129,128]{3,2,1,0:T(8,128)S(1)}, f32[1,8,129,128]{3,2,1,0:T(8,128)}, ...), condition=%wide.region_9.10_spmd.clone, body=%wide.region_8.9_spmd.clone.sunk | while | flops 660483 | bytes 3698807 | solution.py:152
  158.0 4.4 %collective-permute-start = (bf16[1,8,129,128]{3,2,1,0:T(8,128)(2,1)}, bf16[1,8,129,128]{3,2,1,0:T(8,128)(2,1)S(1)}, u32[]{:S(2)}, u32[]{:S(2)}) collective-permute-start(bf16[1,8,129,128]{3,2,1,0:T(8,128)(2,1)} %fusion.88), channel_id=1, source_target_pairs={{0,4},{4,8},{8,12},{1,5},{5,9},{9,13},{2,6},{6,10},{10,14},{3,7},{... | collective-permute-start | bytes 792584 | tf_op jit(solution)/shard_map/while/body/eval_jaxpr/ppermute | solution.py:14
  162.4 4.8 %collective-permute-done = bf16[1,8,129,128]{3,2,1,0:T(8,128)(2,1)S(1)} collective-permute-done((bf16[1,8,129,128]{3,2,1,0:T(8,128)(2,1)}, bf16[1,8,129,128]{3,2,1,0:T(8,128)(2,1)S(1)}, u32[]{:S(2)}, u32[]{:S(2)}) %collective-permute-start) | collective-permute-done | bytes 264224 | tf_op jit(solution)/shard_map/while/body/eval_jaxpr/ppermute | solution.py:14
  169.0 4.3 %collective-permute-start = (bf16[1,8,129,128]{3,2,1,0:T(8,128)(2,1)}, bf16[1,8,129,128]{3,2,1,0:T(8,128)(2,1)S(1)}, u32[]{:S(2)}, u32[]{:S(2)}) collective-permute-start(bf16[1,8,129,128]{3,2,1,0:T(8,128)(2,1)} %fusion.88), channel_id=1, source_target_pairs={{0,4},{4,8},{8,12},{1,5},{5,9},{9,13},{2,6},{6,10},{10,14},{3,7},{... | collective-permute-start | bytes 792584 | tf_op jit(solution)/shard_map/while/body/eval_jaxpr/ppermute | solution.py:14
  173.3 4.3 %collective-permute-done = bf16[1,8,129,128]{3,2,1,0:T(8,128)(2,1)S(1)} collective-permute-done((bf16[1,8,129,128]{3,2,1,0:T(8,128)(2,1)}, bf16[1,8,129,128]{3,2,1,0:T(8,128)(2,1)S(1)}, u32[]{:S(2)}, u32[]{:S(2)}) %collective-permute-start) | collective-permute-done | bytes 264224 | tf_op jit(solution)/shard_map/while/body/eval_jaxpr/ppermute | solution.py:14
  179.6 4.3 %collective-permute-start = (bf16[1,8,129,128]{3,2,1,0:T(8,128)(2,1)}, bf16[1,8,129,128]{3,2,1,0:T(8,128)(2,1)S(1)}, u32[]{:S(2)}, u32[]{:S(2)}) collective-permute-start(bf16[1,8,129,128]{3,2,1,0:T(8,128)(2,1)} %fusion.88), channel_id=1, source_target_pairs={{0,4},{4,8},{8,12},{1,5},{5,9},{9,13},{2,6},{6,10},{10,14},{3,7},{... | collective-permute-start | bytes 792584 | tf_op jit(solution)/shard_map/while/body/eval_jaxpr/ppermute | solution.py:14
  183.9 4.3 %collective-permute-done = bf16[1,8,129,128]{3,2,1,0:T(8,128)(2,1)S(1)} collective-permute-done((bf16[1,8,129,128]{3,2,1,0:T(8,128)(2,1)}, bf16[1,8,129,128]{3,2,1,0:T(8,128)(2,1)S(1)}, u32[]{:S(2)}, u32[]{:S(2)}) %collective-permute-start) | collective-permute-done | bytes 264224 | tf_op jit(solution)/shard_map/while/body/eval_jaxpr/ppermute | solution.py:14
  188.3 4.8 %copy.79 = f32[1,8,129,128]{1,3,2,0:T(8,128)} copy(f32[1,8,129,128]{3,2,1,0:T(8,128)S(1)} %get-tuple-element.36) | data formatting | bytes 1056768 | tf_op jit(solution)/shard_map/while | solution.py:152
  194.4 4.1 %multiply_bitcast_fusion.1 = (f32[64,8,8,128]{3,1,2,0:T(8,128)S(1)}, f32[64,8,8,128]{3,2,1,0:T(8,128)}) fusion(bf16[512,1024]{1,0:T(8,128)(2,1)} %collective-permute-done.4, bf16[1024,1024]{1,0:T(8,128)(2,1)S(1)} %copy-done, bf16[1,512,2048]{2,1,0:T(8,128)(2,1)} %copy-done.5, s32[]{:T(128)S(6)} %select_n.80), kind=kOutput, calls=%fused_computation.41 | convolution fusion | flops 1075314688 | bytes 8388612 | tf_op jit(solution)/shard_map/dot_general | solution.py:105
  199.7 2.6 %copy.90 = bf16[64,8,8,128]{3,2,1,0:T(8,128)(2,1)} copy(bf16[64,8,8,128]{3,1,2,0:T(8,128)(2,1)} %bitcast.50) | data formatting | bytes 2097152
  205.1 2.3 fusion.3
  207.5 2.6 %fusion.2 = (f32[8,512]{1,0:T(8,128)S(1)}, f32[8,512,512]{1,2,0:T(8,128)S(1)}) fusion(pred[512,512]{0,1:T(8,128)(4,1)S(1)} %copy-done.13, bf16[512,8,128]{2,0,1:T(8,128)(2,1)S(1)} %fusion.13, f32[512,8,128]{0,2,1:T(8,128)S(1)} %bitcast.112, f32[512,8]{0,1:T(8,128)S(1)} %add_rsqrt_fusion), kind=kOutput, calls=%fused_computation.8 | convolution fusion | flops 544206848 | bytes 11829248 | tf_op jit(solution)/shard_map/bihd,bjhd->bhij/dot_general | solution.py:23
  210.8 2.4 %fusion.7 = f32[8,128,512]{2,1,0:T(8,128)S(1)} fusion(bf16[512,8,128]{0,2,1:T(8,128)(2,1)S(1)} %bitcast.117, f32[8,512,512]{1,2,0:T(8,128)S(1)} %get-tuple-element.70, f32[8,512]{1,0:T(8,128)S(1)} %add.155, pred[512,512]{0,1:T(8,128)(4,1)S(1)} %copy-done.13), kind=kOutput, calls=%fused_computation.16 | convolution fusion | flops 545259520 | bytes 11812864 | tf_op jit(solution)/shard_map/bhij,bjhd->bihd/dot_general | solution.py:38
  213.2 2.6 %fusion.8 = f32[8,128,512]{2,1,0:T(8,128)S(1)} fusion(bf16[512,8,128]{0,2,1:T(8,128)(2,1)S(1)} %bitcast.118, f32[8,512,512]{1,2,0:T(8,128)S(1)} %get-tuple-element.72, f32[8,512]{1,0:T(8,128)S(1)} %add.155, pred[512,512]{0,1:T(8,128)(4,1)S(1)} %copy-done.12), kind=kOutput, calls=%fused_computation.17 | convolution fusion | flops 545259520 | bytes 11812864 | tf_op jit(solution)/shard_map/bhij,bjhd->bihd/dot_general | solution.py:40
  217.0 3.8 %fusion.29 = bf16[512,1024]{1,0:T(8,128)(2,1)} fusion(bf16[512,1024]{0,1:T(8,128)(2,1)S(1)} %bitcast.120, bf16[1024,2048]{1,0:T(8,128)(2,1)} %all-gather.2.cloned.1.call-done, s32[]{:T(128)S(6)} %select_n.94), kind=kOutput, calls=%fused_computation.44 | convolution fusion | flops 1074266112 | bytes 4194308 | tf_op jit(solution)/shard_map/dot_general | solution.py:182
  220.8 3.0 %collective-permute-done.7 = bf16[512,1024]{1,0:T(8,128)(2,1)} collective-permute-done((bf16[512,1024]{1,0:T(8,128)(2,1)}, bf16[512,1024]{1,0:T(8,128)(2,1)}, u32[]{:S(2)}, u32[]{:S(2)}) %collective-permute-start.7) | collective-permute-done | bytes 1048608 | tf_op jit(solution)/shard_map/ppermute | solution.py:189
  223.8 4.5 %fusion.35 = bf16[1,512,1024]{2,1,0:T(8,128)(2,1)} fusion(bf16[512,1024]{1,0:T(8,128)(2,1)} %collective-permute-done.7, bf16[512,1024]{0,1:T(8,128)(2,1)S(1)} %bitcast.121, bf16[1024,2048]{1,0:T(8,128)(2,1)} %all-gather.2.cloned.1.call-done, s32[]{:T(128)S(6)} %select_n.79, bf16[1,512,2048]{2,1,0:T(8,128)(2,1)} %param.9), kind=kOutput, calls=%fused_computation.47 | convolution fusion | flops 1076363264 | bytes 6292480 | tf_op jit(solution)/shard_map/dot_general | solution.py:182
  (95 shorter events, 40.1 us)
Async XLA Ops:
  6.5 109.7 %copy-start = (bf16[1024,1024]{1,0:T(8,128)(2,1)S(1)}, bf16[1024,1024]{1,0:T(8,128)(2,1)}, u32[]{:S(2)}) copy-start(bf16[1024,1024]{1,0:T(8,128)(2,1)} %param.11) | copy-start | bytes 6291460
  6.5 2.3 copy-start.16
  6.5 210.5 %all-gather.2.cloned.1.call-start = ((), (), s32[]{:S(2)}) async-start(), calls=%async_computation | async-start | bytes 6291456 | tf_op jit(solution)/shard_map/all_gather | solution.py:176
  11.0 1.3 copy-start.5
  12.6 15.0 %collective-permute-start.1 = (bf16[256,1024]{1,0:T(8,128)(2,1)S(1)}, bf16[256,1024]{1,0:T(8,128)(2,1)S(1)}, u32[]{:S(2)}, u32[]{:S(2)}) collective-permute-start(bf16[256,1024]{1,0:T(8,128)(2,1)S(1)} %dynamic-slice_bitcast_fusion), channel_id=1, source_target_pairs={{0,2},{2,0},{1,3},{3,1},{4,6},{6,4},{5,7},{7,5},{8,10},{10,8},{9,1... | collective-permute-start | bytes 1572872 | tf_op jit(solution)/shard_map/ppermute | solution.py:77
  27.5 1.9 collective-permute-start.2
  32.6 6.4 %copy-start.8 = (bf16[512,1024]{1,0:T(8,128)(2,1)}, bf16[512,1024]{1,0:T(8,128)(2,1)S(1)}, u32[]{:S(2)}) copy-start(bf16[512,1024]{1,0:T(8,128)(2,1)S(1)} %bitcast_select_fusion) | copy-start | bytes 3145732
  32.6 8.8 %copy-start.15 = (f32[1,8,512]{2,1,0:T(8,128)S(1)}, f32[1,8,512]{2,1,0:T(8,128)}, u32[]{:S(2)}) copy-start(f32[1,8,512]{2,1,0:T(8,128)} %param.14) | copy-start | bytes 49156
  38.9 48.0 %collective-permute-start.3 = (bf16[2,512,1024]{2,1,0:T(8,128)(2,1)}, bf16[2,512,1024]{2,1,0:T(8,128)(2,1)}, u32[]{:S(2)}, u32[]{:S(2)}) collective-permute-start(bf16[2,512,1024]{2,1,0:T(8,128)(2,1)} %convert_bitcast_fusion), channel_id=1, source_target_pairs={{0,2},{2,0},{1,3},{3,1},{4,6},{6,4},{5,7},{7,5},{8,10},{10,8},{9,1... | collective-permute-start | bytes 6291464 | tf_op jit(solution)/shard_map/ppermute | solution.py:91
  42.7 44.2 %copy-start.6 = (bf16[1,512,2048]{2,1,0:T(8,128)(2,1)S(1)}, bf16[1,512,2048]{2,1,0:T(8,128)(2,1)}, u32[]{:S(2)}) copy-start(bf16[1,512,2048]{2,1,0:T(8,128)(2,1)} %copy-done.5) | copy-start | bytes 6291460
  92.3 2.2 copy-start.3
  103.2 13.1 %copy-start.9 = (bf16[512,1024]{1,0:T(8,128)(2,1)S(1)}, bf16[512,1024]{1,0:T(8,128)(2,1)}, u32[]{:S(2)}) copy-start(bf16[512,1024]{1,0:T(8,128)(2,1)} %copy-done.8) | copy-start | bytes 3145732
  107.8 27.6 %collective-permute-start.5 = (bf16[1,512,1024]{2,1,0:T(8,128)(2,1)}, bf16[1,512,1024]{2,1,0:T(8,128)(2,1)}, u32[]{:S(2)}, u32[]{:S(2)}) collective-permute-start(bf16[1,512,1024]{2,1,0:T(8,128)(2,1)} %get-tuple-element.65), channel_id=1, source_target_pairs={{0,4},{4,8},{8,12},{1,5},{5,9},{9,13},{2,6},{6,10},{10,14},{3,7},{... | collective-permute-start | bytes 3145736 | tf_op jit(solution)/shard_map/ppermute | solution.py:14
  112.5 43.6 %collective-permute-start.6 = (bf16[1,512,1024]{2,1,0:T(8,128)(2,1)}, bf16[1,512,1024]{2,1,0:T(8,128)(2,1)}, u32[]{:S(2)}, u32[]{:S(2)}) collective-permute-start(bf16[1,512,1024]{2,1,0:T(8,128)(2,1)} %slice.55), channel_id=1, source_target_pairs={{0,4},{4,8},{8,12},{1,5},{5,9},{9,13},{2,6},{6,10},{10,14},{3,7},{... | collective-permute-start | bytes 3145736 | tf_op jit(solution)/shard_map/ppermute | solution.py:14
  120.8 73.6 %collective-permute-start.4 = (bf16[512,1024]{1,0:T(8,128)(2,1)}, bf16[512,1024]{1,0:T(8,128)(2,1)}, u32[]{:S(2)}, u32[]{:S(2)}) collective-permute-start(bf16[512,1024]{1,0:T(8,128)(2,1)} %convolution_convert_fusion), channel_id=1, source_target_pairs={{0,2},{2,0},{1,3},{3,1},{4,6},{6,4},{5,7},{7,5},{8,10},{10,8},{9,1... | collective-permute-start | bytes 3145736 | tf_op jit(solution)/shard_map/ppermute | solution.py:91
  158.0 9.2 %collective-permute-start = (bf16[1,8,129,128]{3,2,1,0:T(8,128)(2,1)}, bf16[1,8,129,128]{3,2,1,0:T(8,128)(2,1)S(1)}, u32[]{:S(2)}, u32[]{:S(2)}) collective-permute-start(bf16[1,8,129,128]{3,2,1,0:T(8,128)(2,1)} %fusion.88), channel_id=1, source_target_pairs={{0,4},{4,8},{8,12},{1,5},{5,9},{9,13},{2,6},{6,10},{10,14},{3,7},{... | collective-permute-start | bytes 792584 | tf_op jit(solution)/shard_map/while/body/eval_jaxpr/ppermute | solution.py:14
  169.0 8.6 %collective-permute-start = (bf16[1,8,129,128]{3,2,1,0:T(8,128)(2,1)}, bf16[1,8,129,128]{3,2,1,0:T(8,128)(2,1)S(1)}, u32[]{:S(2)}, u32[]{:S(2)}) collective-permute-start(bf16[1,8,129,128]{3,2,1,0:T(8,128)(2,1)} %fusion.88), channel_id=1, source_target_pairs={{0,4},{4,8},{8,12},{1,5},{5,9},{9,13},{2,6},{6,10},{10,14},{3,7},{... | collective-permute-start | bytes 792584 | tf_op jit(solution)/shard_map/while/body/eval_jaxpr/ppermute | solution.py:14
  179.6 8.6 %collective-permute-start = (bf16[1,8,129,128]{3,2,1,0:T(8,128)(2,1)}, bf16[1,8,129,128]{3,2,1,0:T(8,128)(2,1)S(1)}, u32[]{:S(2)}, u32[]{:S(2)}) collective-permute-start(bf16[1,8,129,128]{3,2,1,0:T(8,128)(2,1)} %fusion.88), channel_id=1, source_target_pairs={{0,4},{4,8},{8,12},{1,5},{5,9},{9,13},{2,6},{6,10},{10,14},{3,7},{... | collective-permute-start | bytes 792584 | tf_op jit(solution)/shard_map/while/body/eval_jaxpr/ppermute | solution.py:14
  199.7 4.2 %copy-start.7 = (f32[64,8,8,128]{3,2,1,0:T(8,128)S(1)}, f32[64,8,8,128]{3,2,1,0:T(8,128)}, u32[]{:S(2)}) copy-start(f32[64,8,8,128]{3,2,1,0:T(8,128)} %get-tuple-element.68) | copy-start | bytes 6291460
  203.9 1.2 copy-start.11
  203.9 1.3 copy-start.12
  205.1 2.3 copy-start.2
  205.1 2.4 %copy-start.13 = (pred[512,512]{0,1:T(8,128)(4,1)S(1)}, pred[512,512]{0,1:T(8,128)(4,1)}, u32[]{:S(2)}) copy-start(pred[512,512]{0,1:T(8,128)(4,1)} %iota_compare_fusion.1) | copy-start | bytes 786436
  207.5 3.3 %copy-start.4 = (bf16[1,512,1024]{1,2,0:T(8,128)(2,1)S(1)}, bf16[1,512,1024]{1,2,0:T(8,128)(2,1)}, u32[]{:S(2)}) copy-start(bf16[1,512,1024]{1,2,0:T(8,128)(2,1)} %copy.86) | copy-start | bytes 3145732
  213.2 2.6 %copy-start.10 = (f32[1,8,129,128]{2,3,1,0:T(8,128)S(1)}, f32[1,8,129,128]{2,3,1,0:T(8,128)}, u32[]{:S(2)}) copy-start(f32[1,8,129,128]{2,3,1,0:T(8,128)} %copy.78) | copy-start | bytes 1585156
  213.2 2.6 %copy-start.14 = (f32[512,8]{0,1:T(8,128)S(1)}, f32[512,8]{0,1:T(8,128)}, u32[]{:S(2)}) copy-start(f32[512,8]{0,1:T(8,128)} %get-tuple-element.61) | copy-start | bytes 49156
  220.8 3.0 %collective-permute-start.7 = (bf16[512,1024]{1,0:T(8,128)(2,1)}, bf16[512,1024]{1,0:T(8,128)(2,1)}, u32[]{:S(2)}, u32[]{:S(2)}) collective-permute-start(bf16[512,1024]{1,0:T(8,128)(2,1)} %fusion.29), channel_id=1, source_target_pairs={{0,1},{1,0},{2,3},{3,2},{4,5},{5,4},{6,7},{7,6},{8,9},{9,8},{10,11... | collective-permute-start | bytes 3145736 | tf_op jit(solution)/shard_map/ppermute | solution.py:189
  220.8 7.5 %copy-start.1 = (bf16[1024,1024]{1,0:T(8,128)(2,1)S(1)}, bf16[1024,1024]{1,0:T(8,128)(2,1)}, u32[]{:S(2)}) copy-start(bf16[1024,1024]{1,0:T(8,128)(2,1)} %param.11) | copy-start | bytes 6291460
Sparse Core Ops, SparseCore 0:
  125.3 64.6 all-gather.1

commit v5 on v4

--- a/solution.py
+++ b/solution.py
@@ -149,9 +149,9 @@
         )
 
     local_both, prior_keys, prior_values = lax.optimization_barrier((local_both, prior_keys, prior_values))
-    entering_both = lax.fori_loop(
-        0, lax.axis_size("seq") - 1, relay_turn, jnp.zeros_like(local_both)
-    )
+    entering_both = jnp.zeros_like(local_both)
+    for turn in range(lax.axis_size("seq") - 1):
+        entering_both = relay_turn(turn, entering_both)
     entering = entering_both[:, :, :head_dim, :]
     entering_mass = entering_both[:, :, head_dim, 0]
     entering = entering * keep[:, None, None, None]

time: 236 us -> 217 us (0.919)
  waiting for transfers between devices: 98.7 us -> 67.5 us
  matrix products: 40.5 us -> 51.5 us
  local copies, waits for them, and re-layouts: 29 us -> 33.1 us
    ppermute x5, waiting for transfers between devices: 40.5 us -> 11.5 us  [shifted(): lax.ppermute(value, axis, [(source, source + steps) for source in range(i...]
    another operation x2 -> x3, other arithmetic: 1.18 us -> 9.5 us
    another operation x2 -> x3, local copies, waits for them, and re-layouts: 1.49 us -> 8.28 us
    while x2 -> x0, local copies, waits for them, and re-layouts: 6.1 us -> none  [shards(): lax.fori_loop(0, lax.axis_size('seq') - 1, relay_turn, jnp.zeros_like(loc...]
    convert_element_type x3, other arithmetic: 5.52 us -> 0.21 us  [relay_turn(): (factor_both * carry + local_both).astype(jnp.bfloat16)]
    slice x1 -> x3, local copies, waits for them, and re-layouts: 0.16 us -> 4.95 us  [the longest x2 4.79 us: shards(): entering = entering_both[:, :, :head_dim, :]]
    dot_general x1, matrix products: 2.59 us -> 7.05 us  [window_mix(): jnp.einsum('bhij,bjhd->bihd', prior_p, prior_values, preferred_element_ty...]
    dot_general x1, matrix products: 2.33 us -> 5.37 us  [window_mix(): jnp.einsum('bihd,bjhd->bhij', queries, prior_keys, preferred_element_type...]
  transfers between devices with their start and end apart: 11 -> 11, of which waited for: 9 -> 5; matrix products, arithmetic and copies ran while one was open for 21% -> 37% of each run, Pallas kernels for 0% -> 0%
where the time goes in v5:
time: 217 us; the launch traced here: 216 us
  waiting for transfers between devices  67.5 us (31%)
  matrix products  51.5 us (24%)
  local copies, waits for them, and re-layouts  33.1 us (15%)
  starting transfers between devices  26.2 us (12%)
  other arithmetic  23.5 us (11%)
  between operations  14.5 us (7%)
    ppermute x2, waiting for transfers between devices, gathered_sum(): lax.ppermute(outgoing, 'wloop', [(source, (source - step) % ways) for sou...  39.3 us
    ppermute x5, starting transfers between devices, shifted(): lax.ppermute(value, axis, [(source, source + steps) for source in range(i...  20 us
    ppermute x1, waiting for transfers between devices, shards(): lax.ppermute(part, 'wloop', [(source, (source + step) % ways) for source...  11.9 us
    ppermute x5, waiting for transfers between devices, shifted(): lax.ppermute(value, axis, [(source, source + steps) for source in range(i...  11.5 us
    dot_general x2, matrix products, shards(): jnp.einsum('td,dje->jte', rows, w_keyvalue, preferred_element_type=jnp.fl...  10.4 us
    another operation x3, other arithmetic  9.5 us
    dot_general x2, matrix products, output_share(): jnp.dot(attended, lax.dynamic_slice_in_dim(w_output_rows, index * share,...  8.32 us
    another operation x3, local copies, waits for them, and re-layouts  8.28 us
  transfers between devices with their start and end apart: 11, of which 5 were waited for; matrix products, arithmetic and copies ran while one was open for 37% of the time, Pallas kernels for 0%

profile of v5, /device:TPU:0, one launch (start us, length us, event | category | flops | bytes accessed | tf_op | source)
XLA Modules:
  0.0 216.4 jit_solution(1277557037998152807)
XLA Ops:
  6.5 2.2 %fusion.2 = f32[512]{0:T(512)S(1)} fusion(bf16[1,512,2048]{2,1,0:T(8,128)(2,1)} %param.7), kind=kLoop, calls=%fused_computation.10 | loop fusion | flops 3145216 | bytes 2099200 | tf_op jit(solution)/shard_map/reduce_sum | solution.py:18
  11.1 3.0 %collective-permute-start = (bf16[256,1024]{1,0:T(8,128)(2,1)S(1)}, bf16[256,1024]{1,0:T(8,128)(2,1)S(1)}, u32[]{:S(2)}, u32[]{:S(2)}) collective-permute-start(bf16[256,1024]{1,0:T(8,128)(2,1)S(1)} %dynamic-slice_bitcast_fusion), channel_id=1, source_target_pairs={{0,2},{2,0},{1,3},{3,1},{4,6},{6,4},{5,7},{7,5},{8,10},{10,8},{9,1... | collective-permute-start | bytes 1572872 | tf_op jit(solution)/shard_map/ppermute | solution.py:77
  14.1 11.9 %collective-permute-done = bf16[256,1024]{1,0:T(8,128)(2,1)S(1)} collective-permute-done((bf16[256,1024]{1,0:T(8,128)(2,1)S(1)}, bf16[256,1024]{1,0:T(8,128)(2,1)S(1)}, u32[]{:S(2)}, u32[]{:S(2)}) %collective-permute-start) | collective-permute-done | bytes 524320 | tf_op jit(solution)/shard_map/ppermute | solution.py:77
  29.0 1.8 gather_fusion
  31.1 6.3 %convert_bitcast_fusion = bf16[2,512,1024]{2,1,0:T(8,128)(2,1)} fusion(bf16[1024,2,1024]{2,1,0:T(2,128)(2,1)} %param.10, bf16[512,1024]{1,0:T(8,128)(2,1)S(1)} %bitcast_select_fusion), kind=kOutput, calls=%fused_computation.41 | convolution fusion | flops 2148532224 | bytes 7340032 | tf_op jit(solution)/shard_map/td,dje->jte/dot_general | solution.py:100
  42.5 3.7 %convolution_convert_fusion = bf16[512,1024]{1,0:T(8,128)(2,1)} fusion(bf16[512,1024]{1,0:T(8,128)(2,1)} %copy-done.13, bf16[1024,1024]{1,0:T(8,128)(2,1)S(1)} %copy-done), kind=kOutput, calls=%fused_computation.43 | convolution fusion | flops 1074266112 | bytes 4194304 | tf_op jit(solution)/shard_map/dot_general | solution.py:105
  46.1 39.3 %collective-permute-done.2 = bf16[2,512,1024]{2,1,0:T(8,128)(2,1)} collective-permute-done((bf16[2,512,1024]{2,1,0:T(8,128)(2,1)}, bf16[2,512,1024]{2,1,0:T(8,128)(2,1)}, u32[]{:S(2)}, u32[]{:S(2)}) %collective-permute-start.2) | collective-permute-done | bytes 2097184 | tf_op jit(solution)/shard_map/ppermute | solution.py:91
  85.4 4.1 %bitcast_add_fusion = f32[2,512,1024]{2,1,0:T(8,128)S(1)} fusion(bf16[2,512,1024]{2,1,0:T(8,128)(2,1)} %collective-permute-done.2, bf16[1024,2,1024]{2,1,0:T(2,128)(2,1)S(1)} %copy-done.17, bf16[1,512,2048]{2,1,0:T(8,128)(2,1)S(1)} %copy-done.8, s32[]{:T(128)S(6)} %select_n.80), kind=kOutput, calls=%fused_computation.13 | convolution fusion | flops 2149580800 | bytes 11534340 | tf_op jit(solution)/shard_map/td,dje->jte/dot_general | solution.py:100
  91.8 4.7 %collective-permute-start.5 = (bf16[1,512,1024]{2,1,0:T(8,128)(2,1)}, bf16[1,512,1024]{2,1,0:T(8,128)(2,1)}, u32[]{:S(2)}, u32[]{:S(2)}) collective-permute-start(bf16[1,512,1024]{2,1,0:T(8,128)(2,1)} %slice.43), channel_id=1, source_target_pairs={{0,4},{4,8},{8,12},{1,5},{5,9},{9,13},{2,6},{6,10},{10,14},{3,7},{... | collective-permute-start | bytes 3145736 | tf_op jit(solution)/shard_map/ppermute | solution.py:14
  98.0 1.8 copy.108
  99.8 2.2 %reduce_sum.56 = f32[512,8]{1,0:T(8,128)S(1)} reduce(f32[512,8,128]{2,1,0:T(8,128)} %bitcast.113, f32[]{:T(128)} %constant.92.clone.1), dimensions={2}, to_apply=%region_2.3 | reduce | flops 520192 | bytes 2113540 | tf_op jit(solution)/shard_map/reduce_sum | solution.py:18
  103.7 3.0 %copy.102 = f32[1,512,1024]{2,1,0:T(8,128)} copy(f32[1,512,1024]{1,2,0:T(8,128)} %bitcast.114) | data formatting | bytes 4194304 | tf_op jit(solution)/shard_map/mul | solution.py:18
  106.7 4.6 %multiply_convert_fusion = (bf16[1,512,1024]{2,1,0:T(8,128)(2,1)}, f32[1,512,1024]{2,1,0:T(8,128)}) fusion(f32[1,512,1024]{2,1,0:T(8,128)} %copy.102, f32[2,512,1024]{2,1,0:T(8,128)} %copy-done.4), kind=kLoop, calls=%fused_computation.33 | loop fusion | flops 1048576 | bytes 7340032 | tf_op jit(solution)/shard_map/convert_element_type | solution.py:108
  111.3 3.5 %collective-permute-start.4 = (bf16[1,512,1024]{2,1,0:T(8,128)(2,1)}, bf16[1,512,1024]{2,1,0:T(8,128)(2,1)}, u32[]{:S(2)}, u32[]{:S(2)}) collective-permute-start(bf16[1,512,1024]{2,1,0:T(8,128)(2,1)} %get-tuple-element.19), channel_id=1, source_target_pairs={{0,4},{4,8},{8,12},{1,5},{5,9},{9,13},{2,6},{6,10},{10,14},{3,7},{... | collective-permute-start | bytes 3145736 | tf_op jit(solution)/shard_map/ppermute | solution.py:14
  116.6 3.2 %copy.101 = f32[1,512,1024]{1,2,0:T(8,128)} copy(f32[1,512,1024]{2,1,0:T(8,128)} %get-tuple-element.20) | data formatting | bytes 4194304 | tf_op jit(solution)/shard_map/reshape;squeeze | solution.py:108
  119.9 3.2 %fusion.36 = f32[1,8,128,128]{3,2,1,0:T(8,128)S(1)} fusion(bf16[512,8,128]{0,2,1:T(8,128)(2,1)S(1)} %bitcast.115, f32[512,8]{0,1:T(8,128)S(1)} %fusion.61, f32[512,8,128]{0,2,1:T(8,128)} %bitcast.110, f32[512,8]{0,1:T(8,128)S(1)} %add_rsqrt_fusion), kind=kOutput, calls=%fused_computation.46 | convolution fusion | flops 807403520 | bytes 3702784 | tf_op jit(solution)/shard_map/bht,bthd,bthe->bhde/dot_general | solution.py:125
  123.5 3.9 %multiply_bitcast_fusion.2 = (f32[64,8,8,128]{3,1,2,0:T(8,128)S(1)}, f32[64,8,8,128]{3,2,1,0:T(8,128)}) fusion(bf16[512,1024]{1,0:T(8,128)(2,1)} %collective-permute-done.3, bf16[1024,1024]{1,0:T(8,128)(2,1)S(1)} %copy-done, bf16[1,512,2048]{2,1,0:T(8,128)(2,1)S(1)} %copy-done.9, s32[]{:T(128)S(6)} %select_n.80), kind=kOutput, calls=%fused_computation.39 | convolution fusion | flops 1075314688 | bytes 8388612 | tf_op jit(solution)/shard_map/dot_general | solution.py:105
  128.7 11.5 %collective-permute-done.4 = bf16[1,512,1024]{2,1,0:T(8,128)(2,1)} collective-permute-done((bf16[1,512,1024]{2,1,0:T(8,128)(2,1)}, bf16[1,512,1024]{2,1,0:T(8,128)(2,1)}, u32[]{:S(2)}, u32[]{:S(2)}) %collective-permute-start.4) | collective-permute-done | bytes 1048608 | tf_op jit(solution)/shard_map/ppermute | solution.py:14
  141.9 4.5 %collective-permute-start.6 = (bf16[1,8,129,128]{3,1,2,0:T(8,128)(2,1)S(1)}, bf16[1,8,129,128]{3,1,2,0:T(8,128)(2,1)S(1)}, u32[]{:S(2)}, u32[]{:S(2)}) collective-permute-start(bf16[1,8,129,128]{3,1,2,0:T(8,128)(2,1)S(1)} %fusion.53), channel_id=1, source_target_pairs={{0,4},{4,8},{8,12},{1,5},{5,9},{9,13},{2,6},{6,10},{10,14},{3,7},{... | collective-permute-start | bytes 792584 | tf_op jit(solution)/shard_map/ppermute | solution.py:14
  147.3 2.6 %fusion = (f32[8,512]{1,0:T(8,128)S(1)}, f32[8,512,512]{1,2,0:T(8,128)S(1)}) fusion(pred[512,512]{0,1:T(8,128)(4,1)S(1)} %copy-done.14, bf16[512,8,128]{2,0,1:T(8,128)(2,1)S(1)} %fusion.11, f32[512,8,128]{0,2,1:T(8,128)S(1)} %bitcast.111, f32[512,8]{0,1:T(8,128)S(1)} %add_rsqrt_fusion), kind=kOutput, calls=%fused_computation.6 | convolution fusion | flops 544206848 | bytes 11829248 | tf_op jit(solution)/shard_map/bihd,bjhd->bhij/dot_general | solution.py:23
  149.9 5.4 %fusion.1 = (f32[8,512]{1,0:T(8,128)S(1)}, f32[8,512,512]{1,2,0:T(8,128)}) fusion(pred[512,512]{0,1:T(8,128)(4,1)S(1)} %fusion.46, bf16[512,8,128]{2,0,1:T(8,128)(2,1)S(1)} %fusion.11, bf16[512,8,128]{2,1,0:T(8,128)(2,1)S(1)} %bitcast.117), kind=kOutput, calls=%fused_computation.7 | convolution fusion | flops 543158272 | bytes 10764288 | tf_op jit(solution)/shard_map/bihd,bjhd->bhij/dot_general | solution.py:27
  155.4 3.5 %collective-permute-start.7 = (bf16[1,8,129,128]{3,1,2,0:T(8,128)(2,1)S(1)}, bf16[1,8,129,128]{3,1,2,0:T(8,128)(2,1)S(1)}, u32[]{:S(2)}, u32[]{:S(2)}) collective-permute-start(bf16[1,8,129,128]{3,1,2,0:T(8,128)(2,1)S(1)} %fusion.55), channel_id=1, source_target_pairs={{0,4},{4,8},{8,12},{1,5},{5,9},{9,13},{2,6},{6,10},{10,14},{3,7},{... | collective-permute-start | bytes 792584 | tf_op jit(solution)/shard_map/ppermute | solution.py:14
  158.9 3.5 %fusion.5 = f32[8,128,512]{2,1,0:T(8,128)} fusion(bf16[512,8,128]{0,2,1:T(8,128)(2,1)S(1)} %bitcast.116, f32[8,512,512]{1,2,0:T(8,128)S(1)} %get-tuple-element.24, f32[8,512]{1,0:T(8,128)S(1)} %add.158, pred[512,512]{0,1:T(8,128)(4,1)S(1)} %copy-done.14), kind=kOutput, calls=%fused_computation.14 | convolution fusion | flops 545259520 | bytes 11812864 | tf_op jit(solution)/shard_map/bhij,bjhd->bihd/dot_general | solution.py:38
  164.0 3.7 %collective-permute-start.8 = (bf16[1,8,129,128]{3,1,2,0:T(8,128)(2,1)S(1)}, bf16[1,8,129,128]{3,1,2,0:T(8,128)(2,1)S(1)}, u32[]{:S(2)}, u32[]{:S(2)}) collective-permute-start(bf16[1,8,129,128]{3,1,2,0:T(8,128)(2,1)S(1)} %fusion.57), channel_id=1, source_target_pairs={{0,4},{4,8},{8,12},{1,5},{5,9},{9,13},{2,6},{6,10},{10,14},{3,7},{... | collective-permute-start | bytes 792584 | tf_op jit(solution)/shard_map/ppermute | solution.py:14
  167.7 7.0 %fusion.6 = f32[8,128,512]{2,1,0:T(8,128)} fusion(bf16[512,8,128]{0,2,1:T(8,128)(2,1)S(1)} %bitcast.118, f32[8,512,512]{1,2,0:T(8,128)} %get-tuple-element.26, f32[8,512]{1,0:T(8,128)S(1)} %add.158, pred[512,512]{0,1:T(8,128)(4,1)S(1)} %fusion.46), kind=kOutput, calls=%fused_computation.15 | convolution fusion | flops 545259520 | bytes 11812864 | tf_op jit(solution)/shard_map/bhij,bjhd->bihd/dot_general | solution.py:40
  174.9 4.8 %copy.95 = f32[1,8,128,128]{1,3,2,0:T(8,128)} copy(f32[1,8,128,128]{3,1,2,0:T(8,128)S(1)} %slice.34) | data formatting | bytes 1048576 | tf_op jit(solution)/shard_map/slice | solution.py:155
  179.7 8.3 %multiply_bitcast_fusion = f32[8,128,128]{0,2,1:T(8,128)} fusion(f32[1,8,128,128]{1,3,2,0:T(8,128)} %copy.95, f32[]{:T(128)} %bitcast.27), kind=kLoop, calls=%fused_computation.1 | loop fusion | flops 131072 | bytes 1048580 | tf_op jit(solution)/shard_map/reshape.51
  188.0 6.8 %copy.96 = f32[8,128,128]{1,2,0:T(8,128)S(1)} copy(f32[8,128,128]{0,2,1:T(8,128)} %multiply_bitcast_fusion) | data formatting | bytes 1048576 | tf_op jit(solution)/shard_map/reshape.51
  194.8 3.4 %fusion.14 = bf16[1,512,8,128]{1,3,2,0:T(8,128)(2,1)S(1)} fusion(f32[8,128,512]{2,1,0:T(8,128)} %fusion.5, f32[8,128,512]{2,1,0:T(8,128)} %fusion.6, f32[8,128,128]{1,2,0:T(8,128)S(1)} %copy.96, bf16[512,8,128]{2,0,1:T(8,128)(2,1)S(1)} %copy-done.12, f32[8]{0:T(128)S(1)} %bitcast.125, f32[512,8]{0,1:T(8,128)S(1)} %get-tuple-element.15), kind=kOutput, calls=%fused_computation.26 | convolution fusion | flops 807927808 | bytes 6832160 | tf_op jit(solution)/shard_map/bthd,bhde->bthe/dot_general | solution.py:159
  198.2 3.8 %fusion.27 = bf16[512,1024]{1,0:T(8,128)(2,1)} fusion(bf16[512,1024]{0,1:T(8,128)(2,1)S(1)} %bitcast.119, bf16[1024,2048]{1,0:T(8,128)(2,1)} %all-gather.2.cloned.1.call-done, s32[]{:T(128)S(6)} %select_n.94), kind=kOutput, calls=%fused_computation.42 | convolution fusion | flops 1074266112 | bytes 4194308 | tf_op jit(solution)/shard_map/dot_general | solution.py:182
  202.1 3.0 %collective-permute-done.9 = bf16[512,1024]{1,0:T(8,128)(2,1)} collective-permute-done((bf16[512,1024]{1,0:T(8,128)(2,1)}, bf16[512,1024]{1,0:T(8,128)(2,1)}, u32[]{:S(2)}, u32[]{:S(2)}) %collective-permute-start.9) | collective-permute-done | bytes 1048608 | tf_op jit(solution)/shard_map/ppermute | solution.py:189
  205.1 4.5 %fusion.33 = bf16[1,512,1024]{2,1,0:T(8,128)(2,1)} fusion(bf16[512,1024]{1,0:T(8,128)(2,1)} %collective-permute-done.9, bf16[512,1024]{0,1:T(8,128)(2,1)S(1)} %bitcast.120, bf16[1024,2048]{1,0:T(8,128)(2,1)} %all-gather.2.cloned.1.call-done, s32[]{:T(128)S(6)} %select_n.79, bf16[1,512,2048]{2,1,0:T(8,128)(2,1)} %param.7), kind=kOutput, calls=%fused_computation.45 | convolution fusion | flops 1076363264 | bytes 6292480 | tf_op jit(solution)/shard_map/dot_general | solution.py:182
  (96 shorter events, 22.9 us)
Async XLA Ops:
  6.5 35.9 %copy-start = (bf16[1024,1024]{1,0:T(8,128)(2,1)S(1)}, bf16[1024,1024]{1,0:T(8,128)(2,1)}, u32[]{:S(2)}) copy-start(bf16[1024,1024]{1,0:T(8,128)(2,1)} %param.9) | copy-start | bytes 6291460
  6.5 2.2 %copy-start.16 = (f32[2048]{0:T(1024)S(1)}, f32[2048]{0:T(1024)}, u32[]{:S(2)}) copy-start(f32[2048]{0:T(1024)} %param.8) | copy-start | bytes 24580
  6.5 191.7 %all-gather.2.cloned.1.call-start = ((), (), s32[]{:S(2)}) async-start(), calls=%async_computation | async-start | bytes 6291456 | tf_op jit(solution)/shard_map/all_gather | solution.py:176
  6.5 2.4 %copy-start.2 = (bf16[1,512,2048]{2,1,0:T(8,128)(2,1)S(1)}, bf16[1,512,2048]{2,1,0:T(8,128)(2,1)}, u32[]{:S(2)}) copy-start(bf16[1,512,2048]{2,1,0:T(8,128)(2,1)} %param.7) | copy-start | bytes 6291460
  9.5 1.3 copy-start.7
  11.1 15.0 %collective-permute-start = (bf16[256,1024]{1,0:T(8,128)(2,1)S(1)}, bf16[256,1024]{1,0:T(8,128)(2,1)S(1)}, u32[]{:S(2)}, u32[]{:S(2)}) collective-permute-start(bf16[256,1024]{1,0:T(8,128)(2,1)S(1)} %dynamic-slice_bitcast_fusion), channel_id=1, source_target_pairs={{0,2},{2,0},{1,3},{3,1},{4,6},{6,4},{5,7},{7,5},{8,10},{10,8},{9,1... | collective-permute-start | bytes 1572872 | tf_op jit(solution)/shard_map/ppermute | solution.py:77
  26.1 1.9 collective-permute-start.1
  31.1 6.3 %copy-start.13 = (bf16[512,1024]{1,0:T(8,128)(2,1)}, bf16[512,1024]{1,0:T(8,128)(2,1)S(1)}, u32[]{:S(2)}) copy-start(bf16[512,1024]{1,0:T(8,128)(2,1)S(1)} %bitcast_select_fusion) | copy-start | bytes 3145732
  31.1 8.7 %copy-start.15 = (f32[1,8,512]{2,1,0:T(8,128)S(1)}, f32[1,8,512]{2,1,0:T(8,128)}, u32[]{:S(2)}) copy-start(f32[1,8,512]{2,1,0:T(8,128)} %param.12) | copy-start | bytes 49156
  37.4 48.0 %collective-permute-start.2 = (bf16[2,512,1024]{2,1,0:T(8,128)(2,1)}, bf16[2,512,1024]{2,1,0:T(8,128)(2,1)}, u32[]{:S(2)}, u32[]{:S(2)}) collective-permute-start(bf16[2,512,1024]{2,1,0:T(8,128)(2,1)} %convert_bitcast_fusion), channel_id=1, source_target_pairs={{0,2},{2,0},{1,3},{3,1},{4,6},{6,4},{5,7},{7,5},{8,10},{10,8},{9,1... | collective-permute-start | bytes 6291464 | tf_op jit(solution)/shard_map/ppermute | solution.py:91
  42.4 43.0 %copy-start.8 = (bf16[1,512,2048]{2,1,0:T(8,128)(2,1)S(1)}, bf16[1,512,2048]{2,1,0:T(8,128)(2,1)}, u32[]{:S(2)}) copy-start(bf16[1,512,2048]{2,1,0:T(8,128)(2,1)} %copy-done.7) | copy-start | bytes 6291460
  42.4 43.0 %copy-start.17 = (bf16[1024,2,1024]{2,1,0:T(2,128)(2,1)S(1)}, bf16[1024,2,1024]{2,1,0:T(2,128)(2,1)}, u32[]{:S(2)}) copy-start(bf16[1024,2,1024]{2,1,0:T(2,128)(2,1)} %param.10) | copy-start | bytes 12582916
  89.5 2.3 %copy-start.4 = (f32[2,512,1024]{2,1,0:T(8,128)}, f32[2,512,1024]{2,1,0:T(8,128)S(1)}, u32[]{:S(2)}) copy-start(f32[2,512,1024]{2,1,0:T(8,128)S(1)} %bitcast_add_fusion) | copy-start | bytes 12582916
  91.8 36.8 %collective-permute-start.5 = (bf16[1,512,1024]{2,1,0:T(8,128)(2,1)}, bf16[1,512,1024]{2,1,0:T(8,128)(2,1)}, u32[]{:S(2)}, u32[]{:S(2)}) collective-permute-start(bf16[1,512,1024]{2,1,0:T(8,128)(2,1)} %slice.43), channel_id=1, source_target_pairs={{0,4},{4,8},{8,12},{1,5},{5,9},{9,13},{2,6},{6,10},{10,14},{3,7},{... | collective-permute-start | bytes 3145736 | tf_op jit(solution)/shard_map/ppermute | solution.py:14
  96.5 27.0 %collective-permute-start.3 = (bf16[512,1024]{1,0:T(8,128)(2,1)}, bf16[512,1024]{1,0:T(8,128)(2,1)}, u32[]{:S(2)}, u32[]{:S(2)}) collective-permute-start(bf16[512,1024]{1,0:T(8,128)(2,1)} %convolution_convert_fusion), channel_id=1, source_target_pairs={{0,2},{2,0},{1,3},{3,1},{4,6},{6,4},{5,7},{7,5},{8,10},{10,8},{9,1... | collective-permute-start | bytes 3145736 | tf_op jit(solution)/shard_map/ppermute | solution.py:91
  111.3 28.9 %collective-permute-start.4 = (bf16[1,512,1024]{2,1,0:T(8,128)(2,1)}, bf16[1,512,1024]{2,1,0:T(8,128)(2,1)}, u32[]{:S(2)}, u32[]{:S(2)}) collective-permute-start(bf16[1,512,1024]{2,1,0:T(8,128)(2,1)} %get-tuple-element.19), channel_id=1, source_target_pairs={{0,4},{4,8},{8,12},{1,5},{5,9},{9,13},{2,6},{6,10},{10,14},{3,7},{... | collective-permute-start | bytes 3145736 | tf_op jit(solution)/shard_map/ppermute | solution.py:14
  116.6 3.3 %copy-start.5 = (bf16[1,512,1024]{1,2,0:T(8,128)(2,1)}, bf16[1,512,1024]{1,2,0:T(8,128)(2,1)S(1)}, u32[]{:S(2)}) copy-start(bf16[1,512,1024]{1,2,0:T(8,128)(2,1)S(1)} %copy.105) | copy-start | bytes 3145732
  119.9 3.6 %copy-start.9 = (bf16[1,512,2048]{2,1,0:T(8,128)(2,1)S(1)}, bf16[1,512,2048]{2,1,0:T(8,128)(2,1)}, u32[]{:S(2)}) copy-start(bf16[1,512,2048]{2,1,0:T(8,128)(2,1)} %copy-done.7) | copy-start | bytes 6291460
  128.6 17.9 %copy-start.10 = (f32[64,8,8,128]{3,2,1,0:T(8,128)S(1)}, f32[64,8,8,128]{3,2,1,0:T(8,128)}, u32[]{:S(2)}) copy-start(f32[64,8,8,128]{3,2,1,0:T(8,128)} %get-tuple-element.22) | copy-start | bytes 6291460
  141.9 5.4 %copy-start.3 = (f32[1,512,1024]{1,2,0:T(8,128)S(1)}, f32[1,512,1024]{1,2,0:T(8,128)}, u32[]{:S(2)}) copy-start(f32[1,512,1024]{1,2,0:T(8,128)} %copy.101) | copy-start | bytes 6291460
  141.9 5.4 %copy-start.14 = (pred[512,512]{0,1:T(8,128)(4,1)S(1)}, pred[512,512]{0,1:T(8,128)(4,1)}, u32[]{:S(2)}) copy-start(pred[512,512]{0,1:T(8,128)(4,1)} %iota_compare_fusion.1) | copy-start | bytes 786436
  141.9 13.4 %collective-permute-start.6 = (bf16[1,8,129,128]{3,1,2,0:T(8,128)(2,1)S(1)}, bf16[1,8,129,128]{3,1,2,0:T(8,128)(2,1)S(1)}, u32[]{:S(2)}, u32[]{:S(2)}) collective-permute-start(bf16[1,8,129,128]{3,1,2,0:T(8,128)(2,1)S(1)} %fusion.53), channel_id=1, source_target_pairs={{0,4},{4,8},{8,12},{1,5},{5,9},{9,13},{2,6},{6,10},{10,14},{3,7},{... | collective-permute-start | bytes 792584 | tf_op jit(solution)/shard_map/ppermute | solution.py:14
  147.2 2.7 %copy-start.11 = (bf16[512,8,128]{2,0,1:T(8,128)(2,1)}, bf16[512,8,128]{2,0,1:T(8,128)(2,1)S(1)}, u32[]{:S(2)}) copy-start(bf16[512,8,128]{2,0,1:T(8,128)(2,1)S(1)} %fusion.11) | copy-start | bytes 3145732
  149.9 9.0 %copy-start.6 = (bf16[1,512,1024]{1,2,0:T(8,128)(2,1)S(1)}, bf16[1,512,1024]{1,2,0:T(8,128)(2,1)}, u32[]{:S(2)}) copy-start(bf16[1,512,1024]{1,2,0:T(8,128)(2,1)} %copy-done.5) | copy-start | bytes 3145732
  155.4 8.5 %collective-permute-start.7 = (bf16[1,8,129,128]{3,1,2,0:T(8,128)(2,1)S(1)}, bf16[1,8,129,128]{3,1,2,0:T(8,128)(2,1)S(1)}, u32[]{:S(2)}, u32[]{:S(2)}) collective-permute-start(bf16[1,8,129,128]{3,1,2,0:T(8,128)(2,1)S(1)} %fusion.55), channel_id=1, source_target_pairs={{0,4},{4,8},{8,12},{1,5},{5,9},{9,13},{2,6},{6,10},{10,14},{3,7},{... | collective-permute-start | bytes 792584 | tf_op jit(solution)/shard_map/ppermute | solution.py:14
  164.0 10.7 %collective-permute-start.8 = (bf16[1,8,129,128]{3,1,2,0:T(8,128)(2,1)S(1)}, bf16[1,8,129,128]{3,1,2,0:T(8,128)(2,1)S(1)}, u32[]{:S(2)}, u32[]{:S(2)}) collective-permute-start(bf16[1,8,129,128]{3,1,2,0:T(8,128)(2,1)S(1)} %fusion.57), channel_id=1, source_target_pairs={{0,4},{4,8},{8,12},{1,5},{5,9},{9,13},{2,6},{6,10},{10,14},{3,7},{... | collective-permute-start | bytes 792584 | tf_op jit(solution)/shard_map/ppermute | solution.py:14
  188.0 6.8 %copy-start.12 = (bf16[512,8,128]{2,0,1:T(8,128)(2,1)S(1)}, bf16[512,8,128]{2,0,1:T(8,128)(2,1)}, u32[]{:S(2)}) copy-start(bf16[512,8,128]{2,0,1:T(8,128)(2,1)} %copy-done.11) | copy-start | bytes 3145732
  202.1 3.0 %collective-permute-start.9 = (bf16[512,1024]{1,0:T(8,128)(2,1)}, bf16[512,1024]{1,0:T(8,128)(2,1)}, u32[]{:S(2)}, u32[]{:S(2)}) collective-permute-start(bf16[512,1024]{1,0:T(8,128)(2,1)} %fusion.27), channel_id=1, source_target_pairs={{0,1},{1,0},{2,3},{3,2},{4,5},{5,4},{6,7},{7,6},{8,9},{9,8},{10,11... | collective-permute-start | bytes 3145736 | tf_op jit(solution)/shard_map/ppermute | solution.py:189
  202.1 7.5 %copy-start.1 = (bf16[1024,1024]{1,0:T(8,128)(2,1)S(1)}, bf16[1024,1024]{1,0:T(8,128)(2,1)}, u32[]{:S(2)}) copy-start(bf16[1024,1024]{1,0:T(8,128)(2,1)} %param.9) | copy-start | bytes 6291460
Sparse Core Ops, SparseCore 0:
  116.7 54.1 all-gather.1

commit v6 on v5

--- a/solution.py
+++ b/solution.py
@@ -122,13 +122,12 @@
     whole = climb[:, :, -1]
     factor = jnp.exp(whole) * keep[:, None]
     weight = jnp.exp(whole[:, :, None] - climb)
+    weighted = weight.transpose(0, 2, 1)[..., None] * lookup_vectors.astype(jnp.float32)
+    weighted_hi = weighted.astype(jnp.bfloat16)
+    weighted_lo = (weighted - weighted_hi.astype(jnp.float32)).astype(jnp.bfloat16)
     local_state = jnp.einsum(
-        "bht,bthd,bthe->bhde",
-        weight,
-        lookup_vectors.astype(jnp.float32),
-        values.astype(jnp.float32),
-        precision=lax.Precision.HIGHEST,
-    )
+        "bthd,bthe->bhde", weighted_hi, values, preferred_element_type=jnp.float32
+    ) + jnp.einsum("bthd,bthe->bhde", weighted_lo, values, preferred_element_type=jnp.float32)
     local_mass = jnp.sum(weight * weight, axis=-1)
 
     local_both = jnp.concatenate(
@@ -157,7 +156,7 @@
     entering = entering * keep[:, None, None, None]
     entering_mass = entering_mass * keep[:, None]
     read = jnp.einsum(
-        "bthd,bhde->bthe", queries.astype(jnp.float32), entering, precision=lax.Precision.HIGHEST
+        "bthd,bhde->bthe", queries, entering.astype(jnp.bfloat16), preferred_element_type=jnp.float32
     )
     read = read * jnp.exp(climb).transpose(0, 2, 1)[..., None]
     read = read / jnp.sqrt(head_dim * (1.0 + entering_mass))[:, None, :, None]

time: 217 us -> 231 us (1.065)
  waiting for transfers between devices: 67.5 us -> 85.1 us
    ppermute x5, waiting for transfers between devices: 11.5 us -> 26.2 us  [shifted(): lax.ppermute(value, axis, [(source, source + steps) for source in range(i...]
    another operation x3 -> x2, other arithmetic: 9.5 us -> 1.16 us
    slice x3 -> x1, local copies, waits for them, and re-layouts: 4.95 us -> 0.16 us  [the longest x2 4.79 us: shards(): entering = entering_both[:, :, :head_dim, :]]
    mul x0 -> x1, local copies, waits for them, and re-layouts: none -> 3.19 us  [shards(): entering = entering * keep[:, None, None, None]]
    ppermute x2, waiting for transfers between devices: 39.3 us -> 42.2 us  [gathered_sum(): lax.ppermute(outgoing, 'wloop', [(source, (source - step) % ways) for sou...]
    convert_element_type x3, other arithmetic: 0.21 us -> 2.63 us  [relay_turn(): (factor_both * carry + local_both).astype(jnp.bfloat16)]
    unnamed x40 -> x38, local copies, waits for them, and re-layouts: 6.12 us -> 8.05 us
    convert_element_type x1 -> x2, other arithmetic: 4.61 us -> 6.44 us  [shards(): rms_rows(pair_raw[0].reshape(trajs, span, heads_here, head_dim), 1e-06)]
  transfers between devices with their start and end apart: 11 -> 11, of which waited for: 5 -> 6; matrix products, arithmetic and copies ran while one was open for 37% -> 26% of each run, Pallas kernels for 0% -> 0%
where the time goes in v6:
time: 231 us; the launch traced here: 230 us
  waiting for transfers between devices  85.1 us (37%)
  matrix products  49.5 us (21%)
  local copies, waits for them, and re-layouts  33.6 us (15%)
  starting transfers between devices  26.2 us (11%)
  other arithmetic  21.4 us (9%)
  between operations  14.4 us (6%)
    ppermute x2, waiting for transfers between devices, gathered_sum(): lax.ppermute(outgoing, 'wloop', [(source, (source - step) % ways) for sou...  42.2 us
    ppermute x5, waiting for transfers between devices, shifted(): lax.ppermute(value, axis, [(source, source + steps) for source in range(i...  26.2 us
    ppermute x5, starting transfers between devices, shifted(): lax.ppermute(value, axis, [(source, source + steps) for source in range(i...  19.9 us
    dot_general x2, matrix products, shards(): jnp.einsum('td,dje->jte', rows, w_keyvalue, preferred_element_type=jnp.fl...  12 us
    ppermute x1, waiting for transfers between devices, shards(): lax.ppermute(part, 'wloop', [(source, (source + step) % ways) for source...  11.9 us
    dot_general x2, matrix products, output_share(): jnp.dot(attended, lax.dynamic_slice_in_dim(w_output_rows, index * share,...  8.32 us
    unnamed x38, local copies, waits for them, and re-layouts  8.05 us
    another operation x3, local copies, waits for them, and re-layouts  7.8 us
  transfers between devices with their start and end apart: 11, of which 6 were waited for; matrix products, arithmetic and copies ran while one was open for 26% of the time, Pallas kernels for 0%

profile of v6, /device:TPU:0, one launch (start us, length us, event | category | flops | bytes accessed | tf_op | source)
XLA Modules:
  0.0 230.2 jit_solution(8067575981914741587)
XLA Ops:
  6.5 2.2 fusion.2
  11.1 3.0 %collective-permute-start = (bf16[256,1024]{1,0:T(8,128)(2,1)S(1)}, bf16[256,1024]{1,0:T(8,128)(2,1)S(1)}, u32[]{:S(2)}, u32[]{:S(2)}) collective-permute-start(bf16[256,1024]{1,0:T(8,128)(2,1)S(1)} %dynamic-slice_bitcast_fusion), channel_id=1, source_target_pairs={{0,2},{2,0},{1,3},{3,1},{4,6},{6,4},{5,7},{7,5},{8,10},{10,8},{9,1... | collective-permute-start | bytes 1572872 | tf_op jit(solution)/shard_map/ppermute | solution.py:77
  14.1 11.9 %collective-permute-done = bf16[256,1024]{1,0:T(8,128)(2,1)S(1)} collective-permute-done((bf16[256,1024]{1,0:T(8,128)(2,1)S(1)}, bf16[256,1024]{1,0:T(8,128)(2,1)S(1)}, u32[]{:S(2)}, u32[]{:S(2)}) %collective-permute-start) | collective-permute-done | bytes 524320 | tf_op jit(solution)/shard_map/ppermute | solution.py:77
  31.1 6.4 %convert_bitcast_fusion.1 = bf16[2,512,1024]{2,1,0:T(8,128)(2,1)} fusion(bf16[1024,2,1024]{2,1,0:T(2,128)(2,1)} %param.10, bf16[512,1024]{1,0:T(8,128)(2,1)S(1)} %bitcast_select_fusion), kind=kOutput, calls=%fused_computation.41 | convolution fusion | flops 2148532224 | bytes 7340032 | tf_op jit(solution)/shard_map/td,dje->jte/dot_general | solution.py:100
  43.2 42.2 %collective-permute-done.2 = bf16[2,512,1024]{2,1,0:T(8,128)(2,1)} collective-permute-done((bf16[2,512,1024]{2,1,0:T(8,128)(2,1)}, bf16[2,512,1024]{2,1,0:T(8,128)(2,1)}, u32[]{:S(2)}, u32[]{:S(2)}) %collective-permute-start.2) | collective-permute-done | bytes 2097184 | tf_op jit(solution)/shard_map/ppermute | solution.py:91
  85.4 5.6 %bitcast_add_fusion = f32[2,512,1024]{2,1,0:T(8,128)S(1)} fusion(bf16[2,512,1024]{2,1,0:T(8,128)(2,1)} %collective-permute-done.2, bf16[1024,2,1024]{2,1,0:T(2,128)(2,1)} %param.10, bf16[1,512,2048]{2,1,0:T(8,128)(2,1)} %copy-done.8, s32[]{:T(128)S(6)} %select_n.80), kind=kOutput, calls=%fused_computation.12 | convolution fusion | flops 2149580800 | bytes 11534340 | tf_op jit(solution)/shard_map/td,dje->jte/dot_general | solution.py:100
  96.0 2.2 reduce_sum.56
  100.0 2.9 %copy.110 = f32[1,512,1024]{2,1,0:T(8,128)} copy(f32[1,512,1024]{1,2,0:T(8,128)} %bitcast.109) | data formatting | bytes 4194304 | tf_op jit(solution)/shard_map/mul | solution.py:18
  102.9 4.6 %multiply_convert_fusion = (bf16[1,512,1024]{2,1,0:T(8,128)(2,1)}, f32[1,512,1024]{2,1,0:T(8,128)}) fusion(f32[1,512,1024]{2,1,0:T(8,128)} %copy.110, f32[2,512,1024]{2,1,0:T(8,128)} %copy-done.3), kind=kLoop, calls=%fused_computation.33 | loop fusion | flops 1048576 | bytes 7340032 | tf_op jit(solution)/shard_map/convert_element_type | solution.py:108
  107.5 4.7 %collective-permute-start.4 = (bf16[1,512,1024]{2,1,0:T(8,128)(2,1)}, bf16[1,512,1024]{2,1,0:T(8,128)(2,1)}, u32[]{:S(2)}, u32[]{:S(2)}) collective-permute-start(bf16[1,512,1024]{2,1,0:T(8,128)(2,1)} %get-tuple-element.19), channel_id=1, source_target_pairs={{0,4},{4,8},{8,12},{1,5},{5,9},{9,13},{2,6},{6,10},{10,14},{3,7},{... | collective-permute-start | bytes 3145736 | tf_op jit(solution)/shard_map/ppermute | solution.py:14
  112.2 3.5 %collective-permute-start.5 = (bf16[1,512,1024]{2,1,0:T(8,128)(2,1)}, bf16[1,512,1024]{2,1,0:T(8,128)(2,1)}, u32[]{:S(2)}, u32[]{:S(2)}) collective-permute-start(bf16[1,512,1024]{2,1,0:T(8,128)(2,1)} %slice.44), channel_id=1, source_target_pairs={{0,4},{4,8},{8,12},{1,5},{5,9},{9,13},{2,6},{6,10},{10,14},{3,7},{... | collective-permute-start | bytes 3145736 | tf_op jit(solution)/shard_map/ppermute | solution.py:14
  115.7 2.3 convolution_convert_fusion
  118.0 2.9 %copy.109 = f32[1,512,1024]{1,2,0:T(8,128)} copy(f32[1,512,1024]{2,1,0:T(8,128)} %get-tuple-element.20) | data formatting | bytes 4194304 | tf_op jit(solution)/shard_map/reshape;squeeze | solution.py:108
  124.3 2.7 %copy.113 = bf16[1,512,1024]{1,2,0:T(8,128)(2,1)} copy(bf16[1,512,1024]{2,1,0:T(8,128)(2,1)} %slice.44) | data formatting | bytes 2097152 | tf_op jit(solution)/shard_map/convert_element_type | solution.py:111
  129.7 5.4 %collective-permute-done.4 = bf16[1,512,1024]{2,1,0:T(8,128)(2,1)} collective-permute-done((bf16[1,512,1024]{2,1,0:T(8,128)(2,1)}, bf16[1,512,1024]{2,1,0:T(8,128)(2,1)}, u32[]{:S(2)}, u32[]{:S(2)}) %collective-permute-start.4) | collective-permute-done | bytes 1048608 | tf_op jit(solution)/shard_map/ppermute | solution.py:14
  135.0 20.8 %collective-permute-done.5 = bf16[1,512,1024]{2,1,0:T(8,128)(2,1)} collective-permute-done((bf16[1,512,1024]{2,1,0:T(8,128)(2,1)}, bf16[1,512,1024]{2,1,0:T(8,128)(2,1)}, u32[]{:S(2)}, u32[]{:S(2)}) %collective-permute-start.5) | collective-permute-done | bytes 1048608 | tf_op jit(solution)/shard_map/ppermute | solution.py:14
  156.8 5.1 %collective-permute-start.6 = (bf16[1,8,129,128]{3,1,2,0:T(8,128)(2,1)}, bf16[1,8,129,128]{3,1,2,0:T(8,128)(2,1)}, u32[]{:S(2)}, u32[]{:S(2)}) collective-permute-start(bf16[1,8,129,128]{3,1,2,0:T(8,128)(2,1)} %fusion.52), channel_id=1, source_target_pairs={{0,4},{4,8},{8,12},{1,5},{5,9},{9,13},{2,6},{6,10},{10,14},{3,7},{... | collective-permute-start | bytes 792584 | tf_op jit(solution)/shard_map/ppermute | solution.py:14
  161.9 2.5 %copy.117 = bf16[64,8,8,128]{3,2,1,0:T(8,128)(2,1)} copy(bf16[64,8,8,128]{3,1,2,0:T(8,128)(2,1)} %bitcast.50) | data formatting | bytes 2097152
  164.3 3.8 %multiply_bitcast_fusion.1 = (f32[64,8,8,128]{3,1,2,0:T(8,128)S(1)}, f32[64,8,8,128]{3,2,1,0:T(8,128)}) fusion(bf16[512,1024]{1,0:T(8,128)(2,1)} %collective-permute-done.3, bf16[1024,1024]{1,0:T(8,128)(2,1)S(1)} %copy-done, bf16[1,512,2048]{2,1,0:T(8,128)(2,1)S(1)} %copy-done.9, s32[]{:T(128)S(6)} %select_n.80), kind=kOutput, calls=%fused_computation.39 | convolution fusion | flops 1075314688 | bytes 8388612 | tf_op jit(solution)/shard_map/dot_general | solution.py:105
  169.4 2.0 fusion.11
  171.5 2.5 %fusion = (f32[8,512]{1,0:T(8,128)S(1)}, f32[8,512,512]{1,2,0:T(8,128)S(1)}) fusion(pred[512,512]{0,1:T(8,128)(4,1)S(1)} %copy-done.14, bf16[512,8,128]{2,0,1:T(8,128)(2,1)S(1)} %fusion.11, bf16[512,8,128]{0,2,1:T(8,128)(2,1)S(1)} %copy-done.5), kind=kOutput, calls=%fused_computation.5 | convolution fusion | flops 543158272 | bytes 10764288 | tf_op jit(solution)/shard_map/bihd,bjhd->bhij/dot_general | solution.py:23
  174.0 5.3 %fusion.1 = (f32[8,512]{1,0:T(8,128)S(1)}, f32[8,512,512]{1,2,0:T(8,128)}) fusion(pred[512,512]{0,1:T(8,128)(4,1)S(1)} %copy-done.13, bf16[512,8,128]{2,0,1:T(8,128)(2,1)S(1)} %fusion.11, bf16[512,8,128]{2,1,0:T(8,128)(2,1)S(1)} %bitcast.113), kind=kOutput, calls=%fused_computation.6 | convolution fusion | flops 543158272 | bytes 10764288 | tf_op jit(solution)/shard_map/bihd,bjhd->bhij/dot_general | solution.py:27
  181.0 2.8 %collective-permute-start.7 = (bf16[1,8,129,128]{3,1,2,0:T(8,128)(2,1)}, bf16[1,8,129,128]{3,1,2,0:T(8,128)(2,1)S(1)}, u32[]{:S(2)}, u32[]{:S(2)}) collective-permute-start(bf16[1,8,129,128]{3,1,2,0:T(8,128)(2,1)} %fusion.54), channel_id=1, source_target_pairs={{0,4},{4,8},{8,12},{1,5},{5,9},{9,13},{2,6},{6,10},{10,14},{3,7},{... | collective-permute-start | bytes 792584 | tf_op jit(solution)/shard_map/ppermute | solution.py:14
  183.8 3.4 %fusion.5 = f32[8,128,512]{2,1,0:T(8,128)} fusion(bf16[512,8,128]{0,2,1:T(8,128)(2,1)S(1)} %bitcast.112, f32[8,512,512]{1,2,0:T(8,128)S(1)} %get-tuple-element.26, f32[8,512]{1,0:T(8,128)S(1)} %add.166, pred[512,512]{0,1:T(8,128)(4,1)S(1)} %copy-done.14), kind=kOutput, calls=%fused_computation.14 | convolution fusion | flops 545259520 | bytes 11812864 | tf_op jit(solution)/shard_map/bhij,bjhd->bihd/dot_general | solution.py:38
  188.8 3.8 %collective-permute-start.8 = (bf16[1,8,129,128]{3,1,2,0:T(8,128)(2,1)S(1)}, bf16[1,8,129,128]{3,1,2,0:T(8,128)(2,1)S(1)}, u32[]{:S(2)}, u32[]{:S(2)}) collective-permute-start(bf16[1,8,129,128]{3,1,2,0:T(8,128)(2,1)S(1)} %fusion.56), channel_id=1, source_target_pairs={{0,4},{4,8},{8,12},{1,5},{5,9},{9,13},{2,6},{6,10},{10,14},{3,7},{... | collective-permute-start | bytes 792584 | tf_op jit(solution)/shard_map/ppermute | solution.py:14
  192.7 7.0 %fusion.6 = f32[8,128,512]{2,1,0:T(8,128)} fusion(bf16[512,8,128]{0,2,1:T(8,128)(2,1)S(1)} %bitcast.114, f32[8,512,512]{1,2,0:T(8,128)} %get-tuple-element.28, f32[8,512]{1,0:T(8,128)S(1)} %add.166, pred[512,512]{0,1:T(8,128)(4,1)} %fusion.45), kind=kOutput, calls=%fused_computation.15 | convolution fusion | flops 545259520 | bytes 11812864 | tf_op jit(solution)/shard_map/bhij,bjhd->bihd/dot_general | solution.py:40
  199.7 3.2 %copy.103 = bf16[1,8,128,128]{1,3,2,0:T(8,128)(2,1)} copy(bf16[1,8,128,128]{3,1,2,0:T(8,128)(2,1)S(1)} %slice_multiply_fusion) | data formatting | bytes 524288 | tf_op jit(solution)/shard_map/mul | solution.py:156
  202.9 6.3 %copy.104 = bf16[8,128,128]{1,2,0:T(8,128)(2,1)S(1)} copy(bf16[8,128,128]{0,2,1:T(8,128)(2,1)} %bitcast.105) | data formatting | bytes 524288 | tf_op jit(solution)/shard_map/reshape.52
  209.3 2.7 %fusion.14 = bf16[1,512,8,128]{1,3,2,0:T(8,128)(2,1)S(1)} fusion(f32[8,128,512]{2,1,0:T(8,128)} %fusion.5, f32[8,128,512]{2,1,0:T(8,128)} %fusion.6, bf16[8,128,128]{1,2,0:T(8,128)(2,1)S(1)} %copy.104, bf16[512,8,128]{2,0,1:T(8,128)(2,1)S(1)} %fusion.11, f32[8]{0:T(128)S(1)} %bitcast.121, f32[512,8]{0,1:T(8,128)S(1)} %get-tuple-element.15), kind=kOutput, calls=%fused_computation.26 | convolution fusion | flops 136839168 | bytes 6570016 | tf_op jit(solution)/shard_map/bthd,bhde->bthe/dot_general | solution.py:158
  212.1 3.8 %fusion.25 = bf16[512,1024]{1,0:T(8,128)(2,1)} fusion(bf16[512,1024]{0,1:T(8,128)(2,1)S(1)} %bitcast.115, bf16[1024,2048]{1,0:T(8,128)(2,1)} %all-gather.2.cloned.1.call-done, s32[]{:T(128)S(6)} %select_n.94), kind=kOutput, calls=%fused_computation.42 | convolution fusion | flops 1074266112 | bytes 4194308 | tf_op jit(solution)/shard_map/dot_general | solution.py:181
  215.9 3.0 %collective-permute-done.9 = bf16[512,1024]{1,0:T(8,128)(2,1)} collective-permute-done((bf16[512,1024]{1,0:T(8,128)(2,1)}, bf16[512,1024]{1,0:T(8,128)(2,1)}, u32[]{:S(2)}, u32[]{:S(2)}) %collective-permute-start.9) | collective-permute-done | bytes 1048608 | tf_op jit(solution)/shard_map/ppermute | solution.py:188
  218.9 4.5 %fusion.33 = bf16[1,512,1024]{2,1,0:T(8,128)(2,1)} fusion(bf16[512,1024]{1,0:T(8,128)(2,1)} %collective-permute-done.9, bf16[512,1024]{0,1:T(8,128)(2,1)S(1)} %bitcast.116, bf16[1024,2048]{1,0:T(8,128)(2,1)} %all-gather.2.cloned.1.call-done, s32[]{:T(128)S(6)} %select_n.79, bf16[1,512,2048]{2,1,0:T(8,128)(2,1)} %param.7), kind=kOutput, calls=%fused_computation.46 | convolution fusion | flops 1076363264 | bytes 6292480 | tf_op jit(solution)/shard_map/dot_general | solution.py:181
  (94 shorter events, 30.7 us)
Async XLA Ops:
  6.5 109.1 %copy-start = (bf16[1024,1024]{1,0:T(8,128)(2,1)S(1)}, bf16[1024,1024]{1,0:T(8,128)(2,1)}, u32[]{:S(2)}) copy-start(bf16[1024,1024]{1,0:T(8,128)(2,1)} %param.9) | copy-start | bytes 6291460
  6.5 2.2 copy-start.16
  6.5 205.5 %all-gather.2.cloned.1.call-start = ((), (), s32[]{:S(2)}) async-start(), calls=%async_computation | async-start | bytes 6291456 | tf_op jit(solution)/shard_map/all_gather | solution.py:175
  6.5 2.4 %copy-start.2 = (bf16[1,512,2048]{2,1,0:T(8,128)(2,1)S(1)}, bf16[1,512,2048]{2,1,0:T(8,128)(2,1)}, u32[]{:S(2)}) copy-start(bf16[1,512,2048]{2,1,0:T(8,128)(2,1)} %param.7) | copy-start | bytes 6291460
  9.5 1.3 copy-start.8
  11.1 15.0 %collective-permute-start = (bf16[256,1024]{1,0:T(8,128)(2,1)S(1)}, bf16[256,1024]{1,0:T(8,128)(2,1)S(1)}, u32[]{:S(2)}, u32[]{:S(2)}) collective-permute-start(bf16[256,1024]{1,0:T(8,128)(2,1)S(1)} %dynamic-slice_bitcast_fusion), channel_id=1, source_target_pairs={{0,2},{2,0},{1,3},{3,1},{4,6},{6,4},{5,7},{7,5},{8,10},{10,8},{9,1... | collective-permute-start | bytes 1572872 | tf_op jit(solution)/shard_map/ppermute | solution.py:77
  26.0 1.9 collective-permute-start.1
  31.1 6.4 %copy-start.10 = (bf16[512,1024]{1,0:T(8,128)(2,1)}, bf16[512,1024]{1,0:T(8,128)(2,1)S(1)}, u32[]{:S(2)}) copy-start(bf16[512,1024]{1,0:T(8,128)(2,1)S(1)} %bitcast_select_fusion) | copy-start | bytes 3145732
  31.1 8.1 %copy-start.15 = (f32[1,8,512]{2,1,0:T(8,128)S(1)}, f32[1,8,512]{2,1,0:T(8,128)}, u32[]{:S(2)}) copy-start(f32[1,8,512]{2,1,0:T(8,128)} %param.12) | copy-start | bytes 49156
  37.5 48.0 %collective-permute-start.2 = (bf16[2,512,1024]{2,1,0:T(8,128)(2,1)}, bf16[2,512,1024]{2,1,0:T(8,128)(2,1)}, u32[]{:S(2)}, u32[]{:S(2)}) collective-permute-start(bf16[2,512,1024]{2,1,0:T(8,128)(2,1)} %convert_bitcast_fusion.1), channel_id=1, source_target_pairs={{0,2},{2,0},{1,3},{3,1},{4,6},{6,4},{5,7},{7,5},{8,10},{10,8},{9,1... | collective-permute-start | bytes 6291464 | tf_op jit(solution)/shard_map/ppermute | solution.py:91
  91.1 1.9 copy-start.3
  102.9 12.8 %copy-start.11 = (bf16[512,1024]{1,0:T(8,128)(2,1)S(1)}, bf16[512,1024]{1,0:T(8,128)(2,1)}, u32[]{:S(2)}) copy-start(bf16[512,1024]{1,0:T(8,128)(2,1)} %copy-done.10) | copy-start | bytes 3145732
  107.5 27.6 %collective-permute-start.4 = (bf16[1,512,1024]{2,1,0:T(8,128)(2,1)}, bf16[1,512,1024]{2,1,0:T(8,128)(2,1)}, u32[]{:S(2)}, u32[]{:S(2)}) collective-permute-start(bf16[1,512,1024]{2,1,0:T(8,128)(2,1)} %get-tuple-element.19), channel_id=1, source_target_pairs={{0,4},{4,8},{8,12},{1,5},{5,9},{9,13},{2,6},{6,10},{10,14},{3,7},{... | collective-permute-start | bytes 3145736 | tf_op jit(solution)/shard_map/ppermute | solution.py:14
  112.2 43.6 %collective-permute-start.5 = (bf16[1,512,1024]{2,1,0:T(8,128)(2,1)}, bf16[1,512,1024]{2,1,0:T(8,128)(2,1)}, u32[]{:S(2)}, u32[]{:S(2)}) collective-permute-start(bf16[1,512,1024]{2,1,0:T(8,128)(2,1)} %slice.44), channel_id=1, source_target_pairs={{0,4},{4,8},{8,12},{1,5},{5,9},{9,13},{2,6},{6,10},{10,14},{3,7},{... | collective-permute-start | bytes 3145736 | tf_op jit(solution)/shard_map/ppermute | solution.py:14
  120.9 43.4 %collective-permute-start.3 = (bf16[512,1024]{1,0:T(8,128)(2,1)}, bf16[512,1024]{1,0:T(8,128)(2,1)}, u32[]{:S(2)}, u32[]{:S(2)}) collective-permute-start(bf16[512,1024]{1,0:T(8,128)(2,1)} %convolution_convert_fusion), channel_id=1, source_target_pairs={{0,2},{2,0},{1,3},{3,1},{4,6},{6,4},{5,7},{7,5},{8,10},{10,8},{9,1... | collective-permute-start | bytes 3145736 | tf_op jit(solution)/shard_map/ppermute | solution.py:91
  124.3 4.5 %copy-start.4 = (bf16[512,8,128]{0,2,1:T(8,128)(2,1)}, bf16[512,8,128]{0,2,1:T(8,128)(2,1)S(1)}, u32[]{:S(2)}) copy-start(bf16[512,8,128]{0,2,1:T(8,128)(2,1)S(1)} %multiply_convert_fusion.1) | copy-start | bytes 3145732
  127.0 1.8 copy-start.6
  129.7 34.7 %copy-start.9 = (bf16[1,512,2048]{2,1,0:T(8,128)(2,1)S(1)}, bf16[1,512,2048]{2,1,0:T(8,128)(2,1)}, u32[]{:S(2)}) copy-start(bf16[1,512,2048]{2,1,0:T(8,128)(2,1)} %copy-done.8) | copy-start | bytes 6291460
  156.8 22.5 %collective-permute-start.6 = (bf16[1,8,129,128]{3,1,2,0:T(8,128)(2,1)}, bf16[1,8,129,128]{3,1,2,0:T(8,128)(2,1)}, u32[]{:S(2)}, u32[]{:S(2)}) collective-permute-start(bf16[1,8,129,128]{3,1,2,0:T(8,128)(2,1)} %fusion.52), channel_id=1, source_target_pairs={{0,4},{4,8},{8,12},{1,5},{5,9},{9,13},{2,6},{6,10},{10,14},{3,7},{... | collective-permute-start | bytes 792584 | tf_op jit(solution)/shard_map/ppermute | solution.py:14
  169.3 2.2 copy-start.5
  169.4 2.1 copy-start.14
  171.4 2.5 %copy-start.12 = (bf16[64,8,8,128]{3,2,1,0:T(8,128)(2,1)S(1)}, bf16[64,8,8,128]{3,2,1,0:T(8,128)(2,1)}, u32[]{:S(2)}) copy-start(bf16[64,8,8,128]{3,2,1,0:T(8,128)(2,1)} %copy.117) | copy-start | bytes 3145732
  171.5 2.5 %copy-start.13 = (pred[512,512]{0,1:T(8,128)(4,1)S(1)}, pred[512,512]{0,1:T(8,128)(4,1)}, u32[]{:S(2)}) copy-start(pred[512,512]{0,1:T(8,128)(4,1)} %fusion.45) | copy-start | bytes 786436
  174.0 9.8 %copy-start.7 = (bf16[1,512,1024]{1,2,0:T(8,128)(2,1)S(1)}, bf16[1,512,1024]{1,2,0:T(8,128)(2,1)}, u32[]{:S(2)}) copy-start(bf16[1,512,1024]{1,2,0:T(8,128)(2,1)} %copy.113) | copy-start | bytes 3145732
  181.0 7.7 %collective-permute-start.7 = (bf16[1,8,129,128]{3,1,2,0:T(8,128)(2,1)}, bf16[1,8,129,128]{3,1,2,0:T(8,128)(2,1)S(1)}, u32[]{:S(2)}, u32[]{:S(2)}) collective-permute-start(bf16[1,8,129,128]{3,1,2,0:T(8,128)(2,1)} %fusion.54), channel_id=1, source_target_pairs={{0,4},{4,8},{8,12},{1,5},{5,9},{9,13},{2,6},{6,10},{10,14},{3,7},{... | collective-permute-start | bytes 792584 | tf_op jit(solution)/shard_map/ppermute | solution.py:14
  188.8 10.8 %collective-permute-start.8 = (bf16[1,8,129,128]{3,1,2,0:T(8,128)(2,1)S(1)}, bf16[1,8,129,128]{3,1,2,0:T(8,128)(2,1)S(1)}, u32[]{:S(2)}, u32[]{:S(2)}) collective-permute-start(bf16[1,8,129,128]{3,1,2,0:T(8,128)(2,1)S(1)} %fusion.56), channel_id=1, source_target_pairs={{0,4},{4,8},{8,12},{1,5},{5,9},{9,13},{2,6},{6,10},{10,14},{3,7},{... | collective-permute-start | bytes 792584 | tf_op jit(solution)/shard_map/ppermute | solution.py:14
  215.9 3.0 %collective-permute-start.9 = (bf16[512,1024]{1,0:T(8,128)(2,1)}, bf16[512,1024]{1,0:T(8,128)(2,1)}, u32[]{:S(2)}, u32[]{:S(2)}) collective-permute-start(bf16[512,1024]{1,0:T(8,128)(2,1)} %fusion.25), channel_id=1, source_target_pairs={{0,1},{1,0},{2,3},{3,2},{4,5},{5,4},{6,7},{7,6},{8,9},{9,8},{10,11... | collective-permute-start | bytes 3145736 | tf_op jit(solution)/shard_map/ppermute | solution.py:188
  215.9 7.5 %copy-start.1 = (bf16[1024,1024]{1,0:T(8,128)(2,1)S(1)}, bf16[1024,1024]{1,0:T(8,128)(2,1)}, u32[]{:S(2)}) copy-start(bf16[1024,1024]{1,0:T(8,128)(2,1)} %param.9) | copy-start | bytes 6291460
Sparse Core Ops, SparseCore 0:
  129.7 60.3 all-gather.1

commit v7 on v5

--- a/solution.py
+++ b/solution.py
@@ -131,16 +131,14 @@
     )
     local_mass = jnp.sum(weight * weight, axis=-1)
 
-    local_both = jnp.concatenate(
-        [local_state, jnp.broadcast_to(local_mass[:, :, None, None], local_state.shape[:2] + (1, head_dim))],
-        axis=2,
-    )
+    def as_block(per_head):
+        padded = jnp.pad(per_head, ((0, 0), (0, head_dim * head_dim - heads_here)))
+        return padded.reshape(trajs, 1, head_dim, head_dim)
+
+    local_both = jnp.concatenate([local_state, as_block(local_mass)], axis=1)
     factor_both = jnp.concatenate(
-        [
-            jnp.broadcast_to(factor[:, :, None, None], local_state.shape),
-            jnp.broadcast_to((factor * factor)[:, :, None, None], local_state.shape[:2] + (1, head_dim)),
-        ],
-        axis=2,
+        [jnp.broadcast_to(factor[:, :, None, None], local_state.shape), as_block(factor * factor)],
+        axis=1,
     )
 
     def relay_turn(turn, carry):
@@ -152,12 +150,12 @@
     entering_both = jnp.zeros_like(local_both)
     for turn in range(lax.axis_size("seq") - 1):
         entering_both = relay_turn(turn, entering_both)
-    entering = entering_both[:, :, :head_dim, :]
-    entering_mass = entering_both[:, :, head_dim, 0]
+    entering = entering_both[:, :heads_here]
+    entering_mass = entering_both[:, heads_here].reshape(trajs, head_dim * head_dim)[:, :heads_here]
     entering = entering * keep[:, None, None, None]
     entering_mass = entering_mass * keep[:, None]
     read = jnp.einsum(
-        "bthd,bhde->bthe", queries.astype(jnp.float32), entering, precision=lax.Precision.HIGHEST
+        "bthd,bhde->bthe", queries, entering.astype(jnp.bfloat16), preferred_element_type=jnp.float32
     )
     read = read * jnp.exp(climb).transpose(0, 2, 1)[..., None]
     read = read / jnp.sqrt(head_dim * (1.0 + entering_mass))[:, None, :, None]

time: 217 us -> 192 us (0.88)
  local copies, waits for them, and re-layouts: 33.1 us -> 21.2 us
  other arithmetic: 23.5 us -> 16.7 us
  matrix products: 51.5 us -> 46.4 us
    another operation x3 -> x2, other arithmetic: 9.5 us -> 1.18 us
    another operation x3 -> x2, local copies, waits for them, and re-layouts: 8.28 us -> 1.5 us
    slice x4 -> x2, local copies, waits for them, and re-layouts: 5.13 us -> 0.17 us  [the longest x2 4.79 us: shards(): entering = entering_both[:, :, :head_dim, :]]
    dot_general x1, matrix products: 3.4 us -> 0.6 us  [shards(): jnp.einsum('bthd,bhde->bthe', queries, entering.astype(jnp.bfloat16), pre...]
    dot_general x1, matrix products: 7.05 us -> 4.83 us  [window_mix(): jnp.einsum('bhij,bjhd->bihd', prior_p, prior_values, preferred_element_ty...]
    unnamed x40 -> x47, local copies, waits for them, and re-layouts: 6.12 us -> 6.09 us
  transfers between devices with their start and end apart: 11 -> 11, of which waited for: 5 -> 5; matrix products, arithmetic and copies ran while one was open for 37% -> 29% of each run, Pallas kernels for 0% -> 0%
where the time goes in v7:
time: 192 us
  waiting for transfers between devices  66.2 us (34%)
  matrix products  46.4 us (24%)
  starting transfers between devices  26.8 us (14%)
  local copies, waits for them, and re-layouts  21.2 us (11%)
  other arithmetic  16.7 us (9%)
  between operations  14.6 us (8%)
    ppermute x2, waiting for transfers between devices, gathered_sum(): lax.ppermute(outgoing, 'wloop', [(source, (source - step) % ways) for sou...  38.1 us
    ppermute x5, starting transfers between devices, shifted(): lax.ppermute(value, axis, [(source, source + steps) for source in range(i...  20.5 us
    ppermute x1, waiting for transfers between devices, shards(): lax.ppermute(part, 'wloop', [(source, (source + step) % ways) for source...  11.9 us
    ppermute x5, waiting for transfers between devices, shifted(): lax.ppermute(value, axis, [(source, source + steps) for source in range(i...  11.4 us
    dot_general x2, matrix products, shards(): jnp.einsum('td,dje->jte', rows, w_keyvalue, preferred_element_type=jnp.fl...  10.4 us
    dot_general x2, matrix products, output_share(): jnp.dot(attended, lax.dynamic_slice_in_dim(w_output_rows, index * share,...  8.32 us
    dot_general x2, matrix products, shards(): jnp.dot(rows, w_query, preferred_element_type=jnp.float32)  7.64 us
    unnamed x47, local copies, waits for them, and re-layouts  6.09 us
  transfers between devices with their start and end apart: 11, of which 5 were waited for; matrix products, arithmetic and copies ran while one was open for 29% of the time, Pallas kernels for 0%

profile of v7, /device:TPU:0, one launch (start us, length us, event | category | flops | bytes accessed | tf_op | source)
XLA Modules:
  0.0 191.9 jit_solution(12848485611637905690)
XLA Ops:
  6.5 2.2 %fusion.2 = f32[512]{0:T(512)S(1)} fusion(bf16[1,512,2048]{2,1,0:T(8,128)(2,1)} %param.7), kind=kLoop, calls=%fused_computation.9 | loop fusion | flops 3145216 | bytes 2099200 | tf_op jit(solution)/shard_map/reduce_sum | solution.py:18
  11.1 3.0 %collective-permute-start = (bf16[256,1024]{1,0:T(8,128)(2,1)S(1)}, bf16[256,1024]{1,0:T(8,128)(2,1)S(1)}, u32[]{:S(2)}, u32[]{:S(2)}) collective-permute-start(bf16[256,1024]{1,0:T(8,128)(2,1)S(1)} %dynamic-slice_bitcast_fusion), channel_id=1, source_target_pairs={{0,2},{2,0},{1,3},{3,1},{4,6},{6,4},{5,7},{7,5},{8,10},{10,8},{9,1... | collective-permute-start | bytes 1572872 | tf_op jit(solution)/shard_map/ppermute | solution.py:77
  14.1 11.9 %collective-permute-done = bf16[256,1024]{1,0:T(8,128)(2,1)S(1)} collective-permute-done((bf16[256,1024]{1,0:T(8,128)(2,1)S(1)}, bf16[256,1024]{1,0:T(8,128)(2,1)S(1)}, u32[]{:S(2)}, u32[]{:S(2)}) %collective-permute-start) | collective-permute-done | bytes 524320 | tf_op jit(solution)/shard_map/ppermute | solution.py:77
  26.2 1.8 collective-permute-done.1
  29.0 1.8 gather_fusion
  31.1 6.3 %convert_bitcast_fusion = bf16[2,512,1024]{2,1,0:T(8,128)(2,1)} fusion(bf16[1024,2,1024]{2,1,0:T(2,128)(2,1)} %param.10, bf16[512,1024]{1,0:T(8,128)(2,1)S(1)} %bitcast_select_fusion), kind=kOutput, calls=%fused_computation.40 | convolution fusion | flops 2148532224 | bytes 7340032 | tf_op jit(solution)/shard_map/td,dje->jte/dot_general | solution.py:100
  37.4 1.7 collective-permute-start.2
  43.7 3.7 %convolution_convert_fusion = bf16[512,1024]{1,0:T(8,128)(2,1)} fusion(bf16[512,1024]{1,0:T(8,128)(2,1)} %copy-done.13, bf16[1024,1024]{1,0:T(8,128)(2,1)S(1)} %copy-done), kind=kOutput, calls=%fused_computation.42 | convolution fusion | flops 1074266112 | bytes 4194304 | tf_op jit(solution)/shard_map/dot_general | solution.py:105
  47.4 38.1 %collective-permute-done.2 = bf16[2,512,1024]{2,1,0:T(8,128)(2,1)} collective-permute-done((bf16[2,512,1024]{2,1,0:T(8,128)(2,1)}, bf16[2,512,1024]{2,1,0:T(8,128)(2,1)}, u32[]{:S(2)}, u32[]{:S(2)}) %collective-permute-start.2) | collective-permute-done | bytes 2097184 | tf_op jit(solution)/shard_map/ppermute | solution.py:91
  85.4 4.1 %bitcast_add_fusion = f32[2,512,1024]{2,1,0:T(8,128)S(1)} fusion(bf16[2,512,1024]{2,1,0:T(8,128)(2,1)} %collective-permute-done.2, bf16[1024,2,1024]{2,1,0:T(2,128)(2,1)S(1)} %copy-done.20, bf16[1,512,2048]{2,1,0:T(8,128)(2,1)S(1)} %copy-done.8, s32[]{:T(128)S(6)} %select_n.80), kind=kOutput, calls=%fused_computation.12 | convolution fusion | flops 2149580800 | bytes 11534340 | tf_op jit(solution)/shard_map/td,dje->jte/dot_general | solution.py:100
  91.8 4.7 %collective-permute-start.5 = (bf16[1,512,1024]{2,1,0:T(8,128)(2,1)}, bf16[1,512,1024]{2,1,0:T(8,128)(2,1)}, u32[]{:S(2)}, u32[]{:S(2)}) collective-permute-start(bf16[1,512,1024]{2,1,0:T(8,128)(2,1)} %slice.63), channel_id=1, source_target_pairs={{0,4},{4,8},{8,12},{1,5},{5,9},{9,13},{2,6},{6,10},{10,14},{3,7},{... | collective-permute-start | bytes 3145736 | tf_op jit(solution)/shard_map/ppermute | solution.py:14
  96.5 1.5 collective-permute-start.3
  98.0 1.8 copy.89
  99.8 2.2 %reduce_sum.58 = f32[512,8]{1,0:T(8,128)S(1)} reduce(f32[512,8,128]{2,1,0:T(8,128)} %bitcast.119, f32[]{:T(128)} %constant.93.clone.1), dimensions={2}, to_apply=%region_2.3 | reduce | flops 520192 | bytes 2113540 | tf_op jit(solution)/shard_map/reduce_sum | solution.py:18
  102.2 1.6 mul.218
  103.8 2.9 %copy.84 = f32[1,512,1024]{2,1,0:T(8,128)} copy(f32[1,512,1024]{1,2,0:T(8,128)} %bitcast.120) | data formatting | bytes 4194304 | tf_op jit(solution)/shard_map/mul | solution.py:18
  106.6 4.5 %multiply_convert_fusion = (bf16[1,512,1024]{2,1,0:T(8,128)(2,1)}, f32[1,512,1024]{2,1,0:T(8,128)}) fusion(f32[1,512,1024]{2,1,0:T(8,128)} %copy.84, f32[2,512,1024]{2,1,0:T(8,128)} %copy-done.4), kind=kLoop, calls=%fused_computation.32 | loop fusion | flops 1048576 | bytes 7340032 | tf_op jit(solution)/shard_map/convert_element_type | solution.py:108
  111.1 3.5 %collective-permute-start.4 = (bf16[1,512,1024]{2,1,0:T(8,128)(2,1)}, bf16[1,512,1024]{2,1,0:T(8,128)(2,1)}, u32[]{:S(2)}, u32[]{:S(2)}) collective-permute-start(bf16[1,512,1024]{2,1,0:T(8,128)(2,1)} %get-tuple-element.19), channel_id=1, source_target_pairs={{0,4},{4,8},{8,12},{1,5},{5,9},{9,13},{2,6},{6,10},{10,14},{3,7},{... | collective-permute-start | bytes 3145736 | tf_op jit(solution)/shard_map/ppermute | solution.py:14
  117.0 3.3 %copy.83 = f32[1,512,1024]{1,2,0:T(8,128)} copy(f32[1,512,1024]{2,1,0:T(8,128)} %get-tuple-element.20) | data formatting | bytes 4194304 | tf_op jit(solution)/shard_map/reshape;squeeze | solution.py:108
  120.3 3.2 %fusion.36 = f32[1,8,128,128]{3,2,1,0:T(8,128)S(1)} fusion(bf16[512,8,128]{0,2,1:T(8,128)(2,1)S(1)} %bitcast.121, f32[512,8]{0,1:T(8,128)} %fusion.65, f32[512,8,128]{0,2,1:T(8,128)} %bitcast.116, f32[512,8]{0,1:T(8,128)S(1)} %add_rsqrt_fusion), kind=kOutput, calls=%fused_computation.45 | convolution fusion | flops 807403520 | bytes 3702784 | tf_op jit(solution)/shard_map/bht,bthd,bthe->bhde/dot_general | solution.py:125
  123.6 3.9 %multiply_bitcast_fusion.1 = (f32[64,8,8,128]{3,1,2,0:T(8,128)S(1)}, f32[64,8,8,128]{3,2,1,0:T(8,128)}) fusion(bf16[512,1024]{1,0:T(8,128)(2,1)} %collective-permute-done.3, bf16[1024,1024]{1,0:T(8,128)(2,1)S(1)} %copy-done, bf16[1,512,2048]{2,1,0:T(8,128)(2,1)S(1)} %copy-done.9, s32[]{:T(128)S(6)} %select_n.80), kind=kOutput, calls=%fused_computation.38 | convolution fusion | flops 1075314688 | bytes 8388612 | tf_op jit(solution)/shard_map/dot_general | solution.py:105
  128.8 11.4 %collective-permute-done.4 = bf16[1,512,1024]{2,1,0:T(8,128)(2,1)} collective-permute-done((bf16[1,512,1024]{2,1,0:T(8,128)(2,1)}, bf16[1,512,1024]{2,1,0:T(8,128)(2,1)}, u32[]{:S(2)}, u32[]{:S(2)}) %collective-permute-start.4) | collective-permute-done | bytes 1048608 | tf_op jit(solution)/shard_map/ppermute | solution.py:14
  141.8 4.5 %collective-permute-start.6 = (bf16[1,9,128,128]{3,2,1,0:T(8,128)(2,1)S(1)}, bf16[1,9,128,128]{3,2,1,0:T(8,128)(2,1)S(1)}, u32[]{:S(2)}, u32[]{:S(2)}) collective-permute-start(bf16[1,9,128,128]{3,2,1,0:T(8,128)(2,1)S(1)} %fusion.53), channel_id=1, source_target_pairs={{0,4},{4,8},{8,12},{1,5},{5,9},{9,13},{2,6},{6,10},{10,14},{3,7},{... | collective-permute-start | bytes 884744 | tf_op jit(solution)/shard_map/ppermute | solution.py:14
  147.1 2.6 %fusion = (f32[8,512]{1,0:T(8,128)S(1)}, f32[8,512,512]{1,2,0:T(8,128)S(1)}) fusion(pred[512,512]{0,1:T(8,128)(4,1)S(1)} %copy-done.15, bf16[512,8,128]{2,0,1:T(8,128)(2,1)S(1)} %fusion.11, f32[512,8,128]{0,2,1:T(8,128)S(1)} %bitcast.117, f32[512,8]{0,1:T(8,128)S(1)} %add_rsqrt_fusion), kind=kOutput, calls=%fused_computation.5 | convolution fusion | flops 544206848 | bytes 11829248 | tf_op jit(solution)/shard_map/bihd,bjhd->bhij/dot_general | solution.py:23
  149.8 5.4 %fusion.1 = (f32[8,512]{1,0:T(8,128)S(1)}, f32[8,512,512]{1,2,0:T(8,128)}) fusion(pred[512,512]{0,1:T(8,128)(4,1)S(1)} %fusion.46, bf16[512,8,128]{2,0,1:T(8,128)(2,1)S(1)} %fusion.11, bf16[512,8,128]{2,1,0:T(8,128)(2,1)S(1)} %bitcast.127), kind=kOutput, calls=%fused_computation.6 | convolution fusion | flops 543158272 | bytes 10764288 | tf_op jit(solution)/shard_map/bihd,bjhd->bhij/dot_general | solution.py:27
  155.3 3.5 %collective-permute-start.7 = (bf16[1,9,128,128]{3,2,1,0:T(8,128)(2,1)S(1)}, bf16[1,9,128,128]{3,2,1,0:T(8,128)(2,1)S(1)}, u32[]{:S(2)}, u32[]{:S(2)}) collective-permute-start(bf16[1,9,128,128]{3,2,1,0:T(8,128)(2,1)S(1)} %fusion.55), channel_id=1, source_target_pairs={{0,4},{4,8},{8,12},{1,5},{5,9},{9,13},{2,6},{6,10},{10,14},{3,7},{... | collective-permute-start | bytes 884744 | tf_op jit(solution)/shard_map/ppermute | solution.py:14
  158.8 3.4 %fusion.5 = f32[8,128,512]{2,1,0:T(8,128)} fusion(bf16[512,8,128]{0,2,1:T(8,128)(2,1)S(1)} %bitcast.122, f32[8,512,512]{1,2,0:T(8,128)S(1)} %get-tuple-element.24, f32[8,512]{1,0:T(8,128)S(1)} %add.155, pred[512,512]{0,1:T(8,128)(4,1)S(1)} %copy-done.15), kind=kOutput, calls=%fused_computation.13 | convolution fusion | flops 545259520 | bytes 11812864 | tf_op jit(solution)/shard_map/bhij,bjhd->bihd/dot_general | solution.py:38
  163.9 4.2 %collective-permute-start.8 = (bf16[1,9,128,128]{3,2,1,0:T(8,128)(2,1)S(1)}, bf16[1,9,128,128]{3,2,1,0:T(8,128)(2,1)S(1)}, u32[]{:S(2)}, u32[]{:S(2)}) collective-permute-start(bf16[1,9,128,128]{3,2,1,0:T(8,128)(2,1)S(1)} %fusion.57), channel_id=1, source_target_pairs={{0,4},{4,8},{8,12},{1,5},{5,9},{9,13},{2,6},{6,10},{10,14},{3,7},{... | collective-permute-start | bytes 884744 | tf_op jit(solution)/shard_map/ppermute | solution.py:14
  168.1 4.8 %fusion.6 = f32[8,128,512]{2,1,0:T(8,128)S(1)} fusion(bf16[512,8,128]{0,2,1:T(8,128)(2,1)S(1)} %bitcast.126, f32[8,512,512]{1,2,0:T(8,128)} %get-tuple-element.26, f32[8,512]{1,0:T(8,128)S(1)} %add.155, pred[512,512]{0,1:T(8,128)(4,1)} %copy-done.14), kind=kOutput, calls=%fused_computation.14 | convolution fusion | flops 545259520 | bytes 11812864 | tf_op jit(solution)/shard_map/bhij,bjhd->bihd/dot_general | solution.py:40
  173.7 3.8 %fusion.27 = bf16[512,1024]{1,0:T(8,128)(2,1)} fusion(bf16[512,1024]{0,1:T(8,128)(2,1)S(1)} %bitcast.128, bf16[1024,2048]{1,0:T(8,128)(2,1)} %all-gather.2.cloned.1.call-done, s32[]{:T(128)S(6)} %select_n.94), kind=kOutput, calls=%fused_computation.41 | convolution fusion | flops 1074266112 | bytes 4194308 | tf_op jit(solution)/shard_map/dot_general | solution.py:180
  177.6 3.0 %collective-permute-done.9 = bf16[512,1024]{1,0:T(8,128)(2,1)} collective-permute-done((bf16[512,1024]{1,0:T(8,128)(2,1)}, bf16[512,1024]{1,0:T(8,128)(2,1)}, u32[]{:S(2)}, u32[]{:S(2)}) %collective-permute-start.9) | collective-permute-done | bytes 1048608 | tf_op jit(solution)/shard_map/ppermute | solution.py:187
  180.6 4.5 %fusion.33 = bf16[1,512,1024]{2,1,0:T(8,128)(2,1)} fusion(bf16[512,1024]{1,0:T(8,128)(2,1)} %collective-permute-done.9, bf16[512,1024]{0,1:T(8,128)(2,1)S(1)} %bitcast.129, bf16[1024,2048]{1,0:T(8,128)(2,1)} %all-gather.2.cloned.1.call-done, s32[]{:T(128)S(6)} %select_n.79, bf16[1,512,2048]{2,1,0:T(8,128)(2,1)} %param.7), kind=kOutput, calls=%fused_computation.44 | convolution fusion | flops 1076363264 | bytes 6292480 | tf_op jit(solution)/shard_map/dot_general | solution.py:180
  (99 shorter events, 18.3 us)
Async XLA Ops:
  6.5 37.1 %copy-start = (bf16[1024,1024]{1,0:T(8,128)(2,1)S(1)}, bf16[1024,1024]{1,0:T(8,128)(2,1)}, u32[]{:S(2)}) copy-start(bf16[1024,1024]{1,0:T(8,128)(2,1)} %param.9) | copy-start | bytes 6291460
  6.5 2.2 %copy-start.18 = (f32[2048]{0:T(1024)S(1)}, f32[2048]{0:T(1024)}, u32[]{:S(2)}) copy-start(f32[2048]{0:T(1024)} %param.8) | copy-start | bytes 24580
  6.5 167.2 %all-gather.2.cloned.1.call-start = ((), (), s32[]{:S(2)}) async-start(), calls=%async_computation | async-start | bytes 6291456 | tf_op jit(solution)/shard_map/all_gather | solution.py:174
  6.5 2.4 %copy-start.2 = (bf16[1,512,2048]{2,1,0:T(8,128)(2,1)S(1)}, bf16[1,512,2048]{2,1,0:T(8,128)(2,1)}, u32[]{:S(2)}) copy-start(bf16[1,512,2048]{2,1,0:T(8,128)(2,1)} %param.7) | copy-start | bytes 6291460
  11.1 15.0 %collective-permute-start = (bf16[256,1024]{1,0:T(8,128)(2,1)S(1)}, bf16[256,1024]{1,0:T(8,128)(2,1)S(1)}, u32[]{:S(2)}, u32[]{:S(2)}) collective-permute-start(bf16[256,1024]{1,0:T(8,128)(2,1)S(1)} %dynamic-slice_bitcast_fusion), channel_id=1, source_target_pairs={{0,2},{2,0},{1,3},{3,1},{4,6},{6,4},{5,7},{7,5},{8,10},{10,8},{9,1... | collective-permute-start | bytes 1572872 | tf_op jit(solution)/shard_map/ppermute | solution.py:77
  26.1 1.9 collective-permute-start.1
  31.1 6.4 %copy-start.13 = (bf16[512,1024]{1,0:T(8,128)(2,1)}, bf16[512,1024]{1,0:T(8,128)(2,1)S(1)}, u32[]{:S(2)}) copy-start(bf16[512,1024]{1,0:T(8,128)(2,1)S(1)} %bitcast_select_fusion) | copy-start | bytes 3145732
  31.1 8.8 %copy-start.17 = (f32[1,8,512]{2,1,0:T(8,128)S(1)}, f32[1,8,512]{2,1,0:T(8,128)}, u32[]{:S(2)}) copy-start(f32[1,8,512]{2,1,0:T(8,128)} %param.12) | copy-start | bytes 49156
  37.4 48.0 %collective-permute-start.2 = (bf16[2,512,1024]{2,1,0:T(8,128)(2,1)}, bf16[2,512,1024]{2,1,0:T(8,128)(2,1)}, u32[]{:S(2)}, u32[]{:S(2)}) collective-permute-start(bf16[2,512,1024]{2,1,0:T(8,128)(2,1)} %convert_bitcast_fusion), channel_id=1, source_target_pairs={{0,2},{2,0},{1,3},{3,1},{4,6},{6,4},{5,7},{7,5},{8,10},{10,8},{9,1... | collective-permute-start | bytes 6291464 | tf_op jit(solution)/shard_map/ppermute | solution.py:91
  42.9 106.8 %copy-start.14 = (pred[512,512]{0,1:T(8,128)(4,1)}, pred[512,512]{0,1:T(8,128)(4,1)S(1)}, u32[]{:S(2)}) copy-start(pred[512,512]{0,1:T(8,128)(4,1)S(1)} %fusion.46) | copy-start | bytes 786436
  43.7 41.8 %copy-start.8 = (bf16[1,512,2048]{2,1,0:T(8,128)(2,1)S(1)}, bf16[1,512,2048]{2,1,0:T(8,128)(2,1)}, u32[]{:S(2)}) copy-start(bf16[1,512,2048]{2,1,0:T(8,128)(2,1)} %copy-done.7) | copy-start | bytes 6291460
  43.7 41.8 %copy-start.20 = (bf16[1024,2,1024]{2,1,0:T(2,128)(2,1)S(1)}, bf16[1024,2,1024]{2,1,0:T(2,128)(2,1)}, u32[]{:S(2)}) copy-start(bf16[1024,2,1024]{2,1,0:T(2,128)(2,1)} %param.10) | copy-start | bytes 12582916
  89.5 2.3 %copy-start.4 = (f32[2,512,1024]{2,1,0:T(8,128)}, f32[2,512,1024]{2,1,0:T(8,128)S(1)}, u32[]{:S(2)}) copy-start(f32[2,512,1024]{2,1,0:T(8,128)S(1)} %bitcast_add_fusion) | copy-start | bytes 12582916
  91.8 36.9 %collective-permute-start.5 = (bf16[1,512,1024]{2,1,0:T(8,128)(2,1)}, bf16[1,512,1024]{2,1,0:T(8,128)(2,1)}, u32[]{:S(2)}, u32[]{:S(2)}) collective-permute-start(bf16[1,512,1024]{2,1,0:T(8,128)(2,1)} %slice.63), channel_id=1, source_target_pairs={{0,4},{4,8},{8,12},{1,5},{5,9},{9,13},{2,6},{6,10},{10,14},{3,7},{... | collective-permute-start | bytes 3145736 | tf_op jit(solution)/shard_map/ppermute | solution.py:14
  96.5 27.0 %collective-permute-start.3 = (bf16[512,1024]{1,0:T(8,128)(2,1)}, bf16[512,1024]{1,0:T(8,128)(2,1)}, u32[]{:S(2)}, u32[]{:S(2)}) collective-permute-start(bf16[512,1024]{1,0:T(8,128)(2,1)} %convolution_convert_fusion), channel_id=1, source_target_pairs={{0,2},{2,0},{1,3},{3,1},{4,6},{6,4},{5,7},{7,5},{8,10},{10,8},{9,1... | collective-permute-start | bytes 3145736 | tf_op jit(solution)/shard_map/ppermute | solution.py:91
  111.1 29.0 %collective-permute-start.4 = (bf16[1,512,1024]{2,1,0:T(8,128)(2,1)}, bf16[1,512,1024]{2,1,0:T(8,128)(2,1)}, u32[]{:S(2)}, u32[]{:S(2)}) collective-permute-start(bf16[1,512,1024]{2,1,0:T(8,128)(2,1)} %get-tuple-element.19), channel_id=1, source_target_pairs={{0,4},{4,8},{8,12},{1,5},{5,9},{9,13},{2,6},{6,10},{10,14},{3,7},{... | collective-permute-start | bytes 3145736 | tf_op jit(solution)/shard_map/ppermute | solution.py:14
  117.0 3.3 %copy-start.5 = (bf16[1,512,1024]{1,2,0:T(8,128)(2,1)}, bf16[1,512,1024]{1,2,0:T(8,128)(2,1)S(1)}, u32[]{:S(2)}) copy-start(bf16[1,512,1024]{1,2,0:T(8,128)(2,1)S(1)} %copy.86) | copy-start | bytes 3145732
  120.3 3.3 %copy-start.9 = (bf16[1,512,2048]{2,1,0:T(8,128)(2,1)S(1)}, bf16[1,512,2048]{2,1,0:T(8,128)(2,1)}, u32[]{:S(2)}) copy-start(bf16[1,512,2048]{2,1,0:T(8,128)(2,1)} %copy-done.7) | copy-start | bytes 6291460
  128.0 13.7 %copy-start.19 = (f32[9]{0:T(128)S(1)}, f32[9]{0:T(128)}, u32[]{:S(2)}) copy-start(f32[9]{0:T(128)} %pad.9.clone) | copy-start | bytes 112
  128.7 17.7 %copy-start.10 = (f32[64,8,8,128]{3,2,1,0:T(8,128)S(1)}, f32[64,8,8,128]{3,2,1,0:T(8,128)}, u32[]{:S(2)}) copy-start(f32[64,8,8,128]{3,2,1,0:T(8,128)} %get-tuple-element.22) | copy-start | bytes 6291460
  141.7 5.4 %copy-start.3 = (f32[1,512,1024]{1,2,0:T(8,128)S(1)}, f32[1,512,1024]{1,2,0:T(8,128)}, u32[]{:S(2)}) copy-start(f32[1,512,1024]{1,2,0:T(8,128)} %copy.83) | copy-start | bytes 6291460
  141.7 5.4 %copy-start.15 = (pred[512,512]{0,1:T(8,128)(4,1)S(1)}, pred[512,512]{0,1:T(8,128)(4,1)}, u32[]{:S(2)}) copy-start(pred[512,512]{0,1:T(8,128)(4,1)} %iota_compare_fusion.1) | copy-start | bytes 786436
  141.8 13.3 %collective-permute-start.6 = (bf16[1,9,128,128]{3,2,1,0:T(8,128)(2,1)S(1)}, bf16[1,9,128,128]{3,2,1,0:T(8,128)(2,1)S(1)}, u32[]{:S(2)}, u32[]{:S(2)}) collective-permute-start(bf16[1,9,128,128]{3,2,1,0:T(8,128)(2,1)S(1)} %fusion.53), channel_id=1, source_target_pairs={{0,4},{4,8},{8,12},{1,5},{5,9},{9,13},{2,6},{6,10},{10,14},{3,7},{... | collective-permute-start | bytes 884744 | tf_op jit(solution)/shard_map/ppermute | solution.py:14
  147.1 2.6 %copy-start.11 = (bf16[512,8,128]{2,0,1:T(8,128)(2,1)}, bf16[512,8,128]{2,0,1:T(8,128)(2,1)S(1)}, u32[]{:S(2)}) copy-start(bf16[512,8,128]{2,0,1:T(8,128)(2,1)S(1)} %fusion.11) | copy-start | bytes 3145732
  149.7 9.0 %copy-start.6 = (bf16[1,512,1024]{1,2,0:T(8,128)(2,1)S(1)}, bf16[1,512,1024]{1,2,0:T(8,128)(2,1)}, u32[]{:S(2)}) copy-start(bf16[1,512,1024]{1,2,0:T(8,128)(2,1)} %copy-done.5) | copy-start | bytes 3145732
  155.3 8.4 %collective-permute-start.7 = (bf16[1,9,128,128]{3,2,1,0:T(8,128)(2,1)S(1)}, bf16[1,9,128,128]{3,2,1,0:T(8,128)(2,1)S(1)}, u32[]{:S(2)}, u32[]{:S(2)}) collective-permute-start(bf16[1,9,128,128]{3,2,1,0:T(8,128)(2,1)S(1)} %fusion.55), channel_id=1, source_target_pairs={{0,4},{4,8},{8,12},{1,5},{5,9},{9,13},{2,6},{6,10},{10,14},{3,7},{... | collective-permute-start | bytes 884744 | tf_op jit(solution)/shard_map/ppermute | solution.py:14
  163.9 9.1 %collective-permute-start.8 = (bf16[1,9,128,128]{3,2,1,0:T(8,128)(2,1)S(1)}, bf16[1,9,128,128]{3,2,1,0:T(8,128)(2,1)S(1)}, u32[]{:S(2)}, u32[]{:S(2)}) collective-permute-start(bf16[1,9,128,128]{3,2,1,0:T(8,128)(2,1)S(1)} %fusion.57), channel_id=1, source_target_pairs={{0,4},{4,8},{8,12},{1,5},{5,9},{9,13},{2,6},{6,10},{10,14},{3,7},{... | collective-permute-start | bytes 884744 | tf_op jit(solution)/shard_map/ppermute | solution.py:14
  168.1 5.0 %copy-start.12 = (bf16[512,8,128]{2,0,1:T(8,128)(2,1)S(1)}, bf16[512,8,128]{2,0,1:T(8,128)(2,1)}, u32[]{:S(2)}) copy-start(bf16[512,8,128]{2,0,1:T(8,128)(2,1)} %copy-done.11) | copy-start | bytes 3145732
  168.1 5.0 %copy-start.16 = (f32[512,8]{0,1:T(8,128)S(1)}, f32[512,8]{0,1:T(8,128)}, u32[]{:S(2)}) copy-start(f32[512,8]{0,1:T(8,128)} %get-tuple-element.17) | copy-start | bytes 49156
  168.1 5.0 %copy-start.21 = (f32[8,128,512]{2,1,0:T(8,128)S(1)}, f32[8,128,512]{2,1,0:T(8,128)}, u32[]{:S(2)}) copy-start(f32[8,128,512]{2,1,0:T(8,128)} %fusion.5) | copy-start | bytes 6291460
  177.6 3.0 %collective-permute-start.9 = (bf16[512,1024]{1,0:T(8,128)(2,1)}, bf16[512,1024]{1,0:T(8,128)(2,1)}, u32[]{:S(2)}, u32[]{:S(2)}) collective-permute-start(bf16[512,1024]{1,0:T(8,128)(2,1)} %fusion.27), channel_id=1, source_target_pairs={{0,1},{1,0},{2,3},{3,2},{4,5},{5,4},{6,7},{7,6},{8,9},{9,8},{10,11... | collective-permute-start | bytes 3145736 | tf_op jit(solution)/shard_map/ppermute | solution.py:187
  177.6 7.5 %copy-start.1 = (bf16[1024,1024]{1,0:T(8,128)(2,1)S(1)}, bf16[1024,1024]{1,0:T(8,128)(2,1)}, u32[]{:S(2)}) copy-start(bf16[1024,1024]{1,0:T(8,128)(2,1)} %param.9) | copy-start | bytes 6291460
  (1 other events, 1.3 us)
Sparse Core Ops, SparseCore 0:
  117.2 54.1 all-gather.1

commit v8 on v7

--- a/solution.py
+++ b/solution.py
@@ -95,10 +95,12 @@
             ).astype(jnp.float32)
         return total
 
-    pair_raw = gathered_sum(
+    pair_raw = jnp.stack(
         [
-            jnp.einsum("td,dje->jte", rows, w_keyvalue, preferred_element_type=jnp.float32)
-            for rows in stacked
+            gathered_sum(
+                [jnp.dot(rows, w_keyvalue[:, kind, :], preferred_element_type=jnp.float32) for rows in stacked]
+            )
+            for kind in range(2)
         ]
     )
     query_raw = gathered_sum(
@@ -109,11 +111,15 @@
         jnp.bfloat16
     )
     values = pair_raw[1].reshape(trajs, span, heads_here, head_dim).astype(jnp.bfloat16)
-    prior_keys, prior_values = shifted(
-        (lookup_vectors.reshape(trajs, span, inner_here), values.reshape(trajs, span, inner_here)),
+    prior_both = shifted(
+        jnp.concatenate(
+            [lookup_vectors.reshape(trajs, span, inner_here), values.reshape(trajs, span, inner_here)],
+            axis=-1,
+        ),
         "seq",
         1,
     )
+    prior_keys, prior_values = prior_both[..., :inner_here], prior_both[..., inner_here:]
     queries = rms_rows(query_raw.reshape(trajs, span, heads_here, head_dim), 1e-06).astype(
         jnp.bfloat16
     )

time: 192 us -> 197 us (1.026)
  local copies, waits for them, and re-layouts: 21.2 us -> 25.8 us
  starting transfers between devices: 26.8 us -> 23.9 us
  other arithmetic: 16.7 us -> 19.3 us
    ppermute x5 -> x4, waiting for transfers between devices: 11.4 us -> 24.6 us  [shifted(): lax.ppermute(value, axis, [(source, source + steps) for source in range(i...]
    ppermute x1, waiting for transfers between devices: 11.9 us -> 2.78 us  [shards(): lax.ppermute(part, 'wloop', [(source, (source + step) % ways) for source...]
    slice x2 -> x3, local copies, waits for them, and re-layouts: 1.4 us -> 8.87 us  [the longest x1 7 us: shards(): w_keyvalue[:, kind, :]]
    ppermute x5 -> x4, starting transfers between devices: 20.5 us -> 17 us  [shifted(): lax.ppermute(value, axis, [(source, source + steps) for source in range(i...]
    ppermute x2 -> x3, waiting for transfers between devices: 38.1 us -> 34.7 us  [gathered_sum(): lax.ppermute(outgoing, 'wloop', [(source, (source - step) % ways) for sou...]
    unnamed x47, local copies, waits for them, and re-layouts: 6.09 us -> 3.83 us
    dot_general x2 -> x4, matrix products: 10.4 us -> 12.6 us  [shards(): jnp.dot(rows, w_keyvalue[:, kind, :], preferred_element_type=jnp.float32)]
  transfers between devices with their start and end apart: 11 -> 11, of which waited for: 5 -> 6; matrix products, arithmetic and copies ran while one was open for 29% -> 35% of each run, Pallas kernels for 0% -> 0%
where the time goes in v8:
time: 197 us
  waiting for transfers between devices  66 us (34%)
  matrix products  47 us (24%)
  local copies, waits for them, and re-layouts  25.8 us (13%)
  starting transfers between devices  23.9 us (12%)
  other arithmetic  19.3 us (10%)
  between operations  14.6 us (7%)
    ppermute x3, waiting for transfers between devices, gathered_sum(): lax.ppermute(outgoing, 'wloop', [(source, (source - step) % ways) for sou...  34.7 us
    ppermute x4, waiting for transfers between devices, shifted(): lax.ppermute(value, axis, [(source, source + steps) for source in range(i...  24.6 us
    ppermute x4, starting transfers between devices, shifted(): lax.ppermute(value, axis, [(source, source + steps) for source in range(i...  17 us
    dot_general x4, matrix products, shards(): jnp.dot(rows, w_keyvalue[:, kind, :], preferred_element_type=jnp.float32)  12.6 us
    dot_general x2, matrix products, output_share(): jnp.dot(attended, lax.dynamic_slice_in_dim(w_output_rows, index * share,...  8.32 us
    slice x1, local copies, waits for them, and re-layouts, shards(): w_keyvalue[:, kind, :]  7 us
    dot_general x2, matrix products, shards(): jnp.dot(rows, w_query, preferred_element_type=jnp.float32)  6.16 us
    dot_general x1, matrix products, window_mix(): jnp.einsum('bihd,bjhd->bhij', queries, prior_keys, preferred_element_type...  5.26 us
  transfers between devices with their start and end apart: 11, of which 6 were waited for; matrix products, arithmetic and copies ran while one was open for 35% of the time, Pallas kernels for 0%

profile of v8, /device:TPU:0, one launch (start us, length us, event | category | flops | bytes accessed | tf_op | source)
XLA Modules:
  0.0 196.6 jit_solution(6764068396404386035)
XLA Ops:
  6.5 2.2 %fusion.2 = f32[512]{0:T(512)S(1)} fusion(bf16[1,512,2048]{2,1,0:T(8,128)(2,1)} %param.7), kind=kLoop, calls=%fused_computation.9 | loop fusion | flops 3145216 | bytes 2099200 | tf_op jit(solution)/shard_map/reduce_sum | solution.py:18
  8.8 2.3 %fusion.4 = bf16[1,512,2048]{2,1,0:T(8,128)(2,1)S(1)} fusion(bf16[1,512,2048]{2,1,0:T(8,128)(2,1)} %param.7, f32[2048]{0:T(1024)S(1)} %copy-done.20, f32[512]{0:T(512)S(1)} %add_rsqrt_fusion.2), kind=kLoop, calls=%fused_computation.11 | loop fusion | flops 4194304 | bytes 4204544 | tf_op jit(solution)/shard_map/convert_element_type | solution.py:50
  11.4 3.0 %collective-permute-start = (bf16[256,1024]{1,0:T(8,128)(2,1)S(1)}, bf16[256,1024]{1,0:T(8,128)(2,1)S(1)}, u32[]{:S(2)}, u32[]{:S(2)}) collective-permute-start(bf16[256,1024]{1,0:T(8,128)(2,1)S(1)} %dynamic-slice_bitcast_fusion), channel_id=1, source_target_pairs={{0,2},{2,0},{1,3},{3,1},{4,6},{6,4},{5,7},{7,5},{8,10},{10,8},{9,1... | collective-permute-start | bytes 1572872 | tf_op jit(solution)/shard_map/ppermute | solution.py:77
  14.5 7.0 %fusion.82 = (bf16[1024,1,1024]{2,1,0:T(2,128)(2,1)}, bf16[1024,1,1024]{2,1,0:T(2,128)(2,1)}) fusion(bf16[1024,2,1024]{2,1,0:T(2,128)(2,1)S(1)} %copy-done.3), kind=kLoop, calls=%fused_computation.127 | loop fusion | bytes 8388608 | tf_op jit(solution)/shard_map/slice | solution.py:101
  23.6 2.8 %collective-permute-done = bf16[256,1024]{1,0:T(8,128)(2,1)S(1)} collective-permute-done((bf16[256,1024]{1,0:T(8,128)(2,1)S(1)}, bf16[256,1024]{1,0:T(8,128)(2,1)S(1)}, u32[]{:S(2)}, u32[]{:S(2)}) %collective-permute-start) | collective-permute-done | bytes 524320 | tf_op jit(solution)/shard_map/ppermute | solution.py:77
  29.4 1.8 gather_fusion
  31.4 4.8 %convolution_convert_fusion = bf16[512,1024]{1,0:T(8,128)(2,1)} fusion(bf16[512,1024]{1,0:T(8,128)(2,1)S(1)} %bitcast.144, bf16[1024,1,1024]{2,1,0:T(2,128)(2,1)} %get-tuple-element.19), kind=kOutput, calls=%fused_computation.41 | convolution fusion | flops 1074266112 | bytes 4194304 | tf_op jit(solution)/shard_map/dot_general | solution.py:101
  38.9 3.8 %convolution_convert_fusion.2 = bf16[512,1024]{1,0:T(8,128)(2,1)S(1)} fusion(bf16[512,1024]{1,0:T(8,128)(2,1)} %bitcast.145, bf16[1024,1,1024]{2,1,0:T(2,128)(2,1)} %get-tuple-element.20), kind=kOutput, calls=%fused_computation.43 | convolution fusion | flops 1074266112 | bytes 4194304 | tf_op jit(solution)/shard_map/dot_general | solution.py:101
  43.3 2.2 %convolution_convert_fusion.1 = bf16[512,1024]{1,0:T(8,128)(2,1)} fusion(bf16[512,1024]{1,0:T(8,128)(2,1)S(1)} %bitcast_select_fusion, bf16[1024,1024]{1,0:T(8,128)(2,1)S(1)} %copy-done), kind=kOutput, calls=%fused_computation.42 | convolution fusion | flops 1074266112 | bytes 4194304 | tf_op jit(solution)/shard_map/dot_general | solution.py:107
  45.5 17.0 %collective-permute-done.3 = bf16[512,1024]{1,0:T(8,128)(2,1)} collective-permute-done((bf16[512,1024]{1,0:T(8,128)(2,1)}, bf16[512,1024]{1,0:T(8,128)(2,1)}, u32[]{:S(2)}, u32[]{:S(2)}) %collective-permute-start.3) | collective-permute-done | bytes 1048608 | tf_op jit(solution)/shard_map/ppermute | solution.py:91
  62.6 2.6 %convert_add_fusion.2 = f32[512,1024]{1,0:T(8,128)S(1)} fusion(bf16[512,1024]{1,0:T(8,128)(2,1)} %collective-permute-done.3, bf16[1024,1,1024]{2,1,0:T(2,128)(2,1)S(1)} %copy-done.9, bf16[1,512,2048]{2,1,0:T(8,128)(2,1)S(1)} %copy-done.11, s32[]{:T(128)S(6)} %select_n.95), kind=kOutput, calls=%fused_computation.38 | convolution fusion | flops 1074790400 | bytes 8388612 | tf_op jit(solution)/shard_map/dot_general | solution.py:101
  66.5 17.6 %collective-permute-done.2 = bf16[512,1024]{1,0:T(8,128)(2,1)S(1)} collective-permute-done((bf16[512,1024]{1,0:T(8,128)(2,1)S(1)}, bf16[512,1024]{1,0:T(8,128)(2,1)S(1)}, u32[]{:S(2)}, u32[]{:S(2)}) %collective-permute-start.2) | collective-permute-done | bytes 1048608 | tf_op jit(solution)/shard_map/ppermute | solution.py:91
  85.5 1.8 collective-permute-start.4
  89.1 2.2 %reduce_sum.58 = f32[512,8]{1,0:T(8,128)S(1)} reduce(f32[512,8,128]{2,1,0:T(8,128)} %bitcast.135, f32[]{:T(128)} %constant.93.clone.1), dimensions={2}, to_apply=%region_2.3 | reduce | flops 520192 | bytes 2113540 | tf_op jit(solution)/shard_map/reduce_sum | solution.py:18
  93.1 2.9 %copy.82 = f32[512,1024]{1,0:T(8,128)} copy(f32[512,1024]{0,1:T(8,128)} %bitcast.136) | data formatting | bytes 4194304 | tf_op jit(solution)/shard_map/mul | solution.py:18
  96.0 2.5 %fusion.33 = bf16[1,512,1024]{2,1,0:T(8,128)(2,1)S(1)} fusion(f32[512,1024]{1,0:T(8,128)} %copy-done.2, f32[512,1024]{1,0:T(8,128)} %copy.82), kind=kLoop, calls=%fused_computation.49 | loop fusion | flops 1048576 | bytes 5242880 | tf_op jit(solution)/shard_map/convert_element_type | solution.py:110
  100.1 4.8 %collective-permute-start.5 = (bf16[1,512,2048]{2,1,0:T(8,128)(2,1)}, bf16[1,512,2048]{2,1,0:T(8,128)(2,1)}, u32[]{:S(2)}, u32[]{:S(2)}) collective-permute-start(bf16[1,512,2048]{2,1,0:T(8,128)(2,1)} %pad_maximum_fusion.1), channel_id=1, source_target_pairs={{0,4},{4,8},{8,12},{1,5},{5,9},{9,13},{2,6},{6,10},{10,14},{3,7},{... | collective-permute-start | bytes 6291464 | tf_op jit(solution)/shard_map/ppermute | solution.py:14
  106.8 3.3 %copy.81 = f32[512,1024]{0,1:T(8,128)} copy(f32[512,1024]{1,0:T(8,128)} %copy-done.2) | data formatting | bytes 4194304 | tf_op jit(solution)/shard_map/reshape;squeeze;stack | solution.py:110
  110.1 2.9 %fusion.30 = f32[1,8,128,128]{3,2,1,0:T(8,128)S(1)} fusion(bf16[512,8,128]{0,2,1:T(8,128)(2,1)S(1)} %bitcast.137, f32[512,8]{0,1:T(8,128)S(1)} %fusion.65, f32[512,8,128]{0,2,1:T(8,128)} %bitcast.132, f32[512,8]{0,1:T(8,128)S(1)} %add_rsqrt_fusion), kind=kOutput, calls=%fused_computation.48 | convolution fusion | flops 807403520 | bytes 3702784 | tf_op jit(solution)/shard_map/bht,bthd,bthe->bhde/dot_general | solution.py:131
  113.1 3.9 %multiply_bitcast_fusion.1 = (f32[64,8,8,128]{3,1,2,0:T(8,128)S(1)}, f32[64,8,8,128]{3,2,1,0:T(8,128)}) fusion(bf16[512,1024]{1,0:T(8,128)(2,1)} %collective-permute-done.4, bf16[1024,1024]{1,0:T(8,128)(2,1)S(1)} %copy-done, bf16[1,512,2048]{2,1,0:T(8,128)(2,1)S(1)} %copy-done.12, s32[]{:T(128)S(6)} %select_n.95), kind=kOutput, calls=%fused_computation.36 | convolution fusion | flops 1075314688 | bytes 8388612 | tf_op jit(solution)/shard_map/dot_general | solution.py:107
  118.3 2.3 %fusion.7 = bf16[512,8,128]{2,0,1:T(8,128)(2,1)S(1)} fusion(f32[64,8,8,128]{3,2,1,0:T(8,128)} %get-tuple-element.22, f32[512,8]{0,1:T(8,128)S(1)} %add_rsqrt_fusion.1), kind=kLoop, calls=%fused_computation.16 | loop fusion | flops 1048576 | bytes 3162112 | tf_op jit(solution)/shard_map/convert_element_type | solution.py:123
  120.7 2.6 %fusion = (f32[8,512]{1,0:T(8,128)S(1)}, f32[8,512,512]{1,2,0:T(8,128)S(1)}) fusion(pred[512,512]{0,1:T(8,128)(4,1)S(1)} %copy-done.17, bf16[512,8,128]{2,0,1:T(8,128)(2,1)S(1)} %fusion.7, f32[512,8,128]{0,2,1:T(8,128)S(1)} %bitcast.133, f32[512,8]{0,1:T(8,128)S(1)} %add_rsqrt_fusion), kind=kOutput, calls=%fused_computation.5 | convolution fusion | flops 544206848 | bytes 11829248 | tf_op jit(solution)/shard_map/bihd,bjhd->bhij/dot_general | solution.py:23
  123.3 24.6 %collective-permute-done.5 = bf16[1,512,2048]{2,1,0:T(8,128)(2,1)} collective-permute-done((bf16[1,512,2048]{2,1,0:T(8,128)(2,1)}, bf16[1,512,2048]{2,1,0:T(8,128)(2,1)}, u32[]{:S(2)}, u32[]{:S(2)}) %collective-permute-start.5) | collective-permute-done | bytes 2097184 | tf_op jit(solution)/shard_map/ppermute | solution.py:14
  150.0 4.4 %collective-permute-start.6 = (bf16[1,9,128,128]{3,2,1,0:T(8,128)(2,1)S(1)}, bf16[1,9,128,128]{3,2,1,0:T(8,128)(2,1)S(1)}, u32[]{:S(2)}, u32[]{:S(2)}) collective-permute-start(bf16[1,9,128,128]{3,2,1,0:T(8,128)(2,1)S(1)} %fusion.53), channel_id=1, source_target_pairs={{0,4},{4,8},{8,12},{1,5},{5,9},{9,13},{2,6},{6,10},{10,14},{3,7},{... | collective-permute-start | bytes 884744 | tf_op jit(solution)/shard_map/ppermute | solution.py:14
  154.5 5.3 %fusion.1 = (f32[8,512]{1,0:T(8,128)S(1)}, f32[8,512,512]{1,2,0:T(8,128)}) fusion(pred[512,512]{0,1:T(8,128)(4,1)S(1)} %copy-done.16, bf16[512,8,128]{2,0,1:T(8,128)(2,1)S(1)} %fusion.7, bf16[512,8,128]{2,1,0:T(8,128)(2,1)S(1)} %bitcast.147), kind=kOutput, calls=%fused_computation.6 | convolution fusion | flops 543158272 | bytes 10764288 | tf_op jit(solution)/shard_map/bihd,bjhd->bhij/dot_general | solution.py:27
  159.9 3.6 %collective-permute-start.7 = (bf16[1,9,128,128]{3,2,1,0:T(8,128)(2,1)S(1)}, bf16[1,9,128,128]{3,2,1,0:T(8,128)(2,1)S(1)}, u32[]{:S(2)}, u32[]{:S(2)}) collective-permute-start(bf16[1,9,128,128]{3,2,1,0:T(8,128)(2,1)S(1)} %fusion.55), channel_id=1, source_target_pairs={{0,4},{4,8},{8,12},{1,5},{5,9},{9,13},{2,6},{6,10},{10,14},{3,7},{... | collective-permute-start | bytes 884744 | tf_op jit(solution)/shard_map/ppermute | solution.py:14
  163.5 3.4 %fusion.5 = f32[8,128,512]{2,1,0:T(8,128)} fusion(bf16[512,8,128]{0,2,1:T(8,128)(2,1)S(1)} %bitcast.138, f32[8,512,512]{1,2,0:T(8,128)S(1)} %get-tuple-element.28, f32[8,512]{1,0:T(8,128)S(1)} %add.159, pred[512,512]{0,1:T(8,128)(4,1)S(1)} %copy-done.18), kind=kOutput, calls=%fused_computation.13 | convolution fusion | flops 545259520 | bytes 11812864 | tf_op jit(solution)/shard_map/bhij,bjhd->bihd/dot_general | solution.py:38
  168.4 4.1 %collective-permute-start.8 = (bf16[1,9,128,128]{3,2,1,0:T(8,128)(2,1)S(1)}, bf16[1,9,128,128]{3,2,1,0:T(8,128)(2,1)S(1)}, u32[]{:S(2)}, u32[]{:S(2)}) collective-permute-start(bf16[1,9,128,128]{3,2,1,0:T(8,128)(2,1)S(1)} %fusion.57), channel_id=1, source_target_pairs={{0,4},{4,8},{8,12},{1,5},{5,9},{9,13},{2,6},{6,10},{10,14},{3,7},{... | collective-permute-start | bytes 884744 | tf_op jit(solution)/shard_map/ppermute | solution.py:14
  172.5 5.2 %fusion.6 = f32[8,128,512]{2,1,0:T(8,128)S(1)} fusion(bf16[512,8,128]{0,2,1:T(8,128)(2,1)} %bitcast.146, f32[8,512,512]{1,2,0:T(8,128)} %get-tuple-element.30, f32[8,512]{1,0:T(8,128)S(1)} %add.159, pred[512,512]{0,1:T(8,128)(4,1)} %fusion.45), kind=kOutput, calls=%fused_computation.14 | convolution fusion | flops 545259520 | bytes 11812864 | tf_op jit(solution)/shard_map/bhij,bjhd->bihd/dot_general | solution.py:40
  178.4 3.8 %fusion.19 = bf16[512,1024]{1,0:T(8,128)(2,1)} fusion(bf16[512,1024]{0,1:T(8,128)(2,1)S(1)} %bitcast.148, bf16[1024,2048]{1,0:T(8,128)(2,1)} %all-gather.2.cloned.1.call-done, s32[]{:T(128)S(6)} %select_n.111), kind=kOutput, calls=%fused_computation.40 | convolution fusion | flops 1074266112 | bytes 4194308 | tf_op jit(solution)/shard_map/dot_general | solution.py:186
  182.3 3.0 %collective-permute-done.9 = bf16[512,1024]{1,0:T(8,128)(2,1)} collective-permute-done((bf16[512,1024]{1,0:T(8,128)(2,1)}, bf16[512,1024]{1,0:T(8,128)(2,1)}, u32[]{:S(2)}, u32[]{:S(2)}) %collective-permute-start.9) | collective-permute-done | bytes 1048608 | tf_op jit(solution)/shard_map/ppermute | solution.py:193
  185.3 4.5 %fusion.27 = bf16[1,512,1024]{2,1,0:T(8,128)(2,1)} fusion(bf16[512,1024]{1,0:T(8,128)(2,1)} %collective-permute-done.9, bf16[512,1024]{0,1:T(8,128)(2,1)S(1)} %bitcast.149, bf16[1024,2048]{1,0:T(8,128)(2,1)} %all-gather.2.cloned.1.call-done, s32[]{:T(128)S(6)} %select_n.94, bf16[1,512,2048]{2,1,0:T(8,128)(2,1)} %param.7), kind=kOutput, calls=%fused_computation.47 | convolution fusion | flops 1076363264 | bytes 6292480 | tf_op jit(solution)/shard_map/dot_general | solution.py:186
  (104 shorter events, 23.6 us)
Async XLA Ops:
  6.5 36.7 %copy-start = (bf16[1024,1024]{1,0:T(8,128)(2,1)S(1)}, bf16[1024,1024]{1,0:T(8,128)(2,1)}, u32[]{:S(2)}) copy-start(bf16[1024,1024]{1,0:T(8,128)(2,1)} %param.9) | copy-start | bytes 6291460
  6.5 2.3 %copy-start.20 = (f32[2048]{0:T(1024)S(1)}, f32[2048]{0:T(1024)}, u32[]{:S(2)}) copy-start(f32[2048]{0:T(1024)} %param.8) | copy-start | bytes 24580
  6.5 171.9 %all-gather.2.cloned.1.call-start = ((), (), s32[]{:S(2)}) async-start(), calls=%async_computation | async-start | bytes 6291456 | tf_op jit(solution)/shard_map/all_gather | solution.py:180
  8.8 5.7 %copy-start.3 = (bf16[1024,2,1024]{2,1,0:T(2,128)(2,1)S(1)}, bf16[1024,2,1024]{2,1,0:T(2,128)(2,1)}, u32[]{:S(2)}) copy-start(bf16[1024,2,1024]{2,1,0:T(2,128)(2,1)} %param.10) | copy-start | bytes 12582916
  11.1 10.4 %copy-start.10 = (bf16[1,512,2048]{2,1,0:T(8,128)(2,1)}, bf16[1,512,2048]{2,1,0:T(8,128)(2,1)S(1)}, u32[]{:S(2)}) copy-start(bf16[1,512,2048]{2,1,0:T(8,128)(2,1)S(1)} %fusion.4) | copy-start | bytes 6291460
  11.4 15.0 %collective-permute-start = (bf16[256,1024]{1,0:T(8,128)(2,1)S(1)}, bf16[256,1024]{1,0:T(8,128)(2,1)S(1)}, u32[]{:S(2)}, u32[]{:S(2)}) collective-permute-start(bf16[256,1024]{1,0:T(8,128)(2,1)S(1)} %dynamic-slice_bitcast_fusion), channel_id=1, source_target_pairs={{0,2},{2,0},{1,3},{3,1},{4,6},{6,4},{5,7},{7,5},{8,10},{10,8},{9,1... | collective-permute-start | bytes 1572872 | tf_op jit(solution)/shard_map/ppermute | solution.py:77
  14.5 7.7 %copy-start.19 = (f32[1,8,512]{2,1,0:T(8,128)S(1)}, f32[1,8,512]{2,1,0:T(8,128)}, u32[]{:S(2)}) copy-start(f32[1,8,512]{2,1,0:T(8,128)} %param.12) | copy-start | bytes 49156
  26.4 1.9 collective-permute-start.1
  31.4 4.9 %copy-start.15 = (bf16[2,256,1024]{2,1,0:T(8,128)(2,1)}, bf16[2,256,1024]{2,1,0:T(8,128)(2,1)S(1)}, u32[]{:S(2)}) copy-start(bf16[2,256,1024]{2,1,0:T(8,128)(2,1)S(1)} %broadcast_select_fusion) | copy-start | bytes 3145732
  36.2 26.3 %collective-permute-start.3 = (bf16[512,1024]{1,0:T(8,128)(2,1)}, bf16[512,1024]{1,0:T(8,128)(2,1)}, u32[]{:S(2)}, u32[]{:S(2)}) collective-permute-start(bf16[512,1024]{1,0:T(8,128)(2,1)} %convolution_convert_fusion), channel_id=1, source_target_pairs={{0,2},{2,0},{1,3},{3,1},{4,6},{6,4},{5,7},{7,5},{8,10},{10,8},{9,1... | collective-permute-start | bytes 3145736 | tf_op jit(solution)/shard_map/ppermute | solution.py:91
  42.7 41.4 %collective-permute-start.2 = (bf16[512,1024]{1,0:T(8,128)(2,1)S(1)}, bf16[512,1024]{1,0:T(8,128)(2,1)S(1)}, u32[]{:S(2)}, u32[]{:S(2)}) collective-permute-start(bf16[512,1024]{1,0:T(8,128)(2,1)S(1)} %convolution_convert_fusion.2), channel_id=1, source_target_pairs={{0,2},{2,0},{1,3},{3,1},{4,6},{6,4},{5,7},{7,5},{8,10},{10,8},{9,1... | collective-permute-start | bytes 3145736 | tf_op jit(solution)/shard_map/ppermute | solution.py:91
  43.3 19.3 %copy-start.9 = (bf16[1024,1,1024]{2,1,0:T(2,128)(2,1)S(1)}, bf16[1024,1,1024]{2,1,0:T(2,128)(2,1)}, u32[]{:S(2)}) copy-start(bf16[1024,1,1024]{2,1,0:T(2,128)(2,1)} %get-tuple-element.19) | copy-start | bytes 6291460
  43.3 19.3 %copy-start.11 = (bf16[1,512,2048]{2,1,0:T(8,128)(2,1)S(1)}, bf16[1,512,2048]{2,1,0:T(8,128)(2,1)}, u32[]{:S(2)}) copy-start(bf16[1,512,2048]{2,1,0:T(8,128)(2,1)} %copy-done.10) | copy-start | bytes 6291460
  65.2 18.9 %copy-start.8 = (bf16[1024,1,1024]{2,1,0:T(2,128)(2,1)S(1)}, bf16[1024,1,1024]{2,1,0:T(2,128)(2,1)}, u32[]{:S(2)}) copy-start(bf16[1024,1,1024]{2,1,0:T(2,128)(2,1)} %get-tuple-element.20) | copy-start | bytes 6291460
  85.5 13.0 %copy-start.7 = (bf16[512,1024]{1,0:T(8,128)(2,1)}, bf16[512,1024]{1,0:T(8,128)(2,1)S(1)}, u32[]{:S(2)}) copy-start(bf16[512,1024]{1,0:T(8,128)(2,1)S(1)} %fusion.23) | copy-start | bytes 3145732
  85.5 27.6 %collective-permute-start.4 = (bf16[512,1024]{1,0:T(8,128)(2,1)}, bf16[512,1024]{1,0:T(8,128)(2,1)}, u32[]{:S(2)}, u32[]{:S(2)}) collective-permute-start(bf16[512,1024]{1,0:T(8,128)(2,1)} %convolution_convert_fusion.1), channel_id=1, source_target_pairs={{0,2},{2,0},{1,3},{3,1},{4,6},{6,4},{5,7},{7,5},{8,10},{10,8},{9,1... | collective-permute-start | bytes 3145736 | tf_op jit(solution)/shard_map/ppermute | solution.py:91
  100.1 47.8 %collective-permute-start.5 = (bf16[1,512,2048]{2,1,0:T(8,128)(2,1)}, bf16[1,512,2048]{2,1,0:T(8,128)(2,1)}, u32[]{:S(2)}, u32[]{:S(2)}) collective-permute-start(bf16[1,512,2048]{2,1,0:T(8,128)(2,1)} %pad_maximum_fusion.1), channel_id=1, source_target_pairs={{0,4},{4,8},{8,12},{1,5},{5,9},{9,13},{2,6},{6,10},{10,14},{3,7},{... | collective-permute-start | bytes 6291464 | tf_op jit(solution)/shard_map/ppermute | solution.py:14
  106.8 3.3 %copy-start.5 = (bf16[512,1024]{0,1:T(8,128)(2,1)}, bf16[512,1024]{0,1:T(8,128)(2,1)S(1)}, u32[]{:S(2)}) copy-start(bf16[512,1024]{0,1:T(8,128)(2,1)S(1)} %copy.86) | copy-start | bytes 3145732
  110.1 3.0 %copy-start.12 = (bf16[1,512,2048]{2,1,0:T(8,128)(2,1)S(1)}, bf16[1,512,2048]{2,1,0:T(8,128)(2,1)}, u32[]{:S(2)}) copy-start(bf16[1,512,2048]{2,1,0:T(8,128)(2,1)} %copy-done.10) | copy-start | bytes 6291460
  118.1 2.6 %copy-start.4 = (f32[512,1024]{0,1:T(8,128)S(1)}, f32[512,1024]{0,1:T(8,128)}, u32[]{:S(2)}) copy-start(f32[512,1024]{0,1:T(8,128)} %copy.81) | copy-start | bytes 6291460
  118.1 2.6 %copy-start.17 = (pred[512,512]{0,1:T(8,128)(4,1)S(1)}, pred[512,512]{0,1:T(8,128)(4,1)}, u32[]{:S(2)}) copy-start(pred[512,512]{0,1:T(8,128)(4,1)} %iota_compare_fusion.1) | copy-start | bytes 786436
  120.7 33.7 %copy-start.13 = (bf16[512,8,128]{2,0,1:T(8,128)(2,1)}, bf16[512,8,128]{2,0,1:T(8,128)(2,1)S(1)}, u32[]{:S(2)}) copy-start(bf16[512,8,128]{2,0,1:T(8,128)(2,1)S(1)} %fusion.7) | copy-start | bytes 3145732
  149.6 4.8 %copy-start.16 = (pred[512,512]{0,1:T(8,128)(4,1)S(1)}, pred[512,512]{0,1:T(8,128)(4,1)}, u32[]{:S(2)}) copy-start(pred[512,512]{0,1:T(8,128)(4,1)} %fusion.45) | copy-start | bytes 786436
  150.0 9.7 %collective-permute-start.6 = (bf16[1,9,128,128]{3,2,1,0:T(8,128)(2,1)S(1)}, bf16[1,9,128,128]{3,2,1,0:T(8,128)(2,1)S(1)}, u32[]{:S(2)}, u32[]{:S(2)}) collective-permute-start(bf16[1,9,128,128]{3,2,1,0:T(8,128)(2,1)S(1)} %fusion.53), channel_id=1, source_target_pairs={{0,4},{4,8},{8,12},{1,5},{5,9},{9,13},{2,6},{6,10},{10,14},{3,7},{... | collective-permute-start | bytes 884744 | tf_op jit(solution)/shard_map/ppermute | solution.py:14
  154.4 9.1 %copy-start.6 = (bf16[512,1024]{0,1:T(8,128)(2,1)S(1)}, bf16[512,1024]{0,1:T(8,128)(2,1)}, u32[]{:S(2)}) copy-start(bf16[512,1024]{0,1:T(8,128)(2,1)} %copy-done.5) | copy-start | bytes 3145732
  154.5 9.1 %copy-start.18 = (pred[512,512]{0,1:T(8,128)(4,1)S(1)}, pred[512,512]{0,1:T(8,128)(4,1)}, u32[]{:S(2)}) copy-start(pred[512,512]{0,1:T(8,128)(4,1)} %iota_compare_fusion.1) | copy-start | bytes 786436
  159.9 8.3 %collective-permute-start.7 = (bf16[1,9,128,128]{3,2,1,0:T(8,128)(2,1)S(1)}, bf16[1,9,128,128]{3,2,1,0:T(8,128)(2,1)S(1)}, u32[]{:S(2)}, u32[]{:S(2)}) collective-permute-start(bf16[1,9,128,128]{3,2,1,0:T(8,128)(2,1)S(1)} %fusion.55), channel_id=1, source_target_pairs={{0,4},{4,8},{8,12},{1,5},{5,9},{9,13},{2,6},{6,10},{10,14},{3,7},{... | collective-permute-start | bytes 884744 | tf_op jit(solution)/shard_map/ppermute | solution.py:14
  168.4 9.3 %collective-permute-start.8 = (bf16[1,9,128,128]{3,2,1,0:T(8,128)(2,1)S(1)}, bf16[1,9,128,128]{3,2,1,0:T(8,128)(2,1)S(1)}, u32[]{:S(2)}, u32[]{:S(2)}) collective-permute-start(bf16[1,9,128,128]{3,2,1,0:T(8,128)(2,1)S(1)} %fusion.57), channel_id=1, source_target_pairs={{0,4},{4,8},{8,12},{1,5},{5,9},{9,13},{2,6},{6,10},{10,14},{3,7},{... | collective-permute-start | bytes 884744 | tf_op jit(solution)/shard_map/ppermute | solution.py:14
  172.5 5.3 %copy-start.14 = (bf16[512,8,128]{2,0,1:T(8,128)(2,1)S(1)}, bf16[512,8,128]{2,0,1:T(8,128)(2,1)}, u32[]{:S(2)}) copy-start(bf16[512,8,128]{2,0,1:T(8,128)(2,1)} %copy-done.13) | copy-start | bytes 3145732
  172.5 5.3 %copy-start.21 = (f32[8,128,512]{2,1,0:T(8,128)S(1)}, f32[8,128,512]{2,1,0:T(8,128)}, u32[]{:S(2)}) copy-start(f32[8,128,512]{2,1,0:T(8,128)} %fusion.5) | copy-start | bytes 6291460
  182.3 3.0 %collective-permute-start.9 = (bf16[512,1024]{1,0:T(8,128)(2,1)}, bf16[512,1024]{1,0:T(8,128)(2,1)}, u32[]{:S(2)}, u32[]{:S(2)}) collective-permute-start(bf16[512,1024]{1,0:T(8,128)(2,1)} %fusion.19), channel_id=1, source_target_pairs={{0,1},{1,0},{2,3},{3,2},{4,5},{5,4},{6,7},{7,6},{8,9},{9,8},{10,11... | collective-permute-start | bytes 3145736 | tf_op jit(solution)/shard_map/ppermute | solution.py:193
  182.3 7.5 %copy-start.1 = (bf16[1024,1024]{1,0:T(8,128)(2,1)S(1)}, bf16[1024,1024]{1,0:T(8,128)(2,1)}, u32[]{:S(2)}) copy-start(bf16[1024,1024]{1,0:T(8,128)(2,1)} %param.9) | copy-start | bytes 6291460
  (1 other events, 1.3 us)
Sparse Core Ops, SparseCore 0:
  110.2 54.8 all-gather.1

commit v9 on v7

--- a/solution.py
+++ b/solution.py
@@ -95,25 +95,36 @@
             ).astype(jnp.float32)
         return total
 
-    pair_raw = gathered_sum(
-        [
-            jnp.einsum("td,dje->jte", rows, w_keyvalue, preferred_element_type=jnp.float32)
-            for rows in stacked
-        ]
-    )
+    kv_partials = [
+        jnp.einsum("td,dje->jte", rows, w_keyvalue, preferred_element_type=jnp.float32)
+        for rows in stacked
+    ]
+    pieces = 2
+    rows_per = count // pieces
+    raw_chunks, key_chunks, value_chunks, prior_chunks = [], [], [], []
+    for piece in range(pieces):
+        raw = gathered_sum([p[:, piece * rows_per : (piece + 1) * rows_per] for p in kv_partials])
+        keys_here = rms_rows(raw[0].reshape(rows_per, heads_here, head_dim), 1e-06).astype(jnp.bfloat16)
+        values_here = raw[1].reshape(rows_per, heads_here, head_dim).astype(jnp.bfloat16)
+        prior_chunks.append(
+            shifted(
+                (keys_here.reshape(rows_per, inner_here), values_here.reshape(rows_per, inner_here)),
+                "seq",
+                1,
+            )
+        )
+        raw_chunks.append(raw)
+        key_chunks.append(keys_here)
+        value_chunks.append(values_here)
+    pair_raw = jnp.concatenate(raw_chunks, axis=1)
     query_raw = gathered_sum(
         [jnp.dot(rows, w_query, preferred_element_type=jnp.float32) for rows in stacked],
         after=pair_raw,
     )
-    lookup_vectors = rms_rows(pair_raw[0].reshape(trajs, span, heads_here, head_dim), 1e-06).astype(
-        jnp.bfloat16
-    )
-    values = pair_raw[1].reshape(trajs, span, heads_here, head_dim).astype(jnp.bfloat16)
-    prior_keys, prior_values = shifted(
-        (lookup_vectors.reshape(trajs, span, inner_here), values.reshape(trajs, span, inner_here)),
-        "seq",
-        1,
-    )
+    lookup_vectors = jnp.concatenate(key_chunks, axis=0).reshape(trajs, span, heads_here, head_dim)
+    values = jnp.concatenate(value_chunks, axis=0).reshape(trajs, span, heads_here, head_dim)
+    prior_keys = jnp.concatenate([p[0] for p in prior_chunks], axis=0).reshape(trajs, span, inner_here)
+    prior_values = jnp.concatenate([p[1] for p in prior_chunks], axis=0).reshape(trajs, span, inner_here)
     queries = rms_rows(query_raw.reshape(trajs, span, heads_here, head_dim), 1e-06).astype(
         jnp.bfloat16
     )

time: 192 us -> 231 us (1.20)
  waiting for transfers between devices: 66.2 us -> 105 us
  matrix products: 46.4 us -> 38 us
  other arithmetic: 16.7 us -> 21.9 us
  starting transfers between devices: 26.8 us -> 31 us
    all_gather x1, waiting for transfers between devices: 0.02 us -> 24.2 us  [shards(): w_output_rows = lax.all_gather(w_output, 'wloop', axis=1, tiled=True)]
    ppermute x5 -> x7, waiting for transfers between devices: 11.4 us -> 30.4 us  [shifted(): lax.ppermute(value, axis, [(source, source + steps) for source in range(i...]
    ppermute x5 -> x7, starting transfers between devices: 20.5 us -> 24.4 us  [shifted(): lax.ppermute(value, axis, [(source, source + steps) for source in range(i...]
    mul x2, local copies, waits for them, and re-layouts: 4.46 us -> 0.66 us  [rms_rows(): values * lax.rsqrt(jnp.mean(values * values, axis=-1, keepdims=True) + eps)]
    add x0 -> x1, other arithmetic: none -> 3.41 us  [gathered_sum(): total + lax.ppermute(outgoing, 'wloop', [(source, (source - step) % ways)...]
    ppermute x1, waiting for transfers between devices: 11.9 us -> 8.93 us  [shards(): lax.ppermute(part, 'wloop', [(source, (source + step) % ways) for source...]
    dot_general x1, matrix products: 5.35 us -> 2.48 us  [window_mix(): jnp.einsum('bihd,bjhd->bhij', queries, prior_keys, preferred_element_type...]
    unnamed x47 -> x61, local copies, waits for them, and re-layouts: 6.09 us -> 8.83 us
  transfers between devices with their start and end apart: 11 -> 14, of which waited for: 5 -> 10; matrix products, arithmetic and copies ran while one was open for 29% -> 18% of each run, Pallas kernels for 0% -> 0%
where the time goes in v9:
time: 231 us
  waiting for transfers between devices  105 us (45%)
  matrix products  38 us (16%)
  starting transfers between devices  31 us (13%)
  other arithmetic  21.9 us (9%)
  local copies, waits for them, and re-layouts  19.3 us (8%)
  between operations  14.8 us (6%)
    ppermute x3, waiting for transfers between devices, gathered_sum(): lax.ppermute(outgoing, 'wloop', [(source, (source - step) % ways) for sou...  37.7 us
    ppermute x7, waiting for transfers between devices, shifted(): lax.ppermute(value, axis, [(source, source + steps) for source in range(i...  30.4 us
    ppermute x7, starting transfers between devices, shifted(): lax.ppermute(value, axis, [(source, source + steps) for source in range(i...  24.4 us
    all_gather x1, waiting for transfers between devices, shards(): w_output_rows = lax.all_gather(w_output, 'wloop', axis=1, tiled=True)  24.2 us
    dot_general x2, matrix products, shards(): jnp.einsum('td,dje->jte', rows, w_keyvalue, preferred_element_type=jnp.fl...  10.1 us
    ppermute x1, waiting for transfers between devices, shards(): lax.ppermute(part, 'wloop', [(source, (source + step) % ways) for source...  8.93 us
    unnamed x61, local copies, waits for them, and re-layouts  8.83 us
    dot_general x2, matrix products, output_share(): jnp.dot(attended, lax.dynamic_slice_in_dim(w_output_rows, index * share,...  8.31 us
  transfers between devices with their start and end apart: 14, of which 10 were waited for; matrix products, arithmetic and copies ran while one was open for 18% of the time, Pallas kernels for 0%

profile of v9, /device:TPU:0, one launch (start us, length us, event | category | flops | bytes accessed | tf_op | source)
XLA Modules:
  0.0 230.5 jit_solution(10864495570081886879)
XLA Ops:
  6.5 2.2 fusion.2
  11.1 3.0 %collective-permute-start = (bf16[256,1024]{1,0:T(8,128)(2,1)S(1)}, bf16[256,1024]{1,0:T(8,128)(2,1)S(1)}, u32[]{:S(2)}, u32[]{:S(2)}) collective-permute-start(bf16[256,1024]{1,0:T(8,128)(2,1)S(1)} %dynamic-slice_bitcast_fusion), channel_id=1, source_target_pairs={{0,2},{2,0},{1,3},{3,1},{4,6},{6,4},{5,7},{7,5},{8,10},{10,8},{9,1... | collective-permute-start | bytes 1572872 | tf_op jit(solution)/shard_map/ppermute | solution.py:77
  17.1 8.9 %collective-permute-done = bf16[256,1024]{1,0:T(8,128)(2,1)S(1)} collective-permute-done((bf16[256,1024]{1,0:T(8,128)(2,1)S(1)}, bf16[256,1024]{1,0:T(8,128)(2,1)S(1)}, u32[]{:S(2)}, u32[]{:S(2)}) %collective-permute-start) | collective-permute-done | bytes 524320 | tf_op jit(solution)/shard_map/ppermute | solution.py:77
  31.1 5.0 %convert_bitcast_fusion = bf16[2,512,1024]{2,1,0:T(8,128)(2,1)S(1)} fusion(bf16[1024,2,1024]{2,1,0:T(2,128)(2,1)} %param.10, bf16[512,1024]{1,0:T(8,128)(2,1)S(1)} %bitcast_select_fusion), kind=kOutput, calls=%fused_computation.30 | convolution fusion | flops 2148532224 | bytes 7340032 | tf_op jit(solution)/shard_map/td,dje->jte/dot_general | solution.py:99
  40.5 5.1 %fusion.11 = f32[2,512,1024]{2,1,0:T(8,128)S(1)} fusion(bf16[1024,2,1024]{2,1,0:T(2,128)(2,1)} %param.10, bf16[1,512,2048]{2,1,0:T(8,128)(2,1)} %copy-done.7, s32[]{:T(128)S(6)} %select_n.80), kind=kOutput, calls=%fused_computation.19 | convolution fusion | flops 2147483648 | bytes 9437188 | tf_op jit(solution)/shard_map/td,dje->jte/dot_general | solution.py:99
  45.6 2.3 convolution_convert_fusion
  47.9 16.0 %collective-permute-done.2 = bf16[2,256,1024]{2,1,0:T(8,128)(2,1)S(1)} collective-permute-done((bf16[2,256,1024]{2,1,0:T(8,128)(2,1)}, bf16[2,256,1024]{2,1,0:T(8,128)(2,1)S(1)}, u32[]{:S(2)}, u32[]{:S(2)}) %collective-permute-start.2) | collective-permute-done | bytes 1048608 | tf_op jit(solution)/shard_map/ppermute | solution.py:91
  63.9 21.7 %collective-permute-done.3 = bf16[2,256,1024]{2,1,0:T(8,128)(2,1)} collective-permute-done((bf16[2,256,1024]{2,1,0:T(8,128)(2,1)}, bf16[2,256,1024]{2,1,0:T(8,128)(2,1)}, u32[]{:S(2)}, u32[]{:S(2)}) %collective-permute-start.3) | collective-permute-done | bytes 1048608 | tf_op jit(solution)/shard_map/ppermute | solution.py:91
  85.6 3.4 %slice_add_fusion = (f32[2,256,1024]{2,1,0:T(8,128)}, f32[2,256,1024]{2,1,0:T(8,128)S(1)}) fusion(f32[2,512,1024]{2,1,0:T(8,128)S(1)} %fusion.11, bf16[2,256,1024]{2,1,0:T(8,128)(2,1)} %collective-permute-done.3, bf16[2,256,1024]{2,1,0:T(8,128)(2,1)S(1)} %collective-permute-done.2), kind=kLoop, calls=%fused_computation.22 | loop fusion | flops 2097152 | bytes 10485760 | tf_op jit(solution)/shard_map/add | solution.py:91
  100.0 3.8 %collective-permute-start.5 = (bf16[256,1024]{1,0:T(8,128)(2,1)S(1)}, bf16[256,1024]{1,0:T(8,128)(2,1)S(1)}, u32[]{:S(2)}, u32[]{:S(2)}) collective-permute-start(bf16[256,1024]{1,0:T(8,128)(2,1)S(1)} %fusion.41), channel_id=1, source_target_pairs={{0,4},{4,8},{8,12},{1,5},{5,9},{9,13},{2,6},{6,10},{10,14},{3,7},{... | collective-permute-start | bytes 1572872 | tf_op jit(solution)/shard_map/ppermute | solution.py:14
  104.4 3.5 %collective-permute-start.6 = (bf16[256,1024]{1,0:T(8,128)(2,1)S(1)}, bf16[256,1024]{1,0:T(8,128)(2,1)S(1)}, u32[]{:S(2)}, u32[]{:S(2)}) collective-permute-start(bf16[256,1024]{1,0:T(8,128)(2,1)S(1)} %fusion.40), channel_id=1, source_target_pairs={{0,4},{4,8},{8,12},{1,5},{5,9},{9,13},{2,6},{6,10},{10,14},{3,7},{... | collective-permute-start | bytes 1572872 | tf_op jit(solution)/shard_map/ppermute | solution.py:14
  108.2 3.5 %collective-permute-start.7 = (bf16[256,1024]{1,0:T(8,128)(2,1)S(1)}, bf16[256,1024]{1,0:T(8,128)(2,1)S(1)}, u32[]{:S(2)}, u32[]{:S(2)}) collective-permute-start(bf16[256,1024]{1,0:T(8,128)(2,1)S(1)} %get-tuple-element.23), channel_id=1, source_target_pairs={{0,4},{4,8},{8,12},{1,5},{5,9},{9,13},{2,6},{6,10},{10,14},{3,7},{... | collective-permute-start | bytes 1572872 | tf_op jit(solution)/shard_map/ppermute | solution.py:14
  111.7 2.1 collective-permute-start.8
  115.5 2.7 %fusion.37 = f32[1,8,128,128]{3,2,1,0:T(8,128)S(1)} fusion(bf16[512,8,128]{2,0,1:T(8,128)(2,1)S(1)} %copy_dynamic-update-slice_fusion, f32[512,8]{0,1:T(8,128)S(1)} %copy-done.22, bf16[256,8,128]{2,0,1:T(8,128)(2,1)S(1)} %get-tuple-element.33, bf16[256,8,128]{2,0,1:T(8,128)(2,1)S(1)} %get-tuple-element.34), kind=kOutput, calls=%fused_computation.44 | convolution fusion | flops 807927808 | bytes 2637824 | tf_op jit(solution)/shard_map/bht,bthd,bthe->bhde/dot_general | solution.py:136
  118.3 9.0 %collective-permute-done.6 = bf16[256,1024]{1,0:T(8,128)(2,1)S(1)} collective-permute-done((bf16[256,1024]{1,0:T(8,128)(2,1)S(1)}, bf16[256,1024]{1,0:T(8,128)(2,1)S(1)}, u32[]{:S(2)}, u32[]{:S(2)}) %collective-permute-start.6) | collective-permute-done | bytes 524320 | tf_op jit(solution)/shard_map/ppermute | solution.py:14
  128.3 10.2 %collective-permute-done.7 = bf16[256,1024]{1,0:T(8,128)(2,1)S(1)} collective-permute-done((bf16[256,1024]{1,0:T(8,128)(2,1)S(1)}, bf16[256,1024]{1,0:T(8,128)(2,1)S(1)}, u32[]{:S(2)}, u32[]{:S(2)}) %collective-permute-start.7) | collective-permute-done | bytes 524320 | tf_op jit(solution)/shard_map/ppermute | solution.py:14
  138.5 9.6 %collective-permute-done.8 = bf16[256,1024]{1,0:T(8,128)(2,1)S(1)} collective-permute-done((bf16[256,1024]{1,0:T(8,128)(2,1)S(1)}, bf16[256,1024]{1,0:T(8,128)(2,1)S(1)}, u32[]{:S(2)}, u32[]{:S(2)}) %collective-permute-start.8) | collective-permute-done | bytes 524320 | tf_op jit(solution)/shard_map/ppermute | solution.py:14
  149.2 4.4 %collective-permute-start.9 = (bf16[1,9,128,128]{3,2,1,0:T(8,128)(2,1)S(1)}, bf16[1,9,128,128]{3,2,1,0:T(8,128)(2,1)S(1)}, u32[]{:S(2)}, u32[]{:S(2)}) collective-permute-start(bf16[1,9,128,128]{3,2,1,0:T(8,128)(2,1)S(1)} %fusion.59), channel_id=1, source_target_pairs={{0,4},{4,8},{8,12},{1,5},{5,9},{9,13},{2,6},{6,10},{10,14},{3,7},{... | collective-permute-start | bytes 884744 | tf_op jit(solution)/shard_map/ppermute | solution.py:14
  155.3 2.5 %copy.112 = bf16[64,8,8,128]{3,2,1,0:T(8,128)(2,1)} copy(bf16[64,8,8,128]{3,1,2,0:T(8,128)(2,1)} %bitcast.152) | data formatting | bytes 2097152
  157.8 2.3 copy.101
  160.9 3.5 %collective-permute-start.10 = (bf16[1,9,128,128]{3,2,1,0:T(8,128)(2,1)}, bf16[1,9,128,128]{3,2,1,0:T(8,128)(2,1)S(1)}, u32[]{:S(2)}, u32[]{:S(2)}) collective-permute-start(bf16[1,9,128,128]{3,2,1,0:T(8,128)(2,1)} %fusion.61), channel_id=1, source_target_pairs={{0,4},{4,8},{8,12},{1,5},{5,9},{9,13},{2,6},{6,10},{10,14},{3,7},{... | collective-permute-start | bytes 884744 | tf_op jit(solution)/shard_map/ppermute | solution.py:14
  164.4 4.4 %multiply_bitcast_fusion = (f32[64,8,8,128]{3,1,2,0:T(8,128)S(1)}, f32[64,8,8,128]{3,2,1,0:T(8,128)}) fusion(bf16[512,1024]{1,0:T(8,128)(2,1)} %collective-permute-done.4, bf16[1024,1024]{1,0:T(8,128)(2,1)S(1)} %copy-done, bf16[1,512,2048]{2,1,0:T(8,128)(2,1)} %copy-done.7, s32[]{:T(128)S(6)} %select_n.80), kind=kOutput, calls=%fused_computation.38 | convolution fusion | flops 1075314688 | bytes 8388612 | tf_op jit(solution)/shard_map/dot_general | solution.py:121
  170.0 2.0 fusion.14
  172.1 2.2 fusion
  174.3 2.5 %fusion.1 = (f32[8,512]{1,0:T(8,128)S(1)}, f32[8,512,512]{1,2,0:T(8,128)S(1)}) fusion(pred[512,512]{0,1:T(8,128)(4,1)S(1)} %copy-done.19, bf16[512,8,128]{2,0,1:T(8,128)(2,1)S(1)} %fusion.14, bf16[512,8,128]{2,1,0:T(8,128)(2,1)S(1)} %bitcast.161), kind=kOutput, calls=%fused_computation.6 | convolution fusion | flops 543158272 | bytes 10764288 | tf_op jit(solution)/shard_map/bihd,bjhd->bhij/dot_general | solution.py:27
  176.8 2.4 %fusion.6 = f32[8,128,512]{2,1,0:T(8,128)S(1)} fusion(bf16[512,8,128]{0,2,1:T(8,128)(2,1)S(1)} %bitcast.160, f32[8,512,512]{1,2,0:T(8,128)S(1)} %get-tuple-element.32, f32[8,512]{1,0:T(8,128)S(1)} %add.172, pred[512,512]{0,1:T(8,128)(4,1)S(1)} %copy-done.19), kind=kOutput, calls=%fused_computation.14 | convolution fusion | flops 545259520 | bytes 11812864 | tf_op jit(solution)/shard_map/bhij,bjhd->bihd/dot_general | solution.py:40
  179.4 3.7 %collective-permute-start.11 = (bf16[1,9,128,128]{3,2,1,0:T(8,128)(2,1)S(1)}, bf16[1,9,128,128]{3,2,1,0:T(8,128)(2,1)S(1)}, u32[]{:S(2)}, u32[]{:S(2)}) collective-permute-start(bf16[1,9,128,128]{3,2,1,0:T(8,128)(2,1)S(1)} %fusion.63), channel_id=1, source_target_pairs={{0,4},{4,8},{8,12},{1,5},{5,9},{9,13},{2,6},{6,10},{10,14},{3,7},{... | collective-permute-start | bytes 884744 | tf_op jit(solution)/shard_map/ppermute | solution.py:14
  183.2 2.6 %fusion.5 = f32[8,128,512]{2,1,0:T(8,128)S(1)} fusion(bf16[512,8,128]{2,0,1:T(8,128)(2,1)S(1)} %copy-done.17, f32[8,512,512]{1,2,0:T(8,128)S(1)} %get-tuple-element.30, f32[8,512]{1,0:T(8,128)S(1)} %add.172, pred[512,512]{0,1:T(8,128)(4,1)S(1)} %copy-done.18), kind=kOutput, calls=%fused_computation.13 | convolution fusion | flops 545259520 | bytes 11812864 | tf_op jit(solution)/shard_map/bhij,bjhd->bihd/dot_general | solution.py:38
  188.2 24.2 %all-gather.2.cloned.1.call-done = bf16[1024,2048]{1,0:T(8,128)(2,1)} async-done(((bf16[1024,1024]{1,0:T(8,128)(2,1)}), bf16[1024,2048]{1,0:T(8,128)(2,1)}) %all-gather.2.cloned.1.call-update) | async-done | bytes 4194320 | tf_op jit(solution)/shard_map/all_gather | solution.py:185
  212.4 3.8 %fusion.28 = bf16[512,1024]{1,0:T(8,128)(2,1)} fusion(bf16[512,1024]{0,1:T(8,128)(2,1)S(1)} %bitcast.162, bf16[1024,2048]{1,0:T(8,128)(2,1)} %all-gather.2.cloned.1.call-done, s32[]{:T(128)S(6)} %select_n.94), kind=kOutput, calls=%fused_computation.40 | convolution fusion | flops 1074266112 | bytes 4194308 | tf_op jit(solution)/shard_map/dot_general | solution.py:191
  216.2 3.0 %collective-permute-done.12 = bf16[512,1024]{1,0:T(8,128)(2,1)} collective-permute-done((bf16[512,1024]{1,0:T(8,128)(2,1)}, bf16[512,1024]{1,0:T(8,128)(2,1)}, u32[]{:S(2)}, u32[]{:S(2)}) %collective-permute-start.12) | collective-permute-done | bytes 1048608 | tf_op jit(solution)/shard_map/ppermute | solution.py:198
  219.2 4.5 %fusion.34 = bf16[1,512,1024]{2,1,0:T(8,128)(2,1)} fusion(bf16[512,1024]{1,0:T(8,128)(2,1)} %collective-permute-done.12, bf16[512,1024]{0,1:T(8,128)(2,1)S(1)} %bitcast.163, bf16[1024,2048]{1,0:T(8,128)(2,1)} %all-gather.2.cloned.1.call-done, s32[]{:T(128)S(6)} %select_n.79, bf16[1,512,2048]{2,1,0:T(8,128)(2,1)} %param.7), kind=kOutput, calls=%fused_computation.43 | convolution fusion | flops 1076363264 | bytes 6292480 | tf_op jit(solution)/shard_map/dot_general | solution.py:191
  (127 shorter events, 36.0 us)
Async XLA Ops:
  6.5 39.1 %copy-start = (bf16[1024,1024]{1,0:T(8,128)(2,1)S(1)}, bf16[1024,1024]{1,0:T(8,128)(2,1)}, u32[]{:S(2)}) copy-start(bf16[1024,1024]{1,0:T(8,128)(2,1)} %param.9) | copy-start | bytes 6291460
  6.5 2.2 copy-start.23
  6.5 205.8 %all-gather.2.cloned.1.call-start = ((), (), s32[]{:S(2)}) async-start(), calls=%async_computation | async-start | bytes 6291456 | tf_op jit(solution)/shard_map/all_gather | solution.py:185
  6.5 2.4 %copy-start.2 = (bf16[1,512,2048]{2,1,0:T(8,128)(2,1)S(1)}, bf16[1,512,2048]{2,1,0:T(8,128)(2,1)}, u32[]{:S(2)}) copy-start(bf16[1,512,2048]{2,1,0:T(8,128)(2,1)} %param.7) | copy-start | bytes 6291460
  8.9 5.3 %copy-start.21 = (f32[1,8,512]{2,1,0:T(8,128)S(1)}, f32[1,8,512]{2,1,0:T(8,128)}, u32[]{:S(2)}) copy-start(f32[1,8,512]{2,1,0:T(8,128)} %param.12) | copy-start | bytes 49156
  11.1 15.0 %collective-permute-start = (bf16[256,1024]{1,0:T(8,128)(2,1)S(1)}, bf16[256,1024]{1,0:T(8,128)(2,1)S(1)}, u32[]{:S(2)}, u32[]{:S(2)}) collective-permute-start(bf16[256,1024]{1,0:T(8,128)(2,1)S(1)} %dynamic-slice_bitcast_fusion), channel_id=1, source_target_pairs={{0,2},{2,0},{1,3},{3,1},{4,6},{6,4},{5,7},{7,5},{8,10},{10,8},{9,1... | collective-permute-start | bytes 1572872 | tf_op jit(solution)/shard_map/ppermute | solution.py:77
  26.1 1.9 collective-permute-start.1
  31.1 5.0 %copy-start.8 = (bf16[512,1024]{1,0:T(8,128)(2,1)}, bf16[512,1024]{1,0:T(8,128)(2,1)S(1)}, u32[]{:S(2)}) copy-start(bf16[512,1024]{1,0:T(8,128)(2,1)S(1)} %bitcast_select_fusion) | copy-start | bytes 3145732
  37.6 26.2 %collective-permute-start.2 = (bf16[2,256,1024]{2,1,0:T(8,128)(2,1)}, bf16[2,256,1024]{2,1,0:T(8,128)(2,1)S(1)}, u32[]{:S(2)}, u32[]{:S(2)}) collective-permute-start(bf16[2,256,1024]{2,1,0:T(8,128)(2,1)} %get-tuple-element.28), channel_id=1, source_target_pairs={{0,2},{2,0},{1,3},{3,1},{4,6},{6,4},{5,7},{7,5},{8,10},{10,8},{9,1... | collective-permute-start | bytes 3145736 | tf_op jit(solution)/shard_map/ppermute | solution.py:91
  39.4 46.2 %collective-permute-start.3 = (bf16[2,256,1024]{2,1,0:T(8,128)(2,1)}, bf16[2,256,1024]{2,1,0:T(8,128)(2,1)}, u32[]{:S(2)}, u32[]{:S(2)}) collective-permute-start(bf16[2,256,1024]{2,1,0:T(8,128)(2,1)} %get-tuple-element.27), channel_id=1, source_target_pairs={{0,2},{2,0},{1,3},{3,1},{4,6},{6,4},{5,7},{7,5},{8,10},{10,8},{9,1... | collective-permute-start | bytes 3145736 | tf_op jit(solution)/shard_map/ppermute | solution.py:91
  40.5 5.1 %copy-start.9 = (bf16[512,1024]{1,0:T(8,128)(2,1)S(1)}, bf16[512,1024]{1,0:T(8,128)(2,1)}, u32[]{:S(2)}) copy-start(bf16[512,1024]{1,0:T(8,128)(2,1)} %copy-done.8) | copy-start | bytes 3145732
  95.3 3.8 %copy-start.3 = (f32[2,256,1024]{2,1,0:T(8,128)S(1)}, f32[2,256,1024]{2,1,0:T(8,128)}, u32[]{:S(2)}) copy-start(f32[2,256,1024]{2,1,0:T(8,128)} %get-tuple-element.19) | copy-start | bytes 6291460
  97.2 18.3 %copy-start.12 = (bf16[256,8,128]{2,0,1:T(8,128)(2,1)}, bf16[256,8,128]{2,0,1:T(8,128)(2,1)S(1)}, u32[]{:S(2)}) copy-start(bf16[256,8,128]{2,0,1:T(8,128)(2,1)S(1)} %get-tuple-element.33) | copy-start | bytes 1572868
  97.2 18.3 %copy-start.14 = (bf16[256,8,128]{2,0,1:T(8,128)(2,1)}, bf16[256,8,128]{2,0,1:T(8,128)(2,1)S(1)}, u32[]{:S(2)}) copy-start(bf16[256,8,128]{2,0,1:T(8,128)(2,1)S(1)} %get-tuple-element.34) | copy-start | bytes 1572868
  97.2 2.4 %copy-start.5 = (f32[2,256,1024]{2,1,0:T(8,128)S(1)}, f32[2,256,1024]{2,1,0:T(8,128)}, u32[]{:S(2)}) copy-start(f32[2,256,1024]{2,1,0:T(8,128)} %copy-done.4) | copy-start | bytes 6291460
  100.0 18.3 %collective-permute-start.5 = (bf16[256,1024]{1,0:T(8,128)(2,1)S(1)}, bf16[256,1024]{1,0:T(8,128)(2,1)S(1)}, u32[]{:S(2)}, u32[]{:S(2)}) collective-permute-start(bf16[256,1024]{1,0:T(8,128)(2,1)S(1)} %fusion.41), channel_id=1, source_target_pairs={{0,4},{4,8},{8,12},{1,5},{5,9},{9,13},{2,6},{6,10},{10,14},{3,7},{... | collective-permute-start | bytes 1572872 | tf_op jit(solution)/shard_map/ppermute | solution.py:14
  104.4 22.8 %collective-permute-start.6 = (bf16[256,1024]{1,0:T(8,128)(2,1)S(1)}, bf16[256,1024]{1,0:T(8,128)(2,1)S(1)}, u32[]{:S(2)}, u32[]{:S(2)}) collective-permute-start(bf16[256,1024]{1,0:T(8,128)(2,1)S(1)} %fusion.40), channel_id=1, source_target_pairs={{0,4},{4,8},{8,12},{1,5},{5,9},{9,13},{2,6},{6,10},{10,14},{3,7},{... | collective-permute-start | bytes 1572872 | tf_op jit(solution)/shard_map/ppermute | solution.py:14
  107.9 7.6 %copy-start.22 = (f32[512,8]{0,1:T(8,128)S(1)}, f32[512,8]{0,1:T(8,128)}, u32[]{:S(2)}) copy-start(f32[512,8]{0,1:T(8,128)} %fusion.74) | copy-start | bytes 49156
  108.2 30.3 %collective-permute-start.7 = (bf16[256,1024]{1,0:T(8,128)(2,1)S(1)}, bf16[256,1024]{1,0:T(8,128)(2,1)S(1)}, u32[]{:S(2)}, u32[]{:S(2)}) collective-permute-start(bf16[256,1024]{1,0:T(8,128)(2,1)S(1)} %get-tuple-element.23), channel_id=1, source_target_pairs={{0,4},{4,8},{8,12},{1,5},{5,9},{9,13},{2,6},{6,10},{10,14},{3,7},{... | collective-permute-start | bytes 1572872 | tf_op jit(solution)/shard_map/ppermute | solution.py:14
  111.7 36.3 %collective-permute-start.8 = (bf16[256,1024]{1,0:T(8,128)(2,1)S(1)}, bf16[256,1024]{1,0:T(8,128)(2,1)S(1)}, u32[]{:S(2)}, u32[]{:S(2)}) collective-permute-start(bf16[256,1024]{1,0:T(8,128)(2,1)S(1)} %get-tuple-element.25), channel_id=1, source_target_pairs={{0,4},{4,8},{8,12},{1,5},{5,9},{9,13},{2,6},{6,10},{10,14},{3,7},{... | collective-permute-start | bytes 1572872 | tf_op jit(solution)/shard_map/ppermute | solution.py:14
  113.8 50.6 %collective-permute-start.4 = (bf16[512,1024]{1,0:T(8,128)(2,1)}, bf16[512,1024]{1,0:T(8,128)(2,1)}, u32[]{:S(2)}, u32[]{:S(2)}) collective-permute-start(bf16[512,1024]{1,0:T(8,128)(2,1)} %convolution_convert_fusion), channel_id=1, source_target_pairs={{0,2},{2,0},{1,3},{3,1},{4,6},{6,4},{5,7},{7,5},{8,10},{10,8},{9,1... | collective-permute-start | bytes 3145736 | tf_op jit(solution)/shard_map/ppermute | solution.py:91
  115.5 2.8 %copy-start.16 = (bf16[512,8,128]{2,0,1:T(8,128)(2,1)}, bf16[512,8,128]{2,0,1:T(8,128)(2,1)S(1)}, u32[]{:S(2)}) copy-start(bf16[512,8,128]{2,0,1:T(8,128)(2,1)S(1)} %copy_dynamic-update-slice_fusion) | copy-start | bytes 3145732
  118.2 30.9 %copy-start.24 = (f32[9]{0:T(128)S(1)}, f32[9]{0:T(128)}, u32[]{:S(2)}) copy-start(f32[9]{0:T(128)} %pad.9.clone) | copy-start | bytes 112
  149.2 10.8 %collective-permute-start.9 = (bf16[1,9,128,128]{3,2,1,0:T(8,128)(2,1)S(1)}, bf16[1,9,128,128]{3,2,1,0:T(8,128)(2,1)S(1)}, u32[]{:S(2)}, u32[]{:S(2)}) collective-permute-start(bf16[1,9,128,128]{3,2,1,0:T(8,128)(2,1)S(1)} %fusion.59), channel_id=1, source_target_pairs={{0,4},{4,8},{8,12},{1,5},{5,9},{9,13},{2,6},{6,10},{10,14},{3,7},{... | collective-permute-start | bytes 884744 | tf_op jit(solution)/shard_map/ppermute | solution.py:14
  160.9 18.3 %collective-permute-start.10 = (bf16[1,9,128,128]{3,2,1,0:T(8,128)(2,1)}, bf16[1,9,128,128]{3,2,1,0:T(8,128)(2,1)S(1)}, u32[]{:S(2)}, u32[]{:S(2)}) collective-permute-start(bf16[1,9,128,128]{3,2,1,0:T(8,128)(2,1)} %fusion.61), channel_id=1, source_target_pairs={{0,4},{4,8},{8,12},{1,5},{5,9},{9,13},{2,6},{6,10},{10,14},{3,7},{... | collective-permute-start | bytes 884744 | tf_op jit(solution)/shard_map/ppermute | solution.py:14
  172.1 2.2 copy-start.11
  174.3 2.5 %copy-start.10 = (bf16[1,512,1024]{1,2,0:T(8,128)(2,1)S(1)}, bf16[1,512,1024]{1,2,0:T(8,128)(2,1)}, u32[]{:S(2)}) copy-start(bf16[1,512,1024]{1,2,0:T(8,128)(2,1)} %copy.101) | copy-start | bytes 3145732
  176.8 6.3 %copy-start.17 = (bf16[512,8,128]{2,0,1:T(8,128)(2,1)S(1)}, bf16[512,8,128]{2,0,1:T(8,128)(2,1)}, u32[]{:S(2)}) copy-start(bf16[512,8,128]{2,0,1:T(8,128)(2,1)} %copy-done.16) | copy-start | bytes 3145732
  179.4 8.0 %collective-permute-start.11 = (bf16[1,9,128,128]{3,2,1,0:T(8,128)(2,1)S(1)}, bf16[1,9,128,128]{3,2,1,0:T(8,128)(2,1)S(1)}, u32[]{:S(2)}, u32[]{:S(2)}) collective-permute-start(bf16[1,9,128,128]{3,2,1,0:T(8,128)(2,1)S(1)} %fusion.63), channel_id=1, source_target_pairs={{0,4},{4,8},{8,12},{1,5},{5,9},{9,13},{2,6},{6,10},{10,14},{3,7},{... | collective-permute-start | bytes 884744 | tf_op jit(solution)/shard_map/ppermute | solution.py:14
  183.2 4.4 %copy-start.20 = (f32[512,8]{0,1:T(8,128)S(1)}, f32[512,8]{0,1:T(8,128)}, u32[]{:S(2)}) copy-start(f32[512,8]{0,1:T(8,128)} %get-tuple-element.17) | copy-start | bytes 49156
  216.2 3.0 %collective-permute-start.12 = (bf16[512,1024]{1,0:T(8,128)(2,1)}, bf16[512,1024]{1,0:T(8,128)(2,1)}, u32[]{:S(2)}, u32[]{:S(2)}) collective-permute-start(bf16[512,1024]{1,0:T(8,128)(2,1)} %fusion.28), channel_id=1, source_target_pairs={{0,1},{1,0},{2,3},{3,2},{4,5},{5,4},{6,7},{7,6},{8,9},{9,8},{10,11... | collective-permute-start | bytes 3145736 | tf_op jit(solution)/shard_map/ppermute | solution.py:198
  216.2 7.5 %copy-start.1 = (bf16[1024,1024]{1,0:T(8,128)(2,1)S(1)}, bf16[1024,1024]{1,0:T(8,128)(2,1)}, u32[]{:S(2)}) copy-start(bf16[1024,1024]{1,0:T(8,128)(2,1)} %param.9) | copy-start | bytes 6291460
  (7 other events, 12.2 us)
Sparse Core Ops, SparseCore 0:
  155.4 56.9 all-gather.1

commit v10 on v9

--- a/solution.py
+++ b/solution.py
@@ -103,9 +103,13 @@
     rows_per = count // pieces
     raw_chunks, key_chunks, value_chunks, prior_chunks = [], [], [], []
     for piece in range(pieces):
-        raw = gathered_sum([p[:, piece * rows_per : (piece + 1) * rows_per] for p in kv_partials])
+        raw = gathered_sum(
+            [p[:, piece * rows_per : (piece + 1) * rows_per] for p in kv_partials],
+            after=key_chunks[-1] if key_chunks else None,
+        )
         keys_here = rms_rows(raw[0].reshape(rows_per, heads_here, head_dim), 1e-06).astype(jnp.bfloat16)
         values_here = raw[1].reshape(rows_per, heads_here, head_dim).astype(jnp.bfloat16)
+        keys_here, values_here = lax.optimization_barrier((keys_here, values_here))
         prior_chunks.append(
             shifted(
                 (keys_here.reshape(rows_per, inner_here), values_here.reshape(rows_per, inner_here)),

time: 231 us -> 209 us (0.905)
  waiting for transfers between devices: 105 us -> 80.5 us
  starting transfers between devices: 31 us -> 35.6 us
    ppermute x7, waiting for transfers between devices: 30.4 us -> 10.9 us  [shifted(): lax.ppermute(value, axis, [(source, source + steps) for source in range(i...]
    ppermute x3, waiting for transfers between devices: 37.7 us -> 29.3 us  [gathered_sum(): lax.ppermute(outgoing, 'wloop', [(source, (source - step) % ways) for sou...]
    ppermute x7, starting transfers between devices: 24.4 us -> 27.5 us  [shifted(): lax.ppermute(value, axis, [(source, source + steps) for source in range(i...]
    optimization_barrier x0 -> x2, local copies, waits for them, and re-layouts: none -> 3.04 us  [shards(): keys_here, values_here = lax.optimization_barrier((keys_here, values_here))]
    dot_general x2, matrix products: 10.1 us -> 7.28 us  [shards(): jnp.einsum('td,dje->jte', rows, w_keyvalue, preferred_element_type=jnp.fl...]
    unnamed x61 -> x49, local copies, waits for them, and re-layouts: 8.83 us -> 9.36 us
  transfers between devices with their start and end apart: 14 -> 14, of which waited for: 10 -> 10; matrix products, arithmetic and copies ran while one was open for 18% -> 24% of each run, Pallas kernels for 0% -> 0%
where the time goes in v10:
time: 209 us
  waiting for transfers between devices  80.5 us (39%)
  matrix products  36.8 us (18%)
  starting transfers between devices  35.6 us (17%)
  other arithmetic  21.1 us (10%)
  local copies, waits for them, and re-layouts  20.2 us (10%)
  between operations  14.6 us (7%)
    ppermute x3, waiting for transfers between devices, gathered_sum(): lax.ppermute(outgoing, 'wloop', [(source, (source - step) % ways) for sou...  29.3 us
    ppermute x7, starting transfers between devices, shifted(): lax.ppermute(value, axis, [(source, source + steps) for source in range(i...  27.5 us
    all_gather x1, waiting for transfers between devices, shards(): w_output_rows = lax.all_gather(w_output, 'wloop', axis=1, tiled=True)  25.7 us
    ppermute x7, waiting for transfers between devices, shifted(): lax.ppermute(value, axis, [(source, source + steps) for source in range(i...  10.9 us
    ppermute x1, waiting for transfers between devices, shards(): lax.ppermute(part, 'wloop', [(source, (source + step) % ways) for source...  10.7 us
    unnamed x49, local copies, waits for them, and re-layouts  9.36 us
    dot_general x2, matrix products, output_share(): jnp.dot(attended, lax.dynamic_slice_in_dim(w_output_rows, index * share,...  8.31 us
    dot_general x2, matrix products, shards(): jnp.einsum('td,dje->jte', rows, w_keyvalue, preferred_element_type=jnp.fl...  7.28 us
  transfers between devices with their start and end apart: 14, of which 10 were waited for; matrix products, arithmetic and copies ran while one was open for 24% of the time, Pallas kernels for 0%

profile of v10, /device:TPU:0, one launch (start us, length us, event | category | flops | bytes accessed | tf_op | source)
XLA Modules:
  0.0 208.8 jit_solution(7583283904627503053)
XLA Ops:
  6.5 2.2 %fusion.2 = f32[512]{0:T(512)S(1)} fusion(bf16[1,512,2048]{2,1,0:T(8,128)(2,1)} %param.7), kind=kLoop, calls=%fused_computation.9 | loop fusion | flops 3145216 | bytes 2099200 | tf_op jit(solution)/shard_map/reduce_sum | solution.py:18
  11.1 3.0 %collective-permute-start = (bf16[256,1024]{1,0:T(8,128)(2,1)S(1)}, bf16[256,1024]{1,0:T(8,128)(2,1)S(1)}, u32[]{:S(2)}, u32[]{:S(2)}) collective-permute-start(bf16[256,1024]{1,0:T(8,128)(2,1)S(1)} %dynamic-slice_bitcast_fusion), channel_id=1, source_target_pairs={{0,2},{2,0},{1,3},{3,1},{4,6},{6,4},{5,7},{7,5},{8,10},{10,8},{9,1... | collective-permute-start | bytes 1572872 | tf_op jit(solution)/shard_map/ppermute | solution.py:77
  15.4 10.7 %collective-permute-done = bf16[256,1024]{1,0:T(8,128)(2,1)S(1)} collective-permute-done((bf16[256,1024]{1,0:T(8,128)(2,1)S(1)}, bf16[256,1024]{1,0:T(8,128)(2,1)S(1)}, u32[]{:S(2)}, u32[]{:S(2)}) %collective-permute-start) | collective-permute-done | bytes 524320 | tf_op jit(solution)/shard_map/ppermute | solution.py:77
  32.1 4.8 %convert_bitcast_fusion = bf16[2,512,1024]{2,1,0:T(8,128)(2,1)S(1)} fusion(bf16[1024,2,1024]{2,1,0:T(2,128)(2,1)} %param.10, bf16[512,1024]{1,0:T(8,128)(2,1)S(1)} %bitcast_select_fusion), kind=kOutput, calls=%fused_computation.30 | convolution fusion | flops 2148532224 | bytes 7340032 | tf_op jit(solution)/shard_map/td,dje->jte/dot_general | solution.py:99
  40.0 2.5 %fusion.11 = f32[2,512,1024]{2,1,0:T(8,128)S(1)} fusion(bf16[1024,2,1024]{2,1,0:T(2,128)(2,1)S(1)} %copy-done.18, bf16[1,512,2048]{2,1,0:T(8,128)(2,1)S(1)} %copy-done.7, s32[]{:T(128)S(6)} %select_n.80), kind=kOutput, calls=%fused_computation.19 | convolution fusion | flops 2147483648 | bytes 9437188 | tf_op jit(solution)/shard_map/td,dje->jte/dot_general | solution.py:99
  42.6 20.6 %collective-permute-done.2 = bf16[2,256,1024]{2,1,0:T(8,128)(2,1)S(1)} collective-permute-done((bf16[2,256,1024]{2,1,0:T(8,128)(2,1)S(1)}, bf16[2,256,1024]{2,1,0:T(8,128)(2,1)S(1)}, u32[]{:S(2)}, u32[]{:S(2)}) %collective-permute-start.2) | collective-permute-done | bytes 1048608 | tf_op jit(solution)/shard_map/ppermute | solution.py:91
  69.6 2.3 %convolution_convert_fusion = bf16[512,1024]{1,0:T(8,128)(2,1)} fusion(bf16[512,1024]{1,0:T(8,128)(2,1)S(1)} %copy-done.11, bf16[1024,1024]{1,0:T(8,128)(2,1)S(1)} %copy-done), kind=kOutput, calls=%fused_computation.41 | convolution fusion | flops 1074266112 | bytes 4194304 | tf_op jit(solution)/shard_map/dot_general | solution.py:125
  72.9 4.3 %collective-permute-start.5 = (bf16[256,1024]{0,1:T(8,128)(2,1)}, bf16[256,1024]{0,1:T(8,128)(2,1)}, u32[]{:S(2)}, u32[]{:S(2)}) collective-permute-start(bf16[256,1024]{0,1:T(8,128)(2,1)} %bitcast.150), channel_id=1, source_target_pairs={{0,4},{4,8},{8,12},{1,5},{5,9},{9,13},{2,6},{6,10},{10,14},{3,7},{... | collective-permute-start | bytes 1572872 | tf_op jit(solution)/shard_map/ppermute | solution.py:14
  78.3 3.5 %collective-permute-start.7 = (bf16[256,1024]{0,1:T(8,128)(2,1)}, bf16[256,1024]{0,1:T(8,128)(2,1)}, u32[]{:S(2)}, u32[]{:S(2)}) collective-permute-start(bf16[256,1024]{0,1:T(8,128)(2,1)} %bitcast.149), channel_id=1, source_target_pairs={{0,4},{4,8},{8,12},{1,5},{5,9},{9,13},{2,6},{6,10},{10,14},{3,7},{... | collective-permute-start | bytes 1572872 | tf_op jit(solution)/shard_map/ppermute | solution.py:14
  83.6 8.6 %collective-permute-done.3 = bf16[2,256,1024]{2,1,0:T(8,128)(2,1)} collective-permute-done((bf16[2,256,1024]{2,1,0:T(8,128)(2,1)}, bf16[2,256,1024]{2,1,0:T(8,128)(2,1)}, u32[]{:S(2)}, u32[]{:S(2)}) %collective-permute-start.3) | collective-permute-done | bytes 1048608 | tf_op jit(solution)/shard_map/ppermute | solution.py:91
  92.2 2.2 %slice_add_fusion = f32[2,256,1024]{2,1,0:T(8,128)S(1)} fusion(f32[2,512,1024]{2,1,0:T(8,128)} %copy-done.5, bf16[2,256,1024]{2,1,0:T(8,128)(2,1)} %collective-permute-done.3), kind=kLoop, calls=%fused_computation.22 | loop fusion | flops 1048576 | bytes 5242880 | tf_op jit(solution)/shard_map/add | solution.py:91
  98.3 2.0 copy.90
  100.3 4.6 %collective-permute-start.6 = (bf16[256,1024]{0,1:T(8,128)(2,1)}, bf16[256,1024]{0,1:T(8,128)(2,1)}, u32[]{:S(2)}, u32[]{:S(2)}) collective-permute-start(bf16[256,1024]{0,1:T(8,128)(2,1)} %bitcast.152), channel_id=1, source_target_pairs={{0,4},{4,8},{8,12},{1,5},{5,9},{9,13},{2,6},{6,10},{10,14},{3,7},{... | collective-permute-start | bytes 1572872 | tf_op jit(solution)/shard_map/ppermute | solution.py:14
  106.0 2.8 %collective-permute-start.8 = (bf16[256,1024]{0,1:T(8,128)(2,1)}, bf16[256,1024]{0,1:T(8,128)(2,1)S(1)}, u32[]{:S(2)}, u32[]{:S(2)}) collective-permute-start(bf16[256,1024]{0,1:T(8,128)(2,1)} %bitcast.151), channel_id=1, source_target_pairs={{0,4},{4,8},{8,12},{1,5},{5,9},{9,13},{2,6},{6,10},{10,14},{3,7},{... | collective-permute-start | bytes 1572872 | tf_op jit(solution)/shard_map/ppermute | solution.py:14
  112.1 4.0 %fusion.37 = f32[1,8,128,128]{3,2,1,0:T(8,128)S(1)} fusion(bf16[512,8,128]{2,0,1:T(8,128)(2,1)} %copy_dynamic-update-slice_fusion, bf16[512,8,128]{2,0,1:T(8,128)(2,1)} %constant_dynamic-update-slice_fusion, f32[512,8]{0,1:T(8,128)S(1)} %fusion.67), kind=kOutput, calls=%fused_computation.44 | convolution fusion | flops 806354944 | bytes 2637824 | tf_op jit(solution)/shard_map/bht,bthd,bthe->bhde/dot_general | solution.py:140
  116.7 2.2 %maximum_bitcast_fusion = bf16[1,512,1024]{1,2,0:T(8,128)(2,1)} fusion(bf16[256,1024]{0,1:T(8,128)(2,1)} %collective-permute-done.6, bf16[256,1024]{0,1:T(8,128)(2,1)} %collective-permute-done.5), kind=kLoop, calls=%fused_computation.50 | loop fusion | flops 2097152 | bytes 2097152 | tf_op jit(solution)/shard_map/reshape | solution.py:130
  118.9 6.4 %collective-permute-done.8 = bf16[256,1024]{0,1:T(8,128)(2,1)S(1)} collective-permute-done((bf16[256,1024]{0,1:T(8,128)(2,1)}, bf16[256,1024]{0,1:T(8,128)(2,1)S(1)}, u32[]{:S(2)}, u32[]{:S(2)}) %collective-permute-start.8) | collective-permute-done | bytes 524320 | tf_op jit(solution)/shard_map/ppermute | solution.py:14
  125.3 2.1 maximum_bitcast_fusion.1
  127.6 4.3 %collective-permute-start.9 = (bf16[1,9,128,128]{3,2,1,0:T(8,128)(2,1)S(1)}, bf16[1,9,128,128]{3,2,1,0:T(8,128)(2,1)S(1)}, u32[]{:S(2)}, u32[]{:S(2)}) collective-permute-start(bf16[1,9,128,128]{3,2,1,0:T(8,128)(2,1)S(1)} %fusion.54), channel_id=1, source_target_pairs={{0,4},{4,8},{8,12},{1,5},{5,9},{9,13},{2,6},{6,10},{10,14},{3,7},{... | collective-permute-start | bytes 884744 | tf_op jit(solution)/shard_map/ppermute | solution.py:14
  133.5 2.5 %collective-permute-done.9 = bf16[1,9,128,128]{3,2,1,0:T(8,128)(2,1)S(1)} collective-permute-done((bf16[1,9,128,128]{3,2,1,0:T(8,128)(2,1)S(1)}, bf16[1,9,128,128]{3,2,1,0:T(8,128)(2,1)S(1)}, u32[]{:S(2)}, u32[]{:S(2)}) %collective-permute-start.9) | collective-permute-done | bytes 294944 | tf_op jit(solution)/shard_map/ppermute | solution.py:14
  137.0 4.4 %collective-permute-start.10 = (bf16[1,9,128,128]{3,2,1,0:T(8,128)(2,1)}, bf16[1,9,128,128]{3,2,1,0:T(8,128)(2,1)S(1)}, u32[]{:S(2)}, u32[]{:S(2)}) collective-permute-start(bf16[1,9,128,128]{3,2,1,0:T(8,128)(2,1)} %fusion.56), channel_id=1, source_target_pairs={{0,4},{4,8},{8,12},{1,5},{5,9},{9,13},{2,6},{6,10},{10,14},{3,7},{... | collective-permute-start | bytes 884744 | tf_op jit(solution)/shard_map/ppermute | solution.py:14
  141.4 4.5 %multiply_bitcast_fusion = (f32[64,8,8,128]{3,1,2,0:T(8,128)S(1)}, f32[64,8,8,128]{3,2,1,0:T(8,128)}) fusion(bf16[512,1024]{1,0:T(8,128)(2,1)} %collective-permute-done.4, bf16[1024,1024]{1,0:T(8,128)(2,1)S(1)} %copy-done, bf16[1,512,2048]{2,1,0:T(8,128)(2,1)} %copy-done.6, s32[]{:T(128)S(6)} %select_n.80), kind=kOutput, calls=%fused_computation.38 | convolution fusion | flops 1075314688 | bytes 8388612 | tf_op jit(solution)/shard_map/dot_general | solution.py:125
  147.1 2.0 fusion.14
  149.2 2.2 %fusion = (f32[8,512]{1,0:T(8,128)S(1)}, f32[8,512,512]{1,2,0:T(8,128)S(1)}) fusion(pred[512,512]{0,1:T(8,128)(4,1)S(1)} %copy-done.14, bf16[512,8,128]{2,0,1:T(8,128)(2,1)S(1)} %fusion.14, bf16[512,8,128]{2,0,1:T(8,128)(2,1)S(1)} %copy-done.8), kind=kOutput, calls=%fused_computation.5 | convolution fusion | flops 543158272 | bytes 10764288 | tf_op jit(solution)/shard_map/bihd,bjhd->bhij/dot_general | solution.py:23
  151.4 2.5 %fusion.1 = (f32[8,512]{1,0:T(8,128)S(1)}, f32[8,512,512]{1,2,0:T(8,128)S(1)}) fusion(pred[512,512]{0,1:T(8,128)(4,1)S(1)} %copy-done.15, bf16[512,8,128]{2,0,1:T(8,128)(2,1)S(1)} %fusion.14, bf16[512,8,128]{0,2,1:T(8,128)(2,1)S(1)} %bitcast.145), kind=kOutput, calls=%fused_computation.6 | convolution fusion | flops 543158272 | bytes 10764288 | tf_op jit(solution)/shard_map/bihd,bjhd->bhij/dot_general | solution.py:27
  153.9 2.4 %fusion.6 = f32[8,128,512]{2,1,0:T(8,128)S(1)} fusion(bf16[512,8,128]{0,2,1:T(8,128)(2,1)S(1)} %bitcast.146, f32[8,512,512]{1,2,0:T(8,128)S(1)} %get-tuple-element.36, f32[8,512]{1,0:T(8,128)S(1)} %add.172, pred[512,512]{0,1:T(8,128)(4,1)S(1)} %copy-done.15), kind=kOutput, calls=%fused_computation.14 | convolution fusion | flops 545259520 | bytes 11812864 | tf_op jit(solution)/shard_map/bhij,bjhd->bihd/dot_general | solution.py:40
  156.6 3.7 %collective-permute-start.11 = (bf16[1,9,128,128]{3,2,1,0:T(8,128)(2,1)S(1)}, bf16[1,9,128,128]{3,2,1,0:T(8,128)(2,1)S(1)}, u32[]{:S(2)}, u32[]{:S(2)}) collective-permute-start(bf16[1,9,128,128]{3,2,1,0:T(8,128)(2,1)S(1)} %fusion.58), channel_id=1, source_target_pairs={{0,4},{4,8},{8,12},{1,5},{5,9},{9,13},{2,6},{6,10},{10,14},{3,7},{... | collective-permute-start | bytes 884744 | tf_op jit(solution)/shard_map/ppermute | solution.py:14
  160.3 2.6 %fusion.5 = f32[8,128,512]{2,1,0:T(8,128)S(1)} fusion(bf16[512,8,128]{2,0,1:T(8,128)(2,1)S(1)} %copy-done.9, f32[8,512,512]{1,2,0:T(8,128)S(1)} %get-tuple-element.34, f32[8,512]{1,0:T(8,128)S(1)} %add.172, pred[512,512]{0,1:T(8,128)(4,1)S(1)} %copy-done.14), kind=kOutput, calls=%fused_computation.13 | convolution fusion | flops 545259520 | bytes 11812864 | tf_op jit(solution)/shard_map/bhij,bjhd->bihd/dot_general | solution.py:38
  165.0 25.7 %all-gather.2.cloned.1.call-done = bf16[1024,2048]{1,0:T(8,128)(2,1)} async-done(((bf16[1024,1024]{1,0:T(8,128)(2,1)}), bf16[1024,2048]{1,0:T(8,128)(2,1)}) %all-gather.2.cloned.1.call-update) | async-done | bytes 4194320 | tf_op jit(solution)/shard_map/all_gather | solution.py:189
  190.6 3.8 %fusion.28 = bf16[512,1024]{1,0:T(8,128)(2,1)} fusion(bf16[512,1024]{0,1:T(8,128)(2,1)S(1)} %bitcast.147, bf16[1024,2048]{1,0:T(8,128)(2,1)} %all-gather.2.cloned.1.call-done, s32[]{:T(128)S(6)} %select_n.94), kind=kOutput, calls=%fused_computation.40 | convolution fusion | flops 1074266112 | bytes 4194308 | tf_op jit(solution)/shard_map/dot_general | solution.py:195
  194.5 3.0 %collective-permute-done.12 = bf16[512,1024]{1,0:T(8,128)(2,1)} collective-permute-done((bf16[512,1024]{1,0:T(8,128)(2,1)}, bf16[512,1024]{1,0:T(8,128)(2,1)}, u32[]{:S(2)}, u32[]{:S(2)}) %collective-permute-start.12) | collective-permute-done | bytes 1048608 | tf_op jit(solution)/shard_map/ppermute | solution.py:202
  197.5 4.5 %fusion.34 = bf16[1,512,1024]{2,1,0:T(8,128)(2,1)} fusion(bf16[512,1024]{1,0:T(8,128)(2,1)} %collective-permute-done.12, bf16[512,1024]{0,1:T(8,128)(2,1)S(1)} %bitcast.148, bf16[1024,2048]{1,0:T(8,128)(2,1)} %all-gather.2.cloned.1.call-done, s32[]{:T(128)S(6)} %select_n.79, bf16[1,512,2048]{2,1,0:T(8,128)(2,1)} %param.7), kind=kOutput, calls=%fused_computation.43 | convolution fusion | flops 1076363264 | bytes 6292480 | tf_op jit(solution)/shard_map/dot_general | solution.py:195
  (115 shorter events, 37.2 us)
Async XLA Ops:
  6.5 63.1 %copy-start = (bf16[1024,1024]{1,0:T(8,128)(2,1)S(1)}, bf16[1024,1024]{1,0:T(8,128)(2,1)}, u32[]{:S(2)}) copy-start(bf16[1024,1024]{1,0:T(8,128)(2,1)} %param.9) | copy-start | bytes 6291460
  6.5 2.2 %copy-start.17 = (f32[2048]{0:T(1024)S(1)}, f32[2048]{0:T(1024)}, u32[]{:S(2)}) copy-start(f32[2048]{0:T(1024)} %param.8) | copy-start | bytes 24580
  6.5 184.1 %all-gather.2.cloned.1.call-start = ((), (), s32[]{:S(2)}) async-start(), calls=%async_computation | async-start | bytes 6291456 | tf_op jit(solution)/shard_map/all_gather | solution.py:189
  6.5 2.4 %copy-start.2 = (bf16[1,512,2048]{2,1,0:T(8,128)(2,1)S(1)}, bf16[1,512,2048]{2,1,0:T(8,128)(2,1)}, u32[]{:S(2)}) copy-start(bf16[1,512,2048]{2,1,0:T(8,128)(2,1)} %param.7) | copy-start | bytes 6291460
  8.9 5.3 %copy-start.16 = (f32[1,8,512]{2,1,0:T(8,128)S(1)}, f32[1,8,512]{2,1,0:T(8,128)}, u32[]{:S(2)}) copy-start(f32[1,8,512]{2,1,0:T(8,128)} %param.12) | copy-start | bytes 49156
  9.5 1.3 copy-start.6
  11.1 15.0 %collective-permute-start = (bf16[256,1024]{1,0:T(8,128)(2,1)S(1)}, bf16[256,1024]{1,0:T(8,128)(2,1)S(1)}, u32[]{:S(2)}, u32[]{:S(2)}) collective-permute-start(bf16[256,1024]{1,0:T(8,128)(2,1)S(1)} %dynamic-slice_bitcast_fusion), channel_id=1, source_target_pairs={{0,2},{2,0},{1,3},{3,1},{4,6},{6,4},{5,7},{7,5},{8,10},{10,8},{9,1... | collective-permute-start | bytes 1572872 | tf_op jit(solution)/shard_map/ppermute | solution.py:77
  26.0 1.9 collective-permute-start.1
  32.1 7.9 %copy-start.18 = (bf16[1024,2,1024]{2,1,0:T(2,128)(2,1)S(1)}, bf16[1024,2,1024]{2,1,0:T(2,128)(2,1)}, u32[]{:S(2)}) copy-start(bf16[1024,2,1024]{2,1,0:T(2,128)(2,1)} %param.10) | copy-start | bytes 12582916
  36.8 3.2 %copy-start.7 = (bf16[1,512,2048]{2,1,0:T(8,128)(2,1)S(1)}, bf16[1,512,2048]{2,1,0:T(8,128)(2,1)}, u32[]{:S(2)}) copy-start(bf16[1,512,2048]{2,1,0:T(8,128)(2,1)} %copy-done.6) | copy-start | bytes 6291460
  38.0 25.2 %collective-permute-start.2 = (bf16[2,256,1024]{2,1,0:T(8,128)(2,1)S(1)}, bf16[2,256,1024]{2,1,0:T(8,128)(2,1)S(1)}, u32[]{:S(2)}, u32[]{:S(2)}) collective-permute-start(bf16[2,256,1024]{2,1,0:T(8,128)(2,1)S(1)} %get-tuple-element.32), channel_id=1, source_target_pairs={{0,2},{2,0},{1,3},{3,1},{4,6},{6,4},{5,7},{7,5},{8,10},{10,8},{9,1... | collective-permute-start | bytes 3145736 | tf_op jit(solution)/shard_map/ppermute | solution.py:91
  42.5 21.0 %copy-start.5 = (f32[2,512,1024]{2,1,0:T(8,128)}, f32[2,512,1024]{2,1,0:T(8,128)S(1)}, u32[]{:S(2)}) copy-start(f32[2,512,1024]{2,1,0:T(8,128)S(1)} %fusion.11) | copy-start | bytes 12582916
  65.1 4.5 %copy-start.11 = (bf16[512,1024]{1,0:T(8,128)(2,1)S(1)}, bf16[512,1024]{1,0:T(8,128)(2,1)}, u32[]{:S(2)}) copy-start(bf16[512,1024]{1,0:T(8,128)(2,1)} %copy-done.10) | copy-start | bytes 3145732
  67.4 24.7 %collective-permute-start.3 = (bf16[2,256,1024]{2,1,0:T(8,128)(2,1)}, bf16[2,256,1024]{2,1,0:T(8,128)(2,1)}, u32[]{:S(2)}, u32[]{:S(2)}) collective-permute-start(bf16[2,256,1024]{2,1,0:T(8,128)(2,1)} %get-tuple-element.17), channel_id=1, source_target_pairs={{0,2},{2,0},{1,3},{3,1},{4,6},{6,4},{5,7},{7,5},{8,10},{10,8},{9,1... | collective-permute-start | bytes 3145736 | tf_op jit(solution)/shard_map/ppermute | solution.py:91
  69.6 2.3 %copy-start.3 = (bf16[256,8,128]{2,0,1:T(8,128)(2,1)S(1)}, bf16[256,8,128]{2,0,1:T(8,128)(2,1)}, u32[]{:S(2)}) copy-start(bf16[256,8,128]{2,0,1:T(8,128)(2,1)} %fusion.45) | copy-start | bytes 1572868
  72.9 43.3 %collective-permute-start.5 = (bf16[256,1024]{0,1:T(8,128)(2,1)}, bf16[256,1024]{0,1:T(8,128)(2,1)}, u32[]{:S(2)}, u32[]{:S(2)}) collective-permute-start(bf16[256,1024]{0,1:T(8,128)(2,1)} %bitcast.150), channel_id=1, source_target_pairs={{0,4},{4,8},{8,12},{1,5},{5,9},{9,13},{2,6},{6,10},{10,14},{3,7},{... | collective-permute-start | bytes 1572872 | tf_op jit(solution)/shard_map/ppermute | solution.py:14
  78.3 40.6 %collective-permute-start.7 = (bf16[256,1024]{0,1:T(8,128)(2,1)}, bf16[256,1024]{0,1:T(8,128)(2,1)}, u32[]{:S(2)}, u32[]{:S(2)}) collective-permute-start(bf16[256,1024]{0,1:T(8,128)(2,1)} %bitcast.149), channel_id=1, source_target_pairs={{0,4},{4,8},{8,12},{1,5},{5,9},{9,13},{2,6},{6,10},{10,14},{3,7},{... | collective-permute-start | bytes 1572872 | tf_op jit(solution)/shard_map/ppermute | solution.py:14
  97.1 12.6 %copy-start.4 = (bf16[256,8,128]{2,0,1:T(8,128)(2,1)S(1)}, bf16[256,8,128]{2,0,1:T(8,128)(2,1)}, u32[]{:S(2)}) copy-start(bf16[256,8,128]{2,0,1:T(8,128)(2,1)} %fusion.44) | copy-start | bytes 1572868
  100.3 16.3 %collective-permute-start.6 = (bf16[256,1024]{0,1:T(8,128)(2,1)}, bf16[256,1024]{0,1:T(8,128)(2,1)}, u32[]{:S(2)}, u32[]{:S(2)}) collective-permute-start(bf16[256,1024]{0,1:T(8,128)(2,1)} %bitcast.152), channel_id=1, source_target_pairs={{0,4},{4,8},{8,12},{1,5},{5,9},{9,13},{2,6},{6,10},{10,14},{3,7},{... | collective-permute-start | bytes 1572872 | tf_op jit(solution)/shard_map/ppermute | solution.py:14
  106.0 19.4 %collective-permute-start.8 = (bf16[256,1024]{0,1:T(8,128)(2,1)}, bf16[256,1024]{0,1:T(8,128)(2,1)S(1)}, u32[]{:S(2)}, u32[]{:S(2)}) collective-permute-start(bf16[256,1024]{0,1:T(8,128)(2,1)} %bitcast.151), channel_id=1, source_target_pairs={{0,4},{4,8},{8,12},{1,5},{5,9},{9,13},{2,6},{6,10},{10,14},{3,7},{... | collective-permute-start | bytes 1572872 | tf_op jit(solution)/shard_map/ppermute | solution.py:14
  110.6 30.7 %collective-permute-start.4 = (bf16[512,1024]{1,0:T(8,128)(2,1)}, bf16[512,1024]{1,0:T(8,128)(2,1)}, u32[]{:S(2)}, u32[]{:S(2)}) collective-permute-start(bf16[512,1024]{1,0:T(8,128)(2,1)} %convolution_convert_fusion), channel_id=1, source_target_pairs={{0,2},{2,0},{1,3},{3,1},{4,6},{6,4},{5,7},{7,5},{8,10},{10,8},{9,1... | collective-permute-start | bytes 3145736 | tf_op jit(solution)/shard_map/ppermute | solution.py:91
  127.6 8.5 %collective-permute-start.9 = (bf16[1,9,128,128]{3,2,1,0:T(8,128)(2,1)S(1)}, bf16[1,9,128,128]{3,2,1,0:T(8,128)(2,1)S(1)}, u32[]{:S(2)}, u32[]{:S(2)}) collective-permute-start(bf16[1,9,128,128]{3,2,1,0:T(8,128)(2,1)S(1)} %fusion.54), channel_id=1, source_target_pairs={{0,4},{4,8},{8,12},{1,5},{5,9},{9,13},{2,6},{6,10},{10,14},{3,7},{... | collective-permute-start | bytes 884744 | tf_op jit(solution)/shard_map/ppermute | solution.py:14
  137.0 19.4 %collective-permute-start.10 = (bf16[1,9,128,128]{3,2,1,0:T(8,128)(2,1)}, bf16[1,9,128,128]{3,2,1,0:T(8,128)(2,1)S(1)}, u32[]{:S(2)}, u32[]{:S(2)}) collective-permute-start(bf16[1,9,128,128]{3,2,1,0:T(8,128)(2,1)} %fusion.56), channel_id=1, source_target_pairs={{0,4},{4,8},{8,12},{1,5},{5,9},{9,13},{2,6},{6,10},{10,14},{3,7},{... | collective-permute-start | bytes 884744 | tf_op jit(solution)/shard_map/ppermute | solution.py:14
  147.0 2.2 %copy-start.8 = (bf16[512,8,128]{2,0,1:T(8,128)(2,1)S(1)}, bf16[512,8,128]{2,0,1:T(8,128)(2,1)}, u32[]{:S(2)}) copy-start(bf16[512,8,128]{2,0,1:T(8,128)(2,1)} %constant_dynamic-update-slice_fusion) | copy-start | bytes 3145732
  147.1 2.1 copy-start.14
  149.1 2.2 %copy-start.12 = (bf16[1,512,1024]{1,2,0:T(8,128)(2,1)S(1)}, bf16[1,512,1024]{1,2,0:T(8,128)(2,1)}, u32[]{:S(2)}) copy-start(bf16[1,512,1024]{1,2,0:T(8,128)(2,1)} %maximum_bitcast_fusion) | copy-start | bytes 3145732
  149.2 2.2 %copy-start.15 = (pred[512,512]{0,1:T(8,128)(4,1)S(1)}, pred[512,512]{0,1:T(8,128)(4,1)}, u32[]{:S(2)}) copy-start(pred[512,512]{0,1:T(8,128)(4,1)} %fusion.47) | copy-start | bytes 786436
  151.4 2.5 %copy-start.13 = (bf16[1,512,1024]{1,2,0:T(8,128)(2,1)S(1)}, bf16[1,512,1024]{1,2,0:T(8,128)(2,1)}, u32[]{:S(2)}) copy-start(bf16[1,512,1024]{1,2,0:T(8,128)(2,1)} %maximum_bitcast_fusion.1) | copy-start | bytes 3145732
  153.9 6.3 %copy-start.9 = (bf16[512,8,128]{2,0,1:T(8,128)(2,1)S(1)}, bf16[512,8,128]{2,0,1:T(8,128)(2,1)}, u32[]{:S(2)}) copy-start(bf16[512,8,128]{2,0,1:T(8,128)(2,1)} %copy_dynamic-update-slice_fusion) | copy-start | bytes 3145732
  156.6 7.7 %collective-permute-start.11 = (bf16[1,9,128,128]{3,2,1,0:T(8,128)(2,1)S(1)}, bf16[1,9,128,128]{3,2,1,0:T(8,128)(2,1)S(1)}, u32[]{:S(2)}, u32[]{:S(2)}) collective-permute-start(bf16[1,9,128,128]{3,2,1,0:T(8,128)(2,1)S(1)} %fusion.58), channel_id=1, source_target_pairs={{0,4},{4,8},{8,12},{1,5},{5,9},{9,13},{2,6},{6,10},{10,14},{3,7},{... | collective-permute-start | bytes 884744 | tf_op jit(solution)/shard_map/ppermute | solution.py:14
  194.5 3.0 %collective-permute-start.12 = (bf16[512,1024]{1,0:T(8,128)(2,1)}, bf16[512,1024]{1,0:T(8,128)(2,1)}, u32[]{:S(2)}, u32[]{:S(2)}) collective-permute-start(bf16[512,1024]{1,0:T(8,128)(2,1)} %fusion.28), channel_id=1, source_target_pairs={{0,1},{1,0},{2,3},{3,2},{4,5},{5,4},{6,7},{7,6},{8,9},{9,8},{10,11... | collective-permute-start | bytes 3145736 | tf_op jit(solution)/shard_map/ppermute | solution.py:202
  194.5 7.5 %copy-start.1 = (bf16[1024,1024]{1,0:T(8,128)(2,1)S(1)}, bf16[1024,1024]{1,0:T(8,128)(2,1)}, u32[]{:S(2)}) copy-start(bf16[1024,1024]{1,0:T(8,128)(2,1)} %param.9) | copy-start | bytes 6291460
  (1 other events, 1.0 us)
Sparse Core Ops, SparseCore 0:
  133.6 56.9 all-gather.1

commit v11 on v10

--- a/solution.py
+++ b/solution.py
@@ -95,16 +95,20 @@
             ).astype(jnp.float32)
         return total
 
-    kv_partials = [
-        jnp.einsum("td,dje->jte", rows, w_keyvalue, preferred_element_type=jnp.float32)
-        for rows in stacked
-    ]
     pieces = 2
     rows_per = count // pieces
     raw_chunks, key_chunks, value_chunks, prior_chunks = [], [], [], []
     for piece in range(pieces):
         raw = gathered_sum(
-            [p[:, piece * rows_per : (piece + 1) * rows_per] for p in kv_partials],
+            [
+                jnp.einsum(
+                    "td,dje->jte",
+                    rows[piece * rows_per : (piece + 1) * rows_per],
+                    w_keyvalue,
+                    preferred_element_type=jnp.float32,
+                )
+                for rows in stacked
+            ],
             after=key_chunks[-1] if key_chunks else None,
         )
         keys_here = rms_rows(raw[0].reshape(rows_per, heads_here, head_dim), 1e-06).astype(jnp.bfloat16)
@@ -123,7 +127,7 @@
     pair_raw = jnp.concatenate(raw_chunks, axis=1)
     query_raw = gathered_sum(
         [jnp.dot(rows, w_query, preferred_element_type=jnp.float32) for rows in stacked],
-        after=pair_raw,
+        after=key_chunks[-1],
     )
     lookup_vectors = jnp.concatenate(key_chunks, axis=0).reshape(trajs, span, heads_here, head_dim)
     values = jnp.concatenate(value_chunks, axis=0).reshape(trajs, span, heads_here, head_dim)
@@ -185,8 +189,16 @@
         scale,
     )
     attended = (window + read).astype(jnp.bfloat16).reshape(count, inner_here)
-    w_output = lax.optimization_barrier((w_output, pair_raw))[0]
-    w_output_rows = lax.all_gather(w_output, "wloop", axis=1, tiled=True)
+    w_output = lax.optimization_barrier((w_output, key_chunks[-1]))[0]
+    out_cols = w_output.shape[1]
+    from_ranks = [w_output] + [
+        lax.ppermute(w_output, "wloop", [(source, (source + step) % ways) for source in range(ways)])
+        for step in range(1, ways)
+    ]
+    rank_order = (me - jnp.arange(ways)) % ways
+    w_output_rows = (
+        jnp.take(jnp.stack(from_ranks), rank_order, axis=0).transpose(1, 0, 2).reshape(w_output.shape[0], ways * out_cols)
+    )
     cores = lax.axis_size("heads")
     core = lax.axis_index("heads")
     share = width // cores

time: 209 us -> 211 us (level)
  waiting for transfers between devices: 80.5 us -> 64.7 us
  between operations: 14.6 us -> 1.26 us
  local copies, waits for them, and re-layouts: 20.2 us -> 32 us
  matrix products: 36.8 us -> 45.5 us
  other arithmetic: 21.1 us -> 29.3 us
    all_gather x1 -> x0, waiting for transfers between devices: 25.7 us -> none  [shards(): w_output_rows = lax.all_gather(w_output, 'wloop', axis=1, tiled=True)]
    ppermute x0 -> x1, waiting for transfers between devices: none -> 14.3 us  [shards(): lax.ppermute(w_output, 'wloop', [(source, (source + step) % ways) for sou...]
    dot_general x2 -> x4, matrix products: 7.28 us -> 17.6 us  [shards(): jnp.einsum('td,dje->jte', rows[piece * rows_per:(piece + 1) * rows_per],...]
    select_n x0 -> x1, local copies, waits for them, and re-layouts: none -> 6.33 us  [shards(): jnp.take(jnp.stack(from_ranks), rank_order, axis=0).transpose(1, 0, 2)]
    gather x0 -> x2, local copies, waits for them, and re-layouts: none -> 5.87 us  [shards(): jnp.take(jnp.stack(from_ranks), rank_order, axis=0).transpose(1, 0, 2)]
    select_n x0 -> x2, other arithmetic: none -> 3.96 us  [shards(): jnp.take(jnp.stack(from_ranks), rank_order, axis=0).transpose(1, 0, 2)]
    another operation x2 -> x3, other arithmetic: 1.17 us -> 4.8 us  [the longest x1 3.62 us: shards(): jnp.stack(from_ranks)]
    ppermute x3, waiting for transfers between devices: 29.3 us -> 26.6 us  [gathered_sum(): lax.ppermute(outgoing, 'wloop', [(source, (source - step) % ways) for sou...]
  transfers between devices with their start and end apart: 14 -> 14, of which waited for: 10 -> 10; matrix products, arithmetic and copies ran while one was open for 24% -> 26% of each run, Pallas kernels for 0% -> 0%
where the time goes in v11:
time: 211 us; the launch traced here: 210 us
  waiting for transfers between devices  64.7 us (31%)
  matrix products  45.5 us (22%)
  starting transfers between devices  37.3 us (18%)
  local copies, waits for them, and re-layouts  32 us (15%)
  other arithmetic  29.3 us (14%)
    ppermute x7, starting transfers between devices, shifted(): lax.ppermute(value, axis, [(source, source + steps) for source in range(i...  27.7 us
    ppermute x3, waiting for transfers between devices, gathered_sum(): lax.ppermute(outgoing, 'wloop', [(source, (source - step) % ways) for sou...  26.6 us
    dot_general x4, matrix products, shards(): jnp.einsum('td,dje->jte', rows[piece * rows_per:(piece + 1) * rows_per],...  17.6 us
    ppermute x1, waiting for transfers between devices, shards(): lax.ppermute(w_output, 'wloop', [(source, (source + step) % ways) for sou...  14.3 us
    unnamed x49, local copies, waits for them, and re-layouts  10 us
    ppermute x1, waiting for transfers between devices, shards(): lax.ppermute(part, 'wloop', [(source, (source + step) % ways) for source...  9.89 us
    ppermute x7, waiting for transfers between devices, shifted(): lax.ppermute(value, axis, [(source, source + steps) for source in range(i...  9.48 us
    dot_general x2, matrix products, output_share(): jnp.dot(attended, lax.dynamic_slice_in_dim(w_output_rows, index * share,...  7.58 us
  transfers between devices with their start and end apart: 14, of which 10 were waited for; matrix products, arithmetic and copies ran while one was open for 26% of the time, Pallas kernels for 0%

profile of v11, /device:TPU:0, one launch (start us, length us, event | category | flops | bytes accessed | tf_op | source)
XLA Modules:
  0.0 210.0 jit_solution(16280725957936259484)
XLA Ops:
  6.1 3.0 %collective-permute-start = (bf16[256,1024]{1,0:T(8,128)(2,1)S(1)}, bf16[256,1024]{1,0:T(8,128)(2,1)S(1)}, u32[]{:S(2)}, u32[]{:S(2)}) collective-permute-start(bf16[256,1024]{1,0:T(8,128)(2,1)S(1)} %dynamic-slice_bitcast_fusion.4), channel_id=1, source_target_pairs={{0,2},{2,0},{1,3},{3,1},{4,6},{6,4},{5,7},{7,5},{8,10},{10,8},{9,1... | collective-permute-start | bytes 1572872 | tf_op jit(solution)/shard_map/ppermute | solution.py:77
  11.1 9.9 %collective-permute-done = bf16[256,1024]{1,0:T(8,128)(2,1)S(1)} collective-permute-done((bf16[256,1024]{1,0:T(8,128)(2,1)S(1)}, bf16[256,1024]{1,0:T(8,128)(2,1)S(1)}, u32[]{:S(2)}, u32[]{:S(2)}) %collective-permute-start) | collective-permute-done | bytes 524320 | tf_op jit(solution)/shard_map/ppermute | solution.py:77
  26.0 5.1 %fusion.46 = bf16[2,256,1024]{2,1,0:T(8,128)(2,1)} fusion(bf16[1024,2,1024]{2,1,0:T(2,128)(2,1)} %param.10, bf16[2,256,1024]{2,1,0:T(8,128)(2,1)S(1)} %broadcast_select_fusion), kind=kOutput, calls=%fused_computation.55 | convolution fusion | flops 1074266112 | bytes 5767168 | tf_op jit(solution)/shard_map/td,dje->jte/dot_general | solution.py:104
  33.4 5.1 %fusion.43 = bf16[2,256,1024]{2,1,0:T(8,128)(2,1)} fusion(bf16[1024,2,1024]{2,1,0:T(2,128)(2,1)} %param.10, bf16[2,256,1024]{2,1,0:T(8,128)(2,1)} %copy-done.10), kind=kOutput, calls=%fused_computation.54 | convolution fusion | flops 1074266112 | bytes 5767168 | tf_op jit(solution)/shard_map/td,dje->jte/dot_general | solution.py:104
  38.4 18.2 %collective-permute-done.2 = bf16[2,256,1024]{2,1,0:T(8,128)(2,1)} collective-permute-done((bf16[2,256,1024]{2,1,0:T(8,128)(2,1)}, bf16[2,256,1024]{2,1,0:T(8,128)(2,1)}, u32[]{:S(2)}, u32[]{:S(2)}) %collective-permute-start.2) | collective-permute-done | bytes 1048608 | tf_op jit(solution)/shard_map/ppermute | solution.py:91
  56.7 3.1 %bitcast_add_fusion.1 = f32[2,256,1024]{2,1,0:T(8,128)S(1)} fusion(bf16[2,256,1024]{2,1,0:T(8,128)(2,1)} %collective-permute-done.2, bf16[1024,2,1024]{2,1,0:T(2,128)(2,1)S(1)} %copy-done.17, bf16[1,512,2048]{2,1,0:T(8,128)(2,1)} %copy-done.6, s32[]{:T(128)S(6)} %select_n.120), kind=kOutput, calls=%fused_computation.39 | convolution fusion | flops 1074790400 | bytes 7864324 | tf_op jit(solution)/shard_map/td,dje->jte/dot_general | solution.py:104
  62.3 2.4 %fusion.60 = bf16[256,8,128]{2,0,1:T(8,128)(2,1)} fusion(f32[256,8,128]{2,1,0:T(8,128)} %bitcast.155, f32[256,8]{0,1:T(8,128)S(1)} %add_rsqrt_fusion.2), kind=kLoop, calls=%fused_computation.71 | loop fusion | flops 524288 | bytes 1581056 | tf_op jit(solution)/shard_map/convert_element_type | solution.py:114
  72.1 4.3 %collective-permute-start.5 = (bf16[256,1024]{0,1:T(8,128)(2,1)}, bf16[256,1024]{0,1:T(8,128)(2,1)}, u32[]{:S(2)}, u32[]{:S(2)}) collective-permute-start(bf16[256,1024]{0,1:T(8,128)(2,1)} %bitcast.171), channel_id=1, source_target_pairs={{0,4},{4,8},{8,12},{1,5},{5,9},{9,13},{2,6},{6,10},{10,14},{3,7},{... | collective-permute-start | bytes 1572872 | tf_op jit(solution)/shard_map/ppermute | solution.py:14
  77.6 3.5 %collective-permute-start.7 = (bf16[256,1024]{0,1:T(8,128)(2,1)}, bf16[256,1024]{0,1:T(8,128)(2,1)}, u32[]{:S(2)}, u32[]{:S(2)}) collective-permute-start(bf16[256,1024]{0,1:T(8,128)(2,1)} %bitcast.170), channel_id=1, source_target_pairs={{0,4},{4,8},{8,12},{1,5},{5,9},{9,13},{2,6},{6,10},{10,14},{3,7},{... | collective-permute-start | bytes 1572872 | tf_op jit(solution)/shard_map/ppermute | solution.py:14
  82.9 8.4 %collective-permute-done.3 = bf16[2,256,1024]{2,1,0:T(8,128)(2,1)} collective-permute-done((bf16[2,256,1024]{2,1,0:T(8,128)(2,1)}, bf16[2,256,1024]{2,1,0:T(8,128)(2,1)}, u32[]{:S(2)}, u32[]{:S(2)}) %collective-permute-start.3) | collective-permute-done | bytes 1048608 | tf_op jit(solution)/shard_map/ppermute | solution.py:91
  91.3 4.3 %bitcast_add_fusion = f32[2,256,1024]{2,1,0:T(8,128)S(1)} fusion(bf16[2,256,1024]{2,1,0:T(8,128)(2,1)} %collective-permute-done.3, bf16[1024,2,1024]{2,1,0:T(2,128)(2,1)} %param.10, bf16[1,512,2048]{2,1,0:T(8,128)(2,1)} %copy-done.6, s32[]{:T(128)S(6)} %add.223, s32[]{:T(128)S(6)} %select_n.120), kind=kOutput, calls=%fused_computation.38 | convolution fusion | flops 1074790400 | bytes 7864328 | tf_op jit(solution)/shard_map/td,dje->jte/dot_general | solution.py:104
  101.6 4.5 %collective-permute-start.6 = (bf16[256,1024]{0,1:T(8,128)(2,1)}, bf16[256,1024]{0,1:T(8,128)(2,1)}, u32[]{:S(2)}, u32[]{:S(2)}) collective-permute-start(bf16[256,1024]{0,1:T(8,128)(2,1)} %bitcast.173), channel_id=1, source_target_pairs={{0,4},{4,8},{8,12},{1,5},{5,9},{9,13},{2,6},{6,10},{10,14},{3,7},{... | collective-permute-start | bytes 1572872 | tf_op jit(solution)/shard_map/ppermute | solution.py:14
  109.6 2.7 %collective-permute-start.8 = (bf16[256,1024]{0,1:T(8,128)(2,1)}, bf16[256,1024]{0,1:T(8,128)(2,1)S(1)}, u32[]{:S(2)}, u32[]{:S(2)}) collective-permute-start(bf16[256,1024]{0,1:T(8,128)(2,1)} %bitcast.172), channel_id=1, source_target_pairs={{0,4},{4,8},{8,12},{1,5},{5,9},{9,13},{2,6},{6,10},{10,14},{3,7},{... | collective-permute-start | bytes 1572872 | tf_op jit(solution)/shard_map/ppermute | solution.py:14
  113.2 4.0 %fusion.54 = f32[1,8,128,128]{3,2,1,0:T(8,128)S(1)} fusion(bf16[512,8,128]{2,0,1:T(8,128)(2,1)} %copy_dynamic-update-slice_fusion, bf16[512,8,128]{2,0,1:T(8,128)(2,1)} %constant_dynamic-update-slice_fusion, f32[512,8]{0,1:T(8,128)S(1)} %fusion.81), kind=kOutput, calls=%fused_computation.57 | convolution fusion | flops 806354944 | bytes 2637824 | tf_op jit(solution)/shard_map/bht,bthd,bthe->bhde/dot_general | solution.py:144
  117.9 2.3 %maximum_bitcast_fusion = bf16[1,512,1024]{1,2,0:T(8,128)(2,1)} fusion(bf16[256,1024]{0,1:T(8,128)(2,1)} %collective-permute-done.6, bf16[256,1024]{0,1:T(8,128)(2,1)} %collective-permute-done.5), kind=kLoop, calls=%fused_computation.63 | loop fusion | flops 2097152 | bytes 2097152 | tf_op jit(solution)/shard_map/reshape | solution.py:134
  120.2 6.4 %collective-permute-done.8 = bf16[256,1024]{0,1:T(8,128)(2,1)S(1)} collective-permute-done((bf16[256,1024]{0,1:T(8,128)(2,1)}, bf16[256,1024]{0,1:T(8,128)(2,1)S(1)}, u32[]{:S(2)}, u32[]{:S(2)}) %collective-permute-start.8) | collective-permute-done | bytes 524320 | tf_op jit(solution)/shard_map/ppermute | solution.py:14
  128.9 4.3 %collective-permute-start.9 = (bf16[1,9,128,128]{3,2,1,0:T(8,128)(2,1)S(1)}, bf16[1,9,128,128]{3,2,1,0:T(8,128)(2,1)S(1)}, u32[]{:S(2)}, u32[]{:S(2)}) collective-permute-start(bf16[1,9,128,128]{3,2,1,0:T(8,128)(2,1)S(1)} %fusion.68), channel_id=1, source_target_pairs={{0,4},{4,8},{8,12},{1,5},{5,9},{9,13},{2,6},{6,10},{10,14},{3,7},{... | collective-permute-start | bytes 884744 | tf_op jit(solution)/shard_map/ppermute | solution.py:14
  138.3 4.6 %collective-permute-start.10 = (bf16[1,9,128,128]{3,2,1,0:T(8,128)(2,1)}, bf16[1,9,128,128]{3,2,1,0:T(8,128)(2,1)S(1)}, u32[]{:S(2)}, u32[]{:S(2)}) collective-permute-start(bf16[1,9,128,128]{3,2,1,0:T(8,128)(2,1)} %fusion.70), channel_id=1, source_target_pairs={{0,4},{4,8},{8,12},{1,5},{5,9},{9,13},{2,6},{6,10},{10,14},{3,7},{... | collective-permute-start | bytes 884744 | tf_op jit(solution)/shard_map/ppermute | solution.py:14
  142.9 2.6 %multiply_bitcast_fusion = (f32[64,8,8,128]{3,1,2,0:T(8,128)S(1)}, f32[64,8,8,128]{3,2,1,0:T(8,128)}) fusion(bf16[512,1024]{1,0:T(8,128)(2,1)S(1)} %collective-permute-done.4, bf16[1024,1024]{1,0:T(8,128)(2,1)S(1)} %copy-done, bf16[1,512,2048]{2,1,0:T(8,128)(2,1)S(1)} %copy-done.7, s32[]{:T(128)S(6)} %select_n.120), kind=kOutput, calls=%fused_computation.47 | convolution fusion | flops 1075314688 | bytes 8388612 | tf_op jit(solution)/shard_map/dot_general | solution.py:129
  151.0 2.5 %fusion.1 = (f32[8,512]{1,0:T(8,128)S(1)}, f32[8,512,512]{1,2,0:T(8,128)S(1)}) fusion(pred[512,512]{0,1:T(8,128)(4,1)S(1)} %copy-done.14, bf16[512,8,128]{2,0,1:T(8,128)(2,1)S(1)} %fusion.17, bf16[512,8,128]{0,2,1:T(8,128)(2,1)S(1)} %bitcast.168), kind=kOutput, calls=%fused_computation.8 | convolution fusion | flops 543158272 | bytes 10764288 | tf_op jit(solution)/shard_map/bihd,bjhd->bhij/dot_general | solution.py:27
  153.6 2.4 %fusion.7 = f32[8,128,512]{2,1,0:T(8,128)S(1)} fusion(bf16[512,8,128]{0,2,1:T(8,128)(2,1)S(1)} %bitcast.169, f32[8,512,512]{1,2,0:T(8,128)S(1)} %get-tuple-element.36, f32[8,512]{1,0:T(8,128)S(1)} %add.202, pred[512,512]{0,1:T(8,128)(4,1)S(1)} %copy-done.14), kind=kOutput, calls=%fused_computation.19 | convolution fusion | flops 545259520 | bytes 11812864 | tf_op jit(solution)/shard_map/bhij,bjhd->bihd/dot_general | solution.py:40
  156.2 3.7 %collective-permute-start.11 = (bf16[1,9,128,128]{3,2,1,0:T(8,128)(2,1)S(1)}, bf16[1,9,128,128]{3,2,1,0:T(8,128)(2,1)S(1)}, u32[]{:S(2)}, u32[]{:S(2)}) collective-permute-start(bf16[1,9,128,128]{3,2,1,0:T(8,128)(2,1)S(1)} %fusion.72), channel_id=1, source_target_pairs={{0,4},{4,8},{8,12},{1,5},{5,9},{9,13},{2,6},{6,10},{10,14},{3,7},{... | collective-permute-start | bytes 884744 | tf_op jit(solution)/shard_map/ppermute | solution.py:14
  159.9 2.6 %fusion.6 = f32[8,128,512]{2,1,0:T(8,128)S(1)} fusion(bf16[512,8,128]{2,0,1:T(8,128)(2,1)S(1)} %copy-done.9, f32[8,512,512]{1,2,0:T(8,128)S(1)} %get-tuple-element.34, f32[8,512]{1,0:T(8,128)S(1)} %add.202, pred[512,512]{0,1:T(8,128)(4,1)S(1)} %copy-done.13), kind=kOutput, calls=%fused_computation.18 | convolution fusion | flops 545259520 | bytes 11812864 | tf_op jit(solution)/shard_map/bhij,bjhd->bihd/dot_general | solution.py:38
  165.7 14.3 %collective-permute-done.12 = bf16[1024,1024]{1,0:T(8,128)(2,1)} collective-permute-done((bf16[1024,1024]{1,0:T(8,128)(2,1)}, bf16[1024,1024]{1,0:T(8,128)(2,1)}, u32[]{:S(2)}, u32[]{:S(2)}) %collective-permute-start.12) | collective-permute-done | bytes 2097184 | tf_op jit(solution)/shard_map/ppermute | solution.py:195
  179.9 3.6 %fusion.16 = (bf16[2,512,1024]{2,1,0:T(8,128)(2,1)}, bf16[2,512,1024]{2,1,0:T(8,128)(2,1)}) fusion(bf16[1,1024,1024]{2,1,0:T(8,128)(2,1)} %bitcast.52, bf16[1,1024,1024]{2,1,0:T(8,128)(2,1)} %bitcast.53), kind=kLoop, calls=%fused_computation.28 | loop fusion | flops 8388608 | bytes 8388608 | tf_op jit(solution)/shard_map/stack | solution.py:200
  183.6 2.3 %gather_fusion.2 = bf16[2,512,1024]{2,1,0:T(8,128)(2,1)S(1)} fusion(bf16[2,512,1024]{2,1,0:T(8,128)(2,1)} %get-tuple-element.30, s32[1024]{0:T(1024)S(1)} %pad_clamp_fusion), kind=kCustom, calls=%fused_computation.2 | custom fusion | bytes 4194312 | tf_op jit(solution)/shard_map/jit(_take)/gather | solution.py:200
  185.8 3.6 %gather_fusion.1 = bf16[2,512,1024]{2,1,0:T(8,128)(2,1)} fusion(bf16[2,512,1024]{2,1,0:T(8,128)(2,1)} %get-tuple-element.29, s32[1024]{0:T(1024)S(1)} %pad_clamp_fusion), kind=kCustom, calls=%fused_computation.1 | custom fusion | bytes 4194312 | tf_op jit(solution)/shard_map/jit(_take)/gather | solution.py:200
  189.4 3.9 %fusion.5 = bf16[1024,2,1024]{2,0,1:T(8,128)(2,1)} fusion(bf16[2,512,1024]{2,1,0:T(8,128)(2,1)S(1)} %gather_fusion.2, bf16[2,512,1024]{2,1,0:T(8,128)(2,1)} %gather_fusion.1, pred[2]{0:T(512)(128)(4,1)S(1)} %get-tuple-element.37), kind=kLoop, calls=%fused_computation.17 | loop fusion | flops 10485760 | bytes 8388610 | tf_op jit(solution)/shard_map/jit(_take)/select_n | solution.py:200
  193.4 6.3 %copy.110 = bf16[1024,2,1024]{0,2,1:T(8,128)(2,1)} copy(bf16[1024,2,1024]{2,0,1:T(8,128)(2,1)} %fusion.5) | data formatting | bytes 8388608 | tf_op jit(solution)/shard_map/jit(_take)/select_n | solution.py:200
  199.7 2.9 %fusion.33 = bf16[512,1024]{1,0:T(8,128)(2,1)S(1)} fusion(bf16[512,1024]{0,1:T(8,128)(2,1)S(1)} %bitcast.183, bf16[1024,2048]{0,1:T(8,128)(2,1)} %bitcast.163, s32[]{:T(128)S(6)} %select_n.141), kind=kOutput, calls=%fused_computation.49 | convolution fusion | flops 1074266112 | bytes 4194308 | tf_op jit(solution)/shard_map/dot_general | solution.py:207
  202.7 2.6 %collective-permute-done.13 = bf16[512,1024]{1,0:T(8,128)(2,1)S(1)} collective-permute-done((bf16[512,1024]{1,0:T(8,128)(2,1)S(1)}, bf16[512,1024]{1,0:T(8,128)(2,1)S(1)}, u32[]{:S(2)}, u32[]{:S(2)}) %collective-permute-start.13) | collective-permute-done | bytes 1048608 | tf_op jit(solution)/shard_map/ppermute | solution.py:214
  205.3 4.7 %fusion.51 = bf16[1,512,1024]{2,1,0:T(8,128)(2,1)} fusion(bf16[512,1024]{1,0:T(8,128)(2,1)S(1)} %collective-permute-done.13, bf16[512,1024]{0,1:T(8,128)(2,1)} %bitcast.182, bf16[1024,2048]{0,1:T(8,128)(2,1)} %bitcast.164, s32[]{:T(128)S(6)} %select_n.119, bf16[1,512,2048]{2,1,0:T(8,128)(2,1)} %param.7), kind=kOutput, calls=%fused_computation.56 | convolution fusion | flops 1076363264 | bytes 6292480 | tf_op jit(solution)/shard_map/dot_general | solution.py:207
  (121 shorter events, 54.4 us)
Async XLA Ops:
  0.0 68.8 %copy-start = (bf16[1024,1024]{1,0:T(8,128)(2,1)S(1)}, bf16[1024,1024]{1,0:T(8,128)(2,1)}, u32[]{:S(2)}) copy-start(bf16[1024,1024]{1,0:T(8,128)(2,1)} %param.9) | copy-start | bytes 6291460
  0.0 2.3 %copy-start.16 = (f32[2048]{0:T(1024)S(1)}, f32[2048]{0:T(1024)}, u32[]{:S(2)}) copy-start(f32[2048]{0:T(1024)} %param.8) | copy-start | bytes 24580
  2.3 7.5 %copy-start.15 = (f32[1,8,512]{2,1,0:T(8,128)S(1)}, f32[1,8,512]{2,1,0:T(8,128)}, u32[]{:S(2)}) copy-start(f32[1,8,512]{2,1,0:T(8,128)} %param.12) | copy-start | bytes 49156
  4.4 1.3 copy-start.6
  6.1 15.0 %collective-permute-start = (bf16[256,1024]{1,0:T(8,128)(2,1)S(1)}, bf16[256,1024]{1,0:T(8,128)(2,1)S(1)}, u32[]{:S(2)}, u32[]{:S(2)}) collective-permute-start(bf16[256,1024]{1,0:T(8,128)(2,1)S(1)} %dynamic-slice_bitcast_fusion.4), channel_id=1, source_target_pairs={{0,2},{2,0},{1,3},{3,1},{4,6},{6,4},{5,7},{7,5},{8,10},{10,8},{9,1... | collective-permute-start | bytes 1572872 | tf_op jit(solution)/shard_map/ppermute | solution.py:77
  21.0 1.9 collective-permute-start.1
  26.0 5.1 %copy-start.10 = (bf16[2,256,1024]{2,1,0:T(8,128)(2,1)}, bf16[2,256,1024]{2,1,0:T(8,128)(2,1)S(1)}, u32[]{:S(2)}) copy-start(bf16[2,256,1024]{2,1,0:T(8,128)(2,1)S(1)} %broadcast_select_fusion) | copy-start | bytes 3145732
  31.1 25.5 %collective-permute-start.2 = (bf16[2,256,1024]{2,1,0:T(8,128)(2,1)}, bf16[2,256,1024]{2,1,0:T(8,128)(2,1)}, u32[]{:S(2)}, u32[]{:S(2)}) collective-permute-start(bf16[2,256,1024]{2,1,0:T(8,128)(2,1)} %fusion.46), channel_id=1, source_target_pairs={{0,2},{2,0},{1,3},{3,1},{4,6},{6,4},{5,7},{7,5},{8,10},{10,8},{9,1... | collective-permute-start | bytes 3145736 | tf_op jit(solution)/shard_map/ppermute | solution.py:91
  33.4 23.3 %copy-start.17 = (bf16[1024,2,1024]{2,1,0:T(2,128)(2,1)S(1)}, bf16[1024,2,1024]{2,1,0:T(2,128)(2,1)}, u32[]{:S(2)}) copy-start(bf16[1024,2,1024]{2,1,0:T(2,128)(2,1)} %param.10) | copy-start | bytes 12582916
  66.6 24.7 %collective-permute-start.3 = (bf16[2,256,1024]{2,1,0:T(8,128)(2,1)}, bf16[2,256,1024]{2,1,0:T(8,128)(2,1)}, u32[]{:S(2)}, u32[]{:S(2)}) collective-permute-start(bf16[2,256,1024]{2,1,0:T(8,128)(2,1)} %fusion.43), channel_id=1, source_target_pairs={{0,2},{2,0},{1,3},{3,1},{4,6},{6,4},{5,7},{7,5},{8,10},{10,8},{9,1... | collective-permute-start | bytes 3145736 | tf_op jit(solution)/shard_map/ppermute | solution.py:91
  68.8 2.3 %copy-start.3 = (bf16[256,8,128]{2,0,1:T(8,128)(2,1)S(1)}, bf16[256,8,128]{2,0,1:T(8,128)(2,1)}, u32[]{:S(2)}) copy-start(bf16[256,8,128]{2,0,1:T(8,128)(2,1)} %fusion.60) | copy-start | bytes 1572868
  68.8 7.6 %copy-start.5 = (bf16[32,8,8,128]{3,2,1,0:T(8,128)(2,1)S(1)}, bf16[32,8,8,128]{3,2,1,0:T(8,128)(2,1)}, u32[]{:S(2)}) copy-start(bf16[32,8,8,128]{3,2,1,0:T(8,128)(2,1)} %copy.121) | copy-start | bytes 1572868
  72.1 45.2 %collective-permute-start.5 = (bf16[256,1024]{0,1:T(8,128)(2,1)}, bf16[256,1024]{0,1:T(8,128)(2,1)}, u32[]{:S(2)}, u32[]{:S(2)}) collective-permute-start(bf16[256,1024]{0,1:T(8,128)(2,1)} %bitcast.171), channel_id=1, source_target_pairs={{0,4},{4,8},{8,12},{1,5},{5,9},{9,13},{2,6},{6,10},{10,14},{3,7},{... | collective-permute-start | bytes 1572872 | tf_op jit(solution)/shard_map/ppermute | solution.py:14
  77.6 42.6 %collective-permute-start.7 = (bf16[256,1024]{0,1:T(8,128)(2,1)}, bf16[256,1024]{0,1:T(8,128)(2,1)}, u32[]{:S(2)}, u32[]{:S(2)}) collective-permute-start(bf16[256,1024]{0,1:T(8,128)(2,1)} %bitcast.170), channel_id=1, source_target_pairs={{0,4},{4,8},{8,12},{1,5},{5,9},{9,13},{2,6},{6,10},{10,14},{3,7},{... | collective-permute-start | bytes 1572872 | tf_op jit(solution)/shard_map/ppermute | solution.py:14
  98.3 14.0 %copy-start.4 = (bf16[256,8,128]{2,0,1:T(8,128)(2,1)S(1)}, bf16[256,8,128]{2,0,1:T(8,128)(2,1)}, u32[]{:S(2)}) copy-start(bf16[256,8,128]{2,0,1:T(8,128)(2,1)} %fusion.59) | copy-start | bytes 1572868
  101.6 16.3 %collective-permute-start.6 = (bf16[256,1024]{0,1:T(8,128)(2,1)}, bf16[256,1024]{0,1:T(8,128)(2,1)}, u32[]{:S(2)}, u32[]{:S(2)}) collective-permute-start(bf16[256,1024]{0,1:T(8,128)(2,1)} %bitcast.173), channel_id=1, source_target_pairs={{0,4},{4,8},{8,12},{1,5},{5,9},{9,13},{2,6},{6,10},{10,14},{3,7},{... | collective-permute-start | bytes 1572872 | tf_op jit(solution)/shard_map/ppermute | solution.py:14
  108.1 34.8 %collective-permute-start.4 = (bf16[512,1024]{1,0:T(8,128)(2,1)}, bf16[512,1024]{1,0:T(8,128)(2,1)S(1)}, u32[]{:S(2)}, u32[]{:S(2)}) collective-permute-start(bf16[512,1024]{1,0:T(8,128)(2,1)} %convolution_convert_fusion), channel_id=1, source_target_pairs={{0,2},{2,0},{1,3},{3,1},{4,6},{6,4},{5,7},{7,5},{8,10},{10,8},{9,1... | collective-permute-start | bytes 3145736 | tf_op jit(solution)/shard_map/ppermute | solution.py:91
  109.6 17.0 %collective-permute-start.8 = (bf16[256,1024]{0,1:T(8,128)(2,1)}, bf16[256,1024]{0,1:T(8,128)(2,1)S(1)}, u32[]{:S(2)}, u32[]{:S(2)}) collective-permute-start(bf16[256,1024]{0,1:T(8,128)(2,1)} %bitcast.172), channel_id=1, source_target_pairs={{0,4},{4,8},{8,12},{1,5},{5,9},{9,13},{2,6},{6,10},{10,14},{3,7},{... | collective-permute-start | bytes 1572872 | tf_op jit(solution)/shard_map/ppermute | solution.py:14
  120.2 22.7 %copy-start.7 = (bf16[1,512,2048]{2,1,0:T(8,128)(2,1)S(1)}, bf16[1,512,2048]{2,1,0:T(8,128)(2,1)}, u32[]{:S(2)}) copy-start(bf16[1,512,2048]{2,1,0:T(8,128)(2,1)} %copy-done.6) | copy-start | bytes 6291460
  128.9 8.5 %collective-permute-start.9 = (bf16[1,9,128,128]{3,2,1,0:T(8,128)(2,1)S(1)}, bf16[1,9,128,128]{3,2,1,0:T(8,128)(2,1)S(1)}, u32[]{:S(2)}, u32[]{:S(2)}) collective-permute-start(bf16[1,9,128,128]{3,2,1,0:T(8,128)(2,1)S(1)} %fusion.68), channel_id=1, source_target_pairs={{0,4},{4,8},{8,12},{1,5},{5,9},{9,13},{2,6},{6,10},{10,14},{3,7},{... | collective-permute-start | bytes 884744 | tf_op jit(solution)/shard_map/ppermute | solution.py:14
  134.8 45.2 %collective-permute-start.12 = (bf16[1024,1024]{1,0:T(8,128)(2,1)}, bf16[1024,1024]{1,0:T(8,128)(2,1)}, u32[]{:S(2)}, u32[]{:S(2)}) collective-permute-start(bf16[1024,1024]{1,0:T(8,128)(2,1)} %param.11), channel_id=1, source_target_pairs={{0,2},{2,0},{1,3},{3,1},{4,6},{6,4},{5,7},{7,5},{8,10},{10,8},{9,1... | collective-permute-start | bytes 6291464 | tf_op jit(solution)/shard_map/ppermute | solution.py:195
  138.3 17.8 %collective-permute-start.10 = (bf16[1,9,128,128]{3,2,1,0:T(8,128)(2,1)}, bf16[1,9,128,128]{3,2,1,0:T(8,128)(2,1)S(1)}, u32[]{:S(2)}, u32[]{:S(2)}) collective-permute-start(bf16[1,9,128,128]{3,2,1,0:T(8,128)(2,1)} %fusion.70), channel_id=1, source_target_pairs={{0,4},{4,8},{8,12},{1,5},{5,9},{9,13},{2,6},{6,10},{10,14},{3,7},{... | collective-permute-start | bytes 884744 | tf_op jit(solution)/shard_map/ppermute | solution.py:14
  146.6 2.2 %copy-start.8 = (bf16[512,8,128]{2,0,1:T(8,128)(2,1)S(1)}, bf16[512,8,128]{2,0,1:T(8,128)(2,1)}, u32[]{:S(2)}) copy-start(bf16[512,8,128]{2,0,1:T(8,128)(2,1)} %constant_dynamic-update-slice_fusion) | copy-start | bytes 3145732
  146.7 2.1 copy-start.13
  148.8 2.2 %copy-start.11 = (bf16[1,512,1024]{1,2,0:T(8,128)(2,1)S(1)}, bf16[1,512,1024]{1,2,0:T(8,128)(2,1)}, u32[]{:S(2)}) copy-start(bf16[1,512,1024]{1,2,0:T(8,128)(2,1)} %maximum_bitcast_fusion) | copy-start | bytes 3145732
  148.8 2.2 %copy-start.14 = (pred[512,512]{0,1:T(8,128)(4,1)S(1)}, pred[512,512]{0,1:T(8,128)(4,1)}, u32[]{:S(2)}) copy-start(pred[512,512]{0,1:T(8,128)(4,1)} %fusion.63) | copy-start | bytes 786436
  151.0 2.5 %copy-start.12 = (bf16[1,512,1024]{1,2,0:T(8,128)(2,1)S(1)}, bf16[1,512,1024]{1,2,0:T(8,128)(2,1)}, u32[]{:S(2)}) copy-start(bf16[1,512,1024]{1,2,0:T(8,128)(2,1)} %maximum_bitcast_fusion.1) | copy-start | bytes 3145732
  153.6 6.4 %copy-start.9 = (bf16[512,8,128]{2,0,1:T(8,128)(2,1)S(1)}, bf16[512,8,128]{2,0,1:T(8,128)(2,1)}, u32[]{:S(2)}) copy-start(bf16[512,8,128]{2,0,1:T(8,128)(2,1)} %copy_dynamic-update-slice_fusion) | copy-start | bytes 3145732
  156.2 7.7 %collective-permute-start.11 = (bf16[1,9,128,128]{3,2,1,0:T(8,128)(2,1)S(1)}, bf16[1,9,128,128]{3,2,1,0:T(8,128)(2,1)S(1)}, u32[]{:S(2)}, u32[]{:S(2)}) collective-permute-start(bf16[1,9,128,128]{3,2,1,0:T(8,128)(2,1)S(1)} %fusion.72), channel_id=1, source_target_pairs={{0,4},{4,8},{8,12},{1,5},{5,9},{9,13},{2,6},{6,10},{10,14},{3,7},{... | collective-permute-start | bytes 884744 | tf_op jit(solution)/shard_map/ppermute | solution.py:14
  193.4 6.3 %copy-start.18 = (bf16[1,512,8,128]{1,3,2,0:T(8,128)(2,1)S(1)}, bf16[1,512,8,128]{1,3,2,0:T(8,128)(2,1)}, u32[]{:S(2)}) copy-start(bf16[1,512,8,128]{1,3,2,0:T(8,128)(2,1)} %fusion.20) | copy-start | bytes 3145732
  202.6 2.7 %collective-permute-start.13 = (bf16[512,1024]{1,0:T(8,128)(2,1)S(1)}, bf16[512,1024]{1,0:T(8,128)(2,1)S(1)}, u32[]{:S(2)}, u32[]{:S(2)}) collective-permute-start(bf16[512,1024]{1,0:T(8,128)(2,1)S(1)} %fusion.33), channel_id=1, source_target_pairs={{0,1},{1,0},{2,3},{3,2},{4,5},{5,4},{6,7},{7,6},{8,9},{9,8},{10,11... | collective-permute-start | bytes 3145736 | tf_op jit(solution)/shard_map/ppermute | solution.py:214
  205.3 4.7 %copy-start.1 = (bf16[1024,1024]{1,0:T(8,128)(2,1)S(1)}, bf16[1024,1024]{1,0:T(8,128)(2,1)}, u32[]{:S(2)}) copy-start(bf16[1024,1024]{1,0:T(8,128)(2,1)} %param.9) | copy-start | bytes 6291460
  (1 other events, 1.0 us)

commit v12 on v7

--- a/solution.py
+++ b/solution.py
@@ -171,17 +171,32 @@
     )
     attended = (window + read).astype(jnp.bfloat16).reshape(count, inner_here)
     w_output = lax.optimization_barrier((w_output, pair_raw))[0]
-    w_output_rows = lax.all_gather(w_output, "wloop", axis=1, tiled=True)
+    out_block = w_output.shape[1]
+    from_ranks = jnp.stack(
+        [w_output]
+        + [
+            lax.ppermute(w_output, "wloop", [(source, (source + step) % ways) for source in range(ways)])
+            for step in range(1, ways)
+        ]
+    )
     cores = lax.axis_size("heads")
     core = lax.axis_index("heads")
     share = width // cores
 
+    blocks_per_share = share // out_block
+
     def output_share(index):
-        return jnp.dot(
-            attended,
-            lax.dynamic_slice_in_dim(w_output_rows, index * share, share, 1),
-            preferred_element_type=jnp.float32,
-        )
+        parts = []
+        for part in range(blocks_per_share):
+            rank = index * blocks_per_share + part
+            parts.append(
+                jnp.dot(
+                    attended,
+                    lax.dynamic_index_in_dim(from_ranks, (me - rank) % ways, 0, keepdims=False),
+                    preferred_element_type=jnp.float32,
+                )
+            )
+        return jnp.concatenate(parts, axis=1) if blocks_per_share > 1 else parts[0]
 
     received = [
         lax.ppermute(

time: 192 us -> 179 us (0.932)
  between operations: 14.6 us -> 1.28 us
    unnamed x47 -> x51, local copies, waits for them, and re-layouts: 6.09 us -> 7.05 us
  transfers between devices with their start and end apart: 11 -> 11, of which waited for: 5 -> 5; matrix products, arithmetic and copies ran while one was open for 29% -> 31% of each run, Pallas kernels for 0% -> 0%
where the time goes in v12:
time: 179 us; the launch traced here: 178 us
  waiting for transfers between devices  65.6 us (37%)
  matrix products  45.1 us (25%)
  starting transfers between devices  27.5 us (15%)
  local copies, waits for them, and re-layouts  22.3 us (12%)
  other arithmetic  16.7 us (9%)
    ppermute x2, waiting for transfers between devices, gathered_sum(): lax.ppermute(outgoing, 'wloop', [(source, (source - step) % ways) for sou...  38.2 us
    ppermute x5, starting transfers between devices, shifted(): lax.ppermute(value, axis, [(source, source + steps) for source in range(i...  20.6 us
    ppermute x1, waiting for transfers between devices, shards(): lax.ppermute(part, 'wloop', [(source, (source + step) % ways) for source...  11.9 us
    ppermute x5, waiting for transfers between devices, shifted(): lax.ppermute(value, axis, [(source, source + steps) for source in range(i...  11.1 us
    dot_general x2, matrix products, shards(): jnp.einsum('td,dje->jte', rows, w_keyvalue, preferred_element_type=jnp.fl...  10.4 us
    dot_general x2, matrix products, output_share(): jnp.dot(attended, lax.dynamic_index_in_dim(from_ranks, (me - rank) % ways...  7.62 us
    dot_general x2, matrix products, shards(): jnp.dot(rows, w_query, preferred_element_type=jnp.float32)  7.45 us
    unnamed x51, local copies, waits for them, and re-layouts  7.05 us
  transfers between devices with their start and end apart: 11, of which 5 were waited for; matrix products, arithmetic and copies ran while one was open for 31% of the time, Pallas kernels for 0%

profile of v12, /device:TPU:0, one launch (start us, length us, event | category | flops | bytes accessed | tf_op | source)
XLA Modules:
  0.0 178.4 jit_solution(5200790553907135945)
XLA Ops:
  0.0 2.2 %fusion.2 = f32[512]{0:T(512)S(1)} fusion(bf16[1,512,2048]{2,1,0:T(8,128)(2,1)} %param.7), kind=kLoop, calls=%fused_computation.13 | loop fusion | flops 3145216 | bytes 2099200 | tf_op jit(solution)/shard_map/reduce_sum | solution.py:18
  4.6 3.0 %collective-permute-start = (bf16[256,1024]{1,0:T(8,128)(2,1)S(1)}, bf16[256,1024]{1,0:T(8,128)(2,1)S(1)}, u32[]{:S(2)}, u32[]{:S(2)}) collective-permute-start(bf16[256,1024]{1,0:T(8,128)(2,1)S(1)} %dynamic-slice_bitcast_fusion), channel_id=1, source_target_pairs={{0,2},{2,0},{1,3},{3,1},{4,6},{6,4},{5,7},{7,5},{8,10},{10,8},{9,1... | collective-permute-start | bytes 1572872 | tf_op jit(solution)/shard_map/ppermute | solution.py:77
  7.6 11.9 %collective-permute-done = bf16[256,1024]{1,0:T(8,128)(2,1)S(1)} collective-permute-done((bf16[256,1024]{1,0:T(8,128)(2,1)S(1)}, bf16[256,1024]{1,0:T(8,128)(2,1)S(1)}, u32[]{:S(2)}, u32[]{:S(2)}) %collective-permute-start) | collective-permute-done | bytes 524320 | tf_op jit(solution)/shard_map/ppermute | solution.py:77
  19.7 1.8 collective-permute-done.1
  22.5 1.8 %gather_fusion = bf16[2,256,1024]{2,1,0:T(8,128)(2,1)S(1)} fusion(bf16[2,256,1024]{2,1,0:T(8,128)(2,1)} %pad_maximum_fusion, s32[1024]{0:T(1024)S(1)} %pad_clamp_fusion), kind=kCustom, calls=%fused_computation | custom fusion | bytes 2097160 | tf_op jit(solution)/shard_map/jit(_take)/gather | solution.py:70
  24.6 6.4 %convert_bitcast_fusion = bf16[2,512,1024]{2,1,0:T(8,128)(2,1)} fusion(bf16[1024,2,1024]{2,1,0:T(2,128)(2,1)} %param.10, bf16[512,1024]{1,0:T(8,128)(2,1)S(1)} %bitcast_select_fusion), kind=kOutput, calls=%fused_computation.46 | convolution fusion | flops 2148532224 | bytes 7340032 | tf_op jit(solution)/shard_map/td,dje->jte/dot_general | solution.py:100
  30.9 1.7 collective-permute-start.2
  37.1 3.6 %convolution_convert_fusion = bf16[512,1024]{1,0:T(8,128)(2,1)} fusion(bf16[512,1024]{1,0:T(8,128)(2,1)} %copy-done.13, bf16[1024,1024]{1,0:T(8,128)(2,1)S(1)} %copy-done), kind=kOutput, calls=%fused_computation.48 | convolution fusion | flops 1074266112 | bytes 4194304 | tf_op jit(solution)/shard_map/dot_general | solution.py:105
  40.7 38.2 %collective-permute-done.2 = bf16[2,512,1024]{2,1,0:T(8,128)(2,1)} collective-permute-done((bf16[2,512,1024]{2,1,0:T(8,128)(2,1)}, bf16[2,512,1024]{2,1,0:T(8,128)(2,1)}, u32[]{:S(2)}, u32[]{:S(2)}) %collective-permute-start.2) | collective-permute-done | bytes 2097184 | tf_op jit(solution)/shard_map/ppermute | solution.py:91
  78.9 4.1 %bitcast_add_fusion = f32[2,512,1024]{2,1,0:T(8,128)S(1)} fusion(bf16[2,512,1024]{2,1,0:T(8,128)(2,1)} %collective-permute-done.2, bf16[1024,2,1024]{2,1,0:T(2,128)(2,1)S(1)} %copy-done.20, bf16[1,512,2048]{2,1,0:T(8,128)(2,1)S(1)} %copy-done.8, s32[]{:T(128)S(6)} %select_n.91), kind=kOutput, calls=%fused_computation.16 | convolution fusion | flops 2149580800 | bytes 11534340 | tf_op jit(solution)/shard_map/td,dje->jte/dot_general | solution.py:100
  85.3 4.8 %collective-permute-start.5 = (bf16[1,512,1024]{2,1,0:T(8,128)(2,1)}, bf16[1,512,1024]{2,1,0:T(8,128)(2,1)}, u32[]{:S(2)}, u32[]{:S(2)}) collective-permute-start(bf16[1,512,1024]{2,1,0:T(8,128)(2,1)} %slice.63), channel_id=1, source_target_pairs={{0,4},{4,8},{8,12},{1,5},{5,9},{9,13},{2,6},{6,10},{10,14},{3,7},{... | collective-permute-start | bytes 3145736 | tf_op jit(solution)/shard_map/ppermute | solution.py:14
  90.0 1.5 collective-permute-start.3
  91.5 1.8 %copy.89 = f32[64,8,8,128]{3,2,1,0:T(8,128)} copy(f32[64,8,8,128]{3,1,2,0:T(8,128)S(1)} %multiply_bitcast_fusion) | data formatting | bytes 4194304
  93.3 2.2 %reduce_sum.58 = f32[512,8]{1,0:T(8,128)S(1)} reduce(f32[512,8,128]{2,1,0:T(8,128)} %bitcast.133, f32[]{:T(128)} %constant.107.clone.1), dimensions={2}, to_apply=%region_2.3 | reduce | flops 520192 | bytes 2113540 | tf_op jit(solution)/shard_map/reduce_sum | solution.py:18
  95.7 1.6 mul.214
  97.3 2.9 %copy.84 = f32[1,512,1024]{2,1,0:T(8,128)} copy(f32[1,512,1024]{1,2,0:T(8,128)} %bitcast.134) | data formatting | bytes 4194304 | tf_op jit(solution)/shard_map/mul | solution.py:18
  100.2 4.5 %multiply_convert_fusion = (bf16[1,512,1024]{2,1,0:T(8,128)(2,1)}, f32[1,512,1024]{2,1,0:T(8,128)}) fusion(f32[1,512,1024]{2,1,0:T(8,128)} %copy.84, f32[2,512,1024]{2,1,0:T(8,128)} %copy-done.4), kind=kLoop, calls=%fused_computation.38 | loop fusion | flops 1048576 | bytes 7340032 | tf_op jit(solution)/shard_map/convert_element_type | solution.py:108
  104.7 3.5 %collective-permute-start.4 = (bf16[1,512,1024]{2,1,0:T(8,128)(2,1)}, bf16[1,512,1024]{2,1,0:T(8,128)(2,1)}, u32[]{:S(2)}, u32[]{:S(2)}) collective-permute-start(bf16[1,512,1024]{2,1,0:T(8,128)(2,1)} %get-tuple-element.19), channel_id=1, source_target_pairs={{0,4},{4,8},{8,12},{1,5},{5,9},{9,13},{2,6},{6,10},{10,14},{3,7},{... | collective-permute-start | bytes 3145736 | tf_op jit(solution)/shard_map/ppermute | solution.py:14
  110.6 3.3 %copy.83 = f32[1,512,1024]{1,2,0:T(8,128)} copy(f32[1,512,1024]{2,1,0:T(8,128)} %get-tuple-element.20) | data formatting | bytes 4194304 | tf_op jit(solution)/shard_map/reshape;squeeze | solution.py:108
  114.4 2.9 %fusion.40 = f32[1,8,128,128]{3,2,1,0:T(8,128)S(1)} fusion(bf16[512,8,128]{0,2,1:T(8,128)(2,1)S(1)} %bitcast.135, f32[512,8]{0,1:T(8,128)} %fusion.69, f32[512,8,128]{0,2,1:T(8,128)} %bitcast.130, f32[512,8]{0,1:T(8,128)S(1)} %add_rsqrt_fusion), kind=kOutput, calls=%fused_computation.51 | convolution fusion | flops 807403520 | bytes 3702784 | tf_op jit(solution)/shard_map/bht,bthd,bthe->bhde/dot_general | solution.py:125
  117.4 3.8 %multiply_bitcast_fusion.1 = (f32[64,8,8,128]{3,1,2,0:T(8,128)S(1)}, f32[64,8,8,128]{3,2,1,0:T(8,128)}) fusion(bf16[512,1024]{1,0:T(8,128)(2,1)} %collective-permute-done.3, bf16[1024,1024]{1,0:T(8,128)(2,1)S(1)} %copy-done, bf16[1,512,2048]{2,1,0:T(8,128)(2,1)S(1)} %copy-done.9, s32[]{:T(128)S(6)} %select_n.91), kind=kOutput, calls=%fused_computation.44 | convolution fusion | flops 1075314688 | bytes 8388612 | tf_op jit(solution)/shard_map/dot_general | solution.py:105
  122.5 11.1 %collective-permute-done.4 = bf16[1,512,1024]{2,1,0:T(8,128)(2,1)} collective-permute-done((bf16[1,512,1024]{2,1,0:T(8,128)(2,1)}, bf16[1,512,1024]{2,1,0:T(8,128)(2,1)}, u32[]{:S(2)}, u32[]{:S(2)}) %collective-permute-start.4) | collective-permute-done | bytes 1048608 | tf_op jit(solution)/shard_map/ppermute | solution.py:14
  135.3 4.5 %collective-permute-start.6 = (bf16[1,9,128,128]{3,2,1,0:T(8,128)(2,1)S(1)}, bf16[1,9,128,128]{3,2,1,0:T(8,128)(2,1)S(1)}, u32[]{:S(2)}, u32[]{:S(2)}) collective-permute-start(bf16[1,9,128,128]{3,2,1,0:T(8,128)(2,1)S(1)} %fusion.57), channel_id=1, source_target_pairs={{0,4},{4,8},{8,12},{1,5},{5,9},{9,13},{2,6},{6,10},{10,14},{3,7},{... | collective-permute-start | bytes 884744 | tf_op jit(solution)/shard_map/ppermute | solution.py:14
  140.6 2.6 %fusion = (f32[8,512]{1,0:T(8,128)S(1)}, f32[8,512,512]{1,2,0:T(8,128)S(1)}) fusion(pred[512,512]{0,1:T(8,128)(4,1)S(1)} %copy-done.15, bf16[512,8,128]{2,0,1:T(8,128)(2,1)S(1)} %fusion.19, f32[512,8,128]{0,2,1:T(8,128)S(1)} %bitcast.131, f32[512,8]{0,1:T(8,128)S(1)} %add_rsqrt_fusion), kind=kOutput, calls=%fused_computation.5 | convolution fusion | flops 544206848 | bytes 11829248 | tf_op jit(solution)/shard_map/bihd,bjhd->bhij/dot_general | solution.py:23
  143.2 5.3 %fusion.1 = (f32[8,512]{1,0:T(8,128)S(1)}, f32[8,512,512]{1,2,0:T(8,128)}) fusion(pred[512,512]{0,1:T(8,128)(4,1)S(1)} %fusion.50, bf16[512,8,128]{2,0,1:T(8,128)(2,1)S(1)} %fusion.19, bf16[512,8,128]{2,1,0:T(8,128)(2,1)S(1)} %bitcast.141), kind=kOutput, calls=%fused_computation.6 | convolution fusion | flops 543158272 | bytes 10764288 | tf_op jit(solution)/shard_map/bihd,bjhd->bhij/dot_general | solution.py:27
  148.6 3.5 %collective-permute-start.7 = (bf16[1,9,128,128]{3,2,1,0:T(8,128)(2,1)S(1)}, bf16[1,9,128,128]{3,2,1,0:T(8,128)(2,1)S(1)}, u32[]{:S(2)}, u32[]{:S(2)}) collective-permute-start(bf16[1,9,128,128]{3,2,1,0:T(8,128)(2,1)S(1)} %fusion.59), channel_id=1, source_target_pairs={{0,4},{4,8},{8,12},{1,5},{5,9},{9,13},{2,6},{6,10},{10,14},{3,7},{... | collective-permute-start | bytes 884744 | tf_op jit(solution)/shard_map/ppermute | solution.py:14
  152.1 3.3 %fusion.5 = f32[8,128,512]{2,1,0:T(8,128)} fusion(bf16[512,8,128]{0,2,1:T(8,128)(2,1)S(1)} %bitcast.136, f32[8,512,512]{1,2,0:T(8,128)S(1)} %get-tuple-element.24, f32[8,512]{1,0:T(8,128)S(1)} %add.164, pred[512,512]{0,1:T(8,128)(4,1)S(1)} %copy-done.15), kind=kOutput, calls=%fused_computation.17 | convolution fusion | flops 545259520 | bytes 11812864 | tf_op jit(solution)/shard_map/bhij,bjhd->bihd/dot_general | solution.py:38
  157.1 4.3 %collective-permute-start.8 = (bf16[1,9,128,128]{3,2,1,0:T(8,128)(2,1)S(1)}, bf16[1,9,128,128]{3,2,1,0:T(8,128)(2,1)S(1)}, u32[]{:S(2)}, u32[]{:S(2)}) collective-permute-start(bf16[1,9,128,128]{3,2,1,0:T(8,128)(2,1)S(1)} %fusion.61), channel_id=1, source_target_pairs={{0,4},{4,8},{8,12},{1,5},{5,9},{9,13},{2,6},{6,10},{10,14},{3,7},{... | collective-permute-start | bytes 884744 | tf_op jit(solution)/shard_map/ppermute | solution.py:14
  161.5 4.8 %fusion.6 = f32[8,128,512]{2,1,0:T(8,128)S(1)} fusion(bf16[512,8,128]{0,2,1:T(8,128)(2,1)S(1)} %bitcast.140, f32[8,512,512]{1,2,0:T(8,128)} %get-tuple-element.26, f32[8,512]{1,0:T(8,128)S(1)} %add.164, pred[512,512]{0,1:T(8,128)(4,1)} %copy-done.14), kind=kOutput, calls=%fused_computation.18 | convolution fusion | flops 545259520 | bytes 11812864 | tf_op jit(solution)/shard_map/bhij,bjhd->bihd/dot_general | solution.py:40
  168.0 2.9 %fusion.33 = bf16[512,1024]{1,0:T(8,128)(2,1)S(1)} fusion(bf16[512,1024]{0,1:T(8,128)(2,1)S(1)} %bitcast.152, s32[]{:T(128)S(6)} %select_n.108, bf16[1,1024,1024]{2,1,0:T(8,128)(2,1)S(1)} %bitcast.151, bf16[1,1024,1024]{2,1,0:T(8,128)(2,1)} %bitcast.40), kind=kOutput, calls=%fused_computation.47 | convolution fusion | flops 1075314688 | bytes 6291460 | tf_op jit(solution)/shard_map/dot_general | solution.py:193
  171.1 2.6 %collective-permute-done.10 = bf16[512,1024]{1,0:T(8,128)(2,1)S(1)} collective-permute-done((bf16[512,1024]{1,0:T(8,128)(2,1)S(1)}, bf16[512,1024]{1,0:T(8,128)(2,1)S(1)}, u32[]{:S(2)}, u32[]{:S(2)}) %collective-permute-start.10) | collective-permute-done | bytes 1048608 | tf_op jit(solution)/shard_map/ppermute | solution.py:202
  173.7 4.7 %fusion.37 = bf16[1,512,1024]{2,1,0:T(8,128)(2,1)} fusion(bf16[512,1024]{1,0:T(8,128)(2,1)S(1)} %collective-permute-done.10, bf16[512,1024]{0,1:T(8,128)(2,1)} %bitcast.153, s32[]{:T(128)S(6)} %select_n.105, bf16[1,1024,1024]{2,1,0:T(8,128)(2,1)} %bitcast.150, bf16[1,1024,1024]{2,1,0:T(8,128)(2,1)} %bitcast.40, bf16[1,512,2048]{2,1,0:T(8,128)(2,1)} %param.7, ...), kind=kOutput, calls=%fused_computation.50 | convolution fusion | flops 1077411840 | bytes 8388616 | tf_op jit(solution)/shard_map/dot_general | solution.py:193
  (102 shorter events, 19.8 us)
Async XLA Ops:
  0.0 37.1 %copy-start = (bf16[1024,1024]{1,0:T(8,128)(2,1)S(1)}, bf16[1024,1024]{1,0:T(8,128)(2,1)}, u32[]{:S(2)}) copy-start(bf16[1024,1024]{1,0:T(8,128)(2,1)} %param.9) | copy-start | bytes 6291460
  0.0 2.4 %copy-start.3 = (bf16[1,512,2048]{2,1,0:T(8,128)(2,1)S(1)}, bf16[1,512,2048]{2,1,0:T(8,128)(2,1)}, u32[]{:S(2)}) copy-start(bf16[1,512,2048]{2,1,0:T(8,128)(2,1)} %param.7) | copy-start | bytes 6291460
  4.6 15.0 %collective-permute-start = (bf16[256,1024]{1,0:T(8,128)(2,1)S(1)}, bf16[256,1024]{1,0:T(8,128)(2,1)S(1)}, u32[]{:S(2)}, u32[]{:S(2)}) collective-permute-start(bf16[256,1024]{1,0:T(8,128)(2,1)S(1)} %dynamic-slice_bitcast_fusion), channel_id=1, source_target_pairs={{0,2},{2,0},{1,3},{3,1},{4,6},{6,4},{5,7},{7,5},{8,10},{10,8},{9,1... | collective-permute-start | bytes 1572872 | tf_op jit(solution)/shard_map/ppermute | solution.py:77
  19.5 1.9 %collective-permute-start.1 = (bf16[256,1024]{1,0:T(8,128)(2,1)S(1)}, bf16[256,1024]{1,0:T(8,128)(2,1)S(1)}, u32[]{:S(2)}, u32[]{:S(2)}) collective-permute-start(bf16[256,1024]{1,0:T(8,128)(2,1)S(1)} %collective-permute-done), channel_id=1, source_target_pairs={{0,1},{1,0},{2,3},{3,2},{4,5},{5,4},{6,7},{7,6},{8,9},{9,8},{10,11... | collective-permute-start | bytes 1572872 | tf_op jit(solution)/shard_map/ppermute | solution.py:67
  24.5 6.4 %copy-start.13 = (bf16[512,1024]{1,0:T(8,128)(2,1)}, bf16[512,1024]{1,0:T(8,128)(2,1)S(1)}, u32[]{:S(2)}) copy-start(bf16[512,1024]{1,0:T(8,128)(2,1)S(1)} %bitcast_select_fusion) | copy-start | bytes 3145732
  24.6 8.8 %copy-start.17 = (f32[1,8,512]{2,1,0:T(8,128)S(1)}, f32[1,8,512]{2,1,0:T(8,128)}, u32[]{:S(2)}) copy-start(f32[1,8,512]{2,1,0:T(8,128)} %param.12) | copy-start | bytes 49156
  30.9 48.0 %collective-permute-start.2 = (bf16[2,512,1024]{2,1,0:T(8,128)(2,1)}, bf16[2,512,1024]{2,1,0:T(8,128)(2,1)}, u32[]{:S(2)}, u32[]{:S(2)}) collective-permute-start(bf16[2,512,1024]{2,1,0:T(8,128)(2,1)} %convert_bitcast_fusion), channel_id=1, source_target_pairs={{0,2},{2,0},{1,3},{3,1},{4,6},{6,4},{5,7},{7,5},{8,10},{10,8},{9,1... | collective-permute-start | bytes 6291464 | tf_op jit(solution)/shard_map/ppermute | solution.py:91
  36.4 106.8 %copy-start.14 = (pred[512,512]{0,1:T(8,128)(4,1)}, pred[512,512]{0,1:T(8,128)(4,1)S(1)}, u32[]{:S(2)}) copy-start(pred[512,512]{0,1:T(8,128)(4,1)S(1)} %fusion.50) | copy-start | bytes 786436
  37.1 41.8 %copy-start.8 = (bf16[1,512,2048]{2,1,0:T(8,128)(2,1)S(1)}, bf16[1,512,2048]{2,1,0:T(8,128)(2,1)}, u32[]{:S(2)}) copy-start(bf16[1,512,2048]{2,1,0:T(8,128)(2,1)} %copy-done.7) | copy-start | bytes 6291460
  37.1 41.8 %copy-start.20 = (bf16[1024,2,1024]{2,1,0:T(2,128)(2,1)S(1)}, bf16[1024,2,1024]{2,1,0:T(2,128)(2,1)}, u32[]{:S(2)}) copy-start(bf16[1024,2,1024]{2,1,0:T(2,128)(2,1)} %param.10) | copy-start | bytes 12582916
  83.0 2.3 %copy-start.4 = (f32[2,512,1024]{2,1,0:T(8,128)}, f32[2,512,1024]{2,1,0:T(8,128)S(1)}, u32[]{:S(2)}) copy-start(f32[2,512,1024]{2,1,0:T(8,128)S(1)} %bitcast_add_fusion) | copy-start | bytes 12582916
  85.3 37.2 %collective-permute-start.5 = (bf16[1,512,1024]{2,1,0:T(8,128)(2,1)}, bf16[1,512,1024]{2,1,0:T(8,128)(2,1)}, u32[]{:S(2)}, u32[]{:S(2)}) collective-permute-start(bf16[1,512,1024]{2,1,0:T(8,128)(2,1)} %slice.63), channel_id=1, source_target_pairs={{0,4},{4,8},{8,12},{1,5},{5,9},{9,13},{2,6},{6,10},{10,14},{3,7},{... | collective-permute-start | bytes 3145736 | tf_op jit(solution)/shard_map/ppermute | solution.py:14
  90.0 27.4 %collective-permute-start.3 = (bf16[512,1024]{1,0:T(8,128)(2,1)}, bf16[512,1024]{1,0:T(8,128)(2,1)}, u32[]{:S(2)}, u32[]{:S(2)}) collective-permute-start(bf16[512,1024]{1,0:T(8,128)(2,1)} %convolution_convert_fusion), channel_id=1, source_target_pairs={{0,2},{2,0},{1,3},{3,1},{4,6},{6,4},{5,7},{7,5},{8,10},{10,8},{9,1... | collective-permute-start | bytes 3145736 | tf_op jit(solution)/shard_map/ppermute | solution.py:91
  104.7 28.9 %collective-permute-start.4 = (bf16[1,512,1024]{2,1,0:T(8,128)(2,1)}, bf16[1,512,1024]{2,1,0:T(8,128)(2,1)}, u32[]{:S(2)}, u32[]{:S(2)}) collective-permute-start(bf16[1,512,1024]{2,1,0:T(8,128)(2,1)} %get-tuple-element.19), channel_id=1, source_target_pairs={{0,4},{4,8},{8,12},{1,5},{5,9},{9,13},{2,6},{6,10},{10,14},{3,7},{... | collective-permute-start | bytes 3145736 | tf_op jit(solution)/shard_map/ppermute | solution.py:14
  110.6 3.9 %copy-start.5 = (bf16[1,512,1024]{1,2,0:T(8,128)(2,1)}, bf16[1,512,1024]{1,2,0:T(8,128)(2,1)S(1)}, u32[]{:S(2)}) copy-start(bf16[1,512,1024]{1,2,0:T(8,128)(2,1)S(1)} %copy.86) | copy-start | bytes 3145732
  113.9 53.2 %collective-permute-start.9 = (bf16[1024,1024]{1,0:T(8,128)(2,1)}, bf16[1024,1024]{1,0:T(8,128)(2,1)}, u32[]{:S(2)}, u32[]{:S(2)}) collective-permute-start(bf16[1024,1024]{1,0:T(8,128)(2,1)} %param.11), channel_id=1, source_target_pairs={{0,2},{2,0},{1,3},{3,1},{4,6},{6,4},{5,7},{7,5},{8,10},{10,8},{9,1... | collective-permute-start | bytes 6291464 | tf_op jit(solution)/shard_map/ppermute | solution.py:178
  114.4 3.0 %copy-start.9 = (bf16[1,512,2048]{2,1,0:T(8,128)(2,1)S(1)}, bf16[1,512,2048]{2,1,0:T(8,128)(2,1)}, u32[]{:S(2)}) copy-start(bf16[1,512,2048]{2,1,0:T(8,128)(2,1)} %copy-done.7) | copy-start | bytes 6291460
  121.8 13.4 %copy-start.19 = (f32[9]{0:T(128)S(1)}, f32[9]{0:T(128)}, u32[]{:S(2)}) copy-start(f32[9]{0:T(128)} %pad.11.clone) | copy-start | bytes 112
  122.5 17.4 %copy-start.10 = (f32[64,8,8,128]{3,2,1,0:T(8,128)S(1)}, f32[64,8,8,128]{3,2,1,0:T(8,128)}, u32[]{:S(2)}) copy-start(f32[64,8,8,128]{3,2,1,0:T(8,128)} %get-tuple-element.22) | copy-start | bytes 6291460
  135.1 5.4 %copy-start.2 = (f32[1,512,1024]{1,2,0:T(8,128)S(1)}, f32[1,512,1024]{1,2,0:T(8,128)}, u32[]{:S(2)}) copy-start(f32[1,512,1024]{1,2,0:T(8,128)} %copy.83) | copy-start | bytes 6291460
  135.1 5.4 %copy-start.15 = (pred[512,512]{0,1:T(8,128)(4,1)S(1)}, pred[512,512]{0,1:T(8,128)(4,1)}, u32[]{:S(2)}) copy-start(pred[512,512]{0,1:T(8,128)(4,1)} %iota_compare_fusion.1) | copy-start | bytes 786436
  135.3 13.2 %collective-permute-start.6 = (bf16[1,9,128,128]{3,2,1,0:T(8,128)(2,1)S(1)}, bf16[1,9,128,128]{3,2,1,0:T(8,128)(2,1)S(1)}, u32[]{:S(2)}, u32[]{:S(2)}) collective-permute-start(bf16[1,9,128,128]{3,2,1,0:T(8,128)(2,1)S(1)} %fusion.57), channel_id=1, source_target_pairs={{0,4},{4,8},{8,12},{1,5},{5,9},{9,13},{2,6},{6,10},{10,14},{3,7},{... | collective-permute-start | bytes 884744 | tf_op jit(solution)/shard_map/ppermute | solution.py:14
  140.6 2.6 %copy-start.11 = (bf16[512,8,128]{2,0,1:T(8,128)(2,1)}, bf16[512,8,128]{2,0,1:T(8,128)(2,1)S(1)}, u32[]{:S(2)}) copy-start(bf16[512,8,128]{2,0,1:T(8,128)(2,1)S(1)} %fusion.19) | copy-start | bytes 3145732
  143.2 8.9 %copy-start.6 = (bf16[1,512,1024]{1,2,0:T(8,128)(2,1)S(1)}, bf16[1,512,1024]{1,2,0:T(8,128)(2,1)}, u32[]{:S(2)}) copy-start(bf16[1,512,1024]{1,2,0:T(8,128)(2,1)} %copy-done.5) | copy-start | bytes 3145732
  148.6 8.3 %collective-permute-start.7 = (bf16[1,9,128,128]{3,2,1,0:T(8,128)(2,1)S(1)}, bf16[1,9,128,128]{3,2,1,0:T(8,128)(2,1)S(1)}, u32[]{:S(2)}, u32[]{:S(2)}) collective-permute-start(bf16[1,9,128,128]{3,2,1,0:T(8,128)(2,1)S(1)} %fusion.59), channel_id=1, source_target_pairs={{0,4},{4,8},{8,12},{1,5},{5,9},{9,13},{2,6},{6,10},{10,14},{3,7},{... | collective-permute-start | bytes 884744 | tf_op jit(solution)/shard_map/ppermute | solution.py:14
  157.1 9.2 %collective-permute-start.8 = (bf16[1,9,128,128]{3,2,1,0:T(8,128)(2,1)S(1)}, bf16[1,9,128,128]{3,2,1,0:T(8,128)(2,1)S(1)}, u32[]{:S(2)}, u32[]{:S(2)}) collective-permute-start(bf16[1,9,128,128]{3,2,1,0:T(8,128)(2,1)S(1)} %fusion.61), channel_id=1, source_target_pairs={{0,4},{4,8},{8,12},{1,5},{5,9},{9,13},{2,6},{6,10},{10,14},{3,7},{... | collective-permute-start | bytes 884744 | tf_op jit(solution)/shard_map/ppermute | solution.py:14
  161.5 5.0 %copy-start.12 = (bf16[512,8,128]{2,0,1:T(8,128)(2,1)S(1)}, bf16[512,8,128]{2,0,1:T(8,128)(2,1)}, u32[]{:S(2)}) copy-start(bf16[512,8,128]{2,0,1:T(8,128)(2,1)} %copy-done.11) | copy-start | bytes 3145732
  161.5 5.0 %copy-start.16 = (f32[512,8]{0,1:T(8,128)S(1)}, f32[512,8]{0,1:T(8,128)}, u32[]{:S(2)}) copy-start(f32[512,8]{0,1:T(8,128)} %get-tuple-element.17) | copy-start | bytes 49156
  161.5 5.0 %copy-start.23 = (f32[8,128,512]{2,1,0:T(8,128)S(1)}, f32[8,128,512]{2,1,0:T(8,128)}, u32[]{:S(2)}) copy-start(f32[8,128,512]{2,1,0:T(8,128)} %fusion.5) | copy-start | bytes 6291460
  167.1 3.9 %copy-start.22 = (bf16[1,512,8,128]{1,3,2,0:T(8,128)(2,1)}, bf16[1,512,8,128]{1,3,2,0:T(8,128)(2,1)S(1)}, u32[]{:S(2)}) copy-start(bf16[1,512,8,128]{1,3,2,0:T(8,128)(2,1)S(1)} %fusion.22) | copy-start | bytes 3145732
  171.0 2.7 %collective-permute-start.10 = (bf16[512,1024]{1,0:T(8,128)(2,1)S(1)}, bf16[512,1024]{1,0:T(8,128)(2,1)S(1)}, u32[]{:S(2)}, u32[]{:S(2)}) collective-permute-start(bf16[512,1024]{1,0:T(8,128)(2,1)S(1)} %fusion.33), channel_id=1, source_target_pairs={{0,1},{1,0},{2,3},{3,2},{4,5},{5,4},{6,7},{7,6},{8,9},{9,8},{10,11... | collective-permute-start | bytes 3145736 | tf_op jit(solution)/shard_map/ppermute | solution.py:202
  173.7 4.7 %copy-start.1 = (bf16[1024,1024]{1,0:T(8,128)(2,1)S(1)}, bf16[1024,1024]{1,0:T(8,128)(2,1)}, u32[]{:S(2)}) copy-start(bf16[1024,1024]{1,0:T(8,128)(2,1)} %param.9) | copy-start | bytes 6291460
  (3 other events, 5.2 us)

commit v13 on v12

--- a/solution.py
+++ b/solution.py
@@ -206,7 +206,7 @@
         )
         for step in range(1, cores)
     ]
-    summed = output_share(core)
+    summed = lax.optimization_barrier(output_share(core))
     for piece in received:
         summed = summed + piece.astype(jnp.float32)
     residual = lax.dynamic_slice_in_dim(

time: 179 us -> 177 us (0.989)
  waiting for transfers between devices: 65.6 us -> 63 us
    ppermute x1, waiting for transfers between devices: 2.62 us -> 0.01 us  [shards(): lax.ppermute(output_share((core + step) % cores).astype(jnp.bfloat16), 'h...]
    unnamed x51 -> x53, local copies, waits for them, and re-layouts: 7.05 us -> 7.06 us
  transfers between devices with their start and end apart: 11 -> 11, of which waited for: 5 -> 4; matrix products, arithmetic and copies ran while one was open for 31% -> 33% of each run, Pallas kernels for 0% -> 0%
where the time goes in v13:
time: 177 us
  waiting for transfers between devices  63 us (36%)
  matrix products  44.7 us (25%)
  starting transfers between devices  27.4 us (15%)
  local copies, waits for them, and re-layouts  22.3 us (13%)
  other arithmetic  18.2 us (10%)
    ppermute x2, waiting for transfers between devices, gathered_sum(): lax.ppermute(outgoing, 'wloop', [(source, (source - step) % ways) for sou...  38.2 us
    ppermute x5, starting transfers between devices, shifted(): lax.ppermute(value, axis, [(source, source + steps) for source in range(i...  20.6 us
    ppermute x1, waiting for transfers between devices, shards(): lax.ppermute(part, 'wloop', [(source, (source + step) % ways) for source...  11.9 us
    ppermute x5, waiting for transfers between devices, shifted(): lax.ppermute(value, axis, [(source, source + steps) for source in range(i...  11.1 us
    dot_general x2, matrix products, shards(): jnp.einsum('td,dje->jte', rows, w_keyvalue, preferred_element_type=jnp.fl...  10.4 us
    dot_general x2, matrix products, shards(): jnp.dot(rows, w_query, preferred_element_type=jnp.float32)  7.44 us
    dot_general x2, matrix products, output_share(): jnp.dot(attended, lax.dynamic_index_in_dim(from_ranks, (me - rank) % ways...  7.28 us
    unnamed x53, local copies, waits for them, and re-layouts  7.06 us
  transfers between devices with their start and end apart: 11, of which 4 were waited for; matrix products, arithmetic and copies ran while one was open for 33% of the time, Pallas kernels for 0%

profile of v13, /device:TPU:0, one launch (start us, length us, event | category | flops | bytes accessed | tf_op | source)
XLA Modules:
  0.0 176.9 jit_solution(15209396842369804102)
XLA Ops:
  0.0 2.2 %fusion.2 = f32[512]{0:T(512)S(1)} fusion(bf16[1,512,2048]{2,1,0:T(8,128)(2,1)} %param.7), kind=kLoop, calls=%fused_computation.13 | loop fusion | flops 3145216 | bytes 2099200 | tf_op jit(solution)/shard_map/reduce_sum | solution.py:18
  4.5 3.0 %collective-permute-start = (bf16[256,1024]{1,0:T(8,128)(2,1)S(1)}, bf16[256,1024]{1,0:T(8,128)(2,1)S(1)}, u32[]{:S(2)}, u32[]{:S(2)}) collective-permute-start(bf16[256,1024]{1,0:T(8,128)(2,1)S(1)} %dynamic-slice_bitcast_fusion), channel_id=1, source_target_pairs={{0,2},{2,0},{1,3},{3,1},{4,6},{6,4},{5,7},{7,5},{8,10},{10,8},{9,1... | collective-permute-start | bytes 1572872 | tf_op jit(solution)/shard_map/ppermute | solution.py:77
  7.6 11.9 %collective-permute-done = bf16[256,1024]{1,0:T(8,128)(2,1)S(1)} collective-permute-done((bf16[256,1024]{1,0:T(8,128)(2,1)S(1)}, bf16[256,1024]{1,0:T(8,128)(2,1)S(1)}, u32[]{:S(2)}, u32[]{:S(2)}) %collective-permute-start) | collective-permute-done | bytes 524320 | tf_op jit(solution)/shard_map/ppermute | solution.py:77
  19.6 1.8 %collective-permute-done.1 = bf16[256,1024]{1,0:T(8,128)(2,1)S(1)} collective-permute-done((bf16[256,1024]{1,0:T(8,128)(2,1)S(1)}, bf16[256,1024]{1,0:T(8,128)(2,1)S(1)}, u32[]{:S(2)}, u32[]{:S(2)}) %collective-permute-start.1) | collective-permute-done | bytes 524320 | tf_op jit(solution)/shard_map/ppermute | solution.py:67
  22.5 1.8 %gather_fusion = bf16[2,256,1024]{2,1,0:T(8,128)(2,1)S(1)} fusion(bf16[2,256,1024]{2,1,0:T(8,128)(2,1)} %pad_maximum_fusion, s32[1024]{0:T(1024)S(1)} %pad_clamp_fusion), kind=kCustom, calls=%fused_computation | custom fusion | bytes 2097160 | tf_op jit(solution)/shard_map/jit(_take)/gather | solution.py:70
  24.6 6.3 %convert_bitcast_fusion = bf16[2,512,1024]{2,1,0:T(8,128)(2,1)} fusion(bf16[1024,2,1024]{2,1,0:T(2,128)(2,1)} %param.10, bf16[512,1024]{1,0:T(8,128)(2,1)S(1)} %bitcast_select_fusion), kind=kOutput, calls=%fused_computation.46 | convolution fusion | flops 2148532224 | bytes 7340032 | tf_op jit(solution)/shard_map/td,dje->jte/dot_general | solution.py:100
  30.9 1.7 collective-permute-start.2
  37.1 3.6 %convolution_convert_fusion = bf16[512,1024]{1,0:T(8,128)(2,1)} fusion(bf16[512,1024]{1,0:T(8,128)(2,1)} %copy-done.14, bf16[1024,1024]{1,0:T(8,128)(2,1)S(1)} %copy-done), kind=kOutput, calls=%fused_computation.48 | convolution fusion | flops 1074266112 | bytes 4194304 | tf_op jit(solution)/shard_map/dot_general | solution.py:105
  40.7 38.2 %collective-permute-done.2 = bf16[2,512,1024]{2,1,0:T(8,128)(2,1)} collective-permute-done((bf16[2,512,1024]{2,1,0:T(8,128)(2,1)}, bf16[2,512,1024]{2,1,0:T(8,128)(2,1)}, u32[]{:S(2)}, u32[]{:S(2)}) %collective-permute-start.2) | collective-permute-done | bytes 2097184 | tf_op jit(solution)/shard_map/ppermute | solution.py:91
  78.9 4.1 %bitcast_add_fusion = f32[2,512,1024]{2,1,0:T(8,128)S(1)} fusion(bf16[2,512,1024]{2,1,0:T(8,128)(2,1)} %collective-permute-done.2, bf16[1024,2,1024]{2,1,0:T(2,128)(2,1)S(1)} %copy-done.21, bf16[1,512,2048]{2,1,0:T(8,128)(2,1)S(1)} %copy-done.9, s32[]{:T(128)S(6)} %select_n.91), kind=kOutput, calls=%fused_computation.16 | convolution fusion | flops 2149580800 | bytes 11534340 | tf_op jit(solution)/shard_map/td,dje->jte/dot_general | solution.py:100
  85.3 4.8 %collective-permute-start.5 = (bf16[1,512,1024]{2,1,0:T(8,128)(2,1)}, bf16[1,512,1024]{2,1,0:T(8,128)(2,1)}, u32[]{:S(2)}, u32[]{:S(2)}) collective-permute-start(bf16[1,512,1024]{2,1,0:T(8,128)(2,1)} %slice.63), channel_id=1, source_target_pairs={{0,4},{4,8},{8,12},{1,5},{5,9},{9,13},{2,6},{6,10},{10,14},{3,7},{... | collective-permute-start | bytes 3145736 | tf_op jit(solution)/shard_map/ppermute | solution.py:14
  91.5 1.8 %copy.89 = f32[64,8,8,128]{3,2,1,0:T(8,128)} copy(f32[64,8,8,128]{3,1,2,0:T(8,128)S(1)} %multiply_bitcast_fusion) | data formatting | bytes 4194304
  93.3 2.2 %reduce_sum.58 = f32[512,8]{1,0:T(8,128)S(1)} reduce(f32[512,8,128]{2,1,0:T(8,128)} %bitcast.129, f32[]{:T(128)} %constant.107.clone.1), dimensions={2}, to_apply=%region_2.3 | reduce | flops 520192 | bytes 2113540 | tf_op jit(solution)/shard_map/reduce_sum | solution.py:18
  95.7 1.6 mul.214
  97.3 2.9 %copy.84 = f32[1,512,1024]{2,1,0:T(8,128)} copy(f32[1,512,1024]{1,2,0:T(8,128)} %bitcast.130) | data formatting | bytes 4194304 | tf_op jit(solution)/shard_map/mul | solution.py:18
  100.2 4.5 %multiply_convert_fusion = (bf16[1,512,1024]{2,1,0:T(8,128)(2,1)}, f32[1,512,1024]{2,1,0:T(8,128)}) fusion(f32[1,512,1024]{2,1,0:T(8,128)} %copy.84, f32[2,512,1024]{2,1,0:T(8,128)} %copy-done.5), kind=kLoop, calls=%fused_computation.38 | loop fusion | flops 1048576 | bytes 7340032 | tf_op jit(solution)/shard_map/convert_element_type | solution.py:108
  104.7 3.5 %collective-permute-start.4 = (bf16[1,512,1024]{2,1,0:T(8,128)(2,1)}, bf16[1,512,1024]{2,1,0:T(8,128)(2,1)}, u32[]{:S(2)}, u32[]{:S(2)}) collective-permute-start(bf16[1,512,1024]{2,1,0:T(8,128)(2,1)} %get-tuple-element.19), channel_id=1, source_target_pairs={{0,4},{4,8},{8,12},{1,5},{5,9},{9,13},{2,6},{6,10},{10,14},{3,7},{... | collective-permute-start | bytes 3145736 | tf_op jit(solution)/shard_map/ppermute | solution.py:14
  109.1 1.5 copy.86
  110.6 3.3 %copy.83 = f32[1,512,1024]{1,2,0:T(8,128)} copy(f32[1,512,1024]{2,1,0:T(8,128)} %get-tuple-element.20) | data formatting | bytes 4194304 | tf_op jit(solution)/shard_map/reshape;squeeze | solution.py:108
  114.4 2.9 %fusion.35 = f32[1,8,128,128]{3,2,1,0:T(8,128)S(1)} fusion(bf16[512,8,128]{0,2,1:T(8,128)(2,1)S(1)} %bitcast.131, f32[512,8]{0,1:T(8,128)} %fusion.65, f32[512,8,128]{0,2,1:T(8,128)} %bitcast.126, f32[512,8]{0,1:T(8,128)S(1)} %add_rsqrt_fusion), kind=kOutput, calls=%fused_computation.50 | convolution fusion | flops 807403520 | bytes 3702784 | tf_op jit(solution)/shard_map/bht,bthd,bthe->bhde/dot_general | solution.py:125
  117.4 3.8 %multiply_bitcast_fusion.1 = (f32[64,8,8,128]{3,1,2,0:T(8,128)S(1)}, f32[64,8,8,128]{3,2,1,0:T(8,128)}) fusion(bf16[512,1024]{1,0:T(8,128)(2,1)} %collective-permute-done.3, bf16[1024,1024]{1,0:T(8,128)(2,1)S(1)} %copy-done, bf16[1,512,2048]{2,1,0:T(8,128)(2,1)S(1)} %copy-done.10, s32[]{:T(128)S(6)} %select_n.91), kind=kOutput, calls=%fused_computation.44 | convolution fusion | flops 1075314688 | bytes 8388612 | tf_op jit(solution)/shard_map/dot_general | solution.py:105
  122.5 11.1 %collective-permute-done.4 = bf16[1,512,1024]{2,1,0:T(8,128)(2,1)} collective-permute-done((bf16[1,512,1024]{2,1,0:T(8,128)(2,1)}, bf16[1,512,1024]{2,1,0:T(8,128)(2,1)}, u32[]{:S(2)}, u32[]{:S(2)}) %collective-permute-start.4) | collective-permute-done | bytes 1048608 | tf_op jit(solution)/shard_map/ppermute | solution.py:14
  135.3 4.5 %collective-permute-start.6 = (bf16[1,9,128,128]{3,2,1,0:T(8,128)(2,1)S(1)}, bf16[1,9,128,128]{3,2,1,0:T(8,128)(2,1)S(1)}, u32[]{:S(2)}, u32[]{:S(2)}) collective-permute-start(bf16[1,9,128,128]{3,2,1,0:T(8,128)(2,1)S(1)} %fusion.53), channel_id=1, source_target_pairs={{0,4},{4,8},{8,12},{1,5},{5,9},{9,13},{2,6},{6,10},{10,14},{3,7},{... | collective-permute-start | bytes 884744 | tf_op jit(solution)/shard_map/ppermute | solution.py:14
  140.6 2.6 %fusion = (f32[8,512]{1,0:T(8,128)S(1)}, f32[8,512,512]{1,2,0:T(8,128)S(1)}) fusion(pred[512,512]{0,1:T(8,128)(4,1)S(1)} %copy-done.16, bf16[512,8,128]{2,0,1:T(8,128)(2,1)S(1)} %fusion.19, f32[512,8,128]{0,2,1:T(8,128)S(1)} %bitcast.127, f32[512,8]{0,1:T(8,128)S(1)} %add_rsqrt_fusion), kind=kOutput, calls=%fused_computation.5 | convolution fusion | flops 544206848 | bytes 11829248 | tf_op jit(solution)/shard_map/bihd,bjhd->bhij/dot_general | solution.py:23
  143.2 5.3 %fusion.1 = (f32[8,512]{1,0:T(8,128)S(1)}, f32[8,512,512]{1,2,0:T(8,128)}) fusion(pred[512,512]{0,1:T(8,128)(4,1)S(1)} %fusion.46, bf16[512,8,128]{2,0,1:T(8,128)(2,1)S(1)} %fusion.19, bf16[512,8,128]{2,1,0:T(8,128)(2,1)S(1)} %bitcast.137), kind=kOutput, calls=%fused_computation.6 | convolution fusion | flops 543158272 | bytes 10764288 | tf_op jit(solution)/shard_map/bihd,bjhd->bhij/dot_general | solution.py:27
  148.6 3.5 %collective-permute-start.7 = (bf16[1,9,128,128]{3,2,1,0:T(8,128)(2,1)S(1)}, bf16[1,9,128,128]{3,2,1,0:T(8,128)(2,1)S(1)}, u32[]{:S(2)}, u32[]{:S(2)}) collective-permute-start(bf16[1,9,128,128]{3,2,1,0:T(8,128)(2,1)S(1)} %fusion.55), channel_id=1, source_target_pairs={{0,4},{4,8},{8,12},{1,5},{5,9},{9,13},{2,6},{6,10},{10,14},{3,7},{... | collective-permute-start | bytes 884744 | tf_op jit(solution)/shard_map/ppermute | solution.py:14
  152.1 3.3 %fusion.5 = f32[8,128,512]{2,1,0:T(8,128)} fusion(bf16[512,8,128]{0,2,1:T(8,128)(2,1)S(1)} %bitcast.132, f32[8,512,512]{1,2,0:T(8,128)S(1)} %get-tuple-element.24, f32[8,512]{1,0:T(8,128)S(1)} %add.164, pred[512,512]{0,1:T(8,128)(4,1)S(1)} %copy-done.16), kind=kOutput, calls=%fused_computation.17 | convolution fusion | flops 545259520 | bytes 11812864 | tf_op jit(solution)/shard_map/bhij,bjhd->bihd/dot_general | solution.py:38
  157.1 4.3 %collective-permute-start.8 = (bf16[1,9,128,128]{3,2,1,0:T(8,128)(2,1)S(1)}, bf16[1,9,128,128]{3,2,1,0:T(8,128)(2,1)S(1)}, u32[]{:S(2)}, u32[]{:S(2)}) collective-permute-start(bf16[1,9,128,128]{3,2,1,0:T(8,128)(2,1)S(1)} %fusion.57), channel_id=1, source_target_pairs={{0,4},{4,8},{8,12},{1,5},{5,9},{9,13},{2,6},{6,10},{10,14},{3,7},{... | collective-permute-start | bytes 884744 | tf_op jit(solution)/shard_map/ppermute | solution.py:14
  161.5 4.8 %fusion.6 = f32[8,128,512]{2,1,0:T(8,128)S(1)} fusion(bf16[512,8,128]{0,2,1:T(8,128)(2,1)S(1)} %bitcast.136, f32[8,512,512]{1,2,0:T(8,128)} %get-tuple-element.26, f32[8,512]{1,0:T(8,128)S(1)} %add.164, pred[512,512]{0,1:T(8,128)(4,1)} %copy-done.15), kind=kOutput, calls=%fused_computation.18 | convolution fusion | flops 545259520 | bytes 11812864 | tf_op jit(solution)/shard_map/bhij,bjhd->bihd/dot_general | solution.py:40
  168.0 3.9 %fusion.31 = bf16[512,1024]{1,0:T(8,128)(2,1)} fusion(bf16[512,1024]{0,1:T(8,128)(2,1)S(1)} %bitcast.148, s32[]{:T(128)S(6)} %select_n.108, bf16[1,1024,1024]{2,1,0:T(8,128)(2,1)S(1)} %bitcast.147, bf16[1,1024,1024]{2,1,0:T(8,128)(2,1)} %bitcast.40), kind=kOutput, calls=%fused_computation.47 | convolution fusion | flops 1075314688 | bytes 6291460 | tf_op jit(solution)/shard_map/dot_general | solution.py:193
  171.9 3.4 %fusion.17 = f32[512,1024]{1,0:T(8,128)S(1)} fusion(bf16[512,1024]{0,1:T(8,128)(2,1)} %bitcast.149, s32[]{:T(128)S(6)} %select_n.105, bf16[1,1024,1024]{2,1,0:T(8,128)(2,1)} %bitcast.146, bf16[1,1024,1024]{2,1,0:T(8,128)(2,1)} %bitcast.40), kind=kOutput, calls=%fused_computation.28 | convolution fusion | flops 1074790400 | bytes 7340036 | tf_op jit(solution)/shard_map/dot_general | solution.py:193
  175.3 1.5 fusion.38
  (105 shorter events, 19.8 us)
Async XLA Ops:
  0.0 37.1 %copy-start = (bf16[1024,1024]{1,0:T(8,128)(2,1)S(1)}, bf16[1024,1024]{1,0:T(8,128)(2,1)}, u32[]{:S(2)}) copy-start(bf16[1024,1024]{1,0:T(8,128)(2,1)} %param.9) | copy-start | bytes 6291460
  0.0 2.4 %copy-start.2 = (bf16[1,512,2048]{2,1,0:T(8,128)(2,1)S(1)}, bf16[1,512,2048]{2,1,0:T(8,128)(2,1)}, u32[]{:S(2)}) copy-start(bf16[1,512,2048]{2,1,0:T(8,128)(2,1)} %param.7) | copy-start | bytes 6291460
  4.5 15.0 %collective-permute-start = (bf16[256,1024]{1,0:T(8,128)(2,1)S(1)}, bf16[256,1024]{1,0:T(8,128)(2,1)S(1)}, u32[]{:S(2)}, u32[]{:S(2)}) collective-permute-start(bf16[256,1024]{1,0:T(8,128)(2,1)S(1)} %dynamic-slice_bitcast_fusion), channel_id=1, source_target_pairs={{0,2},{2,0},{1,3},{3,1},{4,6},{6,4},{5,7},{7,5},{8,10},{10,8},{9,1... | collective-permute-start | bytes 1572872 | tf_op jit(solution)/shard_map/ppermute | solution.py:77
  19.5 1.9 %collective-permute-start.1 = (bf16[256,1024]{1,0:T(8,128)(2,1)S(1)}, bf16[256,1024]{1,0:T(8,128)(2,1)S(1)}, u32[]{:S(2)}, u32[]{:S(2)}) collective-permute-start(bf16[256,1024]{1,0:T(8,128)(2,1)S(1)} %collective-permute-done), channel_id=1, source_target_pairs={{0,1},{1,0},{2,3},{3,2},{4,5},{5,4},{6,7},{7,6},{8,9},{9,8},{10,11... | collective-permute-start | bytes 1572872 | tf_op jit(solution)/shard_map/ppermute | solution.py:67
  24.5 6.4 %copy-start.14 = (bf16[512,1024]{1,0:T(8,128)(2,1)}, bf16[512,1024]{1,0:T(8,128)(2,1)S(1)}, u32[]{:S(2)}) copy-start(bf16[512,1024]{1,0:T(8,128)(2,1)S(1)} %bitcast_select_fusion) | copy-start | bytes 3145732
  24.6 8.8 %copy-start.18 = (f32[1,8,512]{2,1,0:T(8,128)S(1)}, f32[1,8,512]{2,1,0:T(8,128)}, u32[]{:S(2)}) copy-start(f32[1,8,512]{2,1,0:T(8,128)} %param.12) | copy-start | bytes 49156
  30.9 48.0 %collective-permute-start.2 = (bf16[2,512,1024]{2,1,0:T(8,128)(2,1)}, bf16[2,512,1024]{2,1,0:T(8,128)(2,1)}, u32[]{:S(2)}, u32[]{:S(2)}) collective-permute-start(bf16[2,512,1024]{2,1,0:T(8,128)(2,1)} %convert_bitcast_fusion), channel_id=1, source_target_pairs={{0,2},{2,0},{1,3},{3,1},{4,6},{6,4},{5,7},{7,5},{8,10},{10,8},{9,1... | collective-permute-start | bytes 6291464 | tf_op jit(solution)/shard_map/ppermute | solution.py:91
  36.4 106.8 %copy-start.15 = (pred[512,512]{0,1:T(8,128)(4,1)}, pred[512,512]{0,1:T(8,128)(4,1)S(1)}, u32[]{:S(2)}) copy-start(pred[512,512]{0,1:T(8,128)(4,1)S(1)} %fusion.46) | copy-start | bytes 786436
  37.1 41.8 %copy-start.9 = (bf16[1,512,2048]{2,1,0:T(8,128)(2,1)S(1)}, bf16[1,512,2048]{2,1,0:T(8,128)(2,1)}, u32[]{:S(2)}) copy-start(bf16[1,512,2048]{2,1,0:T(8,128)(2,1)} %copy-done.8) | copy-start | bytes 6291460
  37.1 41.8 %copy-start.21 = (bf16[1024,2,1024]{2,1,0:T(2,128)(2,1)S(1)}, bf16[1024,2,1024]{2,1,0:T(2,128)(2,1)}, u32[]{:S(2)}) copy-start(bf16[1024,2,1024]{2,1,0:T(2,128)(2,1)} %param.10) | copy-start | bytes 12582916
  85.3 37.2 %collective-permute-start.5 = (bf16[1,512,1024]{2,1,0:T(8,128)(2,1)}, bf16[1,512,1024]{2,1,0:T(8,128)(2,1)}, u32[]{:S(2)}, u32[]{:S(2)}) collective-permute-start(bf16[1,512,1024]{2,1,0:T(8,128)(2,1)} %slice.63), channel_id=1, source_target_pairs={{0,4},{4,8},{8,12},{1,5},{5,9},{9,13},{2,6},{6,10},{10,14},{3,7},{... | collective-permute-start | bytes 3145736 | tf_op jit(solution)/shard_map/ppermute | solution.py:14
  90.0 27.4 %collective-permute-start.3 = (bf16[512,1024]{1,0:T(8,128)(2,1)}, bf16[512,1024]{1,0:T(8,128)(2,1)}, u32[]{:S(2)}, u32[]{:S(2)}) collective-permute-start(bf16[512,1024]{1,0:T(8,128)(2,1)} %convolution_convert_fusion), channel_id=1, source_target_pairs={{0,2},{2,0},{1,3},{3,1},{4,6},{6,4},{5,7},{7,5},{8,10},{10,8},{9,1... | collective-permute-start | bytes 3145736 | tf_op jit(solution)/shard_map/ppermute | solution.py:91
  104.7 28.9 %collective-permute-start.4 = (bf16[1,512,1024]{2,1,0:T(8,128)(2,1)}, bf16[1,512,1024]{2,1,0:T(8,128)(2,1)}, u32[]{:S(2)}, u32[]{:S(2)}) collective-permute-start(bf16[1,512,1024]{2,1,0:T(8,128)(2,1)} %get-tuple-element.19), channel_id=1, source_target_pairs={{0,4},{4,8},{8,12},{1,5},{5,9},{9,13},{2,6},{6,10},{10,14},{3,7},{... | collective-permute-start | bytes 3145736 | tf_op jit(solution)/shard_map/ppermute | solution.py:14
  110.6 3.8 %copy-start.6 = (bf16[1,512,1024]{1,2,0:T(8,128)(2,1)}, bf16[1,512,1024]{1,2,0:T(8,128)(2,1)S(1)}, u32[]{:S(2)}) copy-start(bf16[1,512,1024]{1,2,0:T(8,128)(2,1)S(1)} %copy.86) | copy-start | bytes 3145732
  113.9 53.2 %collective-permute-start.9 = (bf16[1024,1024]{1,0:T(8,128)(2,1)}, bf16[1024,1024]{1,0:T(8,128)(2,1)}, u32[]{:S(2)}, u32[]{:S(2)}) collective-permute-start(bf16[1024,1024]{1,0:T(8,128)(2,1)} %param.11), channel_id=1, source_target_pairs={{0,2},{2,0},{1,3},{3,1},{4,6},{6,4},{5,7},{7,5},{8,10},{10,8},{9,1... | collective-permute-start | bytes 6291464 | tf_op jit(solution)/shard_map/ppermute | solution.py:178
  114.4 3.0 %copy-start.10 = (bf16[1,512,2048]{2,1,0:T(8,128)(2,1)S(1)}, bf16[1,512,2048]{2,1,0:T(8,128)(2,1)}, u32[]{:S(2)}) copy-start(bf16[1,512,2048]{2,1,0:T(8,128)(2,1)} %copy-done.8) | copy-start | bytes 6291460
  121.7 13.4 %copy-start.20 = (f32[9]{0:T(128)S(1)}, f32[9]{0:T(128)}, u32[]{:S(2)}) copy-start(f32[9]{0:T(128)} %pad.11.clone) | copy-start | bytes 112
  122.5 17.4 %copy-start.11 = (f32[64,8,8,128]{3,2,1,0:T(8,128)S(1)}, f32[64,8,8,128]{3,2,1,0:T(8,128)}, u32[]{:S(2)}) copy-start(f32[64,8,8,128]{3,2,1,0:T(8,128)} %get-tuple-element.22) | copy-start | bytes 6291460
  135.1 5.4 %copy-start.4 = (f32[1,512,1024]{1,2,0:T(8,128)S(1)}, f32[1,512,1024]{1,2,0:T(8,128)}, u32[]{:S(2)}) copy-start(f32[1,512,1024]{1,2,0:T(8,128)} %copy.83) | copy-start | bytes 6291460
  135.1 5.4 %copy-start.16 = (pred[512,512]{0,1:T(8,128)(4,1)S(1)}, pred[512,512]{0,1:T(8,128)(4,1)}, u32[]{:S(2)}) copy-start(pred[512,512]{0,1:T(8,128)(4,1)} %iota_compare_fusion.1) | copy-start | bytes 786436
  135.3 13.2 %collective-permute-start.6 = (bf16[1,9,128,128]{3,2,1,0:T(8,128)(2,1)S(1)}, bf16[1,9,128,128]{3,2,1,0:T(8,128)(2,1)S(1)}, u32[]{:S(2)}, u32[]{:S(2)}) collective-permute-start(bf16[1,9,128,128]{3,2,1,0:T(8,128)(2,1)S(1)} %fusion.53), channel_id=1, source_target_pairs={{0,4},{4,8},{8,12},{1,5},{5,9},{9,13},{2,6},{6,10},{10,14},{3,7},{... | collective-permute-start | bytes 884744 | tf_op jit(solution)/shard_map/ppermute | solution.py:14
  140.6 2.6 %copy-start.12 = (bf16[512,8,128]{2,0,1:T(8,128)(2,1)}, bf16[512,8,128]{2,0,1:T(8,128)(2,1)S(1)}, u32[]{:S(2)}) copy-start(bf16[512,8,128]{2,0,1:T(8,128)(2,1)S(1)} %fusion.19) | copy-start | bytes 3145732
  143.2 8.9 %copy-start.7 = (bf16[1,512,1024]{1,2,0:T(8,128)(2,1)S(1)}, bf16[1,512,1024]{1,2,0:T(8,128)(2,1)}, u32[]{:S(2)}) copy-start(bf16[1,512,1024]{1,2,0:T(8,128)(2,1)} %copy-done.6) | copy-start | bytes 3145732
  148.6 8.3 %collective-permute-start.7 = (bf16[1,9,128,128]{3,2,1,0:T(8,128)(2,1)S(1)}, bf16[1,9,128,128]{3,2,1,0:T(8,128)(2,1)S(1)}, u32[]{:S(2)}, u32[]{:S(2)}) collective-permute-start(bf16[1,9,128,128]{3,2,1,0:T(8,128)(2,1)S(1)} %fusion.55), channel_id=1, source_target_pairs={{0,4},{4,8},{8,12},{1,5},{5,9},{9,13},{2,6},{6,10},{10,14},{3,7},{... | collective-permute-start | bytes 884744 | tf_op jit(solution)/shard_map/ppermute | solution.py:14
  157.1 9.2 %collective-permute-start.8 = (bf16[1,9,128,128]{3,2,1,0:T(8,128)(2,1)S(1)}, bf16[1,9,128,128]{3,2,1,0:T(8,128)(2,1)S(1)}, u32[]{:S(2)}, u32[]{:S(2)}) collective-permute-start(bf16[1,9,128,128]{3,2,1,0:T(8,128)(2,1)S(1)} %fusion.57), channel_id=1, source_target_pairs={{0,4},{4,8},{8,12},{1,5},{5,9},{9,13},{2,6},{6,10},{10,14},{3,7},{... | collective-permute-start | bytes 884744 | tf_op jit(solution)/shard_map/ppermute | solution.py:14
  161.4 5.0 %copy-start.13 = (bf16[512,8,128]{2,0,1:T(8,128)(2,1)S(1)}, bf16[512,8,128]{2,0,1:T(8,128)(2,1)}, u32[]{:S(2)}) copy-start(bf16[512,8,128]{2,0,1:T(8,128)(2,1)} %copy-done.12) | copy-start | bytes 3145732
  161.4 5.0 %copy-start.17 = (f32[512,8]{0,1:T(8,128)S(1)}, f32[512,8]{0,1:T(8,128)}, u32[]{:S(2)}) copy-start(f32[512,8]{0,1:T(8,128)} %get-tuple-element.17) | copy-start | bytes 49156
  161.4 5.0 %copy-start.24 = (f32[8,128,512]{2,1,0:T(8,128)S(1)}, f32[8,128,512]{2,1,0:T(8,128)}, u32[]{:S(2)}) copy-start(f32[8,128,512]{2,1,0:T(8,128)} %fusion.5) | copy-start | bytes 6291460
  167.0 4.9 %copy-start.23 = (bf16[1,512,8,128]{1,3,2,0:T(8,128)(2,1)}, bf16[1,512,8,128]{1,3,2,0:T(8,128)(2,1)S(1)}, u32[]{:S(2)}) copy-start(bf16[1,512,8,128]{1,3,2,0:T(8,128)(2,1)S(1)} %fusion.22) | copy-start | bytes 3145732
  171.9 3.4 %collective-permute-start.10 = (bf16[512,1024]{1,0:T(8,128)(2,1)}, bf16[512,1024]{1,0:T(8,128)(2,1)S(1)}, u32[]{:S(2)}, u32[]{:S(2)}) collective-permute-start(bf16[512,1024]{1,0:T(8,128)(2,1)} %fusion.31), channel_id=1, source_target_pairs={{0,1},{1,0},{2,3},{3,2},{4,5},{5,4},{6,7},{7,6},{8,9},{9,8},{10,11... | collective-permute-start | bytes 3145736 | tf_op jit(solution)/shard_map/ppermute | solution.py:202
  171.9 3.4 %copy-start.3 = (bf16[1,512,2048]{2,1,0:T(8,128)(2,1)S(1)}, bf16[1,512,2048]{2,1,0:T(8,128)(2,1)}, u32[]{:S(2)}) copy-start(bf16[1,512,2048]{2,1,0:T(8,128)(2,1)} %param.7) | copy-start | bytes 6291460
  171.9 5.0 %copy-start.1 = (bf16[1024,1024]{1,0:T(8,128)(2,1)S(1)}, bf16[1024,1024]{1,0:T(8,128)(2,1)}, u32[]{:S(2)}) copy-start(bf16[1024,1024]{1,0:T(8,128)(2,1)} %param.9) | copy-start | bytes 6291460
  (4 other events, 7.4 us)

commit v14 on v10

--- a/solution.py
+++ b/solution.py
@@ -186,17 +186,32 @@
     )
     attended = (window + read).astype(jnp.bfloat16).reshape(count, inner_here)
     w_output = lax.optimization_barrier((w_output, pair_raw))[0]
-    w_output_rows = lax.all_gather(w_output, "wloop", axis=1, tiled=True)
+    out_block = w_output.shape[1]
+    from_ranks = jnp.stack(
+        [w_output]
+        + [
+            lax.ppermute(w_output, "wloop", [(source, (source + step) % ways) for source in range(ways)])
+            for step in range(1, ways)
+        ]
+    )
     cores = lax.axis_size("heads")
     core = lax.axis_index("heads")
     share = width // cores
 
+    blocks_per_share = share // out_block
+
     def output_share(index):
-        return jnp.dot(
-            attended,
-            lax.dynamic_slice_in_dim(w_output_rows, index * share, share, 1),
-            preferred_element_type=jnp.float32,
-        )
+        parts = []
+        for part in range(blocks_per_share):
+            rank = index * blocks_per_share + part
+            parts.append(
+                jnp.dot(
+                    attended,
+                    lax.dynamic_index_in_dim(from_ranks, (me - rank) % ways, 0, keepdims=False),
+                    preferred_element_type=jnp.float32,
+                )
+            )
+        return jnp.concatenate(parts, axis=1) if blocks_per_share > 1 else parts[0]
 
     received = [
         lax.ppermute(
@@ -206,7 +221,7 @@
         )
         for step in range(1, cores)
     ]
-    summed = output_share(core)
+    summed = lax.optimization_barrier(output_share(core))
     for piece in received:
         summed = summed + piece.astype(jnp.float32)
     residual = lax.dynamic_slice_in_dim(

time: 209 us -> 182 us (0.87)
  waiting for transfers between devices: 80.5 us -> 64.4 us
  between operations: 14.6 us -> 1.29 us
    all_gather x1 -> x0, waiting for transfers between devices: 25.7 us -> none  [shards(): w_output_rows = lax.all_gather(w_output, 'wloop', axis=1, tiled=True)]
    ppermute x0 -> x1, waiting for transfers between devices: none -> 14.2 us  [shards(): lax.ppermute(w_output, 'wloop', [(source, (source + step) % ways) for sou...]
    ppermute x1, waiting for transfers between devices: 3 us -> 0.01 us  [shards(): lax.ppermute(output_share((core + step) % cores).astype(jnp.bfloat16), 'h...]
    unnamed x49 -> x55, local copies, waits for them, and re-layouts: 9.36 us -> 9.41 us
  transfers between devices with their start and end apart: 14 -> 14, of which waited for: 10 -> 9; matrix products, arithmetic and copies ran while one was open for 24% -> 30% of each run, Pallas kernels for 0% -> 0%
where the time goes in v14:
time: 182 us; the launch traced here: 181 us
  waiting for transfers between devices  64.4 us (35%)
  starting transfers between devices  37.1 us (20%)
  matrix products  35.4 us (19%)
  other arithmetic  22.7 us (12%)
  local copies, waits for them, and re-layouts  20.4 us (11%)
    ppermute x3, waiting for transfers between devices, gathered_sum(): lax.ppermute(outgoing, 'wloop', [(source, (source - step) % ways) for sou...  29.2 us
    ppermute x7, starting transfers between devices, shifted(): lax.ppermute(value, axis, [(source, source + steps) for source in range(i...  27.5 us
    ppermute x1, waiting for transfers between devices, shards(): lax.ppermute(w_output, 'wloop', [(source, (source + step) % ways) for sou...  14.2 us
    ppermute x1, waiting for transfers between devices, shards(): lax.ppermute(part, 'wloop', [(source, (source + step) % ways) for source...  10.7 us
    unnamed x55, local copies, waits for them, and re-layouts  9.41 us
    ppermute x7, waiting for transfers between devices, shifted(): lax.ppermute(value, axis, [(source, source + steps) for source in range(i...  9.36 us
    dot_general x2, matrix products, output_share(): jnp.dot(attended, lax.dynamic_index_in_dim(from_ranks, (me - rank) % ways...  7.32 us
    dot_general x2, matrix products, shards(): jnp.einsum('td,dje->jte', rows, w_keyvalue, preferred_element_type=jnp.fl...  7.27 us
  transfers between devices with their start and end apart: 14, of which 9 were waited for; matrix products, arithmetic and copies ran while one was open for 30% of the time, Pallas kernels for 0%

profile of v14, /device:TPU:0, one launch (start us, length us, event | category | flops | bytes accessed | tf_op | source)
XLA Modules:
  0.0 181.2 jit_solution(17052618747257791197)
XLA Ops:
  0.0 2.2 %fusion.2 = f32[512]{0:T(512)S(1)} fusion(bf16[1,512,2048]{2,1,0:T(8,128)(2,1)} %param.7), kind=kLoop, calls=%fused_computation.13 | loop fusion | flops 3145216 | bytes 2099200 | tf_op jit(solution)/shard_map/reduce_sum | solution.py:18
  4.5 3.0 %collective-permute-start = (bf16[256,1024]{1,0:T(8,128)(2,1)S(1)}, bf16[256,1024]{1,0:T(8,128)(2,1)S(1)}, u32[]{:S(2)}, u32[]{:S(2)}) collective-permute-start(bf16[256,1024]{1,0:T(8,128)(2,1)S(1)} %dynamic-slice_bitcast_fusion), channel_id=1, source_target_pairs={{0,2},{2,0},{1,3},{3,1},{4,6},{6,4},{5,7},{7,5},{8,10},{10,8},{9,1... | collective-permute-start | bytes 1572872 | tf_op jit(solution)/shard_map/ppermute | solution.py:77
  8.8 10.7 %collective-permute-done = bf16[256,1024]{1,0:T(8,128)(2,1)S(1)} collective-permute-done((bf16[256,1024]{1,0:T(8,128)(2,1)S(1)}, bf16[256,1024]{1,0:T(8,128)(2,1)S(1)}, u32[]{:S(2)}, u32[]{:S(2)}) %collective-permute-start) | collective-permute-done | bytes 524320 | tf_op jit(solution)/shard_map/ppermute | solution.py:77
  22.5 1.8 %gather_fusion = bf16[2,256,1024]{2,1,0:T(8,128)(2,1)S(1)} fusion(bf16[2,256,1024]{2,1,0:T(8,128)(2,1)} %pad_maximum_fusion.1, s32[1024]{0:T(1024)S(1)} %pad_clamp_fusion), kind=kCustom, calls=%fused_computation | custom fusion | bytes 2097160 | tf_op jit(solution)/shard_map/jit(_take)/gather | solution.py:70
  25.5 4.8 %convert_bitcast_fusion = bf16[2,512,1024]{2,1,0:T(8,128)(2,1)S(1)} fusion(bf16[1024,2,1024]{2,1,0:T(2,128)(2,1)} %param.10, bf16[512,1024]{1,0:T(8,128)(2,1)S(1)} %bitcast_select_fusion), kind=kOutput, calls=%fused_computation.40 | convolution fusion | flops 2148532224 | bytes 7340032 | tf_op jit(solution)/shard_map/td,dje->jte/dot_general | solution.py:99
  33.5 2.5 %fusion.11 = f32[2,512,1024]{2,1,0:T(8,128)S(1)} fusion(bf16[1024,2,1024]{2,1,0:T(2,128)(2,1)S(1)} %copy-done.19, bf16[1,512,2048]{2,1,0:T(8,128)(2,1)S(1)} %copy-done.8, s32[]{:T(128)S(6)} %select_n.91), kind=kOutput, calls=%fused_computation.23 | convolution fusion | flops 2147483648 | bytes 9437188 | tf_op jit(solution)/shard_map/td,dje->jte/dot_general | solution.py:99
  36.0 20.6 %collective-permute-done.2 = bf16[2,256,1024]{2,1,0:T(8,128)(2,1)S(1)} collective-permute-done((bf16[2,256,1024]{2,1,0:T(8,128)(2,1)S(1)}, bf16[2,256,1024]{2,1,0:T(8,128)(2,1)S(1)}, u32[]{:S(2)}, u32[]{:S(2)}) %collective-permute-start.2) | collective-permute-done | bytes 1048608 | tf_op jit(solution)/shard_map/ppermute | solution.py:91
  60.9 1.8 collective-permute-start.3
  63.1 2.3 %convolution_convert_fusion = bf16[512,1024]{1,0:T(8,128)(2,1)} fusion(bf16[512,1024]{1,0:T(8,128)(2,1)S(1)} %copy-done.12, bf16[1024,1024]{1,0:T(8,128)(2,1)S(1)} %copy-done), kind=kOutput, calls=%fused_computation.47 | convolution fusion | flops 1074266112 | bytes 4194304 | tf_op jit(solution)/shard_map/dot_general | solution.py:125
  66.4 4.3 %collective-permute-start.5 = (bf16[256,1024]{0,1:T(8,128)(2,1)}, bf16[256,1024]{0,1:T(8,128)(2,1)}, u32[]{:S(2)}, u32[]{:S(2)}) collective-permute-start(bf16[256,1024]{0,1:T(8,128)(2,1)} %bitcast.158), channel_id=1, source_target_pairs={{0,4},{4,8},{8,12},{1,5},{5,9},{9,13},{2,6},{6,10},{10,14},{3,7},{... | collective-permute-start | bytes 1572872 | tf_op jit(solution)/shard_map/ppermute | solution.py:14
  71.9 3.4 %collective-permute-start.7 = (bf16[256,1024]{0,1:T(8,128)(2,1)}, bf16[256,1024]{0,1:T(8,128)(2,1)}, u32[]{:S(2)}, u32[]{:S(2)}) collective-permute-start(bf16[256,1024]{0,1:T(8,128)(2,1)} %bitcast.157), channel_id=1, source_target_pairs={{0,4},{4,8},{8,12},{1,5},{5,9},{9,13},{2,6},{6,10},{10,14},{3,7},{... | collective-permute-start | bytes 1572872 | tf_op jit(solution)/shard_map/ppermute | solution.py:14
  77.1 8.5 %collective-permute-done.3 = bf16[2,256,1024]{2,1,0:T(8,128)(2,1)} collective-permute-done((bf16[2,256,1024]{2,1,0:T(8,128)(2,1)}, bf16[2,256,1024]{2,1,0:T(8,128)(2,1)}, u32[]{:S(2)}, u32[]{:S(2)}) %collective-permute-start.3) | collective-permute-done | bytes 1048608 | tf_op jit(solution)/shard_map/ppermute | solution.py:91
  85.6 2.2 %slice_add_fusion = f32[2,256,1024]{2,1,0:T(8,128)S(1)} fusion(f32[2,512,1024]{2,1,0:T(8,128)} %copy-done.6, bf16[2,256,1024]{2,1,0:T(8,128)(2,1)} %collective-permute-done.3), kind=kLoop, calls=%fused_computation.32 | loop fusion | flops 1048576 | bytes 5242880 | tf_op jit(solution)/shard_map/add | solution.py:91
  91.7 2.0 %copy.90 = bf16[256,8,128]{0,2,1:T(8,128)(2,1)} copy(bf16[256,8,128]{2,0,1:T(8,128)(2,1)} %fusion.44) | data formatting | bytes 1048576 | tf_op jit(solution)/shard_map/optimization_barrier | solution.py:112
  93.8 4.5 %collective-permute-start.6 = (bf16[256,1024]{0,1:T(8,128)(2,1)}, bf16[256,1024]{0,1:T(8,128)(2,1)}, u32[]{:S(2)}, u32[]{:S(2)}) collective-permute-start(bf16[256,1024]{0,1:T(8,128)(2,1)} %bitcast.160), channel_id=1, source_target_pairs={{0,4},{4,8},{8,12},{1,5},{5,9},{9,13},{2,6},{6,10},{10,14},{3,7},{... | collective-permute-start | bytes 1572872 | tf_op jit(solution)/shard_map/ppermute | solution.py:14
  99.4 2.9 %collective-permute-start.8 = (bf16[256,1024]{0,1:T(8,128)(2,1)}, bf16[256,1024]{0,1:T(8,128)(2,1)S(1)}, u32[]{:S(2)}, u32[]{:S(2)}) collective-permute-start(bf16[256,1024]{0,1:T(8,128)(2,1)} %bitcast.159), channel_id=1, source_target_pairs={{0,4},{4,8},{8,12},{1,5},{5,9},{9,13},{2,6},{6,10},{10,14},{3,7},{... | collective-permute-start | bytes 1572872 | tf_op jit(solution)/shard_map/ppermute | solution.py:14
  105.6 4.0 %fusion.36 = f32[1,8,128,128]{3,2,1,0:T(8,128)S(1)} fusion(bf16[512,8,128]{2,0,1:T(8,128)(2,1)} %copy_dynamic-update-slice_fusion, bf16[512,8,128]{2,0,1:T(8,128)(2,1)} %constant_dynamic-update-slice_fusion, f32[512,8]{0,1:T(8,128)S(1)} %fusion.67), kind=kOutput, calls=%fused_computation.49 | convolution fusion | flops 806354944 | bytes 2637824 | tf_op jit(solution)/shard_map/bht,bthd,bthe->bhde/dot_general | solution.py:140
  110.1 2.2 %maximum_bitcast_fusion = bf16[1,512,1024]{1,2,0:T(8,128)(2,1)} fusion(bf16[256,1024]{0,1:T(8,128)(2,1)} %collective-permute-done.6, bf16[256,1024]{0,1:T(8,128)(2,1)} %collective-permute-done.5), kind=kLoop, calls=%fused_computation.56 | loop fusion | flops 2097152 | bytes 2097152 | tf_op jit(solution)/shard_map/reshape | solution.py:130
  112.3 6.4 %collective-permute-done.8 = bf16[256,1024]{0,1:T(8,128)(2,1)S(1)} collective-permute-done((bf16[256,1024]{0,1:T(8,128)(2,1)}, bf16[256,1024]{0,1:T(8,128)(2,1)S(1)}, u32[]{:S(2)}, u32[]{:S(2)}) %collective-permute-start.8) | collective-permute-done | bytes 524320 | tf_op jit(solution)/shard_map/ppermute | solution.py:14
  118.8 2.2 %maximum_bitcast_fusion.1 = bf16[1,512,1024]{1,2,0:T(8,128)(2,1)} fusion(bf16[256,1024]{0,1:T(8,128)(2,1)S(1)} %collective-permute-done.8, bf16[256,1024]{0,1:T(8,128)(2,1)} %collective-permute-done.7), kind=kLoop, calls=%fused_computation.57 | loop fusion | flops 2097152 | bytes 2097152 | tf_op jit(solution)/shard_map/reshape | solution.py:131
  121.1 4.3 %collective-permute-start.9 = (bf16[1,9,128,128]{3,2,1,0:T(8,128)(2,1)S(1)}, bf16[1,9,128,128]{3,2,1,0:T(8,128)(2,1)S(1)}, u32[]{:S(2)}, u32[]{:S(2)}) collective-permute-start(bf16[1,9,128,128]{3,2,1,0:T(8,128)(2,1)S(1)} %fusion.54), channel_id=1, source_target_pairs={{0,4},{4,8},{8,12},{1,5},{5,9},{9,13},{2,6},{6,10},{10,14},{3,7},{... | collective-permute-start | bytes 884744 | tf_op jit(solution)/shard_map/ppermute | solution.py:14
  130.5 4.4 %collective-permute-start.10 = (bf16[1,9,128,128]{3,2,1,0:T(8,128)(2,1)}, bf16[1,9,128,128]{3,2,1,0:T(8,128)(2,1)S(1)}, u32[]{:S(2)}, u32[]{:S(2)}) collective-permute-start(bf16[1,9,128,128]{3,2,1,0:T(8,128)(2,1)} %fusion.56), channel_id=1, source_target_pairs={{0,4},{4,8},{8,12},{1,5},{5,9},{9,13},{2,6},{6,10},{10,14},{3,7},{... | collective-permute-start | bytes 884744 | tf_op jit(solution)/shard_map/ppermute | solution.py:14
  134.9 4.1 %multiply_bitcast_fusion = (f32[64,8,8,128]{3,1,2,0:T(8,128)S(1)}, f32[64,8,8,128]{3,2,1,0:T(8,128)}) fusion(bf16[512,1024]{1,0:T(8,128)(2,1)} %collective-permute-done.4, bf16[1024,1024]{1,0:T(8,128)(2,1)S(1)} %copy-done, bf16[1,512,2048]{2,1,0:T(8,128)(2,1)} %copy-done.7, s32[]{:T(128)S(6)} %select_n.91), kind=kOutput, calls=%fused_computation.44 | convolution fusion | flops 1075314688 | bytes 8388612 | tf_op jit(solution)/shard_map/dot_general | solution.py:125
  140.2 2.0 %fusion.22 = bf16[512,8,128]{2,0,1:T(8,128)(2,1)S(1)} fusion(f32[64,8,8,128]{3,2,1,0:T(8,128)} %get-tuple-element.30, f32[512,8]{0,1:T(8,128)S(1)} %add_rsqrt_fusion), kind=kLoop, calls=%fused_computation.31 | loop fusion | flops 1048576 | bytes 3162112 | tf_op jit(solution)/shard_map/convert_element_type | solution.py:132
  142.3 2.2 %fusion = (f32[8,512]{1,0:T(8,128)S(1)}, f32[8,512,512]{1,2,0:T(8,128)S(1)}) fusion(pred[512,512]{0,1:T(8,128)(4,1)S(1)} %copy-done.15, bf16[512,8,128]{2,0,1:T(8,128)(2,1)S(1)} %fusion.22, bf16[512,8,128]{2,0,1:T(8,128)(2,1)S(1)} %copy-done.9), kind=kOutput, calls=%fused_computation.5 | convolution fusion | flops 543158272 | bytes 10764288 | tf_op jit(solution)/shard_map/bihd,bjhd->bhij/dot_general | solution.py:23
  144.5 2.5 %fusion.1 = (f32[8,512]{1,0:T(8,128)S(1)}, f32[8,512,512]{1,2,0:T(8,128)S(1)}) fusion(pred[512,512]{0,1:T(8,128)(4,1)S(1)} %copy-done.16, bf16[512,8,128]{2,0,1:T(8,128)(2,1)S(1)} %fusion.22, bf16[512,8,128]{0,2,1:T(8,128)(2,1)S(1)} %bitcast.155), kind=kOutput, calls=%fused_computation.6 | convolution fusion | flops 543158272 | bytes 10764288 | tf_op jit(solution)/shard_map/bihd,bjhd->bhij/dot_general | solution.py:27
  147.0 2.4 %fusion.6 = f32[8,128,512]{2,1,0:T(8,128)S(1)} fusion(bf16[512,8,128]{0,2,1:T(8,128)(2,1)S(1)} %bitcast.156, f32[8,512,512]{1,2,0:T(8,128)S(1)} %get-tuple-element.36, f32[8,512]{1,0:T(8,128)S(1)} %add.181, pred[512,512]{0,1:T(8,128)(4,1)S(1)} %copy-done.16), kind=kOutput, calls=%fused_computation.18 | convolution fusion | flops 545259520 | bytes 11812864 | tf_op jit(solution)/shard_map/bhij,bjhd->bihd/dot_general | solution.py:40
  149.7 3.7 %collective-permute-start.11 = (bf16[1,9,128,128]{3,2,1,0:T(8,128)(2,1)S(1)}, bf16[1,9,128,128]{3,2,1,0:T(8,128)(2,1)S(1)}, u32[]{:S(2)}, u32[]{:S(2)}) collective-permute-start(bf16[1,9,128,128]{3,2,1,0:T(8,128)(2,1)S(1)} %fusion.58), channel_id=1, source_target_pairs={{0,4},{4,8},{8,12},{1,5},{5,9},{9,13},{2,6},{6,10},{10,14},{3,7},{... | collective-permute-start | bytes 884744 | tf_op jit(solution)/shard_map/ppermute | solution.py:14
  153.4 2.6 %fusion.5 = f32[8,128,512]{2,1,0:T(8,128)S(1)} fusion(bf16[512,8,128]{2,0,1:T(8,128)(2,1)S(1)} %copy-done.10, f32[8,512,512]{1,2,0:T(8,128)S(1)} %get-tuple-element.34, f32[8,512]{1,0:T(8,128)S(1)} %add.181, pred[512,512]{0,1:T(8,128)(4,1)S(1)} %copy-done.15), kind=kOutput, calls=%fused_computation.17 | convolution fusion | flops 545259520 | bytes 11812864 | tf_op jit(solution)/shard_map/bhij,bjhd->bihd/dot_general | solution.py:38
  158.1 14.2 %collective-permute-done.12 = bf16[1024,1024]{1,0:T(8,128)(2,1)} collective-permute-done((bf16[1024,1024]{1,0:T(8,128)(2,1)}, bf16[1024,1024]{1,0:T(8,128)(2,1)}, u32[]{:S(2)}, u32[]{:S(2)}) %collective-permute-start.12) | collective-permute-done | bytes 2097184 | tf_op jit(solution)/shard_map/ppermute | solution.py:193
  172.3 3.9 %fusion.32 = bf16[512,1024]{1,0:T(8,128)(2,1)} fusion(bf16[512,1024]{0,1:T(8,128)(2,1)S(1)} %bitcast.171, s32[]{:T(128)S(6)} %select_n.108, bf16[1,1024,1024]{2,1,0:T(8,128)(2,1)S(1)} %bitcast.170, bf16[1,1024,1024]{2,1,0:T(8,128)(2,1)} %bitcast.45), kind=kOutput, calls=%fused_computation.46 | convolution fusion | flops 1075314688 | bytes 6291460 | tf_op jit(solution)/shard_map/dot_general | solution.py:208
  176.3 3.4 %fusion.20 = f32[512,1024]{1,0:T(8,128)S(1)} fusion(bf16[512,1024]{0,1:T(8,128)(2,1)} %bitcast.172, s32[]{:T(128)S(6)} %select_n.105, bf16[1,1024,1024]{2,1,0:T(8,128)(2,1)} %bitcast.169, bf16[1,1024,1024]{2,1,0:T(8,128)(2,1)} %bitcast.45), kind=kOutput, calls=%fused_computation.29 | convolution fusion | flops 1074790400 | bytes 7340036 | tf_op jit(solution)/shard_map/dot_general | solution.py:208
  (121 shorter events, 37.7 us)
Async XLA Ops:
  0.0 63.1 %copy-start = (bf16[1024,1024]{1,0:T(8,128)(2,1)S(1)}, bf16[1024,1024]{1,0:T(8,128)(2,1)}, u32[]{:S(2)}) copy-start(bf16[1024,1024]{1,0:T(8,128)(2,1)} %param.9) | copy-start | bytes 6291460
  0.0 2.2 %copy-start.18 = (f32[2048]{0:T(1024)S(1)}, f32[2048]{0:T(1024)}, u32[]{:S(2)}) copy-start(f32[2048]{0:T(1024)} %param.8) | copy-start | bytes 24580
  0.0 2.4 %copy-start.2 = (bf16[1,512,2048]{2,1,0:T(8,128)(2,1)S(1)}, bf16[1,512,2048]{2,1,0:T(8,128)(2,1)}, u32[]{:S(2)}) copy-start(bf16[1,512,2048]{2,1,0:T(8,128)(2,1)} %param.7) | copy-start | bytes 6291460
  2.4 5.3 %copy-start.17 = (f32[1,8,512]{2,1,0:T(8,128)S(1)}, f32[1,8,512]{2,1,0:T(8,128)}, u32[]{:S(2)}) copy-start(f32[1,8,512]{2,1,0:T(8,128)} %param.12) | copy-start | bytes 49156
  4.5 15.0 %collective-permute-start = (bf16[256,1024]{1,0:T(8,128)(2,1)S(1)}, bf16[256,1024]{1,0:T(8,128)(2,1)S(1)}, u32[]{:S(2)}, u32[]{:S(2)}) collective-permute-start(bf16[256,1024]{1,0:T(8,128)(2,1)S(1)} %dynamic-slice_bitcast_fusion), channel_id=1, source_target_pairs={{0,2},{2,0},{1,3},{3,1},{4,6},{6,4},{5,7},{7,5},{8,10},{10,8},{9,1... | collective-permute-start | bytes 1572872 | tf_op jit(solution)/shard_map/ppermute | solution.py:77
  19.5 1.9 %collective-permute-start.1 = (bf16[256,1024]{1,0:T(8,128)(2,1)S(1)}, bf16[256,1024]{1,0:T(8,128)(2,1)S(1)}, u32[]{:S(2)}, u32[]{:S(2)}) collective-permute-start(bf16[256,1024]{1,0:T(8,128)(2,1)S(1)} %collective-permute-done), channel_id=1, source_target_pairs={{0,1},{1,0},{2,3},{3,2},{4,5},{5,4},{6,7},{7,6},{8,9},{9,8},{10,11... | collective-permute-start | bytes 1572872 | tf_op jit(solution)/shard_map/ppermute | solution.py:67
  25.5 8.0 %copy-start.19 = (bf16[1024,2,1024]{2,1,0:T(2,128)(2,1)S(1)}, bf16[1024,2,1024]{2,1,0:T(2,128)(2,1)}, u32[]{:S(2)}) copy-start(bf16[1024,2,1024]{2,1,0:T(2,128)(2,1)} %param.10) | copy-start | bytes 12582916
  30.3 3.2 %copy-start.8 = (bf16[1,512,2048]{2,1,0:T(8,128)(2,1)S(1)}, bf16[1,512,2048]{2,1,0:T(8,128)(2,1)}, u32[]{:S(2)}) copy-start(bf16[1,512,2048]{2,1,0:T(8,128)(2,1)} %copy-done.7) | copy-start | bytes 6291460
  31.5 25.2 %collective-permute-start.2 = (bf16[2,256,1024]{2,1,0:T(8,128)(2,1)S(1)}, bf16[2,256,1024]{2,1,0:T(8,128)(2,1)S(1)}, u32[]{:S(2)}, u32[]{:S(2)}) collective-permute-start(bf16[2,256,1024]{2,1,0:T(8,128)(2,1)S(1)} %get-tuple-element.32), channel_id=1, source_target_pairs={{0,2},{2,0},{1,3},{3,1},{4,6},{6,4},{5,7},{7,5},{8,10},{10,8},{9,1... | collective-permute-start | bytes 3145736 | tf_op jit(solution)/shard_map/ppermute | solution.py:91
  36.0 21.0 %copy-start.6 = (f32[2,512,1024]{2,1,0:T(8,128)}, f32[2,512,1024]{2,1,0:T(8,128)S(1)}, u32[]{:S(2)}) copy-start(f32[2,512,1024]{2,1,0:T(8,128)S(1)} %fusion.11) | copy-start | bytes 12582916
  58.6 4.5 %copy-start.12 = (bf16[512,1024]{1,0:T(8,128)(2,1)S(1)}, bf16[512,1024]{1,0:T(8,128)(2,1)}, u32[]{:S(2)}) copy-start(bf16[512,1024]{1,0:T(8,128)(2,1)} %copy-done.11) | copy-start | bytes 3145732
  60.9 24.7 %collective-permute-start.3 = (bf16[2,256,1024]{2,1,0:T(8,128)(2,1)}, bf16[2,256,1024]{2,1,0:T(8,128)(2,1)}, u32[]{:S(2)}, u32[]{:S(2)}) collective-permute-start(bf16[2,256,1024]{2,1,0:T(8,128)(2,1)} %get-tuple-element.17), channel_id=1, source_target_pairs={{0,2},{2,0},{1,3},{3,1},{4,6},{6,4},{5,7},{7,5},{8,10},{10,8},{9,1... | collective-permute-start | bytes 3145736 | tf_op jit(solution)/shard_map/ppermute | solution.py:91
  63.1 2.3 %copy-start.4 = (bf16[256,8,128]{2,0,1:T(8,128)(2,1)S(1)}, bf16[256,8,128]{2,0,1:T(8,128)(2,1)}, u32[]{:S(2)}) copy-start(bf16[256,8,128]{2,0,1:T(8,128)(2,1)} %fusion.45) | copy-start | bytes 1572868
  66.4 43.2 %collective-permute-start.5 = (bf16[256,1024]{0,1:T(8,128)(2,1)}, bf16[256,1024]{0,1:T(8,128)(2,1)}, u32[]{:S(2)}, u32[]{:S(2)}) collective-permute-start(bf16[256,1024]{0,1:T(8,128)(2,1)} %bitcast.158), channel_id=1, source_target_pairs={{0,4},{4,8},{8,12},{1,5},{5,9},{9,13},{2,6},{6,10},{10,14},{3,7},{... | collective-permute-start | bytes 1572872 | tf_op jit(solution)/shard_map/ppermute | solution.py:14
  71.9 40.4 %collective-permute-start.7 = (bf16[256,1024]{0,1:T(8,128)(2,1)}, bf16[256,1024]{0,1:T(8,128)(2,1)}, u32[]{:S(2)}, u32[]{:S(2)}) collective-permute-start(bf16[256,1024]{0,1:T(8,128)(2,1)} %bitcast.157), channel_id=1, source_target_pairs={{0,4},{4,8},{8,12},{1,5},{5,9},{9,13},{2,6},{6,10},{10,14},{3,7},{... | collective-permute-start | bytes 1572872 | tf_op jit(solution)/shard_map/ppermute | solution.py:14
  90.5 12.7 %copy-start.5 = (bf16[256,8,128]{2,0,1:T(8,128)(2,1)S(1)}, bf16[256,8,128]{2,0,1:T(8,128)(2,1)}, u32[]{:S(2)}) copy-start(bf16[256,8,128]{2,0,1:T(8,128)(2,1)} %fusion.44) | copy-start | bytes 1572868
  93.8 16.3 %collective-permute-start.6 = (bf16[256,1024]{0,1:T(8,128)(2,1)}, bf16[256,1024]{0,1:T(8,128)(2,1)}, u32[]{:S(2)}, u32[]{:S(2)}) collective-permute-start(bf16[256,1024]{0,1:T(8,128)(2,1)} %bitcast.160), channel_id=1, source_target_pairs={{0,4},{4,8},{8,12},{1,5},{5,9},{9,13},{2,6},{6,10},{10,14},{3,7},{... | collective-permute-start | bytes 1572872 | tf_op jit(solution)/shard_map/ppermute | solution.py:14
  99.4 19.4 %collective-permute-start.8 = (bf16[256,1024]{0,1:T(8,128)(2,1)}, bf16[256,1024]{0,1:T(8,128)(2,1)S(1)}, u32[]{:S(2)}, u32[]{:S(2)}) collective-permute-start(bf16[256,1024]{0,1:T(8,128)(2,1)} %bitcast.159), channel_id=1, source_target_pairs={{0,4},{4,8},{8,12},{1,5},{5,9},{9,13},{2,6},{6,10},{10,14},{3,7},{... | collective-permute-start | bytes 1572872 | tf_op jit(solution)/shard_map/ppermute | solution.py:14
  104.1 30.7 %collective-permute-start.4 = (bf16[512,1024]{1,0:T(8,128)(2,1)}, bf16[512,1024]{1,0:T(8,128)(2,1)}, u32[]{:S(2)}, u32[]{:S(2)}) collective-permute-start(bf16[512,1024]{1,0:T(8,128)(2,1)} %convolution_convert_fusion), channel_id=1, source_target_pairs={{0,2},{2,0},{1,3},{3,1},{4,6},{6,4},{5,7},{7,5},{8,10},{10,8},{9,1... | collective-permute-start | bytes 3145736 | tf_op jit(solution)/shard_map/ppermute | solution.py:91
  121.1 8.5 %collective-permute-start.9 = (bf16[1,9,128,128]{3,2,1,0:T(8,128)(2,1)S(1)}, bf16[1,9,128,128]{3,2,1,0:T(8,128)(2,1)S(1)}, u32[]{:S(2)}, u32[]{:S(2)}) collective-permute-start(bf16[1,9,128,128]{3,2,1,0:T(8,128)(2,1)S(1)} %fusion.54), channel_id=1, source_target_pairs={{0,4},{4,8},{8,12},{1,5},{5,9},{9,13},{2,6},{6,10},{10,14},{3,7},{... | collective-permute-start | bytes 884744 | tf_op jit(solution)/shard_map/ppermute | solution.py:14
  127.0 45.3 %collective-permute-start.12 = (bf16[1024,1024]{1,0:T(8,128)(2,1)}, bf16[1024,1024]{1,0:T(8,128)(2,1)}, u32[]{:S(2)}, u32[]{:S(2)}) collective-permute-start(bf16[1024,1024]{1,0:T(8,128)(2,1)} %param.11), channel_id=1, source_target_pairs={{0,2},{2,0},{1,3},{3,1},{4,6},{6,4},{5,7},{7,5},{8,10},{10,8},{9,1... | collective-permute-start | bytes 6291464 | tf_op jit(solution)/shard_map/ppermute | solution.py:193
  130.5 19.0 %collective-permute-start.10 = (bf16[1,9,128,128]{3,2,1,0:T(8,128)(2,1)}, bf16[1,9,128,128]{3,2,1,0:T(8,128)(2,1)S(1)}, u32[]{:S(2)}, u32[]{:S(2)}) collective-permute-start(bf16[1,9,128,128]{3,2,1,0:T(8,128)(2,1)} %fusion.56), channel_id=1, source_target_pairs={{0,4},{4,8},{8,12},{1,5},{5,9},{9,13},{2,6},{6,10},{10,14},{3,7},{... | collective-permute-start | bytes 884744 | tf_op jit(solution)/shard_map/ppermute | solution.py:14
  142.2 2.2 %copy-start.13 = (bf16[1,512,1024]{1,2,0:T(8,128)(2,1)S(1)}, bf16[1,512,1024]{1,2,0:T(8,128)(2,1)}, u32[]{:S(2)}) copy-start(bf16[1,512,1024]{1,2,0:T(8,128)(2,1)} %maximum_bitcast_fusion) | copy-start | bytes 3145732
  142.3 2.2 %copy-start.16 = (pred[512,512]{0,1:T(8,128)(4,1)S(1)}, pred[512,512]{0,1:T(8,128)(4,1)}, u32[]{:S(2)}) copy-start(pred[512,512]{0,1:T(8,128)(4,1)} %fusion.47) | copy-start | bytes 786436
  144.5 2.5 %copy-start.14 = (bf16[1,512,1024]{1,2,0:T(8,128)(2,1)S(1)}, bf16[1,512,1024]{1,2,0:T(8,128)(2,1)}, u32[]{:S(2)}) copy-start(bf16[1,512,1024]{1,2,0:T(8,128)(2,1)} %maximum_bitcast_fusion.1) | copy-start | bytes 3145732
  147.0 6.4 %copy-start.10 = (bf16[512,8,128]{2,0,1:T(8,128)(2,1)S(1)}, bf16[512,8,128]{2,0,1:T(8,128)(2,1)}, u32[]{:S(2)}) copy-start(bf16[512,8,128]{2,0,1:T(8,128)(2,1)} %copy_dynamic-update-slice_fusion) | copy-start | bytes 3145732
  149.7 7.7 %collective-permute-start.11 = (bf16[1,9,128,128]{3,2,1,0:T(8,128)(2,1)S(1)}, bf16[1,9,128,128]{3,2,1,0:T(8,128)(2,1)S(1)}, u32[]{:S(2)}, u32[]{:S(2)}) collective-permute-start(bf16[1,9,128,128]{3,2,1,0:T(8,128)(2,1)S(1)} %fusion.58), channel_id=1, source_target_pairs={{0,4},{4,8},{8,12},{1,5},{5,9},{9,13},{2,6},{6,10},{10,14},{3,7},{... | collective-permute-start | bytes 884744 | tf_op jit(solution)/shard_map/ppermute | solution.py:14
  157.5 14.8 %copy-start.20 = (bf16[1024,1024]{1,0:T(8,128)(2,1)S(1)}, bf16[1024,1024]{1,0:T(8,128)(2,1)}, u32[]{:S(2)}) copy-start(bf16[1024,1024]{1,0:T(8,128)(2,1)} %param.11) | copy-start | bytes 6291460
  158.1 18.1 %copy-start.21 = (bf16[1,512,8,128]{1,3,2,0:T(8,128)(2,1)}, bf16[1,512,8,128]{1,3,2,0:T(8,128)(2,1)S(1)}, u32[]{:S(2)}) copy-start(bf16[1,512,8,128]{1,3,2,0:T(8,128)(2,1)S(1)} %fusion.25) | copy-start | bytes 3145732
  176.2 3.4 %collective-permute-start.13 = (bf16[512,1024]{1,0:T(8,128)(2,1)}, bf16[512,1024]{1,0:T(8,128)(2,1)S(1)}, u32[]{:S(2)}, u32[]{:S(2)}) collective-permute-start(bf16[512,1024]{1,0:T(8,128)(2,1)} %fusion.32), channel_id=1, source_target_pairs={{0,1},{1,0},{2,3},{3,2},{4,5},{5,4},{6,7},{7,6},{8,9},{9,8},{10,11... | collective-permute-start | bytes 3145736 | tf_op jit(solution)/shard_map/ppermute | solution.py:217
  176.2 3.4 %copy-start.3 = (bf16[1,512,2048]{2,1,0:T(8,128)(2,1)S(1)}, bf16[1,512,2048]{2,1,0:T(8,128)(2,1)}, u32[]{:S(2)}) copy-start(bf16[1,512,2048]{2,1,0:T(8,128)(2,1)} %param.7) | copy-start | bytes 6291460
  176.2 5.0 %copy-start.1 = (bf16[1024,1024]{1,0:T(8,128)(2,1)S(1)}, bf16[1024,1024]{1,0:T(8,128)(2,1)}, u32[]{:S(2)}) copy-start(bf16[1024,1024]{1,0:T(8,128)(2,1)} %param.9) | copy-start | bytes 6291460
  (4 other events, 6.5 us)

commit v15 on v14

--- a/solution.py
+++ b/solution.py
@@ -187,10 +187,21 @@
     attended = (window + read).astype(jnp.bfloat16).reshape(count, inner_here)
     w_output = lax.optimization_barrier((w_output, pair_raw))[0]
     out_block = w_output.shape[1]
+    half_rows = w_output.shape[0] // 2
     from_ranks = jnp.stack(
         [w_output]
         + [
-            lax.ppermute(w_output, "wloop", [(source, (source + step) % ways) for source in range(ways)])
+            jnp.concatenate(
+                [
+                    lax.ppermute(
+                        w_output[half * half_rows : (half + 1) * half_rows],
+                        "wloop",
+                        [(source, (source + step) % ways) for source in range(ways)],
+                    )
+                    for half in range(2)
+                ],
+                axis=0,
+            )
             for step in range(1, ways)
         ]
     )

time: 182 us -> 185 us (1.016)
  local copies, waits for them, and re-layouts: 20.4 us -> 23.4 us
  waiting for transfers between devices: 64.4 us -> 61.6 us
  other arithmetic: 22.7 us -> 24.6 us
    ppermute x3, waiting for transfers between devices: 29.2 us -> 25.3 us  [gathered_sum(): lax.ppermute(outgoing, 'wloop', [(source, (source - step) % ways) for sou...]
    ppermute x1 -> x2, waiting for transfers between devices: 14.2 us -> 17.3 us  [shards(): lax.ppermute(w_output[half * half_rows:(half + 1) * half_rows], 'wloop',...]
    dot_general x2, matrix products: 7.27 us -> 9.98 us  [shards(): jnp.einsum('td,dje->jte', rows, w_keyvalue, preferred_element_type=jnp.fl...]
    ppermute x7, waiting for transfers between devices: 9.36 us -> 7.38 us  [shifted(): lax.ppermute(value, axis, [(source, source + steps) for source in range(i...]
    unnamed x55 -> x59, local copies, waits for them, and re-layouts: 9.41 us -> 10.4 us
  transfers between devices with their start and end apart: 14 -> 15, of which waited for: 9 -> 8; matrix products, arithmetic and copies ran while one was open for 30% -> 31% of each run, Pallas kernels for 0% -> 0%
where the time goes in v15:
time: 185 us; the launch traced here: 184 us
  waiting for transfers between devices  61.6 us (33%)
  starting transfers between devices  38 us (21%)
  matrix products  35 us (19%)
  other arithmetic  24.6 us (13%)
  local copies, waits for them, and re-layouts  23.4 us (13%)
    ppermute x7, starting transfers between devices, shifted(): lax.ppermute(value, axis, [(source, source + steps) for source in range(i...  27.9 us
    ppermute x3, waiting for transfers between devices, gathered_sum(): lax.ppermute(outgoing, 'wloop', [(source, (source - step) % ways) for sou...  25.3 us
    ppermute x2, waiting for transfers between devices, shards(): lax.ppermute(w_output[half * half_rows:(half + 1) * half_rows], 'wloop',...  17.3 us
    unnamed x59, local copies, waits for them, and re-layouts  10.4 us
    dot_general x2, matrix products, shards(): jnp.einsum('td,dje->jte', rows, w_keyvalue, preferred_element_type=jnp.fl...  9.98 us
    ppermute x1, waiting for transfers between devices, shards(): lax.ppermute(part, 'wloop', [(source, (source + step) % ways) for source...  9.8 us
    ppermute x7, waiting for transfers between devices, shifted(): lax.ppermute(value, axis, [(source, source + steps) for source in range(i...  7.38 us
    dot_general x2, matrix products, output_share(): jnp.dot(attended, lax.dynamic_index_in_dim(from_ranks, (me - rank) % ways...  5.74 us
  transfers between devices with their start and end apart: 15, of which 8 were waited for; matrix products, arithmetic and copies ran while one was open for 31% of the time, Pallas kernels for 0%

profile of v15, /device:TPU:0, one launch (start us, length us, event | category | flops | bytes accessed | tf_op | source)
XLA Modules:
  0.0 183.9 jit_solution(8101814504640217386)
XLA Ops:
  0.0 2.2 %fusion.2 = f32[512]{0:T(512)S(1)} fusion(bf16[1,512,2048]{2,1,0:T(8,128)(2,1)} %param.7), kind=kLoop, calls=%fused_computation.13 | loop fusion | flops 3145216 | bytes 2099200 | tf_op jit(solution)/shard_map/reduce_sum | solution.py:18
  4.6 3.0 %collective-permute-start = (bf16[256,1024]{1,0:T(8,128)(2,1)S(1)}, bf16[256,1024]{1,0:T(8,128)(2,1)S(1)}, u32[]{:S(2)}, u32[]{:S(2)}) collective-permute-start(bf16[256,1024]{1,0:T(8,128)(2,1)S(1)} %dynamic-slice_bitcast_fusion), channel_id=1, source_target_pairs={{0,2},{2,0},{1,3},{3,1},{4,6},{6,4},{5,7},{7,5},{8,10},{10,8},{9,1... | collective-permute-start | bytes 1572872 | tf_op jit(solution)/shard_map/ppermute | solution.py:77
  9.7 9.8 %collective-permute-done = bf16[256,1024]{1,0:T(8,128)(2,1)S(1)} collective-permute-done((bf16[256,1024]{1,0:T(8,128)(2,1)S(1)}, bf16[256,1024]{1,0:T(8,128)(2,1)S(1)}, u32[]{:S(2)}, u32[]{:S(2)}) %collective-permute-start) | collective-permute-done | bytes 524320 | tf_op jit(solution)/shard_map/ppermute | solution.py:77
  19.6 1.8 collective-permute-done.1
  22.5 1.8 gather_fusion
  24.6 5.0 %convert_bitcast_fusion = bf16[2,512,1024]{2,1,0:T(8,128)(2,1)S(1)} fusion(bf16[1024,2,1024]{2,1,0:T(2,128)(2,1)} %param.10, bf16[512,1024]{1,0:T(8,128)(2,1)S(1)} %bitcast_select_fusion), kind=kOutput, calls=%fused_computation.41 | convolution fusion | flops 2148532224 | bytes 7340032 | tf_op jit(solution)/shard_map/td,dje->jte/dot_general | solution.py:99
  34.2 5.0 %fusion.11 = f32[2,512,1024]{2,1,0:T(8,128)S(1)} fusion(bf16[1024,2,1024]{2,1,0:T(2,128)(2,1)} %param.10, bf16[1,512,2048]{2,1,0:T(8,128)(2,1)} %copy-done.7, s32[]{:T(128)S(6)} %select_n.91), kind=kOutput, calls=%fused_computation.23 | convolution fusion | flops 2147483648 | bytes 9437188 | tf_op jit(solution)/shard_map/td,dje->jte/dot_general | solution.py:99
  39.2 17.4 %collective-permute-done.2 = bf16[2,256,1024]{2,1,0:T(8,128)(2,1)S(1)} collective-permute-done((bf16[2,256,1024]{2,1,0:T(8,128)(2,1)}, bf16[2,256,1024]{2,1,0:T(8,128)(2,1)S(1)}, u32[]{:S(2)}, u32[]{:S(2)}) %collective-permute-start.2) | collective-permute-done | bytes 1048608 | tf_op jit(solution)/shard_map/ppermute | solution.py:91
  63.5 2.3 %convolution_convert_fusion = bf16[512,1024]{1,0:T(8,128)(2,1)} fusion(bf16[512,1024]{1,0:T(8,128)(2,1)S(1)} %copy-done.15, bf16[1024,1024]{1,0:T(8,128)(2,1)S(1)} %copy-done), kind=kOutput, calls=%fused_computation.48 | convolution fusion | flops 1074266112 | bytes 4194304 | tf_op jit(solution)/shard_map/dot_general | solution.py:125
  66.9 4.3 %collective-permute-start.5 = (bf16[256,1024]{0,1:T(8,128)(2,1)}, bf16[256,1024]{0,1:T(8,128)(2,1)}, u32[]{:S(2)}, u32[]{:S(2)}) collective-permute-start(bf16[256,1024]{0,1:T(8,128)(2,1)} %bitcast.161), channel_id=1, source_target_pairs={{0,4},{4,8},{8,12},{1,5},{5,9},{9,13},{2,6},{6,10},{10,14},{3,7},{... | collective-permute-start | bytes 1572872 | tf_op jit(solution)/shard_map/ppermute | solution.py:14
  72.3 3.5 %collective-permute-start.7 = (bf16[256,1024]{0,1:T(8,128)(2,1)}, bf16[256,1024]{0,1:T(8,128)(2,1)}, u32[]{:S(2)}, u32[]{:S(2)}) collective-permute-start(bf16[256,1024]{0,1:T(8,128)(2,1)} %bitcast.160), channel_id=1, source_target_pairs={{0,4},{4,8},{8,12},{1,5},{5,9},{9,13},{2,6},{6,10},{10,14},{3,7},{... | collective-permute-start | bytes 1572872 | tf_op jit(solution)/shard_map/ppermute | solution.py:14
  77.6 8.0 %collective-permute-done.3 = bf16[2,256,1024]{2,1,0:T(8,128)(2,1)} collective-permute-done((bf16[2,256,1024]{2,1,0:T(8,128)(2,1)}, bf16[2,256,1024]{2,1,0:T(8,128)(2,1)}, u32[]{:S(2)}, u32[]{:S(2)}) %collective-permute-start.3) | collective-permute-done | bytes 1048608 | tf_op jit(solution)/shard_map/ppermute | solution.py:91
  85.6 2.2 %slice_add_fusion = f32[2,256,1024]{2,1,0:T(8,128)S(1)} fusion(f32[2,512,1024]{2,1,0:T(8,128)} %copy-done.6, bf16[2,256,1024]{2,1,0:T(8,128)(2,1)} %collective-permute-done.3), kind=kLoop, calls=%fused_computation.32 | loop fusion | flops 1048576 | bytes 5242880 | tf_op jit(solution)/shard_map/add | solution.py:91
  91.7 2.0 %copy.90 = bf16[256,8,128]{0,2,1:T(8,128)(2,1)} copy(bf16[256,8,128]{2,0,1:T(8,128)(2,1)} %fusion.44) | data formatting | bytes 1048576 | tf_op jit(solution)/shard_map/optimization_barrier | solution.py:112
  93.7 4.6 %collective-permute-start.6 = (bf16[256,1024]{0,1:T(8,128)(2,1)}, bf16[256,1024]{0,1:T(8,128)(2,1)}, u32[]{:S(2)}, u32[]{:S(2)}) collective-permute-start(bf16[256,1024]{0,1:T(8,128)(2,1)} %bitcast.163), channel_id=1, source_target_pairs={{0,4},{4,8},{8,12},{1,5},{5,9},{9,13},{2,6},{6,10},{10,14},{3,7},{... | collective-permute-start | bytes 1572872 | tf_op jit(solution)/shard_map/ppermute | solution.py:14
  99.4 2.8 %collective-permute-start.8 = (bf16[256,1024]{0,1:T(8,128)(2,1)}, bf16[256,1024]{0,1:T(8,128)(2,1)S(1)}, u32[]{:S(2)}, u32[]{:S(2)}) collective-permute-start(bf16[256,1024]{0,1:T(8,128)(2,1)} %bitcast.162), channel_id=1, source_target_pairs={{0,4},{4,8},{8,12},{1,5},{5,9},{9,13},{2,6},{6,10},{10,14},{3,7},{... | collective-permute-start | bytes 1572872 | tf_op jit(solution)/shard_map/ppermute | solution.py:14
  105.5 4.0 %fusion.36 = f32[1,8,128,128]{3,2,1,0:T(8,128)S(1)} fusion(bf16[512,8,128]{2,0,1:T(8,128)(2,1)} %copy_dynamic-update-slice_fusion, bf16[512,8,128]{2,0,1:T(8,128)(2,1)} %constant_dynamic-update-slice_fusion, f32[512,8]{0,1:T(8,128)S(1)} %fusion.67), kind=kOutput, calls=%fused_computation.50 | convolution fusion | flops 806354944 | bytes 2637824 | tf_op jit(solution)/shard_map/bht,bthd,bthe->bhde/dot_general | solution.py:140
  110.0 2.4 %maximum_bitcast_fusion.1 = bf16[1,512,1024]{1,2,0:T(8,128)(2,1)} fusion(bf16[256,1024]{0,1:T(8,128)(2,1)} %collective-permute-done.6, bf16[256,1024]{0,1:T(8,128)(2,1)} %collective-permute-done.5), kind=kLoop, calls=%fused_computation.57 | loop fusion | flops 2097152 | bytes 2097152 | tf_op jit(solution)/shard_map/reshape | solution.py:130
  112.4 6.3 %collective-permute-done.8 = bf16[256,1024]{0,1:T(8,128)(2,1)S(1)} collective-permute-done((bf16[256,1024]{0,1:T(8,128)(2,1)}, bf16[256,1024]{0,1:T(8,128)(2,1)S(1)}, u32[]{:S(2)}, u32[]{:S(2)}) %collective-permute-start.8) | collective-permute-done | bytes 524320 | tf_op jit(solution)/shard_map/ppermute | solution.py:14
  118.7 2.2 %maximum_bitcast_fusion.2 = bf16[1,512,1024]{1,2,0:T(8,128)(2,1)} fusion(bf16[256,1024]{0,1:T(8,128)(2,1)S(1)} %collective-permute-done.8, bf16[256,1024]{0,1:T(8,128)(2,1)} %collective-permute-done.7), kind=kLoop, calls=%fused_computation.58 | loop fusion | flops 2097152 | bytes 2097152 | tf_op jit(solution)/shard_map/reshape | solution.py:131
  121.0 4.4 %collective-permute-start.9 = (bf16[1,9,128,128]{3,2,1,0:T(8,128)(2,1)S(1)}, bf16[1,9,128,128]{3,2,1,0:T(8,128)(2,1)S(1)}, u32[]{:S(2)}, u32[]{:S(2)}) collective-permute-start(bf16[1,9,128,128]{3,2,1,0:T(8,128)(2,1)S(1)} %fusion.54), channel_id=1, source_target_pairs={{0,4},{4,8},{8,12},{1,5},{5,9},{9,13},{2,6},{6,10},{10,14},{3,7},{... | collective-permute-start | bytes 884744 | tf_op jit(solution)/shard_map/ppermute | solution.py:14
  130.5 4.6 %collective-permute-start.10 = (bf16[1,9,128,128]{3,2,1,0:T(8,128)(2,1)}, bf16[1,9,128,128]{3,2,1,0:T(8,128)(2,1)S(1)}, u32[]{:S(2)}, u32[]{:S(2)}) collective-permute-start(bf16[1,9,128,128]{3,2,1,0:T(8,128)(2,1)} %fusion.56), channel_id=1, source_target_pairs={{0,4},{4,8},{8,12},{1,5},{5,9},{9,13},{2,6},{6,10},{10,14},{3,7},{... | collective-permute-start | bytes 884744 | tf_op jit(solution)/shard_map/ppermute | solution.py:14
  135.2 2.6 %multiply_bitcast_fusion = (f32[64,8,8,128]{3,1,2,0:T(8,128)S(1)}, f32[64,8,8,128]{3,2,1,0:T(8,128)}) fusion(bf16[512,1024]{1,0:T(8,128)(2,1)S(1)} %collective-permute-done.4, bf16[1024,1024]{1,0:T(8,128)(2,1)S(1)} %copy-done, bf16[1,512,2048]{2,1,0:T(8,128)(2,1)S(1)} %copy-done.8, s32[]{:T(128)S(6)} %select_n.91), kind=kOutput, calls=%fused_computation.45 | convolution fusion | flops 1075314688 | bytes 8388612 | tf_op jit(solution)/shard_map/dot_general | solution.py:125
  139.0 2.0 %fusion.22 = bf16[512,8,128]{2,0,1:T(8,128)(2,1)S(1)} fusion(f32[64,8,8,128]{3,2,1,0:T(8,128)} %get-tuple-element.30, f32[512,8]{0,1:T(8,128)S(1)} %add_rsqrt_fusion), kind=kLoop, calls=%fused_computation.31 | loop fusion | flops 1048576 | bytes 3162112 | tf_op jit(solution)/shard_map/convert_element_type | solution.py:132
  141.1 2.2 %fusion = (f32[8,512]{1,0:T(8,128)S(1)}, f32[8,512,512]{1,2,0:T(8,128)S(1)}) fusion(pred[512,512]{0,1:T(8,128)(4,1)S(1)} %copy-done.18, bf16[512,8,128]{2,0,1:T(8,128)(2,1)S(1)} %fusion.22, bf16[512,8,128]{2,0,1:T(8,128)(2,1)S(1)} %copy-done.9), kind=kOutput, calls=%fused_computation.5 | convolution fusion | flops 543158272 | bytes 10764288 | tf_op jit(solution)/shard_map/bihd,bjhd->bhij/dot_general | solution.py:23
  143.3 2.5 %fusion.1 = (f32[8,512]{1,0:T(8,128)S(1)}, f32[8,512,512]{1,2,0:T(8,128)S(1)}) fusion(pred[512,512]{0,1:T(8,128)(4,1)S(1)} %copy-done.19, bf16[512,8,128]{2,0,1:T(8,128)(2,1)S(1)} %fusion.22, bf16[512,8,128]{0,2,1:T(8,128)(2,1)S(1)} %bitcast.158), kind=kOutput, calls=%fused_computation.6 | convolution fusion | flops 543158272 | bytes 10764288 | tf_op jit(solution)/shard_map/bihd,bjhd->bhij/dot_general | solution.py:27
  145.8 2.4 %fusion.6 = f32[8,128,512]{2,1,0:T(8,128)S(1)} fusion(bf16[512,8,128]{0,2,1:T(8,128)(2,1)S(1)} %bitcast.159, f32[8,512,512]{1,2,0:T(8,128)S(1)} %get-tuple-element.38, f32[8,512]{1,0:T(8,128)S(1)} %add.181, pred[512,512]{0,1:T(8,128)(4,1)S(1)} %copy-done.19), kind=kOutput, calls=%fused_computation.18 | convolution fusion | flops 545259520 | bytes 11812864 | tf_op jit(solution)/shard_map/bhij,bjhd->bihd/dot_general | solution.py:40
  148.5 3.7 %collective-permute-start.11 = (bf16[1,9,128,128]{3,2,1,0:T(8,128)(2,1)S(1)}, bf16[1,9,128,128]{3,2,1,0:T(8,128)(2,1)S(1)}, u32[]{:S(2)}, u32[]{:S(2)}) collective-permute-start(bf16[1,9,128,128]{3,2,1,0:T(8,128)(2,1)S(1)} %fusion.58), channel_id=1, source_target_pairs={{0,4},{4,8},{8,12},{1,5},{5,9},{9,13},{2,6},{6,10},{10,14},{3,7},{... | collective-permute-start | bytes 884744 | tf_op jit(solution)/shard_map/ppermute | solution.py:14
  152.2 2.6 %fusion.5 = f32[8,128,512]{2,1,0:T(8,128)S(1)} fusion(bf16[512,8,128]{2,0,1:T(8,128)(2,1)S(1)} %copy-done.10, f32[8,512,512]{1,2,0:T(8,128)S(1)} %get-tuple-element.36, f32[8,512]{1,0:T(8,128)S(1)} %add.181, pred[512,512]{0,1:T(8,128)(4,1)S(1)} %copy-done.18), kind=kOutput, calls=%fused_computation.17 | convolution fusion | flops 545259520 | bytes 11812864 | tf_op jit(solution)/shard_map/bhij,bjhd->bihd/dot_general | solution.py:38
  154.8 17.3 %collective-permute-done.13 = bf16[512,1024]{1,0:T(8,128)(2,1)} collective-permute-done((bf16[512,1024]{1,0:T(8,128)(2,1)}, bf16[512,1024]{1,0:T(8,128)(2,1)}, u32[]{:S(2)}, u32[]{:S(2)}) %collective-permute-start.13) | collective-permute-done | bytes 1048608 | tf_op jit(solution)/shard_map/ppermute | solution.py:196
  176.6 2.4 %fusion.32 = bf16[512,1024]{1,0:T(8,128)(2,1)} fusion(bf16[512,1024]{0,1:T(8,128)(2,1)S(1)} %bitcast.172, s32[]{:T(128)S(6)} %select_n.108, bf16[1,1024,1024]{2,1,0:T(8,128)(2,1)S(1)} %bitcast.154, bf16[1,1024,1024]{2,1,0:T(8,128)(2,1)S(1)} %maximum_bitcast_fusion), kind=kOutput, calls=%fused_computation.47 | convolution fusion | flops 1075314688 | bytes 6291460 | tf_op jit(solution)/shard_map/dot_general | solution.py:219
  178.9 3.4 %fusion.20 = f32[512,1024]{1,0:T(8,128)S(1)} fusion(bf16[512,1024]{0,1:T(8,128)(2,1)} %bitcast.173, s32[]{:T(128)S(6)} %select_n.105, bf16[1,1024,1024]{2,1,0:T(8,128)(2,1)} %bitcast.153, bf16[1,1024,1024]{2,1,0:T(8,128)(2,1)} %copy-done.13), kind=kOutput, calls=%fused_computation.29 | convolution fusion | flops 1074790400 | bytes 7340036 | tf_op jit(solution)/shard_map/dot_general | solution.py:219
  (129 shorter events, 42.0 us)
Async XLA Ops:
  0.0 63.5 %copy-start = (bf16[1024,1024]{1,0:T(8,128)(2,1)S(1)}, bf16[1024,1024]{1,0:T(8,128)(2,1)}, u32[]{:S(2)}) copy-start(bf16[1024,1024]{1,0:T(8,128)(2,1)} %param.9) | copy-start | bytes 6291460
  0.0 2.4 %copy-start.2 = (bf16[1,512,2048]{2,1,0:T(8,128)(2,1)S(1)}, bf16[1,512,2048]{2,1,0:T(8,128)(2,1)}, u32[]{:S(2)}) copy-start(bf16[1,512,2048]{2,1,0:T(8,128)(2,1)} %param.7) | copy-start | bytes 6291460
  2.4 5.3 %copy-start.20 = (f32[1,8,512]{2,1,0:T(8,128)S(1)}, f32[1,8,512]{2,1,0:T(8,128)}, u32[]{:S(2)}) copy-start(f32[1,8,512]{2,1,0:T(8,128)} %param.12) | copy-start | bytes 49156
  4.6 15.0 %collective-permute-start = (bf16[256,1024]{1,0:T(8,128)(2,1)S(1)}, bf16[256,1024]{1,0:T(8,128)(2,1)S(1)}, u32[]{:S(2)}, u32[]{:S(2)}) collective-permute-start(bf16[256,1024]{1,0:T(8,128)(2,1)S(1)} %dynamic-slice_bitcast_fusion), channel_id=1, source_target_pairs={{0,2},{2,0},{1,3},{3,1},{4,6},{6,4},{5,7},{7,5},{8,10},{10,8},{9,1... | collective-permute-start | bytes 1572872 | tf_op jit(solution)/shard_map/ppermute | solution.py:77
  19.5 1.9 %collective-permute-start.1 = (bf16[256,1024]{1,0:T(8,128)(2,1)S(1)}, bf16[256,1024]{1,0:T(8,128)(2,1)S(1)}, u32[]{:S(2)}, u32[]{:S(2)}) collective-permute-start(bf16[256,1024]{1,0:T(8,128)(2,1)S(1)} %collective-permute-done), channel_id=1, source_target_pairs={{0,1},{1,0},{2,3},{3,2},{4,5},{5,4},{6,7},{7,6},{8,9},{9,8},{10,11... | collective-permute-start | bytes 1572872 | tf_op jit(solution)/shard_map/ppermute | solution.py:67
  24.6 5.0 %copy-start.14 = (bf16[512,1024]{1,0:T(8,128)(2,1)}, bf16[512,1024]{1,0:T(8,128)(2,1)S(1)}, u32[]{:S(2)}) copy-start(bf16[512,1024]{1,0:T(8,128)(2,1)S(1)} %bitcast_select_fusion) | copy-start | bytes 3145732
  31.1 25.4 %collective-permute-start.2 = (bf16[2,256,1024]{2,1,0:T(8,128)(2,1)}, bf16[2,256,1024]{2,1,0:T(8,128)(2,1)S(1)}, u32[]{:S(2)}, u32[]{:S(2)}) collective-permute-start(bf16[2,256,1024]{2,1,0:T(8,128)(2,1)} %get-tuple-element.34), channel_id=1, source_target_pairs={{0,2},{2,0},{1,3},{3,1},{4,6},{6,4},{5,7},{7,5},{8,10},{10,8},{9,1... | collective-permute-start | bytes 3145736 | tf_op jit(solution)/shard_map/ppermute | solution.py:91
  39.2 17.7 %copy-start.6 = (f32[2,512,1024]{2,1,0:T(8,128)}, f32[2,512,1024]{2,1,0:T(8,128)S(1)}, u32[]{:S(2)}) copy-start(f32[2,512,1024]{2,1,0:T(8,128)S(1)} %fusion.11) | copy-start | bytes 12582916
  58.5 5.0 %copy-start.15 = (bf16[512,1024]{1,0:T(8,128)(2,1)S(1)}, bf16[512,1024]{1,0:T(8,128)(2,1)}, u32[]{:S(2)}) copy-start(bf16[512,1024]{1,0:T(8,128)(2,1)} %copy-done.14) | copy-start | bytes 3145732
  60.8 24.7 %collective-permute-start.3 = (bf16[2,256,1024]{2,1,0:T(8,128)(2,1)}, bf16[2,256,1024]{2,1,0:T(8,128)(2,1)}, u32[]{:S(2)}, u32[]{:S(2)}) collective-permute-start(bf16[2,256,1024]{2,1,0:T(8,128)(2,1)} %get-tuple-element.17), channel_id=1, source_target_pairs={{0,2},{2,0},{1,3},{3,1},{4,6},{6,4},{5,7},{7,5},{8,10},{10,8},{9,1... | collective-permute-start | bytes 3145736 | tf_op jit(solution)/shard_map/ppermute | solution.py:91
  63.5 2.3 %copy-start.4 = (bf16[256,8,128]{2,0,1:T(8,128)(2,1)S(1)}, bf16[256,8,128]{2,0,1:T(8,128)(2,1)}, u32[]{:S(2)}) copy-start(bf16[256,8,128]{2,0,1:T(8,128)(2,1)} %fusion.45) | copy-start | bytes 1572868
  66.9 42.7 %collective-permute-start.5 = (bf16[256,1024]{0,1:T(8,128)(2,1)}, bf16[256,1024]{0,1:T(8,128)(2,1)}, u32[]{:S(2)}, u32[]{:S(2)}) collective-permute-start(bf16[256,1024]{0,1:T(8,128)(2,1)} %bitcast.161), channel_id=1, source_target_pairs={{0,4},{4,8},{8,12},{1,5},{5,9},{9,13},{2,6},{6,10},{10,14},{3,7},{... | collective-permute-start | bytes 1572872 | tf_op jit(solution)/shard_map/ppermute | solution.py:14
  72.3 40.1 %collective-permute-start.7 = (bf16[256,1024]{0,1:T(8,128)(2,1)}, bf16[256,1024]{0,1:T(8,128)(2,1)}, u32[]{:S(2)}, u32[]{:S(2)}) collective-permute-start(bf16[256,1024]{0,1:T(8,128)(2,1)} %bitcast.160), channel_id=1, source_target_pairs={{0,4},{4,8},{8,12},{1,5},{5,9},{9,13},{2,6},{6,10},{10,14},{3,7},{... | collective-permute-start | bytes 1572872 | tf_op jit(solution)/shard_map/ppermute | solution.py:14
  90.5 12.7 %copy-start.5 = (bf16[256,8,128]{2,0,1:T(8,128)(2,1)S(1)}, bf16[256,8,128]{2,0,1:T(8,128)(2,1)}, u32[]{:S(2)}) copy-start(bf16[256,8,128]{2,0,1:T(8,128)(2,1)} %fusion.44) | copy-start | bytes 1572868
  93.7 16.3 %collective-permute-start.6 = (bf16[256,1024]{0,1:T(8,128)(2,1)}, bf16[256,1024]{0,1:T(8,128)(2,1)}, u32[]{:S(2)}, u32[]{:S(2)}) collective-permute-start(bf16[256,1024]{0,1:T(8,128)(2,1)} %bitcast.163), channel_id=1, source_target_pairs={{0,4},{4,8},{8,12},{1,5},{5,9},{9,13},{2,6},{6,10},{10,14},{3,7},{... | collective-permute-start | bytes 1572872 | tf_op jit(solution)/shard_map/ppermute | solution.py:14
  99.4 4.6 %copy-start.22 = (bf16[512,1024]{1,0:T(8,128)(2,1)S(1)}, bf16[512,1024]{1,0:T(8,128)(2,1)}, u32[]{:S(2)}) copy-start(bf16[512,1024]{1,0:T(8,128)(2,1)} %convolution_convert_fusion) | copy-start | bytes 3145732
  99.4 19.3 %collective-permute-start.8 = (bf16[256,1024]{0,1:T(8,128)(2,1)}, bf16[256,1024]{0,1:T(8,128)(2,1)S(1)}, u32[]{:S(2)}, u32[]{:S(2)}) collective-permute-start(bf16[256,1024]{0,1:T(8,128)(2,1)} %bitcast.162), channel_id=1, source_target_pairs={{0,4},{4,8},{8,12},{1,5},{5,9},{9,13},{2,6},{6,10},{10,14},{3,7},{... | collective-permute-start | bytes 1572872 | tf_op jit(solution)/shard_map/ppermute | solution.py:14
  104.0 31.1 %collective-permute-start.4 = (bf16[512,1024]{1,0:T(8,128)(2,1)S(1)}, bf16[512,1024]{1,0:T(8,128)(2,1)S(1)}, u32[]{:S(2)}, u32[]{:S(2)}) collective-permute-start(bf16[512,1024]{1,0:T(8,128)(2,1)S(1)} %copy-done.22), channel_id=1, source_target_pairs={{0,2},{2,0},{1,3},{3,1},{4,6},{6,4},{5,7},{7,5},{8,10},{10,8},{9,1... | collective-permute-start | bytes 3145736 | tf_op jit(solution)/shard_map/ppermute | solution.py:91
  109.6 15.9 %copy-start.11 = (bf16[1024,1024]{1,0:T(8,128)(2,1)S(1)}, bf16[1024,1024]{1,0:T(8,128)(2,1)}, u32[]{:S(2)}) copy-start(bf16[1024,1024]{1,0:T(8,128)(2,1)} %param.11) | copy-start | bytes 6291460
  121.0 14.1 %copy-start.8 = (bf16[1,512,2048]{2,1,0:T(8,128)(2,1)S(1)}, bf16[1,512,2048]{2,1,0:T(8,128)(2,1)}, u32[]{:S(2)}) copy-start(bf16[1,512,2048]{2,1,0:T(8,128)(2,1)} %copy-done.7) | copy-start | bytes 6291460
  121.0 8.6 %collective-permute-start.9 = (bf16[1,9,128,128]{3,2,1,0:T(8,128)(2,1)S(1)}, bf16[1,9,128,128]{3,2,1,0:T(8,128)(2,1)S(1)}, u32[]{:S(2)}, u32[]{:S(2)}) collective-permute-start(bf16[1,9,128,128]{3,2,1,0:T(8,128)(2,1)S(1)} %fusion.54), channel_id=1, source_target_pairs={{0,4},{4,8},{8,12},{1,5},{5,9},{9,13},{2,6},{6,10},{10,14},{3,7},{... | collective-permute-start | bytes 884744 | tf_op jit(solution)/shard_map/ppermute | solution.py:14
  127.0 27.9 %collective-permute-start.12 = (bf16[512,1024]{1,0:T(8,128)(2,1)}, bf16[512,1024]{1,0:T(8,128)(2,1)}, u32[]{:S(2)}, u32[]{:S(2)}) collective-permute-start(bf16[512,1024]{1,0:T(8,128)(2,1)} %get-tuple-element.31), channel_id=1, source_target_pairs={{0,2},{2,0},{1,3},{3,1},{4,6},{6,4},{5,7},{7,5},{8,10},{10,8},{9,1... | collective-permute-start | bytes 3145736 | tf_op jit(solution)/shard_map/ppermute | solution.py:196
  128.5 43.6 %collective-permute-start.13 = (bf16[512,1024]{1,0:T(8,128)(2,1)}, bf16[512,1024]{1,0:T(8,128)(2,1)}, u32[]{:S(2)}, u32[]{:S(2)}) collective-permute-start(bf16[512,1024]{1,0:T(8,128)(2,1)} %get-tuple-element.32), channel_id=1, source_target_pairs={{0,2},{2,0},{1,3},{3,1},{4,6},{6,4},{5,7},{7,5},{8,10},{10,8},{9,1... | collective-permute-start | bytes 3145736 | tf_op jit(solution)/shard_map/ppermute | solution.py:196
  130.5 17.8 %collective-permute-start.10 = (bf16[1,9,128,128]{3,2,1,0:T(8,128)(2,1)}, bf16[1,9,128,128]{3,2,1,0:T(8,128)(2,1)S(1)}, u32[]{:S(2)}, u32[]{:S(2)}) collective-permute-start(bf16[1,9,128,128]{3,2,1,0:T(8,128)(2,1)} %fusion.56), channel_id=1, source_target_pairs={{0,4},{4,8},{8,12},{1,5},{5,9},{9,13},{2,6},{6,10},{10,14},{3,7},{... | collective-permute-start | bytes 884744 | tf_op jit(solution)/shard_map/ppermute | solution.py:14
  143.3 2.5 %copy-start.17 = (bf16[1,512,1024]{1,2,0:T(8,128)(2,1)S(1)}, bf16[1,512,1024]{1,2,0:T(8,128)(2,1)}, u32[]{:S(2)}) copy-start(bf16[1,512,1024]{1,2,0:T(8,128)(2,1)} %maximum_bitcast_fusion.2) | copy-start | bytes 3145732
  145.8 6.4 %copy-start.10 = (bf16[512,8,128]{2,0,1:T(8,128)(2,1)S(1)}, bf16[512,8,128]{2,0,1:T(8,128)(2,1)}, u32[]{:S(2)}) copy-start(bf16[512,8,128]{2,0,1:T(8,128)(2,1)} %copy_dynamic-update-slice_fusion) | copy-start | bytes 3145732
  148.5 25.4 %collective-permute-start.11 = (bf16[1,9,128,128]{3,2,1,0:T(8,128)(2,1)S(1)}, bf16[1,9,128,128]{3,2,1,0:T(8,128)(2,1)S(1)}, u32[]{:S(2)}, u32[]{:S(2)}) collective-permute-start(bf16[1,9,128,128]{3,2,1,0:T(8,128)(2,1)S(1)} %fusion.58), channel_id=1, source_target_pairs={{0,4},{4,8},{8,12},{1,5},{5,9},{9,13},{2,6},{6,10},{10,14},{3,7},{... | collective-permute-start | bytes 884744 | tf_op jit(solution)/shard_map/ppermute | solution.py:14
  173.9 2.6 %copy-start.12 = (bf16[1024,1024]{1,0:T(8,128)(2,1)S(1)}, bf16[1024,1024]{1,0:T(8,128)(2,1)}, u32[]{:S(2)}) copy-start(bf16[1024,1024]{1,0:T(8,128)(2,1)} %param.11) | copy-start | bytes 6291460
  174.6 4.3 %copy-start.23 = (bf16[1,512,8,128]{1,3,2,0:T(8,128)(2,1)}, bf16[1,512,8,128]{1,3,2,0:T(8,128)(2,1)S(1)}, u32[]{:S(2)}) copy-start(bf16[1,512,8,128]{1,3,2,0:T(8,128)(2,1)S(1)} %fusion.25) | copy-start | bytes 3145732
  178.9 3.4 %collective-permute-start.14 = (bf16[512,1024]{1,0:T(8,128)(2,1)}, bf16[512,1024]{1,0:T(8,128)(2,1)S(1)}, u32[]{:S(2)}, u32[]{:S(2)}) collective-permute-start(bf16[512,1024]{1,0:T(8,128)(2,1)} %fusion.32), channel_id=1, source_target_pairs={{0,1},{1,0},{2,3},{3,2},{4,5},{5,4},{6,7},{7,6},{8,9},{9,8},{10,11... | collective-permute-start | bytes 3145736 | tf_op jit(solution)/shard_map/ppermute | solution.py:228
  178.9 3.4 %copy-start.3 = (bf16[1,512,2048]{2,1,0:T(8,128)(2,1)S(1)}, bf16[1,512,2048]{2,1,0:T(8,128)(2,1)}, u32[]{:S(2)}) copy-start(bf16[1,512,2048]{2,1,0:T(8,128)(2,1)} %param.7) | copy-start | bytes 6291460
  178.9 5.0 %copy-start.1 = (bf16[1024,1024]{1,0:T(8,128)(2,1)S(1)}, bf16[1024,1024]{1,0:T(8,128)(2,1)}, u32[]{:S(2)}) copy-start(bf16[1024,1024]{1,0:T(8,128)(2,1)} %param.9) | copy-start | bytes 6291460
  (7 other events, 13.6 us)

commit v16 on v13

--- a/solution.py
+++ b/solution.py
@@ -82,17 +82,21 @@
             )
         )
 
+    arrived = []
+
     def gathered_sum(partials, after=None):
         total = partials[0]
         for step in range(1, ways):
             outgoing = partials[step].astype(jnp.bfloat16)
             if after is not None:
                 outgoing = lax.optimization_barrier((outgoing, after))[0]
-            total = total + lax.ppermute(
+            incoming = lax.ppermute(
                 outgoing,
                 "wloop",
                 [(source, (source - step) % ways) for source in range(ways)],
-            ).astype(jnp.float32)
+            )
+            arrived.append(incoming)
+            total = total + incoming.astype(jnp.float32)
         return total
 
     pair_raw = gathered_sum(
@@ -103,7 +107,7 @@
     )
     query_raw = gathered_sum(
         [jnp.dot(rows, w_query, preferred_element_type=jnp.float32) for rows in stacked],
-        after=pair_raw,
+        after=tuple(arrived),
     )
     lookup_vectors = rms_rows(pair_raw[0].reshape(trajs, span, heads_here, head_dim), 1e-06).astype(
         jnp.bfloat16
@@ -170,7 +174,7 @@
         scale,
     )
     attended = (window + read).astype(jnp.bfloat16).reshape(count, inner_here)
-    w_output = lax.optimization_barrier((w_output, pair_raw))[0]
+    w_output = lax.optimization_barrier((w_output, arrived[0]))[0]
     out_block = w_output.shape[1]
     from_ranks = jnp.stack(
         [w_output]

time: 177 us -> 179 us (1.011)
  waiting for transfers between devices: 63 us -> 67 us
  local copies, waits for them, and re-layouts: 22.3 us -> 18.5 us
  other arithmetic: 18.2 us -> 20.6 us
    ppermute x5, waiting for transfers between devices: 11.1 us -> 16 us  [shifted(): lax.ppermute(value, axis, [(source, source + steps) for source in range(i...]
    unnamed x1 -> x2, other arithmetic: 0.23 us -> 3.25 us
    mul x2, local copies, waits for them, and re-layouts: 4.54 us -> 2.07 us  [rms_rows(): values * lax.rsqrt(jnp.mean(values * values, axis=-1, keepdims=True) + eps)]
    unnamed x53 -> x47, local copies, waits for them, and re-layouts: 7.06 us -> 7.12 us
  transfers between devices with their start and end apart: 11 -> 11, of which waited for: 4 -> 5; matrix products, arithmetic and copies ran while one was open for 33% -> 31% of each run, Pallas kernels for 0% -> 0%
where the time goes in v16:
time: 179 us; the launch traced here: 178 us
  waiting for transfers between devices  67 us (37%)
  matrix products  43.7 us (24%)
  starting transfers between devices  27 us (15%)
  other arithmetic  20.6 us (12%)
  local copies, waits for them, and re-layouts  18.5 us (10%)
    ppermute x2, waiting for transfers between devices, gathered_sum(): lax.ppermute(outgoing, 'wloop', [(source, (source - step) % ways) for sou...  37.3 us
    ppermute x5, starting transfers between devices, shifted(): lax.ppermute(value, axis, [(source, source + steps) for source in range(i...  19.9 us
    ppermute x5, waiting for transfers between devices, shifted(): lax.ppermute(value, axis, [(source, source + steps) for source in range(i...  16 us
    ppermute x1, waiting for transfers between devices, shards(): lax.ppermute(part, 'wloop', [(source, (source + step) % ways) for source...  11.9 us
    dot_general x2, matrix products, shards(): jnp.einsum('td,dje->jte', rows, w_keyvalue, preferred_element_type=jnp.fl...  10.4 us
    dot_general x2, matrix products, output_share(): jnp.dot(attended, lax.dynamic_index_in_dim(from_ranks, (me - rank) % ways...  7.29 us
    unnamed x47, local copies, waits for them, and re-layouts  7.12 us
    dot_general x2, matrix products, shards(): jnp.dot(rows, w_query, preferred_element_type=jnp.float32)  6.24 us
  transfers between devices with their start and end apart: 11, of which 5 were waited for; matrix products, arithmetic and copies ran while one was open for 31% of the time, Pallas kernels for 0%

profile of v16, /device:TPU:0, one launch (start us, length us, event | category | flops | bytes accessed | tf_op | source)
XLA Modules:
  0.0 178.0 jit_solution(16459354897182492237)
XLA Ops:
  0.0 2.2 %fusion.2 = f32[512]{0:T(512)S(1)} fusion(bf16[1,512,2048]{2,1,0:T(8,128)(2,1)} %param.7), kind=kLoop, calls=%fused_computation.13 | loop fusion | flops 3145216 | bytes 2099200 | tf_op jit(solution)/shard_map/reduce_sum | solution.py:18
  4.6 3.0 %collective-permute-start = (bf16[256,1024]{1,0:T(8,128)(2,1)S(1)}, bf16[256,1024]{1,0:T(8,128)(2,1)S(1)}, u32[]{:S(2)}, u32[]{:S(2)}) collective-permute-start(bf16[256,1024]{1,0:T(8,128)(2,1)S(1)} %dynamic-slice_bitcast_fusion), channel_id=1, source_target_pairs={{0,2},{2,0},{1,3},{3,1},{4,6},{6,4},{5,7},{7,5},{8,10},{10,8},{9,1... | collective-permute-start | bytes 1572872 | tf_op jit(solution)/shard_map/ppermute | solution.py:77
  7.6 11.9 %collective-permute-done = bf16[256,1024]{1,0:T(8,128)(2,1)S(1)} collective-permute-done((bf16[256,1024]{1,0:T(8,128)(2,1)S(1)}, bf16[256,1024]{1,0:T(8,128)(2,1)S(1)}, u32[]{:S(2)}, u32[]{:S(2)}) %collective-permute-start) | collective-permute-done | bytes 524320 | tf_op jit(solution)/shard_map/ppermute | solution.py:77
  19.7 1.8 collective-permute-done.1
  22.5 1.8 %gather_fusion = bf16[2,256,1024]{2,1,0:T(8,128)(2,1)S(1)} fusion(bf16[2,256,1024]{2,1,0:T(8,128)(2,1)} %pad_maximum_fusion, s32[1024]{0:T(1024)S(1)} %pad_clamp_fusion), kind=kCustom, calls=%fused_computation | custom fusion | bytes 2097160 | tf_op jit(solution)/shard_map/jit(_take)/gather | solution.py:70
  24.6 6.4 %convert_bitcast_fusion = bf16[2,512,1024]{2,1,0:T(8,128)(2,1)} fusion(bf16[1024,2,1024]{2,1,0:T(2,128)(2,1)} %param.10, bf16[512,1024]{1,0:T(8,128)(2,1)S(1)} %bitcast_select_fusion), kind=kOutput, calls=%fused_computation.46 | convolution fusion | flops 2148532224 | bytes 7340032 | tf_op jit(solution)/shard_map/td,dje->jte/dot_general | solution.py:104
  31.0 1.7 collective-permute-start.2
  37.2 3.9 %fusion.41 = f32[512,1024]{1,0:T(8,128)} fusion(bf16[1024,1024]{1,0:T(8,128)(2,1)S(1)} %copy-done, bf16[1,512,2048]{2,1,0:T(8,128)(2,1)} %copy-done.7, s32[]{:T(128)S(6)} %select_n.91), kind=kOutput, calls=%fused_computation.56 | convolution fusion | flops 1073741824 | bytes 5242884 | tf_op jit(solution)/shard_map/dot_general | solution.py:109
  41.1 2.4 %convolution_convert_fusion = bf16[512,1024]{1,0:T(8,128)(2,1)} fusion(bf16[512,1024]{1,0:T(8,128)(2,1)S(1)} %copy-done.11, bf16[1024,1024]{1,0:T(8,128)(2,1)S(1)} %copy-done), kind=kOutput, calls=%fused_computation.48 | convolution fusion | flops 1074266112 | bytes 4194304 | tf_op jit(solution)/shard_map/dot_general | solution.py:109
  43.5 35.5 %collective-permute-done.2 = bf16[2,512,1024]{2,1,0:T(8,128)(2,1)} collective-permute-done((bf16[2,512,1024]{2,1,0:T(8,128)(2,1)}, bf16[2,512,1024]{2,1,0:T(8,128)(2,1)}, u32[]{:S(2)}, u32[]{:S(2)}) %collective-permute-start.2) | collective-permute-done | bytes 2097184 | tf_op jit(solution)/shard_map/ppermute | solution.py:93
  79.0 4.1 %bitcast_add_fusion = f32[2,512,1024]{2,1,0:T(8,128)S(1)} fusion(bf16[2,512,1024]{2,1,0:T(8,128)(2,1)} %collective-permute-done.2, bf16[1024,2,1024]{2,1,0:T(2,128)(2,1)S(1)} %copy-done.18, bf16[1,512,2048]{2,1,0:T(8,128)(2,1)S(1)} %copy-done.8, s32[]{:T(128)S(6)} %select_n.91), kind=kOutput, calls=%fused_computation.16 | convolution fusion | flops 2149580800 | bytes 11534340 | tf_op jit(solution)/shard_map/td,dje->jte/dot_general | solution.py:104
  85.4 1.7 collective-permute-start.3
  87.1 4.5 %collective-permute-start.5 = (bf16[1,512,1024]{2,1,0:T(8,128)(2,1)}, bf16[1,512,1024]{2,1,0:T(8,128)(2,1)}, u32[]{:S(2)}, u32[]{:S(2)}) collective-permute-start(bf16[1,512,1024]{2,1,0:T(8,128)(2,1)} %slice.63), channel_id=1, source_target_pairs={{0,4},{4,8},{8,12},{1,5},{5,9},{9,13},{2,6},{6,10},{10,14},{3,7},{... | collective-permute-start | bytes 3145736 | tf_op jit(solution)/shard_map/ppermute | solution.py:14
  93.0 1.8 %copy.84 = f32[1,512,1024]{2,1,0:T(8,128)} copy(f32[1,512,1024]{1,2,0:T(8,128)S(1)} %bitcast.128) | data formatting | bytes 4194304 | tf_op jit(solution)/shard_map/mul | solution.py:18
  94.9 3.8 %multiply_convert_fusion = (bf16[1,512,1024]{2,1,0:T(8,128)(2,1)}, f32[1,512,1024]{2,1,0:T(8,128)S(1)}) fusion(f32[1,512,1024]{2,1,0:T(8,128)} %copy.84, f32[2,512,1024]{2,1,0:T(8,128)} %copy-done.6), kind=kLoop, calls=%fused_computation.38 | loop fusion | flops 1048576 | bytes 7340032 | tf_op jit(solution)/shard_map/convert_element_type | solution.py:112
  98.7 3.5 %collective-permute-start.4 = (bf16[1,512,1024]{2,1,0:T(8,128)(2,1)}, bf16[1,512,1024]{2,1,0:T(8,128)(2,1)}, u32[]{:S(2)}, u32[]{:S(2)}) collective-permute-start(bf16[1,512,1024]{2,1,0:T(8,128)(2,1)} %get-tuple-element.19), channel_id=1, source_target_pairs={{0,4},{4,8},{8,12},{1,5},{5,9},{9,13},{2,6},{6,10},{10,14},{3,7},{... | collective-permute-start | bytes 3145736 | tf_op jit(solution)/shard_map/ppermute | solution.py:14
  104.5 1.9 %copy.83 = f32[1,512,1024]{1,2,0:T(8,128)} copy(f32[1,512,1024]{2,1,0:T(8,128)S(1)} %get-tuple-element.20) | data formatting | bytes 4194304 | tf_op jit(solution)/shard_map/reshape;squeeze | solution.py:112
  107.0 2.9 %fusion.35 = f32[1,8,128,128]{3,2,1,0:T(8,128)S(1)} fusion(bf16[512,8,128]{0,2,1:T(8,128)(2,1)S(1)} %bitcast.129, f32[512,8]{0,1:T(8,128)} %fusion.65, f32[512,8,128]{0,2,1:T(8,128)} %bitcast.124, f32[512,8]{0,1:T(8,128)S(1)} %add_rsqrt_fusion), kind=kOutput, calls=%fused_computation.50 | convolution fusion | flops 807403520 | bytes 3702784 | tf_op jit(solution)/shard_map/bht,bthd,bthe->bhde/dot_general | solution.py:129
  109.9 1.8 %collective-permute-done.3 = bf16[512,1024]{1,0:T(8,128)(2,1)} collective-permute-done((bf16[512,1024]{1,0:T(8,128)(2,1)}, bf16[512,1024]{1,0:T(8,128)(2,1)}, u32[]{:S(2)}, u32[]{:S(2)}) %collective-permute-start.3) | collective-permute-done | bytes 1048608 | tf_op jit(solution)/shard_map/ppermute | solution.py:93
  111.7 3.0 %multiply_bitcast_fusion.1 = (f32[64,8,8,128]{3,1,2,0:T(8,128)S(1)}, f32[64,8,8,128]{3,2,1,0:T(8,128)}) fusion(f32[512,1024]{1,0:T(8,128)S(1)} %copy-done.9, bf16[512,1024]{1,0:T(8,128)(2,1)} %collective-permute-done.3), kind=kLoop, calls=%fused_computation.44 | loop fusion | flops 1572864 | bytes 7340032
  114.8 1.8 %copy.88 = f32[64,8,8,128]{3,2,1,0:T(8,128)} copy(f32[64,8,8,128]{3,1,2,0:T(8,128)S(1)} %get-tuple-element.21) | data formatting | bytes 4194304
  116.6 2.2 %reduce_sum.57 = f32[512,8]{1,0:T(8,128)S(1)} reduce(f32[512,8,128]{2,1,0:T(8,128)} %bitcast.126, f32[]{:T(128)} %constant.107.clone.1), dimensions={2}, to_apply=%region_1.2 | reduce | flops 520192 | bytes 2113540 | tf_op jit(solution)/shard_map/reduce_sum | solution.py:18
  118.9 16.0 %collective-permute-done.4 = bf16[1,512,1024]{2,1,0:T(8,128)(2,1)} collective-permute-done((bf16[1,512,1024]{2,1,0:T(8,128)(2,1)}, bf16[1,512,1024]{2,1,0:T(8,128)(2,1)}, u32[]{:S(2)}, u32[]{:S(2)}) %collective-permute-start.4) | collective-permute-done | bytes 1048608 | tf_op jit(solution)/shard_map/ppermute | solution.py:14
  136.6 4.5 %collective-permute-start.6 = (bf16[1,9,128,128]{3,2,1,0:T(8,128)(2,1)S(1)}, bf16[1,9,128,128]{3,2,1,0:T(8,128)(2,1)S(1)}, u32[]{:S(2)}, u32[]{:S(2)}) collective-permute-start(bf16[1,9,128,128]{3,2,1,0:T(8,128)(2,1)S(1)} %fusion.53), channel_id=1, source_target_pairs={{0,4},{4,8},{8,12},{1,5},{5,9},{9,13},{2,6},{6,10},{10,14},{3,7},{... | collective-permute-start | bytes 884744 | tf_op jit(solution)/shard_map/ppermute | solution.py:14
  141.9 2.6 %fusion = (f32[8,512]{1,0:T(8,128)S(1)}, f32[8,512,512]{1,2,0:T(8,128)S(1)}) fusion(pred[512,512]{0,1:T(8,128)(4,1)S(1)} %copy-done.13, bf16[512,8,128]{2,0,1:T(8,128)(2,1)S(1)} %fusion.19, f32[512,8,128]{0,2,1:T(8,128)S(1)} %bitcast.125, f32[512,8]{0,1:T(8,128)S(1)} %add_rsqrt_fusion), kind=kOutput, calls=%fused_computation.5 | convolution fusion | flops 544206848 | bytes 11829248 | tf_op jit(solution)/shard_map/bihd,bjhd->bhij/dot_general | solution.py:23
  144.5 5.4 %fusion.1 = (f32[8,512]{1,0:T(8,128)S(1)}, f32[8,512,512]{1,2,0:T(8,128)}) fusion(pred[512,512]{0,1:T(8,128)(4,1)S(1)} %fusion.46, bf16[512,8,128]{2,0,1:T(8,128)(2,1)S(1)} %fusion.19, bf16[512,8,128]{2,1,0:T(8,128)(2,1)S(1)} %bitcast.135), kind=kOutput, calls=%fused_computation.6 | convolution fusion | flops 543158272 | bytes 10764288 | tf_op jit(solution)/shard_map/bihd,bjhd->bhij/dot_general | solution.py:27
  150.0 3.5 %collective-permute-start.7 = (bf16[1,9,128,128]{3,2,1,0:T(8,128)(2,1)S(1)}, bf16[1,9,128,128]{3,2,1,0:T(8,128)(2,1)S(1)}, u32[]{:S(2)}, u32[]{:S(2)}) collective-permute-start(bf16[1,9,128,128]{3,2,1,0:T(8,128)(2,1)S(1)} %fusion.55), channel_id=1, source_target_pairs={{0,4},{4,8},{8,12},{1,5},{5,9},{9,13},{2,6},{6,10},{10,14},{3,7},{... | collective-permute-start | bytes 884744 | tf_op jit(solution)/shard_map/ppermute | solution.py:14
  153.5 3.4 %fusion.5 = f32[8,128,512]{2,1,0:T(8,128)} fusion(bf16[512,8,128]{0,2,1:T(8,128)(2,1)S(1)} %bitcast.130, f32[8,512,512]{1,2,0:T(8,128)S(1)} %get-tuple-element.24, f32[8,512]{1,0:T(8,128)S(1)} %add.164, pred[512,512]{0,1:T(8,128)(4,1)S(1)} %copy-done.13), kind=kOutput, calls=%fused_computation.17 | convolution fusion | flops 545259520 | bytes 11812864 | tf_op jit(solution)/shard_map/bhij,bjhd->bihd/dot_general | solution.py:38
  158.6 4.0 %collective-permute-start.8 = (bf16[1,9,128,128]{3,2,1,0:T(8,128)(2,1)S(1)}, bf16[1,9,128,128]{3,2,1,0:T(8,128)(2,1)S(1)}, u32[]{:S(2)}, u32[]{:S(2)}) collective-permute-start(bf16[1,9,128,128]{3,2,1,0:T(8,128)(2,1)S(1)} %fusion.57), channel_id=1, source_target_pairs={{0,4},{4,8},{8,12},{1,5},{5,9},{9,13},{2,6},{6,10},{10,14},{3,7},{... | collective-permute-start | bytes 884744 | tf_op jit(solution)/shard_map/ppermute | solution.py:14
  162.6 4.8 %fusion.6 = f32[8,128,512]{2,1,0:T(8,128)S(1)} fusion(bf16[512,8,128]{0,2,1:T(8,128)(2,1)S(1)} %bitcast.134, f32[8,512,512]{1,2,0:T(8,128)} %get-tuple-element.26, f32[8,512]{1,0:T(8,128)S(1)} %add.164, pred[512,512]{0,1:T(8,128)(4,1)} %copy-done.12), kind=kOutput, calls=%fused_computation.18 | convolution fusion | flops 545259520 | bytes 11812864 | tf_op jit(solution)/shard_map/bhij,bjhd->bihd/dot_general | solution.py:40
  169.1 3.9 %fusion.31 = bf16[512,1024]{1,0:T(8,128)(2,1)} fusion(bf16[512,1024]{0,1:T(8,128)(2,1)S(1)} %bitcast.146, s32[]{:T(128)S(6)} %select_n.108, bf16[1,1024,1024]{2,1,0:T(8,128)(2,1)S(1)} %bitcast.145, bf16[1,1024,1024]{2,1,0:T(8,128)(2,1)} %bitcast.40), kind=kOutput, calls=%fused_computation.47 | convolution fusion | flops 1075314688 | bytes 6291460 | tf_op jit(solution)/shard_map/dot_general | solution.py:197
  173.1 3.4 %fusion.17 = f32[512,1024]{1,0:T(8,128)S(1)} fusion(bf16[512,1024]{0,1:T(8,128)(2,1)} %bitcast.147, s32[]{:T(128)S(6)} %select_n.105, bf16[1,1024,1024]{2,1,0:T(8,128)(2,1)} %bitcast.144, bf16[1,1024,1024]{2,1,0:T(8,128)(2,1)} %bitcast.40), kind=kOutput, calls=%fused_computation.28 | convolution fusion | flops 1074790400 | bytes 7340036 | tf_op jit(solution)/shard_map/dot_general | solution.py:197
  (100 shorter events, 21.7 us)
Async XLA Ops:
  0.0 37.2 %copy-start = (bf16[1024,1024]{1,0:T(8,128)(2,1)S(1)}, bf16[1024,1024]{1,0:T(8,128)(2,1)}, u32[]{:S(2)}) copy-start(bf16[1024,1024]{1,0:T(8,128)(2,1)} %param.9) | copy-start | bytes 6291460
  0.0 2.2 %copy-start.16 = (f32[2048]{0:T(1024)S(1)}, f32[2048]{0:T(1024)}, u32[]{:S(2)}) copy-start(f32[2048]{0:T(1024)} %param.8) | copy-start | bytes 24580
  0.0 2.4 %copy-start.2 = (bf16[1,512,2048]{2,1,0:T(8,128)(2,1)S(1)}, bf16[1,512,2048]{2,1,0:T(8,128)(2,1)}, u32[]{:S(2)}) copy-start(bf16[1,512,2048]{2,1,0:T(8,128)(2,1)} %param.7) | copy-start | bytes 6291460
  4.6 15.0 %collective-permute-start = (bf16[256,1024]{1,0:T(8,128)(2,1)S(1)}, bf16[256,1024]{1,0:T(8,128)(2,1)S(1)}, u32[]{:S(2)}, u32[]{:S(2)}) collective-permute-start(bf16[256,1024]{1,0:T(8,128)(2,1)S(1)} %dynamic-slice_bitcast_fusion), channel_id=1, source_target_pairs={{0,2},{2,0},{1,3},{3,1},{4,6},{6,4},{5,7},{7,5},{8,10},{10,8},{9,1... | collective-permute-start | bytes 1572872 | tf_op jit(solution)/shard_map/ppermute | solution.py:77
  19.5 1.9 %collective-permute-start.1 = (bf16[256,1024]{1,0:T(8,128)(2,1)S(1)}, bf16[256,1024]{1,0:T(8,128)(2,1)S(1)}, u32[]{:S(2)}, u32[]{:S(2)}) collective-permute-start(bf16[256,1024]{1,0:T(8,128)(2,1)S(1)} %collective-permute-done), channel_id=1, source_target_pairs={{0,1},{1,0},{2,3},{3,2},{4,5},{5,4},{6,7},{7,6},{8,9},{9,8},{10,11... | collective-permute-start | bytes 1572872 | tf_op jit(solution)/shard_map/ppermute | solution.py:67
  24.6 6.4 %copy-start.10 = (bf16[512,1024]{1,0:T(8,128)(2,1)}, bf16[512,1024]{1,0:T(8,128)(2,1)S(1)}, u32[]{:S(2)}) copy-start(bf16[512,1024]{1,0:T(8,128)(2,1)S(1)} %bitcast_select_fusion) | copy-start | bytes 3145732
  24.6 8.8 %copy-start.15 = (f32[1,8,512]{2,1,0:T(8,128)S(1)}, f32[1,8,512]{2,1,0:T(8,128)}, u32[]{:S(2)}) copy-start(f32[1,8,512]{2,1,0:T(8,128)} %param.12) | copy-start | bytes 49156
  31.0 48.0 %collective-permute-start.2 = (bf16[2,512,1024]{2,1,0:T(8,128)(2,1)}, bf16[2,512,1024]{2,1,0:T(8,128)(2,1)}, u32[]{:S(2)}, u32[]{:S(2)}) collective-permute-start(bf16[2,512,1024]{2,1,0:T(8,128)(2,1)} %convert_bitcast_fusion), channel_id=1, source_target_pairs={{0,2},{2,0},{1,3},{3,1},{4,6},{6,4},{5,7},{7,5},{8,10},{10,8},{9,1... | collective-permute-start | bytes 6291464 | tf_op jit(solution)/shard_map/ppermute | solution.py:93
  36.5 108.0 %copy-start.12 = (pred[512,512]{0,1:T(8,128)(4,1)}, pred[512,512]{0,1:T(8,128)(4,1)S(1)}, u32[]{:S(2)}) copy-start(pred[512,512]{0,1:T(8,128)(4,1)S(1)} %fusion.46) | copy-start | bytes 786436
  37.2 3.9 %copy-start.11 = (bf16[512,1024]{1,0:T(8,128)(2,1)S(1)}, bf16[512,1024]{1,0:T(8,128)(2,1)}, u32[]{:S(2)}) copy-start(bf16[512,1024]{1,0:T(8,128)(2,1)} %copy-done.10) | copy-start | bytes 3145732
  41.1 37.9 %copy-start.8 = (bf16[1,512,2048]{2,1,0:T(8,128)(2,1)S(1)}, bf16[1,512,2048]{2,1,0:T(8,128)(2,1)}, u32[]{:S(2)}) copy-start(bf16[1,512,2048]{2,1,0:T(8,128)(2,1)} %copy-done.7) | copy-start | bytes 6291460
  41.1 37.9 %copy-start.18 = (bf16[1024,2,1024]{2,1,0:T(2,128)(2,1)S(1)}, bf16[1024,2,1024]{2,1,0:T(2,128)(2,1)}, u32[]{:S(2)}) copy-start(bf16[1024,2,1024]{2,1,0:T(2,128)(2,1)} %param.10) | copy-start | bytes 12582916
  83.1 2.3 %copy-start.6 = (f32[2,512,1024]{2,1,0:T(8,128)}, f32[2,512,1024]{2,1,0:T(8,128)S(1)}, u32[]{:S(2)}) copy-start(f32[2,512,1024]{2,1,0:T(8,128)S(1)} %bitcast_add_fusion) | copy-start | bytes 12582916
  85.4 26.3 %collective-permute-start.3 = (bf16[512,1024]{1,0:T(8,128)(2,1)}, bf16[512,1024]{1,0:T(8,128)(2,1)}, u32[]{:S(2)}, u32[]{:S(2)}) collective-permute-start(bf16[512,1024]{1,0:T(8,128)(2,1)} %convolution_convert_fusion), channel_id=1, source_target_pairs={{0,2},{2,0},{1,3},{3,1},{4,6},{6,4},{5,7},{7,5},{8,10},{10,8},{9,1... | collective-permute-start | bytes 3145736 | tf_op jit(solution)/shard_map/ppermute | solution.py:93
  87.1 31.8 %collective-permute-start.5 = (bf16[1,512,1024]{2,1,0:T(8,128)(2,1)}, bf16[1,512,1024]{2,1,0:T(8,128)(2,1)}, u32[]{:S(2)}, u32[]{:S(2)}) collective-permute-start(bf16[1,512,1024]{2,1,0:T(8,128)(2,1)} %slice.63), channel_id=1, source_target_pairs={{0,4},{4,8},{8,12},{1,5},{5,9},{9,13},{2,6},{6,10},{10,14},{3,7},{... | collective-permute-start | bytes 3145736 | tf_op jit(solution)/shard_map/ppermute | solution.py:14
  98.7 36.3 %collective-permute-start.4 = (bf16[1,512,1024]{2,1,0:T(8,128)(2,1)}, bf16[1,512,1024]{2,1,0:T(8,128)(2,1)}, u32[]{:S(2)}, u32[]{:S(2)}) collective-permute-start(bf16[1,512,1024]{2,1,0:T(8,128)(2,1)} %get-tuple-element.19), channel_id=1, source_target_pairs={{0,4},{4,8},{8,12},{1,5},{5,9},{9,13},{2,6},{6,10},{10,14},{3,7},{... | collective-permute-start | bytes 3145736 | tf_op jit(solution)/shard_map/ppermute | solution.py:14
  106.4 61.7 %collective-permute-start.9 = (bf16[1024,1024]{1,0:T(8,128)(2,1)}, bf16[1024,1024]{1,0:T(8,128)(2,1)}, u32[]{:S(2)}, u32[]{:S(2)}) collective-permute-start(bf16[1024,1024]{1,0:T(8,128)(2,1)} %param.11), channel_id=1, source_target_pairs={{0,2},{2,0},{1,3},{3,1},{4,6},{6,4},{5,7},{7,5},{8,10},{10,8},{9,1... | collective-permute-start | bytes 6291464 | tf_op jit(solution)/shard_map/ppermute | solution.py:182
  107.0 4.8 %copy-start.9 = (f32[512,1024]{1,0:T(8,128)S(1)}, f32[512,1024]{1,0:T(8,128)}, u32[]{:S(2)}) copy-start(f32[512,1024]{1,0:T(8,128)} %fusion.41) | copy-start | bytes 6291460
  116.6 19.9 %copy-start.17 = (f32[9]{0:T(128)S(1)}, f32[9]{0:T(128)}, u32[]{:S(2)}) copy-start(f32[9]{0:T(128)} %pad.11.clone) | copy-start | bytes 112
  118.9 22.3 %copy-start.4 = (f32[64,8,8,128]{3,2,1,0:T(8,128)S(1)}, f32[64,8,8,128]{3,2,1,0:T(8,128)}, u32[]{:S(2)}) copy-start(f32[64,8,8,128]{3,2,1,0:T(8,128)} %get-tuple-element.22) | copy-start | bytes 6291460
  136.5 5.4 %copy-start.5 = (f32[1,512,1024]{1,2,0:T(8,128)S(1)}, f32[1,512,1024]{1,2,0:T(8,128)}, u32[]{:S(2)}) copy-start(f32[1,512,1024]{1,2,0:T(8,128)} %copy.83) | copy-start | bytes 6291460
  136.5 5.4 %copy-start.13 = (pred[512,512]{0,1:T(8,128)(4,1)S(1)}, pred[512,512]{0,1:T(8,128)(4,1)}, u32[]{:S(2)}) copy-start(pred[512,512]{0,1:T(8,128)(4,1)} %iota_compare_fusion.1) | copy-start | bytes 786436
  136.6 13.2 %collective-permute-start.6 = (bf16[1,9,128,128]{3,2,1,0:T(8,128)(2,1)S(1)}, bf16[1,9,128,128]{3,2,1,0:T(8,128)(2,1)S(1)}, u32[]{:S(2)}, u32[]{:S(2)}) collective-permute-start(bf16[1,9,128,128]{3,2,1,0:T(8,128)(2,1)S(1)} %fusion.53), channel_id=1, source_target_pairs={{0,4},{4,8},{8,12},{1,5},{5,9},{9,13},{2,6},{6,10},{10,14},{3,7},{... | collective-permute-start | bytes 884744 | tf_op jit(solution)/shard_map/ppermute | solution.py:14
  150.0 8.4 %collective-permute-start.7 = (bf16[1,9,128,128]{3,2,1,0:T(8,128)(2,1)S(1)}, bf16[1,9,128,128]{3,2,1,0:T(8,128)(2,1)S(1)}, u32[]{:S(2)}, u32[]{:S(2)}) collective-permute-start(bf16[1,9,128,128]{3,2,1,0:T(8,128)(2,1)S(1)} %fusion.55), channel_id=1, source_target_pairs={{0,4},{4,8},{8,12},{1,5},{5,9},{9,13},{2,6},{6,10},{10,14},{3,7},{... | collective-permute-start | bytes 884744 | tf_op jit(solution)/shard_map/ppermute | solution.py:14
  158.6 8.8 %collective-permute-start.8 = (bf16[1,9,128,128]{3,2,1,0:T(8,128)(2,1)S(1)}, bf16[1,9,128,128]{3,2,1,0:T(8,128)(2,1)S(1)}, u32[]{:S(2)}, u32[]{:S(2)}) collective-permute-start(bf16[1,9,128,128]{3,2,1,0:T(8,128)(2,1)S(1)} %fusion.57), channel_id=1, source_target_pairs={{0,4},{4,8},{8,12},{1,5},{5,9},{9,13},{2,6},{6,10},{10,14},{3,7},{... | collective-permute-start | bytes 884744 | tf_op jit(solution)/shard_map/ppermute | solution.py:14
  162.6 5.0 %copy-start.14 = (f32[512,8]{0,1:T(8,128)S(1)}, f32[512,8]{0,1:T(8,128)}, u32[]{:S(2)}) copy-start(f32[512,8]{0,1:T(8,128)} %get-tuple-element.17) | copy-start | bytes 49156
  162.6 5.0 %copy-start.21 = (f32[8,128,512]{2,1,0:T(8,128)S(1)}, f32[8,128,512]{2,1,0:T(8,128)}, u32[]{:S(2)}) copy-start(f32[8,128,512]{2,1,0:T(8,128)} %fusion.5) | copy-start | bytes 6291460
  167.5 1.6 copy-start.19
  168.2 4.9 %copy-start.20 = (bf16[1,512,8,128]{1,3,2,0:T(8,128)(2,1)}, bf16[1,512,8,128]{1,3,2,0:T(8,128)(2,1)S(1)}, u32[]{:S(2)}) copy-start(bf16[1,512,8,128]{1,3,2,0:T(8,128)(2,1)S(1)} %fusion.22) | copy-start | bytes 3145732
  173.0 3.4 %collective-permute-start.10 = (bf16[512,1024]{1,0:T(8,128)(2,1)}, bf16[512,1024]{1,0:T(8,128)(2,1)S(1)}, u32[]{:S(2)}, u32[]{:S(2)}) collective-permute-start(bf16[512,1024]{1,0:T(8,128)(2,1)} %fusion.31), channel_id=1, source_target_pairs={{0,1},{1,0},{2,3},{3,2},{4,5},{5,4},{6,7},{7,6},{8,9},{9,8},{10,11... | collective-permute-start | bytes 3145736 | tf_op jit(solution)/shard_map/ppermute | solution.py:206
  173.0 3.4 %copy-start.3 = (bf16[1,512,2048]{2,1,0:T(8,128)(2,1)S(1)}, bf16[1,512,2048]{2,1,0:T(8,128)(2,1)}, u32[]{:S(2)}) copy-start(bf16[1,512,2048]{2,1,0:T(8,128)(2,1)} %param.7) | copy-start | bytes 6291460
  173.0 5.0 %copy-start.1 = (bf16[1024,1024]{1,0:T(8,128)(2,1)S(1)}, bf16[1024,1024]{1,0:T(8,128)(2,1)}, u32[]{:S(2)}) copy-start(bf16[1024,1024]{1,0:T(8,128)(2,1)} %param.9) | copy-start | bytes 6291460
  (1 other events, 1.4 us)

commit v17 on v13

--- a/solution.py
+++ b/solution.py
@@ -95,11 +95,18 @@
             ).astype(jnp.float32)
         return total
 
-    pair_raw = gathered_sum(
+    half_rows = count // 2
+    pair_raw = jnp.concatenate(
         [
-            jnp.einsum("td,dje->jte", rows, w_keyvalue, preferred_element_type=jnp.float32)
-            for rows in stacked
-        ]
+            gathered_sum(
+                [
+                    jnp.einsum("td,dje->jte", rows[lo:hi], w_keyvalue, preferred_element_type=jnp.float32)
+                    for rows in stacked
+                ]
+            )
+            for lo, hi in ((0, half_rows), (half_rows, count))
+        ],
+        axis=1,
     )
     query_raw = gathered_sum(
         [jnp.dot(rows, w_query, preferred_element_type=jnp.float32) for rows in stacked],

time: 177 us -> 173 us (0.977)
  waiting for transfers between devices: 63 us -> 60 us
  other arithmetic: 18.2 us -> 21.1 us
  matrix products: 44.7 us -> 41.9 us
  local copies, waits for them, and re-layouts: 22.3 us -> 20.2 us
    ppermute x2 -> x3, waiting for transfers between devices: 38.2 us -> 43.8 us  [gathered_sum(): lax.ppermute(outgoing, 'wloop', [(source, (source - step) % ways) for sou...]
    ppermute x1, waiting for transfers between devices: 11.9 us -> 7.5 us  [shards(): lax.ppermute(part, 'wloop', [(source, (source + step) % ways) for source...]
    ppermute x5, waiting for transfers between devices: 11.1 us -> 8.03 us  [shifted(): lax.ppermute(value, axis, [(source, source + steps) for source in range(i...]
    dot_general x2 -> x4, matrix products: 10.4 us -> 8.97 us  [shards(): jnp.einsum('td,dje->jte', rows[lo:hi], w_keyvalue, preferred_element_type...]
    ppermute x2 -> x3, starting transfers between devices: 3.23 us -> 3.68 us  [gathered_sum(): lax.ppermute(outgoing, 'wloop', [(source, (source - step) % ways) for sou...]
  transfers between devices with their start and end apart: 11 -> 12, of which waited for: 4 -> 6; matrix products, arithmetic and copies ran while one was open for 33% -> 35% of each run, Pallas kernels for 0% -> 0%
where the time goes in v17:
time: 173 us; the launch traced here: 172 us
  waiting for transfers between devices  60 us (35%)
  matrix products  41.9 us (24%)
  starting transfers between devices  27.9 us (16%)
  other arithmetic  21.1 us (12%)
  local copies, waits for them, and re-layouts  20.2 us (12%)
    ppermute x3, waiting for transfers between devices, gathered_sum(): lax.ppermute(outgoing, 'wloop', [(source, (source - step) % ways) for sou...  43.8 us
    ppermute x5, starting transfers between devices, shifted(): lax.ppermute(value, axis, [(source, source + steps) for source in range(i...  20.7 us
    dot_general x4, matrix products, shards(): jnp.einsum('td,dje->jte', rows[lo:hi], w_keyvalue, preferred_element_type...  8.97 us
    ppermute x5, waiting for transfers between devices, shifted(): lax.ppermute(value, axis, [(source, source + steps) for source in range(i...  8.03 us
    ppermute x1, waiting for transfers between devices, shards(): lax.ppermute(part, 'wloop', [(source, (source + step) % ways) for source...  7.5 us
    dot_general x2, matrix products, output_share(): jnp.dot(attended, lax.dynamic_index_in_dim(from_ranks, (me - rank) % ways...  7.3 us
    unnamed x53, local copies, waits for them, and re-layouts  6.28 us
    dot_general x2, matrix products, shards(): jnp.dot(rows, w_query, preferred_element_type=jnp.float32)  6.09 us
  transfers between devices with their start and end apart: 12, of which 6 were waited for; matrix products, arithmetic and copies ran while one was open for 35% of the time, Pallas kernels for 0%

profile of v17, /device:TPU:0, one launch (start us, length us, event | category | flops | bytes accessed | tf_op | source)
XLA Modules:
  0.0 172.4 jit_solution(1176224432354415139)
XLA Ops:
  0.0 2.2 %fusion.2 = f32[512]{0:T(512)S(1)} fusion(bf16[1,512,2048]{2,1,0:T(8,128)(2,1)} %param.7), kind=kLoop, calls=%fused_computation.18 | loop fusion | flops 3145216 | bytes 2099200 | tf_op jit(solution)/shard_map/reduce_sum | solution.py:18
  4.6 3.0 %collective-permute-start = (bf16[256,1024]{1,0:T(8,128)(2,1)S(1)}, bf16[256,1024]{1,0:T(8,128)(2,1)S(1)}, u32[]{:S(2)}, u32[]{:S(2)}) collective-permute-start(bf16[256,1024]{1,0:T(8,128)(2,1)S(1)} %dynamic-slice_bitcast_fusion.4), channel_id=1, source_target_pairs={{0,2},{2,0},{1,3},{3,1},{4,6},{6,4},{5,7},{7,5},{8,10},{10,8},{9,1... | collective-permute-start | bytes 1572872 | tf_op jit(solution)/shard_map/ppermute | solution.py:77
  12.0 7.5 %collective-permute-done = bf16[256,1024]{1,0:T(8,128)(2,1)S(1)} collective-permute-done((bf16[256,1024]{1,0:T(8,128)(2,1)S(1)}, bf16[256,1024]{1,0:T(8,128)(2,1)S(1)}, u32[]{:S(2)}, u32[]{:S(2)}) %collective-permute-start) | collective-permute-done | bytes 524320 | tf_op jit(solution)/shard_map/ppermute | solution.py:77
  22.5 1.8 %gather_fusion = bf16[2,256,1024]{2,1,0:T(8,128)(2,1)S(1)} fusion(bf16[2,256,1024]{2,1,0:T(8,128)(2,1)} %pad_maximum_fusion.1, s32[1024]{0:T(1024)S(1)} %pad_clamp_fusion), kind=kCustom, calls=%fused_computation | custom fusion | bytes 2097160 | tf_op jit(solution)/shard_map/jit(_take)/gather | solution.py:70
  24.5 3.9 %fusion.51 = bf16[2,256,1024]{2,1,0:T(8,128)(2,1)S(1)} fusion(bf16[1024,2,1024]{2,1,0:T(2,128)(2,1)} %param.10, bf16[2,256,1024]{2,1,0:T(8,128)(2,1)S(1)} %broadcast_select_fusion), kind=kOutput, calls=%fused_computation.64 | convolution fusion | flops 1074266112 | bytes 5767168 | tf_op jit(solution)/shard_map/td,dje->jte/dot_general | solution.py:103
  28.4 1.8 %collective-permute-start.2 = (bf16[2,256,1024]{2,1,0:T(8,128)(2,1)S(1)}, bf16[2,256,1024]{2,1,0:T(8,128)(2,1)S(1)}, u32[]{:S(2)}, u32[]{:S(2)}) collective-permute-start(bf16[2,256,1024]{2,1,0:T(8,128)(2,1)S(1)} %fusion.51), channel_id=1, source_target_pairs={{0,2},{2,0},{1,3},{3,1},{4,6},{6,4},{5,7},{7,5},{8,10},{10,8},{9,1... | collective-permute-start | bytes 3145736 | tf_op jit(solution)/shard_map/ppermute | solution.py:91
  32.4 2.3 %convolution_convert_fusion = bf16[512,1024]{1,0:T(8,128)(2,1)} fusion(bf16[512,1024]{1,0:T(8,128)(2,1)S(1)} %bitcast_select_fusion, bf16[1024,1024]{1,0:T(8,128)(2,1)S(1)} %copy-done), kind=kOutput, calls=%fused_computation.61 | convolution fusion | flops 1074266112 | bytes 4194304 | tf_op jit(solution)/shard_map/dot_general | solution.py:112
  34.7 19.8 %collective-permute-done.2 = bf16[2,256,1024]{2,1,0:T(8,128)(2,1)S(1)} collective-permute-done((bf16[2,256,1024]{2,1,0:T(8,128)(2,1)S(1)}, bf16[2,256,1024]{2,1,0:T(8,128)(2,1)S(1)}, u32[]{:S(2)}, u32[]{:S(2)}) %collective-permute-start.2) | collective-permute-done | bytes 1048608 | tf_op jit(solution)/shard_map/ppermute | solution.py:91
  54.5 1.7 %bitcast_add_fusion.1 = f32[2,256,1024]{2,1,0:T(8,128)S(1)} fusion(bf16[2,256,1024]{2,1,0:T(8,128)(2,1)S(1)} %collective-permute-done.2, bf16[1024,2,1024]{2,1,0:T(2,128)(2,1)S(1)} %copy-done.20, bf16[1,512,2048]{2,1,0:T(8,128)(2,1)S(1)} %copy-done.8, s32[]{:T(128)S(6)} %select_n.93), kind=kOutput, calls=%fused_computation.49 | convolution fusion | flops 1074790400 | bytes 7864324 | tf_op jit(solution)/shard_map/td,dje->jte/dot_general | solution.py:103
  56.3 19.9 %collective-permute-done.3 = bf16[2,256,1024]{2,1,0:T(8,128)(2,1)S(1)} collective-permute-done((bf16[2,256,1024]{2,1,0:T(8,128)(2,1)S(1)}, bf16[2,256,1024]{2,1,0:T(8,128)(2,1)S(1)}, u32[]{:S(2)}, u32[]{:S(2)}) %collective-permute-start.3) | collective-permute-done | bytes 1048608 | tf_op jit(solution)/shard_map/ppermute | solution.py:91
  76.2 1.7 %bitcast_add_fusion = f32[2,256,1024]{2,1,0:T(8,128)S(1)} fusion(bf16[2,256,1024]{2,1,0:T(8,128)(2,1)S(1)} %collective-permute-done.3, bf16[1024,2,1024]{2,1,0:T(2,128)(2,1)S(1)} %copy-done.20, bf16[1,512,2048]{2,1,0:T(8,128)(2,1)S(1)} %copy-done.8, s32[]{:T(128)S(6)} %add.188, s32[]{:T(128)S(6)} %select_n.93), kind=kOutput, calls=%fused_computation.48 | convolution fusion | flops 1074790400 | bytes 7864328 | tf_op jit(solution)/shard_map/td,dje->jte/dot_general | solution.py:103
  79.0 1.7 %multiply_bitcast_fusion = (f32[64,8,8,128]{3,1,2,0:T(8,128)S(1)}, f32[1,512,1024]{2,1,0:T(8,128)}) fusion(f32[2,256,1024]{2,1,0:T(8,128)S(1)} %bitcast_add_fusion, f32[2,256,1024]{2,1,0:T(8,128)S(1)} %bitcast_add_fusion.1), kind=kLoop, calls=%fused_computation.55 | loop fusion | flops 1048576 | bytes 8388608
  80.8 4.8 %collective-permute-start.6 = (bf16[1,512,1024]{2,1,0:T(8,128)(2,1)}, bf16[1,512,1024]{2,1,0:T(8,128)(2,1)}, u32[]{:S(2)}, u32[]{:S(2)}) collective-permute-start(bf16[1,512,1024]{2,1,0:T(8,128)(2,1)} %fusion.24), channel_id=1, source_target_pairs={{0,4},{4,8},{8,12},{1,5},{5,9},{9,13},{2,6},{6,10},{10,14},{3,7},{... | collective-permute-start | bytes 3145736 | tf_op jit(solution)/shard_map/ppermute | solution.py:14
  85.6 1.8 %copy.99 = f32[64,8,8,128]{3,2,1,0:T(8,128)} copy(f32[64,8,8,128]{3,1,2,0:T(8,128)S(1)} %get-tuple-element.19) | data formatting | bytes 4194304
  87.4 2.2 %reduce_sum.58 = f32[512,8]{1,0:T(8,128)S(1)} reduce(f32[512,8,128]{2,1,0:T(8,128)} %bitcast.143, f32[]{:T(128)} %constant.107.clone.1), dimensions={2}, to_apply=%region_2.3 | reduce | flops 520192 | bytes 2113540 | tf_op jit(solution)/shard_map/reduce_sum | solution.py:18
  92.8 2.9 %copy.94 = f32[1,512,1024]{2,1,0:T(8,128)} copy(f32[1,512,1024]{1,2,0:T(8,128)} %bitcast.144) | data formatting | bytes 4194304 | tf_op jit(solution)/shard_map/mul | solution.py:18
  95.7 3.5 %multiply_convert_fusion = bf16[1,512,1024]{2,1,0:T(8,128)(2,1)} fusion(f32[1,512,1024]{2,1,0:T(8,128)} %get-tuple-element.20, f32[1,512,1024]{2,1,0:T(8,128)} %copy.94), kind=kLoop, calls=%fused_computation.50 | loop fusion | flops 1048576 | bytes 5242880 | tf_op jit(solution)/shard_map/convert_element_type | solution.py:115
  99.3 3.6 %collective-permute-start.5 = (bf16[1,512,1024]{2,1,0:T(8,128)(2,1)}, bf16[1,512,1024]{2,1,0:T(8,128)(2,1)}, u32[]{:S(2)}, u32[]{:S(2)}) collective-permute-start(bf16[1,512,1024]{2,1,0:T(8,128)(2,1)} %multiply_convert_fusion), channel_id=1, source_target_pairs={{0,4},{4,8},{8,12},{1,5},{5,9},{9,13},{2,6},{6,10},{10,14},{3,7},{... | collective-permute-start | bytes 3145736 | tf_op jit(solution)/shard_map/ppermute | solution.py:14
  105.2 3.3 %copy.93 = f32[1,512,1024]{1,2,0:T(8,128)} copy(f32[1,512,1024]{2,1,0:T(8,128)} %get-tuple-element.20) | data formatting | bytes 4194304 | tf_op jit(solution)/shard_map/reshape;squeeze | solution.py:115
  109.0 2.9 %fusion.54 = f32[1,8,128,128]{3,2,1,0:T(8,128)S(1)} fusion(bf16[512,8,128]{0,2,1:T(8,128)(2,1)S(1)} %bitcast.145, f32[512,8]{0,1:T(8,128)} %fusion.81, f32[512,8,128]{0,2,1:T(8,128)} %bitcast.140, f32[512,8]{0,1:T(8,128)S(1)} %add_rsqrt_fusion), kind=kOutput, calls=%fused_computation.65 | convolution fusion | flops 807403520 | bytes 3702784 | tf_op jit(solution)/shard_map/bht,bthd,bthe->bhde/dot_general | solution.py:132
  112.0 4.0 %collective-permute-done.4 = bf16[512,1024]{1,0:T(8,128)(2,1)} collective-permute-done((bf16[512,1024]{1,0:T(8,128)(2,1)}, bf16[512,1024]{1,0:T(8,128)(2,1)}, u32[]{:S(2)}, u32[]{:S(2)}) %collective-permute-start.4) | collective-permute-done | bytes 1048608 | tf_op jit(solution)/shard_map/ppermute | solution.py:91
  116.1 3.8 %multiply_bitcast_fusion.1 = (f32[64,8,8,128]{3,1,2,0:T(8,128)S(1)}, f32[64,8,8,128]{3,2,1,0:T(8,128)}) fusion(bf16[512,1024]{1,0:T(8,128)(2,1)} %collective-permute-done.4, bf16[1024,1024]{1,0:T(8,128)(2,1)S(1)} %copy-done, bf16[1,512,2048]{2,1,0:T(8,128)(2,1)S(1)} %copy-done.9, s32[]{:T(128)S(6)} %select_n.93), kind=kOutput, calls=%fused_computation.56 | convolution fusion | flops 1075314688 | bytes 8388612 | tf_op jit(solution)/shard_map/dot_general | solution.py:112
  121.1 8.0 %collective-permute-done.5 = bf16[1,512,1024]{2,1,0:T(8,128)(2,1)} collective-permute-done((bf16[1,512,1024]{2,1,0:T(8,128)(2,1)}, bf16[1,512,1024]{2,1,0:T(8,128)(2,1)}, u32[]{:S(2)}, u32[]{:S(2)}) %collective-permute-start.5) | collective-permute-done | bytes 1048608 | tf_op jit(solution)/shard_map/ppermute | solution.py:14
  130.8 4.5 %collective-permute-start.7 = (bf16[1,9,128,128]{3,2,1,0:T(8,128)(2,1)S(1)}, bf16[1,9,128,128]{3,2,1,0:T(8,128)(2,1)S(1)}, u32[]{:S(2)}, u32[]{:S(2)}) collective-permute-start(bf16[1,9,128,128]{3,2,1,0:T(8,128)(2,1)S(1)} %fusion.69), channel_id=1, source_target_pairs={{0,4},{4,8},{8,12},{1,5},{5,9},{9,13},{2,6},{6,10},{10,14},{3,7},{... | collective-permute-start | bytes 884744 | tf_op jit(solution)/shard_map/ppermute | solution.py:14
  136.1 2.6 %fusion = (f32[8,512]{1,0:T(8,128)S(1)}, f32[8,512,512]{1,2,0:T(8,128)S(1)}) fusion(pred[512,512]{0,1:T(8,128)(4,1)S(1)} %copy-done.14, bf16[512,8,128]{2,0,1:T(8,128)(2,1)S(1)} %fusion.26, f32[512,8,128]{0,2,1:T(8,128)S(1)} %bitcast.141, f32[512,8]{0,1:T(8,128)S(1)} %add_rsqrt_fusion), kind=kOutput, calls=%fused_computation.5 | convolution fusion | flops 544206848 | bytes 11829248 | tf_op jit(solution)/shard_map/bihd,bjhd->bhij/dot_general | solution.py:23
  138.7 5.3 %fusion.1 = (f32[8,512]{1,0:T(8,128)S(1)}, f32[8,512,512]{1,2,0:T(8,128)}) fusion(pred[512,512]{0,1:T(8,128)(4,1)S(1)} %fusion.64, bf16[512,8,128]{2,0,1:T(8,128)(2,1)S(1)} %fusion.26, bf16[512,8,128]{2,1,0:T(8,128)(2,1)S(1)} %bitcast.151), kind=kOutput, calls=%fused_computation.6 | convolution fusion | flops 543158272 | bytes 10764288 | tf_op jit(solution)/shard_map/bihd,bjhd->bhij/dot_general | solution.py:27
  144.1 3.5 %collective-permute-start.8 = (bf16[1,9,128,128]{3,2,1,0:T(8,128)(2,1)S(1)}, bf16[1,9,128,128]{3,2,1,0:T(8,128)(2,1)S(1)}, u32[]{:S(2)}, u32[]{:S(2)}) collective-permute-start(bf16[1,9,128,128]{3,2,1,0:T(8,128)(2,1)S(1)} %fusion.71), channel_id=1, source_target_pairs={{0,4},{4,8},{8,12},{1,5},{5,9},{9,13},{2,6},{6,10},{10,14},{3,7},{... | collective-permute-start | bytes 884744 | tf_op jit(solution)/shard_map/ppermute | solution.py:14
  147.6 3.3 %fusion.5 = f32[8,128,512]{2,1,0:T(8,128)} fusion(bf16[512,8,128]{0,2,1:T(8,128)(2,1)S(1)} %bitcast.146, f32[8,512,512]{1,2,0:T(8,128)S(1)} %get-tuple-element.24, f32[8,512]{1,0:T(8,128)S(1)} %add.168, pred[512,512]{0,1:T(8,128)(4,1)S(1)} %copy-done.14), kind=kOutput, calls=%fused_computation.21 | convolution fusion | flops 545259520 | bytes 11812864 | tf_op jit(solution)/shard_map/bhij,bjhd->bihd/dot_general | solution.py:38
  152.6 4.3 %collective-permute-start.9 = (bf16[1,9,128,128]{3,2,1,0:T(8,128)(2,1)S(1)}, bf16[1,9,128,128]{3,2,1,0:T(8,128)(2,1)S(1)}, u32[]{:S(2)}, u32[]{:S(2)}) collective-permute-start(bf16[1,9,128,128]{3,2,1,0:T(8,128)(2,1)S(1)} %fusion.73), channel_id=1, source_target_pairs={{0,4},{4,8},{8,12},{1,5},{5,9},{9,13},{2,6},{6,10},{10,14},{3,7},{... | collective-permute-start | bytes 884744 | tf_op jit(solution)/shard_map/ppermute | solution.py:14
  157.0 4.8 %fusion.6 = f32[8,128,512]{2,1,0:T(8,128)S(1)} fusion(bf16[512,8,128]{0,2,1:T(8,128)(2,1)S(1)} %bitcast.150, f32[8,512,512]{1,2,0:T(8,128)} %get-tuple-element.26, f32[8,512]{1,0:T(8,128)S(1)} %add.168, pred[512,512]{0,1:T(8,128)(4,1)} %copy-done.13), kind=kOutput, calls=%fused_computation.22 | convolution fusion | flops 545259520 | bytes 11812864 | tf_op jit(solution)/shard_map/bhij,bjhd->bihd/dot_general | solution.py:40
  163.5 3.9 %fusion.38 = bf16[512,1024]{1,0:T(8,128)(2,1)} fusion(bf16[512,1024]{0,1:T(8,128)(2,1)S(1)} %bitcast.162, s32[]{:T(128)S(6)} %select_n.111, bf16[1,1024,1024]{2,1,0:T(8,128)(2,1)S(1)} %bitcast.161, bf16[1,1024,1024]{2,1,0:T(8,128)(2,1)} %bitcast.48), kind=kOutput, calls=%fused_computation.58 | convolution fusion | flops 1075314688 | bytes 6291460 | tf_op jit(solution)/shard_map/dot_general | solution.py:200
  167.4 3.4 %fusion.21 = f32[512,1024]{1,0:T(8,128)S(1)} fusion(bf16[512,1024]{0,1:T(8,128)(2,1)} %bitcast.163, s32[]{:T(128)S(6)} %select_n.108, bf16[1,1024,1024]{2,1,0:T(8,128)(2,1)} %bitcast.160, bf16[1,1024,1024]{2,1,0:T(8,128)(2,1)} %bitcast.48), kind=kOutput, calls=%fused_computation.36 | convolution fusion | flops 1074790400 | bytes 7340036 | tf_op jit(solution)/shard_map/dot_general | solution.py:200
  (110 shorter events, 27.1 us)
Async XLA Ops:
  0.0 32.4 %copy-start = (bf16[1024,1024]{1,0:T(8,128)(2,1)S(1)}, bf16[1024,1024]{1,0:T(8,128)(2,1)}, u32[]{:S(2)}) copy-start(bf16[1024,1024]{1,0:T(8,128)(2,1)} %param.9) | copy-start | bytes 6291460
  2.4 6.0 %copy-start.16 = (f32[1,8,512]{2,1,0:T(8,128)S(1)}, f32[1,8,512]{2,1,0:T(8,128)}, u32[]{:S(2)}) copy-start(f32[1,8,512]{2,1,0:T(8,128)} %param.12) | copy-start | bytes 49156
  4.6 15.0 %collective-permute-start = (bf16[256,1024]{1,0:T(8,128)(2,1)S(1)}, bf16[256,1024]{1,0:T(8,128)(2,1)S(1)}, u32[]{:S(2)}, u32[]{:S(2)}) collective-permute-start(bf16[256,1024]{1,0:T(8,128)(2,1)S(1)} %dynamic-slice_bitcast_fusion.4), channel_id=1, source_target_pairs={{0,2},{2,0},{1,3},{3,1},{4,6},{6,4},{5,7},{7,5},{8,10},{10,8},{9,1... | collective-permute-start | bytes 1572872 | tf_op jit(solution)/shard_map/ppermute | solution.py:77
  12.0 126.7 %copy-start.13 = (pred[512,512]{0,1:T(8,128)(4,1)}, pred[512,512]{0,1:T(8,128)(4,1)S(1)}, u32[]{:S(2)}) copy-start(pred[512,512]{0,1:T(8,128)(4,1)S(1)} %fusion.64) | copy-start | bytes 786436
  19.5 1.9 %collective-permute-start.1 = (bf16[256,1024]{1,0:T(8,128)(2,1)S(1)}, bf16[256,1024]{1,0:T(8,128)(2,1)S(1)}, u32[]{:S(2)}, u32[]{:S(2)}) collective-permute-start(bf16[256,1024]{1,0:T(8,128)(2,1)S(1)} %collective-permute-done), channel_id=1, source_target_pairs={{0,1},{1,0},{2,3},{3,2},{4,5},{5,4},{6,7},{7,6},{8,9},{9,8},{10,11... | collective-permute-start | bytes 1572872 | tf_op jit(solution)/shard_map/ppermute | solution.py:67
  24.5 5.7 %copy-start.20 = (bf16[1024,2,1024]{2,1,0:T(2,128)(2,1)S(1)}, bf16[1024,2,1024]{2,1,0:T(2,128)(2,1)}, u32[]{:S(2)}) copy-start(bf16[1024,2,1024]{2,1,0:T(2,128)(2,1)} %param.10) | copy-start | bytes 12582916
  28.4 26.1 %collective-permute-start.2 = (bf16[2,256,1024]{2,1,0:T(8,128)(2,1)S(1)}, bf16[2,256,1024]{2,1,0:T(8,128)(2,1)S(1)}, u32[]{:S(2)}, u32[]{:S(2)}) collective-permute-start(bf16[2,256,1024]{2,1,0:T(8,128)(2,1)S(1)} %fusion.51), channel_id=1, source_target_pairs={{0,2},{2,0},{1,3},{3,1},{4,6},{6,4},{5,7},{7,5},{8,10},{10,8},{9,1... | collective-permute-start | bytes 3145736 | tf_op jit(solution)/shard_map/ppermute | solution.py:91
  31.9 44.3 %collective-permute-start.3 = (bf16[2,256,1024]{2,1,0:T(8,128)(2,1)S(1)}, bf16[2,256,1024]{2,1,0:T(8,128)(2,1)S(1)}, u32[]{:S(2)}, u32[]{:S(2)}) collective-permute-start(bf16[2,256,1024]{2,1,0:T(8,128)(2,1)S(1)} %fusion.48), channel_id=1, source_target_pairs={{0,2},{2,0},{1,3},{3,1},{4,6},{6,4},{5,7},{7,5},{8,10},{10,8},{9,1... | collective-permute-start | bytes 3145736 | tf_op jit(solution)/shard_map/ppermute | solution.py:91
  32.4 22.1 %copy-start.8 = (bf16[1,512,2048]{2,1,0:T(8,128)(2,1)S(1)}, bf16[1,512,2048]{2,1,0:T(8,128)(2,1)}, u32[]{:S(2)}) copy-start(bf16[1,512,2048]{2,1,0:T(8,128)(2,1)} %copy-done.7) | copy-start | bytes 6291460
  80.8 40.3 %collective-permute-start.6 = (bf16[1,512,1024]{2,1,0:T(8,128)(2,1)}, bf16[1,512,1024]{2,1,0:T(8,128)(2,1)}, u32[]{:S(2)}, u32[]{:S(2)}) collective-permute-start(bf16[1,512,1024]{2,1,0:T(8,128)(2,1)} %fusion.24), channel_id=1, source_target_pairs={{0,4},{4,8},{8,12},{1,5},{5,9},{9,13},{2,6},{6,10},{10,14},{3,7},{... | collective-permute-start | bytes 3145736 | tf_op jit(solution)/shard_map/ppermute | solution.py:14
  89.7 26.4 %collective-permute-start.4 = (bf16[512,1024]{1,0:T(8,128)(2,1)}, bf16[512,1024]{1,0:T(8,128)(2,1)}, u32[]{:S(2)}, u32[]{:S(2)}) collective-permute-start(bf16[512,1024]{1,0:T(8,128)(2,1)} %convolution_convert_fusion), channel_id=1, source_target_pairs={{0,2},{2,0},{1,3},{3,1},{4,6},{6,4},{5,7},{7,5},{8,10},{10,8},{9,1... | collective-permute-start | bytes 3145736 | tf_op jit(solution)/shard_map/ppermute | solution.py:91
  95.7 7.4 %copy-start.19 = (f32[8]{0:T(128)S(1)}, f32[8]{0:T(128)}, u32[]{:S(2)}) copy-start(f32[8]{0:T(128)} %get-tuple-element.15) | copy-start | bytes 100
  95.7 7.5 %copy-start.23 = (f32[8]{0:T(128)S(1)}, f32[8]{0:T(128)}, u32[]{:S(2)}) copy-start(f32[8]{0:T(128)} %exponential_multiply_fusion) | copy-start | bytes 100
  99.3 29.9 %collective-permute-start.5 = (bf16[1,512,1024]{2,1,0:T(8,128)(2,1)}, bf16[1,512,1024]{2,1,0:T(8,128)(2,1)}, u32[]{:S(2)}, u32[]{:S(2)}) collective-permute-start(bf16[1,512,1024]{2,1,0:T(8,128)(2,1)} %multiply_convert_fusion), channel_id=1, source_target_pairs={{0,4},{4,8},{8,12},{1,5},{5,9},{9,13},{2,6},{6,10},{10,14},{3,7},{... | collective-permute-start | bytes 3145736 | tf_op jit(solution)/shard_map/ppermute | solution.py:14
  105.2 3.8 %copy-start.5 = (bf16[1,512,1024]{1,2,0:T(8,128)(2,1)}, bf16[1,512,1024]{1,2,0:T(8,128)(2,1)S(1)}, u32[]{:S(2)}) copy-start(bf16[1,512,1024]{1,2,0:T(8,128)(2,1)S(1)} %copy.96) | copy-start | bytes 3145732
  108.5 54.1 %collective-permute-start.10 = (bf16[1024,1024]{1,0:T(8,128)(2,1)}, bf16[1024,1024]{1,0:T(8,128)(2,1)}, u32[]{:S(2)}, u32[]{:S(2)}) collective-permute-start(bf16[1024,1024]{1,0:T(8,128)(2,1)} %param.11), channel_id=1, source_target_pairs={{0,2},{2,0},{1,3},{3,1},{4,6},{6,4},{5,7},{7,5},{8,10},{10,8},{9,1... | collective-permute-start | bytes 6291464 | tf_op jit(solution)/shard_map/ppermute | solution.py:185
  109.0 7.0 %copy-start.9 = (bf16[1,512,2048]{2,1,0:T(8,128)(2,1)S(1)}, bf16[1,512,2048]{2,1,0:T(8,128)(2,1)}, u32[]{:S(2)}) copy-start(bf16[1,512,2048]{2,1,0:T(8,128)(2,1)} %copy-done.7) | copy-start | bytes 6291460
  120.4 10.3 %copy-start.18 = (f32[9]{0:T(128)S(1)}, f32[9]{0:T(128)}, u32[]{:S(2)}) copy-start(f32[9]{0:T(128)} %pad.11.clone) | copy-start | bytes 112
  121.1 14.3 %copy-start.10 = (f32[64,8,8,128]{3,2,1,0:T(8,128)S(1)}, f32[64,8,8,128]{3,2,1,0:T(8,128)}, u32[]{:S(2)}) copy-start(f32[64,8,8,128]{3,2,1,0:T(8,128)} %get-tuple-element.22) | copy-start | bytes 6291460
  130.6 5.4 %copy-start.4 = (f32[1,512,1024]{1,2,0:T(8,128)S(1)}, f32[1,512,1024]{1,2,0:T(8,128)}, u32[]{:S(2)}) copy-start(f32[1,512,1024]{1,2,0:T(8,128)} %copy.93) | copy-start | bytes 6291460
  130.7 5.4 %copy-start.14 = (pred[512,512]{0,1:T(8,128)(4,1)S(1)}, pred[512,512]{0,1:T(8,128)(4,1)}, u32[]{:S(2)}) copy-start(pred[512,512]{0,1:T(8,128)(4,1)} %iota_compare_fusion.1) | copy-start | bytes 786436
  130.8 13.2 %collective-permute-start.7 = (bf16[1,9,128,128]{3,2,1,0:T(8,128)(2,1)S(1)}, bf16[1,9,128,128]{3,2,1,0:T(8,128)(2,1)S(1)}, u32[]{:S(2)}, u32[]{:S(2)}) collective-permute-start(bf16[1,9,128,128]{3,2,1,0:T(8,128)(2,1)S(1)} %fusion.69), channel_id=1, source_target_pairs={{0,4},{4,8},{8,12},{1,5},{5,9},{9,13},{2,6},{6,10},{10,14},{3,7},{... | collective-permute-start | bytes 884744 | tf_op jit(solution)/shard_map/ppermute | solution.py:14
  138.7 8.9 %copy-start.6 = (bf16[1,512,1024]{1,2,0:T(8,128)(2,1)S(1)}, bf16[1,512,1024]{1,2,0:T(8,128)(2,1)}, u32[]{:S(2)}) copy-start(bf16[1,512,1024]{1,2,0:T(8,128)(2,1)} %copy-done.5) | copy-start | bytes 3145732
  144.1 8.3 %collective-permute-start.8 = (bf16[1,9,128,128]{3,2,1,0:T(8,128)(2,1)S(1)}, bf16[1,9,128,128]{3,2,1,0:T(8,128)(2,1)S(1)}, u32[]{:S(2)}, u32[]{:S(2)}) collective-permute-start(bf16[1,9,128,128]{3,2,1,0:T(8,128)(2,1)S(1)} %fusion.71), channel_id=1, source_target_pairs={{0,4},{4,8},{8,12},{1,5},{5,9},{9,13},{2,6},{6,10},{10,14},{3,7},{... | collective-permute-start | bytes 884744 | tf_op jit(solution)/shard_map/ppermute | solution.py:14
  152.6 9.2 %collective-permute-start.9 = (bf16[1,9,128,128]{3,2,1,0:T(8,128)(2,1)S(1)}, bf16[1,9,128,128]{3,2,1,0:T(8,128)(2,1)S(1)}, u32[]{:S(2)}, u32[]{:S(2)}) collective-permute-start(bf16[1,9,128,128]{3,2,1,0:T(8,128)(2,1)S(1)} %fusion.73), channel_id=1, source_target_pairs={{0,4},{4,8},{8,12},{1,5},{5,9},{9,13},{2,6},{6,10},{10,14},{3,7},{... | collective-permute-start | bytes 884744 | tf_op jit(solution)/shard_map/ppermute | solution.py:14
  156.9 5.0 %copy-start.12 = (bf16[512,8,128]{2,0,1:T(8,128)(2,1)S(1)}, bf16[512,8,128]{2,0,1:T(8,128)(2,1)}, u32[]{:S(2)}) copy-start(bf16[512,8,128]{2,0,1:T(8,128)(2,1)} %copy-done.11) | copy-start | bytes 3145732
  156.9 5.0 %copy-start.15 = (f32[512,8]{0,1:T(8,128)S(1)}, f32[512,8]{0,1:T(8,128)}, u32[]{:S(2)}) copy-start(f32[512,8]{0,1:T(8,128)} %get-tuple-element.17) | copy-start | bytes 49156
  157.0 5.0 %copy-start.24 = (f32[8,128,512]{2,1,0:T(8,128)S(1)}, f32[8,128,512]{2,1,0:T(8,128)}, u32[]{:S(2)}) copy-start(f32[8,128,512]{2,1,0:T(8,128)} %fusion.5) | copy-start | bytes 6291460
  162.5 4.9 %copy-start.22 = (bf16[1,512,8,128]{1,3,2,0:T(8,128)(2,1)}, bf16[1,512,8,128]{1,3,2,0:T(8,128)(2,1)S(1)}, u32[]{:S(2)}) copy-start(bf16[1,512,8,128]{1,3,2,0:T(8,128)(2,1)S(1)} %fusion.29) | copy-start | bytes 3145732
  167.4 3.4 %collective-permute-start.11 = (bf16[512,1024]{1,0:T(8,128)(2,1)}, bf16[512,1024]{1,0:T(8,128)(2,1)S(1)}, u32[]{:S(2)}, u32[]{:S(2)}) collective-permute-start(bf16[512,1024]{1,0:T(8,128)(2,1)} %fusion.38), channel_id=1, source_target_pairs={{0,1},{1,0},{2,3},{3,2},{4,5},{5,4},{6,7},{7,6},{8,9},{9,8},{10,11... | collective-permute-start | bytes 3145736 | tf_op jit(solution)/shard_map/ppermute | solution.py:209
  167.4 3.4 %copy-start.3 = (bf16[1,512,2048]{2,1,0:T(8,128)(2,1)S(1)}, bf16[1,512,2048]{2,1,0:T(8,128)(2,1)}, u32[]{:S(2)}) copy-start(bf16[1,512,2048]{2,1,0:T(8,128)(2,1)} %param.7) | copy-start | bytes 6291460
  167.4 5.0 %copy-start.1 = (bf16[1024,1024]{1,0:T(8,128)(2,1)S(1)}, bf16[1024,1024]{1,0:T(8,128)(2,1)}, u32[]{:S(2)}) copy-start(bf16[1024,1024]{1,0:T(8,128)(2,1)} %param.9) | copy-start | bytes 6291460
  (5 other events, 10.2 us)

commit v18 on v17

--- a/solution.py
+++ b/solution.py
@@ -205,11 +205,29 @@
             )
         return jnp.concatenate(parts, axis=1) if blocks_per_share > 1 else parts[0]
 
+    def output_rows(index, lo, hi):
+        parts = [
+            jnp.dot(
+                attended[lo:hi],
+                lax.dynamic_index_in_dim(from_ranks, (me - (index * blocks_per_share + part)) % ways, 0, keepdims=False),
+                preferred_element_type=jnp.float32,
+            )
+            for part in range(blocks_per_share)
+        ]
+        return jnp.concatenate(parts, axis=1) if blocks_per_share > 1 else parts[0]
+
+    half_count = count // 2
     received = [
-        lax.ppermute(
-            output_share((core + step) % cores).astype(jnp.bfloat16),
-            "heads",
-            [(source, (source + step) % cores) for source in range(cores)],
+        jnp.concatenate(
+            [
+                lax.ppermute(
+                    output_rows((core + step) % cores, lo, hi).astype(jnp.bfloat16),
+                    "heads",
+                    [(source, (source + step) % cores) for source in range(cores)],
+                )
+                for lo, hi in ((0, half_count), (half_count, count))
+            ],
+            axis=0,
         )
         for step in range(1, cores)
     ]

time: 173 us -> 178 us (1.029)
  matrix products: 41.9 us -> 44.8 us
    dot_general x0 -> x2, matrix products: none -> 7.19 us  [output_rows(): jnp.dot(attended[lo:hi], lax.dynamic_index_in_dim(from_ranks, (me - (inde...]
    dot_general x2 -> x1, matrix products: 7.3 us -> 3.07 us  [output_share(): jnp.dot(attended, lax.dynamic_index_in_dim(from_ranks, (me - rank) % ways...]
    unnamed x53 -> x51, local copies, waits for them, and re-layouts: 6.28 us -> 6.76 us
  transfers between devices with their start and end apart: 12 -> 13, of which waited for: 6 -> 6; matrix products, arithmetic and copies ran while one was open for 35% -> 34% of each run, Pallas kernels for 0% -> 0%
where the time goes in v18:
time: 178 us
  waiting for transfers between devices  59.9 us (34%)
  matrix products  44.8 us (25%)
  starting transfers between devices  28.5 us (16%)
  other arithmetic  22.3 us (13%)
  local copies, waits for them, and re-layouts  20.9 us (12%)
    ppermute x3, waiting for transfers between devices, gathered_sum(): lax.ppermute(outgoing, 'wloop', [(source, (source - step) % ways) for sou...  43.7 us
    ppermute x5, starting transfers between devices, shifted(): lax.ppermute(value, axis, [(source, source + steps) for source in range(i...  20.7 us
    dot_general x4, matrix products, shards(): jnp.einsum('td,dje->jte', rows[lo:hi], w_keyvalue, preferred_element_type...  8.95 us
    ppermute x5, waiting for transfers between devices, shifted(): lax.ppermute(value, axis, [(source, source + steps) for source in range(i...  8.03 us
    ppermute x1, waiting for transfers between devices, shards(): lax.ppermute(part, 'wloop', [(source, (source + step) % ways) for source...  7.55 us
    dot_general x2, matrix products, output_rows(): jnp.dot(attended[lo:hi], lax.dynamic_index_in_dim(from_ranks, (me - (inde...  7.19 us
    unnamed x51, local copies, waits for them, and re-layouts  6.76 us
    dot_general x2, matrix products, shards(): jnp.dot(rows, w_query, preferred_element_type=jnp.float32)  6.08 us
  transfers between devices with their start and end apart: 13, of which 6 were waited for; matrix products, arithmetic and copies ran while one was open for 34% of the time, Pallas kernels for 0%

profile of v18, /device:TPU:0, one launch (start us, length us, event | category | flops | bytes accessed | tf_op | source)
XLA Modules:
  0.0 177.7 jit_solution(3646616467736730868)
XLA Ops:
  0.0 2.2 %fusion.2 = f32[512]{0:T(512)S(1)} fusion(bf16[1,512,2048]{2,1,0:T(8,128)(2,1)} %param.7), kind=kLoop, calls=%fused_computation.18 | loop fusion | flops 3145216 | bytes 2099200 | tf_op jit(solution)/shard_map/reduce_sum | solution.py:18
  4.6 3.0 %collective-permute-start = (bf16[256,1024]{1,0:T(8,128)(2,1)S(1)}, bf16[256,1024]{1,0:T(8,128)(2,1)S(1)}, u32[]{:S(2)}, u32[]{:S(2)}) collective-permute-start(bf16[256,1024]{1,0:T(8,128)(2,1)S(1)} %dynamic-slice_bitcast_fusion.4), channel_id=1, source_target_pairs={{0,2},{2,0},{1,3},{3,1},{4,6},{6,4},{5,7},{7,5},{8,10},{10,8},{9,1... | collective-permute-start | bytes 1572872 | tf_op jit(solution)/shard_map/ppermute | solution.py:77
  12.0 7.5 %collective-permute-done = bf16[256,1024]{1,0:T(8,128)(2,1)S(1)} collective-permute-done((bf16[256,1024]{1,0:T(8,128)(2,1)S(1)}, bf16[256,1024]{1,0:T(8,128)(2,1)S(1)}, u32[]{:S(2)}, u32[]{:S(2)}) %collective-permute-start) | collective-permute-done | bytes 524320 | tf_op jit(solution)/shard_map/ppermute | solution.py:77
  22.5 1.8 %gather_fusion = bf16[2,256,1024]{2,1,0:T(8,128)(2,1)S(1)} fusion(bf16[2,256,1024]{2,1,0:T(8,128)(2,1)} %pad_maximum_fusion.1, s32[1024]{0:T(1024)S(1)} %pad_clamp_fusion), kind=kCustom, calls=%fused_computation | custom fusion | bytes 2097160 | tf_op jit(solution)/shard_map/jit(_take)/gather | solution.py:70
  24.5 3.9 %fusion.46 = bf16[2,256,1024]{2,1,0:T(8,128)(2,1)S(1)} fusion(bf16[1024,2,1024]{2,1,0:T(2,128)(2,1)} %param.10, bf16[2,256,1024]{2,1,0:T(8,128)(2,1)S(1)} %broadcast_select_fusion), kind=kOutput, calls=%fused_computation.62 | convolution fusion | flops 1074266112 | bytes 5767168 | tf_op jit(solution)/shard_map/td,dje->jte/dot_general | solution.py:103
  28.4 1.8 %collective-permute-start.2 = (bf16[2,256,1024]{2,1,0:T(8,128)(2,1)S(1)}, bf16[2,256,1024]{2,1,0:T(8,128)(2,1)S(1)}, u32[]{:S(2)}, u32[]{:S(2)}) collective-permute-start(bf16[2,256,1024]{2,1,0:T(8,128)(2,1)S(1)} %fusion.46), channel_id=1, source_target_pairs={{0,2},{2,0},{1,3},{3,1},{4,6},{6,4},{5,7},{7,5},{8,10},{10,8},{9,1... | collective-permute-start | bytes 3145736 | tf_op jit(solution)/shard_map/ppermute | solution.py:91
  32.4 2.2 %convolution_convert_fusion = bf16[512,1024]{1,0:T(8,128)(2,1)} fusion(bf16[512,1024]{1,0:T(8,128)(2,1)S(1)} %bitcast_select_fusion, bf16[1024,1024]{1,0:T(8,128)(2,1)S(1)} %copy-done), kind=kOutput, calls=%fused_computation.59 | convolution fusion | flops 1074266112 | bytes 4194304 | tf_op jit(solution)/shard_map/dot_general | solution.py:112
  34.7 19.9 %collective-permute-done.2 = bf16[2,256,1024]{2,1,0:T(8,128)(2,1)S(1)} collective-permute-done((bf16[2,256,1024]{2,1,0:T(8,128)(2,1)S(1)}, bf16[2,256,1024]{2,1,0:T(8,128)(2,1)S(1)}, u32[]{:S(2)}, u32[]{:S(2)}) %collective-permute-start.2) | collective-permute-done | bytes 1048608 | tf_op jit(solution)/shard_map/ppermute | solution.py:91
  56.3 19.9 %collective-permute-done.3 = bf16[2,256,1024]{2,1,0:T(8,128)(2,1)S(1)} collective-permute-done((bf16[2,256,1024]{2,1,0:T(8,128)(2,1)S(1)}, bf16[2,256,1024]{2,1,0:T(8,128)(2,1)S(1)}, u32[]{:S(2)}, u32[]{:S(2)}) %collective-permute-start.3) | collective-permute-done | bytes 1048608 | tf_op jit(solution)/shard_map/ppermute | solution.py:91
  79.0 1.7 multiply_bitcast_fusion
  80.8 4.8 %collective-permute-start.6 = (bf16[1,512,1024]{2,1,0:T(8,128)(2,1)}, bf16[1,512,1024]{2,1,0:T(8,128)(2,1)}, u32[]{:S(2)}, u32[]{:S(2)}) collective-permute-start(bf16[1,512,1024]{2,1,0:T(8,128)(2,1)} %fusion.22), channel_id=1, source_target_pairs={{0,4},{4,8},{8,12},{1,5},{5,9},{9,13},{2,6},{6,10},{10,14},{3,7},{... | collective-permute-start | bytes 3145736 | tf_op jit(solution)/shard_map/ppermute | solution.py:14
  85.5 1.8 %copy.99 = f32[64,8,8,128]{3,2,1,0:T(8,128)} copy(f32[64,8,8,128]{3,1,2,0:T(8,128)S(1)} %get-tuple-element.19) | data formatting | bytes 4194304
  87.3 2.2 %reduce_sum.58 = f32[512,8]{1,0:T(8,128)S(1)} reduce(f32[512,8,128]{2,1,0:T(8,128)} %bitcast.145, f32[]{:T(128)} %constant.113.clone.1), dimensions={2}, to_apply=%region_2.3 | reduce | flops 520192 | bytes 2113540 | tf_op jit(solution)/shard_map/reduce_sum | solution.py:18
  92.8 2.9 %copy.94 = f32[1,512,1024]{2,1,0:T(8,128)} copy(f32[1,512,1024]{1,2,0:T(8,128)} %bitcast.146) | data formatting | bytes 4194304 | tf_op jit(solution)/shard_map/mul | solution.py:18
  95.7 3.5 %multiply_convert_fusion = bf16[1,512,1024]{2,1,0:T(8,128)(2,1)} fusion(f32[1,512,1024]{2,1,0:T(8,128)} %get-tuple-element.20, f32[1,512,1024]{2,1,0:T(8,128)} %copy.94), kind=kLoop, calls=%fused_computation.49 | loop fusion | flops 1048576 | bytes 5242880 | tf_op jit(solution)/shard_map/convert_element_type | solution.py:115
  99.2 3.6 %collective-permute-start.5 = (bf16[1,512,1024]{2,1,0:T(8,128)(2,1)}, bf16[1,512,1024]{2,1,0:T(8,128)(2,1)}, u32[]{:S(2)}, u32[]{:S(2)}) collective-permute-start(bf16[1,512,1024]{2,1,0:T(8,128)(2,1)} %multiply_convert_fusion), channel_id=1, source_target_pairs={{0,4},{4,8},{8,12},{1,5},{5,9},{9,13},{2,6},{6,10},{10,14},{3,7},{... | collective-permute-start | bytes 3145736 | tf_op jit(solution)/shard_map/ppermute | solution.py:14
  105.2 3.3 %copy.93 = f32[1,512,1024]{1,2,0:T(8,128)} copy(f32[1,512,1024]{2,1,0:T(8,128)} %get-tuple-element.20) | data formatting | bytes 4194304 | tf_op jit(solution)/shard_map/reshape;squeeze | solution.py:115
  109.1 2.9 %fusion.49 = f32[1,8,128,128]{3,2,1,0:T(8,128)S(1)} fusion(bf16[512,8,128]{0,2,1:T(8,128)(2,1)S(1)} %bitcast.147, f32[512,8]{0,1:T(8,128)} %fusion.76, f32[512,8,128]{0,2,1:T(8,128)} %bitcast.142, f32[512,8]{0,1:T(8,128)S(1)} %add_rsqrt_fusion), kind=kOutput, calls=%fused_computation.65 | convolution fusion | flops 807403520 | bytes 3702784 | tf_op jit(solution)/shard_map/bht,bthd,bthe->bhde/dot_general | solution.py:132
  112.1 4.0 %collective-permute-done.4 = bf16[512,1024]{1,0:T(8,128)(2,1)} collective-permute-done((bf16[512,1024]{1,0:T(8,128)(2,1)}, bf16[512,1024]{1,0:T(8,128)(2,1)}, u32[]{:S(2)}, u32[]{:S(2)}) %collective-permute-start.4) | collective-permute-done | bytes 1048608 | tf_op jit(solution)/shard_map/ppermute | solution.py:91
  116.0 3.8 %multiply_bitcast_fusion.1 = (f32[64,8,8,128]{3,1,2,0:T(8,128)S(1)}, f32[64,8,8,128]{3,2,1,0:T(8,128)}) fusion(bf16[512,1024]{1,0:T(8,128)(2,1)} %collective-permute-done.4, bf16[1024,1024]{1,0:T(8,128)(2,1)S(1)} %copy-done, bf16[1,512,2048]{2,1,0:T(8,128)(2,1)S(1)} %copy-done.9, s32[]{:T(128)S(6)} %select_n.98), kind=kOutput, calls=%fused_computation.55 | convolution fusion | flops 1075314688 | bytes 8388612 | tf_op jit(solution)/shard_map/dot_general | solution.py:112
  121.1 8.0 %collective-permute-done.5 = bf16[1,512,1024]{2,1,0:T(8,128)(2,1)} collective-permute-done((bf16[1,512,1024]{2,1,0:T(8,128)(2,1)}, bf16[1,512,1024]{2,1,0:T(8,128)(2,1)}, u32[]{:S(2)}, u32[]{:S(2)}) %collective-permute-start.5) | collective-permute-done | bytes 1048608 | tf_op jit(solution)/shard_map/ppermute | solution.py:14
  130.8 4.5 %collective-permute-start.7 = (bf16[1,9,128,128]{3,2,1,0:T(8,128)(2,1)S(1)}, bf16[1,9,128,128]{3,2,1,0:T(8,128)(2,1)S(1)}, u32[]{:S(2)}, u32[]{:S(2)}) collective-permute-start(bf16[1,9,128,128]{3,2,1,0:T(8,128)(2,1)S(1)} %fusion.64), channel_id=1, source_target_pairs={{0,4},{4,8},{8,12},{1,5},{5,9},{9,13},{2,6},{6,10},{10,14},{3,7},{... | collective-permute-start | bytes 884744 | tf_op jit(solution)/shard_map/ppermute | solution.py:14
  136.1 2.6 %fusion = (f32[8,512]{1,0:T(8,128)S(1)}, f32[8,512,512]{1,2,0:T(8,128)S(1)}) fusion(pred[512,512]{0,1:T(8,128)(4,1)S(1)} %copy-done.14, bf16[512,8,128]{2,0,1:T(8,128)(2,1)S(1)} %fusion.24, f32[512,8,128]{0,2,1:T(8,128)S(1)} %bitcast.143, f32[512,8]{0,1:T(8,128)S(1)} %add_rsqrt_fusion), kind=kOutput, calls=%fused_computation.5 | convolution fusion | flops 544206848 | bytes 11829248 | tf_op jit(solution)/shard_map/bihd,bjhd->bhij/dot_general | solution.py:23
  138.7 5.2 %fusion.1 = (f32[8,512]{1,0:T(8,128)S(1)}, f32[8,512,512]{1,2,0:T(8,128)}) fusion(pred[512,512]{0,1:T(8,128)(4,1)S(1)} %fusion.59, bf16[512,8,128]{2,0,1:T(8,128)(2,1)S(1)} %fusion.24, bf16[512,8,128]{2,1,0:T(8,128)(2,1)S(1)} %bitcast.154), kind=kOutput, calls=%fused_computation.6 | convolution fusion | flops 543158272 | bytes 10764288 | tf_op jit(solution)/shard_map/bihd,bjhd->bhij/dot_general | solution.py:27
  144.1 3.5 %collective-permute-start.8 = (bf16[1,9,128,128]{3,2,1,0:T(8,128)(2,1)S(1)}, bf16[1,9,128,128]{3,2,1,0:T(8,128)(2,1)S(1)}, u32[]{:S(2)}, u32[]{:S(2)}) collective-permute-start(bf16[1,9,128,128]{3,2,1,0:T(8,128)(2,1)S(1)} %fusion.66), channel_id=1, source_target_pairs={{0,4},{4,8},{8,12},{1,5},{5,9},{9,13},{2,6},{6,10},{10,14},{3,7},{... | collective-permute-start | bytes 884744 | tf_op jit(solution)/shard_map/ppermute | solution.py:14
  147.6 3.3 %fusion.5 = f32[8,128,512]{2,1,0:T(8,128)} fusion(bf16[512,8,128]{0,2,1:T(8,128)(2,1)S(1)} %bitcast.148, f32[8,512,512]{1,2,0:T(8,128)S(1)} %get-tuple-element.26, f32[8,512]{1,0:T(8,128)S(1)} %add.172, pred[512,512]{0,1:T(8,128)(4,1)S(1)} %copy-done.14), kind=kOutput, calls=%fused_computation.21 | convolution fusion | flops 545259520 | bytes 11812864 | tf_op jit(solution)/shard_map/bhij,bjhd->bihd/dot_general | solution.py:38
  152.6 4.3 %collective-permute-start.9 = (bf16[1,9,128,128]{3,2,1,0:T(8,128)(2,1)S(1)}, bf16[1,9,128,128]{3,2,1,0:T(8,128)(2,1)S(1)}, u32[]{:S(2)}, u32[]{:S(2)}) collective-permute-start(bf16[1,9,128,128]{3,2,1,0:T(8,128)(2,1)S(1)} %fusion.68), channel_id=1, source_target_pairs={{0,4},{4,8},{8,12},{1,5},{5,9},{9,13},{2,6},{6,10},{10,14},{3,7},{... | collective-permute-start | bytes 884744 | tf_op jit(solution)/shard_map/ppermute | solution.py:14
  157.0 4.8 %fusion.6 = f32[8,128,512]{2,1,0:T(8,128)S(1)} fusion(bf16[512,8,128]{0,2,1:T(8,128)(2,1)S(1)} %bitcast.153, f32[8,512,512]{1,2,0:T(8,128)} %get-tuple-element.28, f32[8,512]{1,0:T(8,128)S(1)} %add.172, pred[512,512]{0,1:T(8,128)(4,1)} %copy-done.13), kind=kOutput, calls=%fused_computation.22 | convolution fusion | flops 545259520 | bytes 11812864 | tf_op jit(solution)/shard_map/bhij,bjhd->bihd/dot_general | solution.py:40
  164.2 3.6 %convolution_convert_fusion.2 = bf16[256,1024]{1,0:T(8,128)(2,1)} fusion(bf16[256,1024]{0,1:T(8,128)(2,1)S(1)} %bitcast.158, s32[]{:T(128)S(6)} %select_n.116, bf16[1,1024,1024]{2,1,0:T(8,128)(2,1)S(1)} %bitcast.166, bf16[1,1024,1024]{2,1,0:T(8,128)(2,1)} %bitcast.48), kind=kOutput, calls=%fused_computation.64 | convolution fusion | flops 538181632 | bytes 5242884 | tf_op jit(solution)/shard_map/dot_general | solution.py:210
  167.8 3.6 %convolution_convert_fusion.1 = bf16[256,1024]{1,0:T(8,128)(2,1)} fusion(bf16[256,1024]{0,1:T(8,128)(2,1)S(1)} %bitcast.157, s32[]{:T(128)S(6)} %select_n.116, bf16[1,1024,1024]{2,1,0:T(8,128)(2,1)S(1)} %bitcast.167, bf16[1,1024,1024]{2,1,0:T(8,128)(2,1)} %bitcast.48), kind=kOutput, calls=%fused_computation.63 | convolution fusion | flops 538181632 | bytes 5242884 | tf_op jit(solution)/shard_map/dot_general | solution.py:210
  171.9 3.1 %fusion.19 = f32[512,1024]{1,0:T(8,128)S(1)} fusion(bf16[512,1024]{0,1:T(8,128)(2,1)S(1)} %bitcast.152, s32[]{:T(128)S(6)} %select_n.113, bf16[1,1024,1024]{2,1,0:T(8,128)(2,1)} %bitcast.165, bf16[1,1024,1024]{2,1,0:T(8,128)(2,1)} %bitcast.48), kind=kOutput, calls=%fused_computation.35 | convolution fusion | flops 1074790400 | bytes 7340036 | tf_op jit(solution)/shard_map/dot_general | solution.py:200
  175.0 2.8 %fusion.52 = bf16[1,512,1024]{2,1,0:T(8,128)(2,1)} fusion(f32[512,1024]{1,0:T(8,128)S(1)} %fusion.19, bf16[256,1024]{1,0:T(8,128)(2,1)} %collective-permute-done.12, bf16[256,1024]{1,0:T(8,128)(2,1)} %collective-permute-done.11, bf16[1,512,2048]{2,1,0:T(8,128)(2,1)S(1)} %copy-done.3, s32[]{:T(128)S(6)} %select_n.97), kind=kLoop, calls=%fused_computation.66 | loop fusion | flops 4194304 | bytes 5242884 | tf_op jit(solution)/shard_map/reshape | solution.py:240
  (112 shorter events, 30.1 us)
Async XLA Ops:
  0.0 32.4 %copy-start = (bf16[1024,1024]{1,0:T(8,128)(2,1)S(1)}, bf16[1024,1024]{1,0:T(8,128)(2,1)}, u32[]{:S(2)}) copy-start(bf16[1024,1024]{1,0:T(8,128)(2,1)} %param.9) | copy-start | bytes 6291460
  2.4 6.0 %copy-start.16 = (f32[1,8,512]{2,1,0:T(8,128)S(1)}, f32[1,8,512]{2,1,0:T(8,128)}, u32[]{:S(2)}) copy-start(f32[1,8,512]{2,1,0:T(8,128)} %param.12) | copy-start | bytes 49156
  4.6 15.0 %collective-permute-start = (bf16[256,1024]{1,0:T(8,128)(2,1)S(1)}, bf16[256,1024]{1,0:T(8,128)(2,1)S(1)}, u32[]{:S(2)}, u32[]{:S(2)}) collective-permute-start(bf16[256,1024]{1,0:T(8,128)(2,1)S(1)} %dynamic-slice_bitcast_fusion.4), channel_id=1, source_target_pairs={{0,2},{2,0},{1,3},{3,1},{4,6},{6,4},{5,7},{7,5},{8,10},{10,8},{9,1... | collective-permute-start | bytes 1572872 | tf_op jit(solution)/shard_map/ppermute | solution.py:77
  12.0 126.7 %copy-start.13 = (pred[512,512]{0,1:T(8,128)(4,1)}, pred[512,512]{0,1:T(8,128)(4,1)S(1)}, u32[]{:S(2)}) copy-start(pred[512,512]{0,1:T(8,128)(4,1)S(1)} %fusion.59) | copy-start | bytes 786436
  19.5 1.9 %collective-permute-start.1 = (bf16[256,1024]{1,0:T(8,128)(2,1)S(1)}, bf16[256,1024]{1,0:T(8,128)(2,1)S(1)}, u32[]{:S(2)}, u32[]{:S(2)}) collective-permute-start(bf16[256,1024]{1,0:T(8,128)(2,1)S(1)} %collective-permute-done), channel_id=1, source_target_pairs={{0,1},{1,0},{2,3},{3,2},{4,5},{5,4},{6,7},{7,6},{8,9},{9,8},{10,11... | collective-permute-start | bytes 1572872 | tf_op jit(solution)/shard_map/ppermute | solution.py:67
  24.5 5.8 %copy-start.20 = (bf16[1024,2,1024]{2,1,0:T(2,128)(2,1)S(1)}, bf16[1024,2,1024]{2,1,0:T(2,128)(2,1)}, u32[]{:S(2)}) copy-start(bf16[1024,2,1024]{2,1,0:T(2,128)(2,1)} %param.10) | copy-start | bytes 12582916
  28.4 26.1 %collective-permute-start.2 = (bf16[2,256,1024]{2,1,0:T(8,128)(2,1)S(1)}, bf16[2,256,1024]{2,1,0:T(8,128)(2,1)S(1)}, u32[]{:S(2)}, u32[]{:S(2)}) collective-permute-start(bf16[2,256,1024]{2,1,0:T(8,128)(2,1)S(1)} %fusion.46), channel_id=1, source_target_pairs={{0,2},{2,0},{1,3},{3,1},{4,6},{6,4},{5,7},{7,5},{8,10},{10,8},{9,1... | collective-permute-start | bytes 3145736 | tf_op jit(solution)/shard_map/ppermute | solution.py:91
  31.9 44.3 %collective-permute-start.3 = (bf16[2,256,1024]{2,1,0:T(8,128)(2,1)S(1)}, bf16[2,256,1024]{2,1,0:T(8,128)(2,1)S(1)}, u32[]{:S(2)}, u32[]{:S(2)}) collective-permute-start(bf16[2,256,1024]{2,1,0:T(8,128)(2,1)S(1)} %fusion.43), channel_id=1, source_target_pairs={{0,2},{2,0},{1,3},{3,1},{4,6},{6,4},{5,7},{7,5},{8,10},{10,8},{9,1... | collective-permute-start | bytes 3145736 | tf_op jit(solution)/shard_map/ppermute | solution.py:91
  32.4 22.1 %copy-start.8 = (bf16[1,512,2048]{2,1,0:T(8,128)(2,1)S(1)}, bf16[1,512,2048]{2,1,0:T(8,128)(2,1)}, u32[]{:S(2)}) copy-start(bf16[1,512,2048]{2,1,0:T(8,128)(2,1)} %copy-done.7) | copy-start | bytes 6291460
  80.8 40.3 %collective-permute-start.6 = (bf16[1,512,1024]{2,1,0:T(8,128)(2,1)}, bf16[1,512,1024]{2,1,0:T(8,128)(2,1)}, u32[]{:S(2)}, u32[]{:S(2)}) collective-permute-start(bf16[1,512,1024]{2,1,0:T(8,128)(2,1)} %fusion.22), channel_id=1, source_target_pairs={{0,4},{4,8},{8,12},{1,5},{5,9},{9,13},{2,6},{6,10},{10,14},{3,7},{... | collective-permute-start | bytes 3145736 | tf_op jit(solution)/shard_map/ppermute | solution.py:14
  89.7 26.4 %collective-permute-start.4 = (bf16[512,1024]{1,0:T(8,128)(2,1)}, bf16[512,1024]{1,0:T(8,128)(2,1)}, u32[]{:S(2)}, u32[]{:S(2)}) collective-permute-start(bf16[512,1024]{1,0:T(8,128)(2,1)} %convolution_convert_fusion), channel_id=1, source_target_pairs={{0,2},{2,0},{1,3},{3,1},{4,6},{6,4},{5,7},{7,5},{8,10},{10,8},{9,1... | collective-permute-start | bytes 3145736 | tf_op jit(solution)/shard_map/ppermute | solution.py:91
  95.7 7.4 %copy-start.19 = (f32[8]{0:T(128)S(1)}, f32[8]{0:T(128)}, u32[]{:S(2)}) copy-start(f32[8]{0:T(128)} %get-tuple-element.15) | copy-start | bytes 100
  95.7 7.4 %copy-start.22 = (f32[8]{0:T(128)S(1)}, f32[8]{0:T(128)}, u32[]{:S(2)}) copy-start(f32[8]{0:T(128)} %exponential_multiply_fusion) | copy-start | bytes 100
  99.2 29.9 %collective-permute-start.5 = (bf16[1,512,1024]{2,1,0:T(8,128)(2,1)}, bf16[1,512,1024]{2,1,0:T(8,128)(2,1)}, u32[]{:S(2)}, u32[]{:S(2)}) collective-permute-start(bf16[1,512,1024]{2,1,0:T(8,128)(2,1)} %multiply_convert_fusion), channel_id=1, source_target_pairs={{0,4},{4,8},{8,12},{1,5},{5,9},{9,13},{2,6},{6,10},{10,14},{3,7},{... | collective-permute-start | bytes 3145736 | tf_op jit(solution)/shard_map/ppermute | solution.py:14
  105.2 3.8 %copy-start.5 = (bf16[1,512,1024]{1,2,0:T(8,128)(2,1)}, bf16[1,512,1024]{1,2,0:T(8,128)(2,1)S(1)}, u32[]{:S(2)}) copy-start(bf16[1,512,1024]{1,2,0:T(8,128)(2,1)S(1)} %copy.96) | copy-start | bytes 3145732
  108.5 54.2 %collective-permute-start.10 = (bf16[1024,1024]{1,0:T(8,128)(2,1)}, bf16[1024,1024]{1,0:T(8,128)(2,1)}, u32[]{:S(2)}, u32[]{:S(2)}) collective-permute-start(bf16[1024,1024]{1,0:T(8,128)(2,1)} %param.11), channel_id=1, source_target_pairs={{0,2},{2,0},{1,3},{3,1},{4,6},{6,4},{5,7},{7,5},{8,10},{10,8},{9,1... | collective-permute-start | bytes 6291464 | tf_op jit(solution)/shard_map/ppermute | solution.py:185
  109.1 7.0 %copy-start.9 = (bf16[1,512,2048]{2,1,0:T(8,128)(2,1)S(1)}, bf16[1,512,2048]{2,1,0:T(8,128)(2,1)}, u32[]{:S(2)}) copy-start(bf16[1,512,2048]{2,1,0:T(8,128)(2,1)} %copy-done.7) | copy-start | bytes 6291460
  120.3 10.3 %copy-start.18 = (f32[9]{0:T(128)S(1)}, f32[9]{0:T(128)}, u32[]{:S(2)}) copy-start(f32[9]{0:T(128)} %pad.13.clone) | copy-start | bytes 112
  121.1 14.3 %copy-start.10 = (f32[64,8,8,128]{3,2,1,0:T(8,128)S(1)}, f32[64,8,8,128]{3,2,1,0:T(8,128)}, u32[]{:S(2)}) copy-start(f32[64,8,8,128]{3,2,1,0:T(8,128)} %get-tuple-element.22) | copy-start | bytes 6291460
  130.6 5.4 %copy-start.4 = (f32[1,512,1024]{1,2,0:T(8,128)S(1)}, f32[1,512,1024]{1,2,0:T(8,128)}, u32[]{:S(2)}) copy-start(f32[1,512,1024]{1,2,0:T(8,128)} %copy.93) | copy-start | bytes 6291460
  130.6 5.4 %copy-start.14 = (pred[512,512]{0,1:T(8,128)(4,1)S(1)}, pred[512,512]{0,1:T(8,128)(4,1)}, u32[]{:S(2)}) copy-start(pred[512,512]{0,1:T(8,128)(4,1)} %iota_compare_fusion.1) | copy-start | bytes 786436
  130.8 13.2 %collective-permute-start.7 = (bf16[1,9,128,128]{3,2,1,0:T(8,128)(2,1)S(1)}, bf16[1,9,128,128]{3,2,1,0:T(8,128)(2,1)S(1)}, u32[]{:S(2)}, u32[]{:S(2)}) collective-permute-start(bf16[1,9,128,128]{3,2,1,0:T(8,128)(2,1)S(1)} %fusion.64), channel_id=1, source_target_pairs={{0,4},{4,8},{8,12},{1,5},{5,9},{9,13},{2,6},{6,10},{10,14},{3,7},{... | collective-permute-start | bytes 884744 | tf_op jit(solution)/shard_map/ppermute | solution.py:14
  138.7 8.9 %copy-start.6 = (bf16[1,512,1024]{1,2,0:T(8,128)(2,1)S(1)}, bf16[1,512,1024]{1,2,0:T(8,128)(2,1)}, u32[]{:S(2)}) copy-start(bf16[1,512,1024]{1,2,0:T(8,128)(2,1)} %copy-done.5) | copy-start | bytes 3145732
  144.1 8.4 %collective-permute-start.8 = (bf16[1,9,128,128]{3,2,1,0:T(8,128)(2,1)S(1)}, bf16[1,9,128,128]{3,2,1,0:T(8,128)(2,1)S(1)}, u32[]{:S(2)}, u32[]{:S(2)}) collective-permute-start(bf16[1,9,128,128]{3,2,1,0:T(8,128)(2,1)S(1)} %fusion.66), channel_id=1, source_target_pairs={{0,4},{4,8},{8,12},{1,5},{5,9},{9,13},{2,6},{6,10},{10,14},{3,7},{... | collective-permute-start | bytes 884744 | tf_op jit(solution)/shard_map/ppermute | solution.py:14
  152.6 9.2 %collective-permute-start.9 = (bf16[1,9,128,128]{3,2,1,0:T(8,128)(2,1)S(1)}, bf16[1,9,128,128]{3,2,1,0:T(8,128)(2,1)S(1)}, u32[]{:S(2)}, u32[]{:S(2)}) collective-permute-start(bf16[1,9,128,128]{3,2,1,0:T(8,128)(2,1)S(1)} %fusion.68), channel_id=1, source_target_pairs={{0,4},{4,8},{8,12},{1,5},{5,9},{9,13},{2,6},{6,10},{10,14},{3,7},{... | collective-permute-start | bytes 884744 | tf_op jit(solution)/shard_map/ppermute | solution.py:14
  157.0 5.0 %copy-start.12 = (bf16[512,8,128]{2,0,1:T(8,128)(2,1)S(1)}, bf16[512,8,128]{2,0,1:T(8,128)(2,1)}, u32[]{:S(2)}) copy-start(bf16[512,8,128]{2,0,1:T(8,128)(2,1)} %copy-done.11) | copy-start | bytes 3145732
  157.0 5.0 %copy-start.15 = (f32[512,8]{0,1:T(8,128)S(1)}, f32[512,8]{0,1:T(8,128)}, u32[]{:S(2)}) copy-start(f32[512,8]{0,1:T(8,128)} %get-tuple-element.17) | copy-start | bytes 49156
  157.0 5.0 %copy-start.23 = (f32[8,128,512]{2,1,0:T(8,128)S(1)}, f32[8,128,512]{2,1,0:T(8,128)}, u32[]{:S(2)}) copy-start(f32[8,128,512]{2,1,0:T(8,128)} %fusion.5) | copy-start | bytes 6291460
  171.4 3.6 %collective-permute-start.12 = (bf16[256,1024]{1,0:T(8,128)(2,1)}, bf16[256,1024]{1,0:T(8,128)(2,1)}, u32[]{:S(2)}, u32[]{:S(2)}) collective-permute-start(bf16[256,1024]{1,0:T(8,128)(2,1)} %convolution_convert_fusion.1), channel_id=1, source_target_pairs={{0,1},{1,0},{2,3},{3,2},{4,5},{5,4},{6,7},{7,6},{8,9},{9,8},{10,11... | collective-permute-start | bytes 1572872 | tf_op jit(solution)/shard_map/ppermute | solution.py:223
  171.4 3.6 %collective-permute-start.11 = (bf16[256,1024]{1,0:T(8,128)(2,1)}, bf16[256,1024]{1,0:T(8,128)(2,1)}, u32[]{:S(2)}, u32[]{:S(2)}) collective-permute-start(bf16[256,1024]{1,0:T(8,128)(2,1)} %convolution_convert_fusion.2), channel_id=1, source_target_pairs={{0,1},{1,0},{2,3},{3,2},{4,5},{5,4},{6,7},{7,6},{8,9},{9,8},{10,11... | collective-permute-start | bytes 1572872 | tf_op jit(solution)/shard_map/ppermute | solution.py:223
  171.9 3.1 %copy-start.3 = (bf16[1,512,2048]{2,1,0:T(8,128)(2,1)S(1)}, bf16[1,512,2048]{2,1,0:T(8,128)(2,1)}, u32[]{:S(2)}) copy-start(bf16[1,512,2048]{2,1,0:T(8,128)(2,1)} %param.7) | copy-start | bytes 6291460
  171.9 5.9 %copy-start.1 = (bf16[1024,1024]{1,0:T(8,128)(2,1)S(1)}, bf16[1024,1024]{1,0:T(8,128)(2,1)}, u32[]{:S(2)}) copy-start(bf16[1024,1024]{1,0:T(8,128)(2,1)} %param.9) | copy-start | bytes 6291460
  (5 other events, 10.2 us)

commit v19 on v17

--- a/solution.py
+++ b/solution.py
@@ -95,7 +95,7 @@
             ).astype(jnp.float32)
         return total
 
-    half_rows = count // 2
+    piece_rows = count // 4
     pair_raw = jnp.concatenate(
         [
             gathered_sum(
@@ -104,7 +104,7 @@
                     for rows in stacked
                 ]
             )
-            for lo, hi in ((0, half_rows), (half_rows, count))
+            for lo, hi in [(k * piece_rows, (k + 1) * piece_rows) for k in range(4)]
         ],
         axis=1,
     )

time: 173 us -> 176 us (1.017)
  matrix products: 41.9 us -> 48.1 us
  waiting for transfers between devices: 60 us -> 54.3 us
  local copies, waits for them, and re-layouts: 20.2 us -> 22.4 us
    ppermute x3 -> x5, waiting for transfers between devices: 43.8 us -> 35 us  [gathered_sum(): lax.ppermute(outgoing, 'wloop', [(source, (source - step) % ways) for sou...]
    dot_general x4 -> x8, matrix products: 8.97 us -> 15 us  [shards(): jnp.einsum('td,dje->jte', rows[lo:hi], w_keyvalue, preferred_element_type...]
    ppermute x5, waiting for transfers between devices: 8.03 us -> 11.1 us  [shifted(): lax.ppermute(value, axis, [(source, source + steps) for source in range(i...]
    ppermute x3 -> x5, starting transfers between devices: 3.68 us -> 5.68 us  [gathered_sum(): lax.ppermute(outgoing, 'wloop', [(source, (source - step) % ways) for sou...]
    unnamed x53 -> x55, local copies, waits for them, and re-layouts: 6.28 us -> 7.13 us
  transfers between devices with their start and end apart: 12 -> 14, of which waited for: 6 -> 7; matrix products, arithmetic and copies ran while one was open for 35% -> 37% of each run, Pallas kernels for 0% -> 0%
where the time goes in v19:
time: 176 us; the launch traced here: 175 us
  waiting for transfers between devices  54.3 us (31%)
  matrix products  48.1 us (27%)
  starting transfers between devices  29.4 us (17%)
  local copies, waits for them, and re-layouts  22.4 us (13%)
  other arithmetic  19.9 us (11%)
    ppermute x5, waiting for transfers between devices, gathered_sum(): lax.ppermute(outgoing, 'wloop', [(source, (source - step) % ways) for sou...  35 us
    ppermute x5, starting transfers between devices, shifted(): lax.ppermute(value, axis, [(source, source + steps) for source in range(i...  20.1 us
    dot_general x8, matrix products, shards(): jnp.einsum('td,dje->jte', rows[lo:hi], w_keyvalue, preferred_element_type...  15 us
    ppermute x5, waiting for transfers between devices, shifted(): lax.ppermute(value, axis, [(source, source + steps) for source in range(i...  11.1 us
    ppermute x1, waiting for transfers between devices, shards(): lax.ppermute(part, 'wloop', [(source, (source + step) % ways) for source...  7.51 us
    dot_general x2, matrix products, output_share(): jnp.dot(attended, lax.dynamic_index_in_dim(from_ranks, (me - rank) % ways...  7.28 us
    unnamed x55, local copies, waits for them, and re-layouts  7.13 us
    dot_general x2, matrix products, shards(): jnp.dot(rows, w_query, preferred_element_type=jnp.float32)  6.07 us
  transfers between devices with their start and end apart: 14, of which 7 were waited for; matrix products, arithmetic and copies ran while one was open for 37% of the time, Pallas kernels for 0%

profile of v19, /device:TPU:0, one launch (start us, length us, event | category | flops | bytes accessed | tf_op | source)
XLA Modules:
  0.0 175.3 jit_solution(11083205343583846123)
XLA Ops:
  0.0 2.2 %fusion.2 = f32[512]{0:T(512)S(1)} fusion(bf16[1,512,2048]{2,1,0:T(8,128)(2,1)} %param.7), kind=kLoop, calls=%fused_computation.13 | loop fusion | flops 3145216 | bytes 2099200 | tf_op jit(solution)/shard_map/reduce_sum | solution.py:18
  4.6 3.0 %collective-permute-start = (bf16[256,1024]{1,0:T(8,128)(2,1)S(1)}, bf16[256,1024]{1,0:T(8,128)(2,1)S(1)}, u32[]{:S(2)}, u32[]{:S(2)}) collective-permute-start(bf16[256,1024]{1,0:T(8,128)(2,1)S(1)} %dynamic-slice_bitcast_fusion), channel_id=1, source_target_pairs={{0,2},{2,0},{1,3},{3,1},{4,6},{6,4},{5,7},{7,5},{8,10},{10,8},{9,1... | collective-permute-start | bytes 1572872 | tf_op jit(solution)/shard_map/ppermute | solution.py:77
  12.0 7.5 %collective-permute-done = bf16[256,1024]{1,0:T(8,128)(2,1)S(1)} collective-permute-done((bf16[256,1024]{1,0:T(8,128)(2,1)S(1)}, bf16[256,1024]{1,0:T(8,128)(2,1)S(1)}, u32[]{:S(2)}, u32[]{:S(2)}) %collective-permute-start) | collective-permute-done | bytes 524320 | tf_op jit(solution)/shard_map/ppermute | solution.py:77
  22.5 1.8 %gather_fusion = bf16[2,256,1024]{2,1,0:T(8,128)(2,1)S(1)} fusion(bf16[2,256,1024]{2,1,0:T(8,128)(2,1)} %pad_maximum_fusion.1, s32[1024]{0:T(1024)S(1)} %pad_clamp_fusion), kind=kCustom, calls=%fused_computation | custom fusion | bytes 2097160 | tf_op jit(solution)/shard_map/jit(_take)/gather | solution.py:70
  24.6 3.9 %fusion.33 = bf16[2,128,1024]{2,1,0:T(8,128)(2,1)S(1)} fusion(bf16[1024,2,1024]{2,1,0:T(2,128)(2,1)} %param.10, bf16[512,1024]{1,0:T(8,128)(2,1)S(1)} %bitcast_select_fusion), kind=kOutput, calls=%fused_computation.57 | convolution fusion | flops 537133056 | bytes 4980736 | tf_op jit(solution)/shard_map/td,dje->jte/dot_general | solution.py:103
  31.6 1.8 %collective-permute-start.2 = (bf16[2,128,1024]{2,1,0:T(8,128)(2,1)S(1)}, bf16[2,128,1024]{2,1,0:T(8,128)(2,1)S(1)}, u32[]{:S(2)}, u32[]{:S(2)}) collective-permute-start(bf16[2,128,1024]{2,1,0:T(8,128)(2,1)S(1)} %fusion.30), channel_id=1, source_target_pairs={{0,2},{2,0},{1,3},{3,1},{4,6},{6,4},{5,7},{7,5},{8,10},{10,8},{9,1... | collective-permute-start | bytes 1572872 | tf_op jit(solution)/shard_map/ppermute | solution.py:91
  35.3 2.2 %convolution_convert_fusion = bf16[512,1024]{1,0:T(8,128)(2,1)} fusion(bf16[512,1024]{1,0:T(8,128)(2,1)S(1)} %bitcast_select_fusion, bf16[1024,1024]{1,0:T(8,128)(2,1)S(1)} %copy-done), kind=kOutput, calls=%fused_computation.43 | convolution fusion | flops 1074266112 | bytes 4194304 | tf_op jit(solution)/shard_map/dot_general | solution.py:112
  37.5 1.7 collective-permute-start.4
  39.5 6.9 %collective-permute-done.2 = bf16[2,128,1024]{2,1,0:T(8,128)(2,1)S(1)} collective-permute-done((bf16[2,128,1024]{2,1,0:T(8,128)(2,1)S(1)}, bf16[2,128,1024]{2,1,0:T(8,128)(2,1)S(1)}, u32[]{:S(2)}, u32[]{:S(2)}) %collective-permute-start.2) | collective-permute-done | bytes 524320 | tf_op jit(solution)/shard_map/ppermute | solution.py:91
  48.0 9.6 %collective-permute-done.3 = bf16[2,128,1024]{2,1,0:T(8,128)(2,1)S(1)} collective-permute-done((bf16[2,128,1024]{2,1,0:T(8,128)(2,1)S(1)}, bf16[2,128,1024]{2,1,0:T(8,128)(2,1)S(1)}, u32[]{:S(2)}, u32[]{:S(2)}) %collective-permute-start.3) | collective-permute-done | bytes 524320 | tf_op jit(solution)/shard_map/ppermute | solution.py:91
  59.2 9.7 %collective-permute-done.4 = bf16[2,128,1024]{2,1,0:T(8,128)(2,1)S(1)} collective-permute-done((bf16[2,128,1024]{2,1,0:T(8,128)(2,1)S(1)}, bf16[2,128,1024]{2,1,0:T(8,128)(2,1)S(1)}, u32[]{:S(2)}, u32[]{:S(2)}) %collective-permute-start.4) | collective-permute-done | bytes 524320 | tf_op jit(solution)/shard_map/ppermute | solution.py:91
  70.5 8.8 %collective-permute-done.5 = bf16[2,128,1024]{2,1,0:T(8,128)(2,1)S(1)} collective-permute-done((bf16[2,128,1024]{2,1,0:T(8,128)(2,1)S(1)}, bf16[2,128,1024]{2,1,0:T(8,128)(2,1)S(1)}, u32[]{:S(2)}, u32[]{:S(2)}) %collective-permute-start.5) | collective-permute-done | bytes 524320 | tf_op jit(solution)/shard_map/ppermute | solution.py:91
  79.3 1.7 convert_add_fusion.2
  83.9 4.8 %collective-permute-start.8 = (bf16[1,512,1024]{2,1,0:T(8,128)(2,1)}, bf16[1,512,1024]{2,1,0:T(8,128)(2,1)}, u32[]{:S(2)}, u32[]{:S(2)}) collective-permute-start(bf16[1,512,1024]{2,1,0:T(8,128)(2,1)} %slice.123), channel_id=1, source_target_pairs={{0,4},{4,8},{8,12},{1,5},{5,9},{9,13},{2,6},{6,10},{10,14},{3,7},{... | collective-permute-start | bytes 3145736 | tf_op jit(solution)/shard_map/ppermute | solution.py:14
  90.2 1.8 %copy.119 = f32[64,8,8,128]{3,2,1,0:T(8,128)} copy(f32[64,8,8,128]{3,1,2,0:T(8,128)S(1)} %multiply_bitcast_fusion) | data formatting | bytes 4194304
  92.0 2.2 %reduce_sum.58 = f32[512,8]{1,0:T(8,128)S(1)} reduce(f32[512,8,128]{2,1,0:T(8,128)} %bitcast.171, f32[]{:T(128)} %constant.107.clone.1), dimensions={2}, to_apply=%region_2.3 | reduce | flops 520192 | bytes 2113540 | tf_op jit(solution)/shard_map/reduce_sum | solution.py:18
  95.9 2.9 %copy.114 = f32[1,512,1024]{2,1,0:T(8,128)} copy(f32[1,512,1024]{1,2,0:T(8,128)} %bitcast.172) | data formatting | bytes 4194304 | tf_op jit(solution)/shard_map/mul | solution.py:18
  98.9 4.5 %multiply_convert_fusion = (bf16[1,512,1024]{2,1,0:T(8,128)(2,1)}, f32[1,512,1024]{2,1,0:T(8,128)}) fusion(f32[1,512,1024]{2,1,0:T(8,128)} %copy.114, f32[2,512,1024]{2,1,0:T(8,128)} %copy-done.2), kind=kLoop, calls=%fused_computation.34 | loop fusion | flops 1048576 | bytes 7340032 | tf_op jit(solution)/shard_map/convert_element_type | solution.py:115
  103.4 3.5 %collective-permute-start.7 = (bf16[1,512,1024]{2,1,0:T(8,128)(2,1)}, bf16[1,512,1024]{2,1,0:T(8,128)(2,1)}, u32[]{:S(2)}, u32[]{:S(2)}) collective-permute-start(bf16[1,512,1024]{2,1,0:T(8,128)(2,1)} %get-tuple-element.19), channel_id=1, source_target_pairs={{0,4},{4,8},{8,12},{1,5},{5,9},{9,13},{2,6},{6,10},{10,14},{3,7},{... | collective-permute-start | bytes 3145736 | tf_op jit(solution)/shard_map/ppermute | solution.py:14
  109.2 3.3 %copy.113 = f32[1,512,1024]{1,2,0:T(8,128)} copy(f32[1,512,1024]{2,1,0:T(8,128)} %get-tuple-element.20) | data formatting | bytes 4194304 | tf_op jit(solution)/shard_map/reshape;squeeze | solution.py:115
  113.0 2.9 %fusion.27 = f32[1,8,128,128]{3,2,1,0:T(8,128)S(1)} fusion(bf16[512,8,128]{0,2,1:T(8,128)(2,1)S(1)} %bitcast.173, f32[512,8]{0,1:T(8,128)} %fusion.74, f32[512,8,128]{0,2,1:T(8,128)} %bitcast.168, f32[512,8]{0,1:T(8,128)S(1)} %add_rsqrt_fusion), kind=kOutput, calls=%fused_computation.53 | convolution fusion | flops 807403520 | bytes 3702784 | tf_op jit(solution)/shard_map/bht,bthd,bthe->bhde/dot_general | solution.py:132
  116.1 3.8 %multiply_bitcast_fusion.1 = (f32[64,8,8,128]{3,1,2,0:T(8,128)S(1)}, f32[64,8,8,128]{3,2,1,0:T(8,128)}) fusion(bf16[512,1024]{1,0:T(8,128)(2,1)} %collective-permute-done.6, bf16[1024,1024]{1,0:T(8,128)(2,1)S(1)} %copy-done, bf16[1,512,2048]{2,1,0:T(8,128)(2,1)S(1)} %copy-done.10, s32[]{:T(128)S(6)} %select_n.91), kind=kOutput, calls=%fused_computation.40 | convolution fusion | flops 1075314688 | bytes 8388612 | tf_op jit(solution)/shard_map/dot_general | solution.py:112
  121.1 11.1 %collective-permute-done.7 = bf16[1,512,1024]{2,1,0:T(8,128)(2,1)} collective-permute-done((bf16[1,512,1024]{2,1,0:T(8,128)(2,1)}, bf16[1,512,1024]{2,1,0:T(8,128)(2,1)}, u32[]{:S(2)}, u32[]{:S(2)}) %collective-permute-start.7) | collective-permute-done | bytes 1048608 | tf_op jit(solution)/shard_map/ppermute | solution.py:14
  133.9 4.5 %collective-permute-start.9 = (bf16[1,9,128,128]{3,2,1,0:T(8,128)(2,1)S(1)}, bf16[1,9,128,128]{3,2,1,0:T(8,128)(2,1)S(1)}, u32[]{:S(2)}, u32[]{:S(2)}) collective-permute-start(bf16[1,9,128,128]{3,2,1,0:T(8,128)(2,1)S(1)} %fusion.62), channel_id=1, source_target_pairs={{0,4},{4,8},{8,12},{1,5},{5,9},{9,13},{2,6},{6,10},{10,14},{3,7},{... | collective-permute-start | bytes 884744 | tf_op jit(solution)/shard_map/ppermute | solution.py:14
  139.2 2.6 %fusion = (f32[8,512]{1,0:T(8,128)S(1)}, f32[8,512,512]{1,2,0:T(8,128)S(1)}) fusion(pred[512,512]{0,1:T(8,128)(4,1)S(1)} %copy-done.15, bf16[512,8,128]{2,0,1:T(8,128)(2,1)S(1)} %fusion.15, f32[512,8,128]{0,2,1:T(8,128)S(1)} %bitcast.169, f32[512,8]{0,1:T(8,128)S(1)} %add_rsqrt_fusion), kind=kOutput, calls=%fused_computation.5 | convolution fusion | flops 544206848 | bytes 11829248 | tf_op jit(solution)/shard_map/bihd,bjhd->bhij/dot_general | solution.py:23
  141.8 5.3 %fusion.1 = (f32[8,512]{1,0:T(8,128)S(1)}, f32[8,512,512]{1,2,0:T(8,128)}) fusion(pred[512,512]{0,1:T(8,128)(4,1)S(1)} %fusion.41, bf16[512,8,128]{2,0,1:T(8,128)(2,1)S(1)} %fusion.15, bf16[512,8,128]{2,1,0:T(8,128)(2,1)S(1)} %bitcast.179), kind=kOutput, calls=%fused_computation.6 | convolution fusion | flops 543158272 | bytes 10764288 | tf_op jit(solution)/shard_map/bihd,bjhd->bhij/dot_general | solution.py:27
  147.3 3.5 %collective-permute-start.10 = (bf16[1,9,128,128]{3,2,1,0:T(8,128)(2,1)S(1)}, bf16[1,9,128,128]{3,2,1,0:T(8,128)(2,1)S(1)}, u32[]{:S(2)}, u32[]{:S(2)}) collective-permute-start(bf16[1,9,128,128]{3,2,1,0:T(8,128)(2,1)S(1)} %fusion.64), channel_id=1, source_target_pairs={{0,4},{4,8},{8,12},{1,5},{5,9},{9,13},{2,6},{6,10},{10,14},{3,7},{... | collective-permute-start | bytes 884744 | tf_op jit(solution)/shard_map/ppermute | solution.py:14
  150.7 3.6 %fusion.5 = f32[8,128,512]{2,1,0:T(8,128)} fusion(bf16[512,8,128]{0,2,1:T(8,128)(2,1)S(1)} %bitcast.174, f32[8,512,512]{1,2,0:T(8,128)S(1)} %get-tuple-element.24, f32[8,512]{1,0:T(8,128)S(1)} %add.176, pred[512,512]{0,1:T(8,128)(4,1)S(1)} %copy-done.15), kind=kOutput, calls=%fused_computation.17 | convolution fusion | flops 545259520 | bytes 11812864 | tf_op jit(solution)/shard_map/bhij,bjhd->bihd/dot_general | solution.py:38
  156.0 3.9 %collective-permute-start.11 = (bf16[1,9,128,128]{3,2,1,0:T(8,128)(2,1)S(1)}, bf16[1,9,128,128]{3,2,1,0:T(8,128)(2,1)S(1)}, u32[]{:S(2)}, u32[]{:S(2)}) collective-permute-start(bf16[1,9,128,128]{3,2,1,0:T(8,128)(2,1)S(1)} %fusion.66), channel_id=1, source_target_pairs={{0,4},{4,8},{8,12},{1,5},{5,9},{9,13},{2,6},{6,10},{10,14},{3,7},{... | collective-permute-start | bytes 884744 | tf_op jit(solution)/shard_map/ppermute | solution.py:14
  159.9 4.8 %fusion.6 = f32[8,128,512]{2,1,0:T(8,128)S(1)} fusion(bf16[512,8,128]{0,2,1:T(8,128)(2,1)S(1)} %bitcast.178, f32[8,512,512]{1,2,0:T(8,128)} %get-tuple-element.26, f32[8,512]{1,0:T(8,128)S(1)} %add.176, pred[512,512]{0,1:T(8,128)(4,1)} %copy-done.14), kind=kOutput, calls=%fused_computation.18 | convolution fusion | flops 545259520 | bytes 11812864 | tf_op jit(solution)/shard_map/bhij,bjhd->bihd/dot_general | solution.py:40
  166.4 3.9 %fusion.23 = bf16[512,1024]{1,0:T(8,128)(2,1)} fusion(bf16[512,1024]{0,1:T(8,128)(2,1)S(1)} %bitcast.190, s32[]{:T(128)S(6)} %select_n.108, bf16[1,1024,1024]{2,1,0:T(8,128)(2,1)S(1)} %bitcast.189, bf16[1,1024,1024]{2,1,0:T(8,128)(2,1)} %bitcast.56), kind=kOutput, calls=%fused_computation.42 | convolution fusion | flops 1075314688 | bytes 6291460 | tf_op jit(solution)/shard_map/dot_general | solution.py:200
  170.4 3.4 %fusion.13 = f32[512,1024]{1,0:T(8,128)S(1)} fusion(bf16[512,1024]{0,1:T(8,128)(2,1)} %bitcast.191, s32[]{:T(128)S(6)} %select_n.105, bf16[1,1024,1024]{2,1,0:T(8,128)(2,1)} %bitcast.188, bf16[1,1024,1024]{2,1,0:T(8,128)(2,1)} %bitcast.56), kind=kOutput, calls=%fused_computation.24 | convolution fusion | flops 1074790400 | bytes 7340036 | tf_op jit(solution)/shard_map/dot_general | solution.py:200
  (120 shorter events, 36.7 us)
Async XLA Ops:
  0.0 35.3 %copy-start = (bf16[1024,1024]{1,0:T(8,128)(2,1)S(1)}, bf16[1024,1024]{1,0:T(8,128)(2,1)}, u32[]{:S(2)}) copy-start(bf16[1024,1024]{1,0:T(8,128)(2,1)} %param.9) | copy-start | bytes 6291460
  2.4 6.0 %copy-start.17 = (f32[1,8,512]{2,1,0:T(8,128)S(1)}, f32[1,8,512]{2,1,0:T(8,128)}, u32[]{:S(2)}) copy-start(f32[1,8,512]{2,1,0:T(8,128)} %param.12) | copy-start | bytes 49156
  4.6 15.0 %collective-permute-start = (bf16[256,1024]{1,0:T(8,128)(2,1)S(1)}, bf16[256,1024]{1,0:T(8,128)(2,1)S(1)}, u32[]{:S(2)}, u32[]{:S(2)}) collective-permute-start(bf16[256,1024]{1,0:T(8,128)(2,1)S(1)} %dynamic-slice_bitcast_fusion), channel_id=1, source_target_pairs={{0,2},{2,0},{1,3},{3,1},{4,6},{6,4},{5,7},{7,5},{8,10},{10,8},{9,1... | collective-permute-start | bytes 1572872 | tf_op jit(solution)/shard_map/ppermute | solution.py:77
  12.0 129.8 %copy-start.14 = (pred[512,512]{0,1:T(8,128)(4,1)}, pred[512,512]{0,1:T(8,128)(4,1)S(1)}, u32[]{:S(2)}) copy-start(pred[512,512]{0,1:T(8,128)(4,1)S(1)} %fusion.41) | copy-start | bytes 786436
  19.5 1.9 %collective-permute-start.1 = (bf16[256,1024]{1,0:T(8,128)(2,1)S(1)}, bf16[256,1024]{1,0:T(8,128)(2,1)S(1)}, u32[]{:S(2)}, u32[]{:S(2)}) collective-permute-start(bf16[256,1024]{1,0:T(8,128)(2,1)S(1)} %collective-permute-done), channel_id=1, source_target_pairs={{0,1},{1,0},{2,3},{3,2},{4,5},{5,4},{6,7},{7,6},{8,9},{9,8},{10,11... | collective-permute-start | bytes 1572872 | tf_op jit(solution)/shard_map/ppermute | solution.py:67
  24.6 3.9 %copy-start.21 = (bf16[1024,2,1024]{2,1,0:T(2,128)(2,1)S(1)}, bf16[1024,2,1024]{2,1,0:T(2,128)(2,1)}, u32[]{:S(2)}) copy-start(bf16[1024,2,1024]{2,1,0:T(2,128)(2,1)} %param.10) | copy-start | bytes 12582916
  31.6 14.9 %collective-permute-start.2 = (bf16[2,128,1024]{2,1,0:T(8,128)(2,1)S(1)}, bf16[2,128,1024]{2,1,0:T(8,128)(2,1)S(1)}, u32[]{:S(2)}, u32[]{:S(2)}) collective-permute-start(bf16[2,128,1024]{2,1,0:T(8,128)(2,1)S(1)} %fusion.30), channel_id=1, source_target_pairs={{0,2},{2,0},{1,3},{3,1},{4,6},{6,4},{5,7},{7,5},{8,10},{10,8},{9,1... | collective-permute-start | bytes 1572872 | tf_op jit(solution)/shard_map/ppermute | solution.py:91
  34.9 11.5 %copy-start.9 = (bf16[1,512,2048]{2,1,0:T(8,128)(2,1)S(1)}, bf16[1,512,2048]{2,1,0:T(8,128)(2,1)}, u32[]{:S(2)}) copy-start(bf16[1,512,2048]{2,1,0:T(8,128)(2,1)} %copy-done.8) | copy-start | bytes 6291460
  34.9 22.7 %collective-permute-start.3 = (bf16[2,128,1024]{2,1,0:T(8,128)(2,1)S(1)}, bf16[2,128,1024]{2,1,0:T(8,128)(2,1)S(1)}, u32[]{:S(2)}, u32[]{:S(2)}) collective-permute-start(bf16[2,128,1024]{2,1,0:T(8,128)(2,1)S(1)} %fusion.31), channel_id=1, source_target_pairs={{0,2},{2,0},{1,3},{3,1},{4,6},{6,4},{5,7},{7,5},{8,10},{10,8},{9,1... | collective-permute-start | bytes 1572872 | tf_op jit(solution)/shard_map/ppermute | solution.py:91
  37.5 31.4 %collective-permute-start.4 = (bf16[2,128,1024]{2,1,0:T(8,128)(2,1)S(1)}, bf16[2,128,1024]{2,1,0:T(8,128)(2,1)S(1)}, u32[]{:S(2)}, u32[]{:S(2)}) collective-permute-start(bf16[2,128,1024]{2,1,0:T(8,128)(2,1)S(1)} %fusion.32), channel_id=1, source_target_pairs={{0,2},{2,0},{1,3},{3,1},{4,6},{6,4},{5,7},{7,5},{8,10},{10,8},{9,1... | collective-permute-start | bytes 1572872 | tf_op jit(solution)/shard_map/ppermute | solution.py:91
  39.2 40.0 %collective-permute-start.5 = (bf16[2,128,1024]{2,1,0:T(8,128)(2,1)S(1)}, bf16[2,128,1024]{2,1,0:T(8,128)(2,1)S(1)}, u32[]{:S(2)}, u32[]{:S(2)}) collective-permute-start(bf16[2,128,1024]{2,1,0:T(8,128)(2,1)S(1)} %fusion.33), channel_id=1, source_target_pairs={{0,2},{2,0},{1,3},{3,1},{4,6},{6,4},{5,7},{7,5},{8,10},{10,8},{9,1... | collective-permute-start | bytes 1572872 | tf_op jit(solution)/shard_map/ppermute | solution.py:91
  83.9 37.2 %collective-permute-start.8 = (bf16[1,512,1024]{2,1,0:T(8,128)(2,1)}, bf16[1,512,1024]{2,1,0:T(8,128)(2,1)}, u32[]{:S(2)}, u32[]{:S(2)}) collective-permute-start(bf16[1,512,1024]{2,1,0:T(8,128)(2,1)} %slice.123), channel_id=1, source_target_pairs={{0,4},{4,8},{8,12},{1,5},{5,9},{9,13},{2,6},{6,10},{10,14},{3,7},{... | collective-permute-start | bytes 3145736 | tf_op jit(solution)/shard_map/ppermute | solution.py:14
  88.7 27.4 %collective-permute-start.6 = (bf16[512,1024]{1,0:T(8,128)(2,1)}, bf16[512,1024]{1,0:T(8,128)(2,1)}, u32[]{:S(2)}, u32[]{:S(2)}) collective-permute-start(bf16[512,1024]{1,0:T(8,128)(2,1)} %convolution_convert_fusion), channel_id=1, source_target_pairs={{0,2},{2,0},{1,3},{3,1},{4,6},{6,4},{5,7},{7,5},{8,10},{10,8},{9,1... | collective-permute-start | bytes 3145736 | tf_op jit(solution)/shard_map/ppermute | solution.py:91
  98.9 8.2 %copy-start.20 = (f32[8]{0:T(128)S(1)}, f32[8]{0:T(128)}, u32[]{:S(2)}) copy-start(f32[8]{0:T(128)} %get-tuple-element.15) | copy-start | bytes 100
  98.9 8.3 %copy-start.24 = (f32[8]{0:T(128)S(1)}, f32[8]{0:T(128)}, u32[]{:S(2)}) copy-start(f32[8]{0:T(128)} %exponential_multiply_fusion) | copy-start | bytes 100
  103.4 28.9 %collective-permute-start.7 = (bf16[1,512,1024]{2,1,0:T(8,128)(2,1)}, bf16[1,512,1024]{2,1,0:T(8,128)(2,1)}, u32[]{:S(2)}, u32[]{:S(2)}) collective-permute-start(bf16[1,512,1024]{2,1,0:T(8,128)(2,1)} %get-tuple-element.19), channel_id=1, source_target_pairs={{0,4},{4,8},{8,12},{1,5},{5,9},{9,13},{2,6},{6,10},{10,14},{3,7},{... | collective-permute-start | bytes 3145736 | tf_op jit(solution)/shard_map/ppermute | solution.py:14
  109.2 3.8 %copy-start.6 = (bf16[1,512,1024]{1,2,0:T(8,128)(2,1)}, bf16[1,512,1024]{1,2,0:T(8,128)(2,1)S(1)}, u32[]{:S(2)}) copy-start(bf16[1,512,1024]{1,2,0:T(8,128)(2,1)S(1)} %copy.116) | copy-start | bytes 3145732
  112.5 53.0 %collective-permute-start.12 = (bf16[1024,1024]{1,0:T(8,128)(2,1)}, bf16[1024,1024]{1,0:T(8,128)(2,1)}, u32[]{:S(2)}, u32[]{:S(2)}) collective-permute-start(bf16[1024,1024]{1,0:T(8,128)(2,1)} %param.11), channel_id=1, source_target_pairs={{0,2},{2,0},{1,3},{3,1},{4,6},{6,4},{5,7},{7,5},{8,10},{10,8},{9,1... | collective-permute-start | bytes 6291464 | tf_op jit(solution)/shard_map/ppermute | solution.py:185
  120.4 13.4 %copy-start.19 = (f32[9]{0:T(128)S(1)}, f32[9]{0:T(128)}, u32[]{:S(2)}) copy-start(f32[9]{0:T(128)} %pad.11.clone) | copy-start | bytes 112
  121.1 17.4 %copy-start.11 = (f32[64,8,8,128]{3,2,1,0:T(8,128)S(1)}, f32[64,8,8,128]{3,2,1,0:T(8,128)}, u32[]{:S(2)}) copy-start(f32[64,8,8,128]{3,2,1,0:T(8,128)} %get-tuple-element.22) | copy-start | bytes 6291460
  133.7 5.4 %copy-start.5 = (f32[1,512,1024]{1,2,0:T(8,128)S(1)}, f32[1,512,1024]{1,2,0:T(8,128)}, u32[]{:S(2)}) copy-start(f32[1,512,1024]{1,2,0:T(8,128)} %copy.113) | copy-start | bytes 6291460
  133.8 5.4 %copy-start.15 = (pred[512,512]{0,1:T(8,128)(4,1)S(1)}, pred[512,512]{0,1:T(8,128)(4,1)}, u32[]{:S(2)}) copy-start(pred[512,512]{0,1:T(8,128)(4,1)} %iota_compare_fusion.1) | copy-start | bytes 786436
  133.9 13.2 %collective-permute-start.9 = (bf16[1,9,128,128]{3,2,1,0:T(8,128)(2,1)S(1)}, bf16[1,9,128,128]{3,2,1,0:T(8,128)(2,1)S(1)}, u32[]{:S(2)}, u32[]{:S(2)}) collective-permute-start(bf16[1,9,128,128]{3,2,1,0:T(8,128)(2,1)S(1)} %fusion.62), channel_id=1, source_target_pairs={{0,4},{4,8},{8,12},{1,5},{5,9},{9,13},{2,6},{6,10},{10,14},{3,7},{... | collective-permute-start | bytes 884744 | tf_op jit(solution)/shard_map/ppermute | solution.py:14
  141.8 8.9 %copy-start.7 = (bf16[1,512,1024]{1,2,0:T(8,128)(2,1)S(1)}, bf16[1,512,1024]{1,2,0:T(8,128)(2,1)}, u32[]{:S(2)}) copy-start(bf16[1,512,1024]{1,2,0:T(8,128)(2,1)} %copy-done.6) | copy-start | bytes 3145732
  147.3 8.5 %collective-permute-start.10 = (bf16[1,9,128,128]{3,2,1,0:T(8,128)(2,1)S(1)}, bf16[1,9,128,128]{3,2,1,0:T(8,128)(2,1)S(1)}, u32[]{:S(2)}, u32[]{:S(2)}) collective-permute-start(bf16[1,9,128,128]{3,2,1,0:T(8,128)(2,1)S(1)} %fusion.64), channel_id=1, source_target_pairs={{0,4},{4,8},{8,12},{1,5},{5,9},{9,13},{2,6},{6,10},{10,14},{3,7},{... | collective-permute-start | bytes 884744 | tf_op jit(solution)/shard_map/ppermute | solution.py:14
  156.0 8.8 %collective-permute-start.11 = (bf16[1,9,128,128]{3,2,1,0:T(8,128)(2,1)S(1)}, bf16[1,9,128,128]{3,2,1,0:T(8,128)(2,1)S(1)}, u32[]{:S(2)}, u32[]{:S(2)}) collective-permute-start(bf16[1,9,128,128]{3,2,1,0:T(8,128)(2,1)S(1)} %fusion.66), channel_id=1, source_target_pairs={{0,4},{4,8},{8,12},{1,5},{5,9},{9,13},{2,6},{6,10},{10,14},{3,7},{... | collective-permute-start | bytes 884744 | tf_op jit(solution)/shard_map/ppermute | solution.py:14
  159.9 5.0 %copy-start.13 = (bf16[512,8,128]{2,0,1:T(8,128)(2,1)S(1)}, bf16[512,8,128]{2,0,1:T(8,128)(2,1)}, u32[]{:S(2)}) copy-start(bf16[512,8,128]{2,0,1:T(8,128)(2,1)} %copy-done.12) | copy-start | bytes 3145732
  159.9 5.0 %copy-start.16 = (f32[512,8]{0,1:T(8,128)S(1)}, f32[512,8]{0,1:T(8,128)}, u32[]{:S(2)}) copy-start(f32[512,8]{0,1:T(8,128)} %get-tuple-element.17) | copy-start | bytes 49156
  159.9 5.0 %copy-start.25 = (f32[8,128,512]{2,1,0:T(8,128)S(1)}, f32[8,128,512]{2,1,0:T(8,128)}, u32[]{:S(2)}) copy-start(f32[8,128,512]{2,1,0:T(8,128)} %fusion.5) | copy-start | bytes 6291460
  165.5 4.9 %copy-start.23 = (bf16[1,512,8,128]{1,3,2,0:T(8,128)(2,1)}, bf16[1,512,8,128]{1,3,2,0:T(8,128)(2,1)S(1)}, u32[]{:S(2)}) copy-start(bf16[1,512,8,128]{1,3,2,0:T(8,128)(2,1)S(1)} %fusion.18) | copy-start | bytes 3145732
  170.3 3.4 %collective-permute-start.13 = (bf16[512,1024]{1,0:T(8,128)(2,1)}, bf16[512,1024]{1,0:T(8,128)(2,1)S(1)}, u32[]{:S(2)}, u32[]{:S(2)}) collective-permute-start(bf16[512,1024]{1,0:T(8,128)(2,1)} %fusion.23), channel_id=1, source_target_pairs={{0,1},{1,0},{2,3},{3,2},{4,5},{5,4},{6,7},{7,6},{8,9},{9,8},{10,11... | collective-permute-start | bytes 3145736 | tf_op jit(solution)/shard_map/ppermute | solution.py:209
  170.4 5.0 %copy-start.1 = (bf16[1024,1024]{1,0:T(8,128)(2,1)S(1)}, bf16[1024,1024]{1,0:T(8,128)(2,1)}, u32[]{:S(2)}) copy-start(bf16[1024,1024]{1,0:T(8,128)(2,1)} %param.9) | copy-start | bytes 6291460
  (8 other events, 18.9 us)

commit v20 on v17

--- a/solution.py
+++ b/solution.py
@@ -82,17 +82,21 @@
             )
         )
 
+    arrived = []
+
     def gathered_sum(partials, after=None):
         total = partials[0]
         for step in range(1, ways):
             outgoing = partials[step].astype(jnp.bfloat16)
             if after is not None:
                 outgoing = lax.optimization_barrier((outgoing, after))[0]
-            total = total + lax.ppermute(
+            incoming = lax.ppermute(
                 outgoing,
                 "wloop",
                 [(source, (source - step) % ways) for source in range(ways)],
-            ).astype(jnp.float32)
+            )
+            arrived.append(incoming)
+            total = total + incoming.astype(jnp.float32)
         return total
 
     half_rows = count // 2
@@ -110,7 +114,7 @@
     )
     query_raw = gathered_sum(
         [jnp.dot(rows, w_query, preferred_element_type=jnp.float32) for rows in stacked],
-        after=pair_raw,
+        after=tuple(arrived),
     )
     lookup_vectors = rms_rows(pair_raw[0].reshape(trajs, span, heads_here, head_dim), 1e-06).astype(
         jnp.bfloat16
@@ -177,7 +181,7 @@
         scale,
     )
     attended = (window + read).astype(jnp.bfloat16).reshape(count, inner_here)
-    w_output = lax.optimization_barrier((w_output, pair_raw))[0]
+    w_output = lax.optimization_barrier((w_output, arrived[ways - 1]))[0]
     out_block = w_output.shape[1]
     from_ranks = jnp.stack(
         [w_output]

time: 173 us -> 189 us (1.092)
  waiting for transfers between devices: 60 us -> 72 us
  other arithmetic: 21.1 us -> 24.6 us
    ppermute x5, waiting for transfers between devices: 8.03 us -> 23.3 us  [shifted(): lax.ppermute(value, axis, [(source, source + steps) for source in range(i...]
    ppermute x3, waiting for transfers between devices: 43.8 us -> 39.8 us  [gathered_sum(): lax.ppermute(outgoing, 'wloop', [(source, (source - step) % ways) for sou...]
    unnamed x53 -> x51, local copies, waits for them, and re-layouts: 6.28 us -> 8.36 us
where the time goes in v20:
time: 189 us; the launch traced here: 188 us
  waiting for transfers between devices  72 us (38%)
  matrix products  41.1 us (22%)
  starting transfers between devices  27.4 us (14%)
  other arithmetic  24.6 us (13%)
  local copies, waits for them, and re-layouts  22 us (12%)
    ppermute x3, waiting for transfers between devices, gathered_sum(): lax.ppermute(outgoing, 'wloop', [(source, (source - step) % ways) for sou...  39.8 us
    ppermute x5, waiting for transfers between devices, shifted(): lax.ppermute(value, axis, [(source, source + steps) for source in range(i...  23.3 us
    ppermute x5, starting transfers between devices, shifted(): lax.ppermute(value, axis, [(source, source + steps) for source in range(i...  20 us
    dot_general x4, matrix products, shards(): jnp.einsum('td,dje->jte', rows[lo:hi], w_keyvalue, preferred_element_type...  8.97 us
    unnamed x51, local copies, waits for them, and re-layouts  8.36 us
    ppermute x1, waiting for transfers between devices, shards(): lax.ppermute(part, 'wloop', [(source, (source + step) % ways) for source...  8.24 us
    dot_general x2, matrix products, output_share(): jnp.dot(attended, lax.dynamic_index_in_dim(from_ranks, (me - rank) % ways...  7.28 us
    reduce_sum x3, other arithmetic, rms_rows(): jnp.mean(values * values, axis=-1, keepdims=True) + eps  6.66 us
  transfers between devices with their start and end apart: 12, of which 6 were waited for; matrix products, arithmetic and copies ran while one was open for 35% of the time, Pallas kernels for 0%

profile of v20, /device:TPU:0, one launch (start us, length us, event | category | flops | bytes accessed | tf_op | source)
XLA Modules:
  0.0 188.4 jit_solution(16131226029283386948)
XLA Ops:
  0.0 2.2 %fusion.2 = f32[512]{0:T(512)S(1)} fusion(bf16[1,512,2048]{2,1,0:T(8,128)(2,1)} %param.7), kind=kLoop, calls=%fused_computation.13 | loop fusion | flops 3145216 | bytes 2099200 | tf_op jit(solution)/shard_map/reduce_sum | solution.py:18
  2.3 2.1 %fusion.4 = bf16[1,512,2048]{2,1,0:T(8,128)(2,1)S(1)} fusion(bf16[1,512,2048]{2,1,0:T(8,128)(2,1)} %param.7, f32[2048]{0:T(1024)S(1)} %copy-done.18, f32[512]{0:T(512)S(1)} %add_rsqrt_fusion.2), kind=kLoop, calls=%fused_computation.15 | loop fusion | flops 4194304 | bytes 4204544 | tf_op jit(solution)/shard_map/convert_element_type | solution.py:50
  6.1 3.0 %collective-permute-start = (bf16[256,1024]{1,0:T(8,128)(2,1)S(1)}, bf16[256,1024]{1,0:T(8,128)(2,1)S(1)}, u32[]{:S(2)}, u32[]{:S(2)}) collective-permute-start(bf16[256,1024]{1,0:T(8,128)(2,1)S(1)} %dynamic-slice_bitcast_fusion.4), channel_id=1, source_target_pairs={{0,2},{2,0},{1,3},{3,1},{4,6},{6,4},{5,7},{7,5},{8,10},{10,8},{9,1... | collective-permute-start | bytes 1572872 | tf_op jit(solution)/shard_map/ppermute | solution.py:77
  12.8 8.2 %collective-permute-done = bf16[256,1024]{1,0:T(8,128)(2,1)S(1)} collective-permute-done((bf16[256,1024]{1,0:T(8,128)(2,1)S(1)}, bf16[256,1024]{1,0:T(8,128)(2,1)S(1)}, u32[]{:S(2)}, u32[]{:S(2)}) %collective-permute-start) | collective-permute-done | bytes 524320 | tf_op jit(solution)/shard_map/ppermute | solution.py:77
  24.0 1.8 gather_fusion
  26.0 3.9 %fusion.50 = bf16[2,256,1024]{2,1,0:T(8,128)(2,1)S(1)} fusion(bf16[1024,2,1024]{2,1,0:T(2,128)(2,1)} %param.10, bf16[2,256,1024]{2,1,0:T(8,128)(2,1)S(1)} %broadcast_select_fusion), kind=kOutput, calls=%fused_computation.61 | convolution fusion | flops 1074266112 | bytes 5767168 | tf_op jit(solution)/shard_map/td,dje->jte/dot_general | solution.py:107
  31.6 1.8 collective-permute-start.2
  34.5 2.6 %fusion.57 = f32[512,1024]{1,0:T(8,128)} fusion(bf16[1024,1024]{1,0:T(8,128)(2,1)S(1)} %copy-done, bf16[1,512,2048]{2,1,0:T(8,128)(2,1)S(1)} %copy-done.11, s32[]{:T(128)S(6)} %select_n.93), kind=kOutput, calls=%fused_computation.66 | convolution fusion | flops 1073741824 | bytes 5242884 | tf_op jit(solution)/shard_map/dot_general | solution.py:116
  37.3 2.3 %convolution_convert_fusion = bf16[512,1024]{1,0:T(8,128)(2,1)} fusion(bf16[512,1024]{1,0:T(8,128)(2,1)S(1)} %bitcast_select_fusion, bf16[1024,1024]{1,0:T(8,128)(2,1)S(1)} %copy-done), kind=kOutput, calls=%fused_computation.58 | convolution fusion | flops 1074266112 | bytes 4194304 | tf_op jit(solution)/shard_map/dot_general | solution.py:116
  39.5 18.1 %collective-permute-done.2 = bf16[2,256,1024]{2,1,0:T(8,128)(2,1)S(1)} collective-permute-done((bf16[2,256,1024]{2,1,0:T(8,128)(2,1)S(1)}, bf16[2,256,1024]{2,1,0:T(8,128)(2,1)S(1)}, u32[]{:S(2)}, u32[]{:S(2)}) %collective-permute-start.2) | collective-permute-done | bytes 1048608 | tf_op jit(solution)/shard_map/ppermute | solution.py:93
  57.7 21.6 %collective-permute-done.3 = bf16[2,256,1024]{2,1,0:T(8,128)(2,1)S(1)} collective-permute-done((bf16[2,256,1024]{2,1,0:T(8,128)(2,1)S(1)}, bf16[2,256,1024]{2,1,0:T(8,128)(2,1)S(1)}, u32[]{:S(2)}, u32[]{:S(2)}) %collective-permute-start.3) | collective-permute-done | bytes 1048608 | tf_op jit(solution)/shard_map/ppermute | solution.py:93
  85.9 1.8 copy.99
  87.7 2.2 %reduce_sum.58 = f32[512,8]{1,0:T(8,128)S(1)} reduce(f32[512,8,128]{2,1,0:T(8,128)} %bitcast.141, f32[]{:T(128)} %constant.107.clone.1), dimensions={2}, to_apply=%region_2.3 | reduce | flops 520192 | bytes 2113540 | tf_op jit(solution)/shard_map/reduce_sum | solution.py:18
  91.6 2.9 %copy.94 = f32[1,512,1024]{2,1,0:T(8,128)} copy(f32[1,512,1024]{1,2,0:T(8,128)} %bitcast.142) | data formatting | bytes 4194304 | tf_op jit(solution)/shard_map/mul | solution.py:18
  94.6 3.0 %multiply_convert_fusion = bf16[1,512,1024]{2,1,0:T(8,128)(2,1)} fusion(f32[1,512,1024]{2,1,0:T(8,128)S(1)} %get-tuple-element.20, f32[1,512,1024]{2,1,0:T(8,128)} %copy.94), kind=kLoop, calls=%fused_computation.47 | loop fusion | flops 1048576 | bytes 5242880 | tf_op jit(solution)/shard_map/convert_element_type | solution.py:119
  97.6 4.5 %collective-permute-start.5 = (bf16[1,512,1024]{2,1,0:T(8,128)(2,1)}, bf16[1,512,1024]{2,1,0:T(8,128)(2,1)}, u32[]{:S(2)}, u32[]{:S(2)}) collective-permute-start(bf16[1,512,1024]{2,1,0:T(8,128)(2,1)} %multiply_convert_fusion), channel_id=1, source_target_pairs={{0,4},{4,8},{8,12},{1,5},{5,9},{9,13},{2,6},{6,10},{10,14},{3,7},{... | collective-permute-start | bytes 3145736 | tf_op jit(solution)/shard_map/ppermute | solution.py:14
  102.3 3.6 %collective-permute-start.6 = (bf16[1,512,1024]{2,1,0:T(8,128)(2,1)S(1)}, bf16[1,512,1024]{2,1,0:T(8,128)(2,1)}, u32[]{:S(2)}, u32[]{:S(2)}) collective-permute-start(bf16[1,512,1024]{2,1,0:T(8,128)(2,1)S(1)} %fusion.16), channel_id=1, source_target_pairs={{0,4},{4,8},{8,12},{1,5},{5,9},{9,13},{2,6},{6,10},{10,14},{3,7},{... | collective-permute-start | bytes 3145736 | tf_op jit(solution)/shard_map/ppermute | solution.py:14
  109.3 1.8 copy.93
  111.6 3.2 %fusion.53 = f32[1,8,128,128]{3,2,1,0:T(8,128)S(1)} fusion(bf16[512,8,128]{0,2,1:T(8,128)(2,1)} %bitcast.143, f32[512,8]{0,1:T(8,128)} %fusion.80, f32[512,8,128]{0,2,1:T(8,128)} %bitcast.138, f32[512,8]{0,1:T(8,128)S(1)} %add_rsqrt_fusion), kind=kOutput, calls=%fused_computation.62 | convolution fusion | flops 807403520 | bytes 3702784 | tf_op jit(solution)/shard_map/bht,bthd,bthe->bhde/dot_general | solution.py:136
  114.9 3.0 %multiply_bitcast_fusion.1 = (f32[64,8,8,128]{3,1,2,0:T(8,128)S(1)}, f32[64,8,8,128]{3,2,1,0:T(8,128)}) fusion(f32[512,1024]{1,0:T(8,128)S(1)} %copy-done.12, bf16[512,1024]{1,0:T(8,128)(2,1)} %collective-permute-done.4), kind=kLoop, calls=%fused_computation.53 | loop fusion | flops 1572864 | bytes 7340032
  119.7 2.2 %reduce_sum.57 = f32[512,8]{1,0:T(8,128)S(1)} reduce(f32[512,8,128]{2,1,0:T(8,128)} %bitcast.140, f32[]{:T(128)} %constant.107.clone.1), dimensions={2}, to_apply=%region_1.2 | reduce | flops 520192 | bytes 2113540 | tf_op jit(solution)/shard_map/reduce_sum | solution.py:18
  122.1 2.9 %collective-permute-done.5 = bf16[1,512,1024]{2,1,0:T(8,128)(2,1)} collective-permute-done((bf16[1,512,1024]{2,1,0:T(8,128)(2,1)}, bf16[1,512,1024]{2,1,0:T(8,128)(2,1)}, u32[]{:S(2)}, u32[]{:S(2)}) %collective-permute-start.5) | collective-permute-done | bytes 1048608 | tf_op jit(solution)/shard_map/ppermute | solution.py:14
  124.9 20.4 %collective-permute-done.6 = bf16[1,512,1024]{2,1,0:T(8,128)(2,1)} collective-permute-done((bf16[1,512,1024]{2,1,0:T(8,128)(2,1)S(1)}, bf16[1,512,1024]{2,1,0:T(8,128)(2,1)}, u32[]{:S(2)}, u32[]{:S(2)}) %collective-permute-start.6) | collective-permute-done | bytes 1048608 | tf_op jit(solution)/shard_map/ppermute | solution.py:14
  147.0 4.6 %collective-permute-start.7 = (bf16[1,9,128,128]{3,2,1,0:T(8,128)(2,1)S(1)}, bf16[1,9,128,128]{3,2,1,0:T(8,128)(2,1)S(1)}, u32[]{:S(2)}, u32[]{:S(2)}) collective-permute-start(bf16[1,9,128,128]{3,2,1,0:T(8,128)(2,1)S(1)} %fusion.68), channel_id=1, source_target_pairs={{0,4},{4,8},{8,12},{1,5},{5,9},{9,13},{2,6},{6,10},{10,14},{3,7},{... | collective-permute-start | bytes 884744 | tf_op jit(solution)/shard_map/ppermute | solution.py:14
  152.4 2.6 %fusion = (f32[8,512]{1,0:T(8,128)S(1)}, f32[8,512,512]{1,2,0:T(8,128)S(1)}) fusion(pred[512,512]{0,1:T(8,128)(4,1)S(1)} %iota_compare_fusion.1, bf16[512,8,128]{2,0,1:T(8,128)(2,1)S(1)} %fusion.25, f32[512,8,128]{0,2,1:T(8,128)S(1)} %bitcast.139, f32[512,8]{0,1:T(8,128)S(1)} %add_rsqrt_fusion), kind=kOutput, calls=%fused_computation.5 | convolution fusion | flops 544206848 | bytes 11829248 | tf_op jit(solution)/shard_map/bihd,bjhd->bhij/dot_general | solution.py:23
  155.0 5.3 %fusion.1 = (f32[8,512]{1,0:T(8,128)S(1)}, f32[8,512,512]{1,2,0:T(8,128)}) fusion(pred[512,512]{0,1:T(8,128)(4,1)S(1)} %copy-done.15, bf16[512,8,128]{2,0,1:T(8,128)(2,1)S(1)} %fusion.25, bf16[512,8,128]{2,1,0:T(8,128)(2,1)S(1)} %bitcast.149), kind=kOutput, calls=%fused_computation.6 | convolution fusion | flops 543158272 | bytes 10764288 | tf_op jit(solution)/shard_map/bihd,bjhd->bhij/dot_general | solution.py:27
  160.4 3.5 %collective-permute-start.8 = (bf16[1,9,128,128]{3,2,1,0:T(8,128)(2,1)S(1)}, bf16[1,9,128,128]{3,2,1,0:T(8,128)(2,1)S(1)}, u32[]{:S(2)}, u32[]{:S(2)}) collective-permute-start(bf16[1,9,128,128]{3,2,1,0:T(8,128)(2,1)S(1)} %fusion.70), channel_id=1, source_target_pairs={{0,4},{4,8},{8,12},{1,5},{5,9},{9,13},{2,6},{6,10},{10,14},{3,7},{... | collective-permute-start | bytes 884744 | tf_op jit(solution)/shard_map/ppermute | solution.py:14
  164.0 3.3 %fusion.5 = f32[8,128,512]{2,1,0:T(8,128)} fusion(bf16[512,8,128]{0,2,1:T(8,128)(2,1)S(1)} %bitcast.144, f32[8,512,512]{1,2,0:T(8,128)S(1)} %get-tuple-element.24, f32[8,512]{1,0:T(8,128)S(1)} %add.168, pred[512,512]{0,1:T(8,128)(4,1)S(1)} %copy-done.14), kind=kOutput, calls=%fused_computation.18 | convolution fusion | flops 545259520 | bytes 11812864 | tf_op jit(solution)/shard_map/bhij,bjhd->bihd/dot_general | solution.py:38
  169.0 3.8 %collective-permute-start.9 = (bf16[1,9,128,128]{3,2,1,0:T(8,128)(2,1)S(1)}, bf16[1,9,128,128]{3,2,1,0:T(8,128)(2,1)S(1)}, u32[]{:S(2)}, u32[]{:S(2)}) collective-permute-start(bf16[1,9,128,128]{3,2,1,0:T(8,128)(2,1)S(1)} %fusion.72), channel_id=1, source_target_pairs={{0,4},{4,8},{8,12},{1,5},{5,9},{9,13},{2,6},{6,10},{10,14},{3,7},{... | collective-permute-start | bytes 884744 | tf_op jit(solution)/shard_map/ppermute | solution.py:14
  172.8 5.0 %fusion.6 = f32[8,128,512]{2,1,0:T(8,128)S(1)} fusion(bf16[512,8,128]{0,2,1:T(8,128)(2,1)S(1)} %bitcast.148, f32[8,512,512]{1,2,0:T(8,128)} %get-tuple-element.26, f32[8,512]{1,0:T(8,128)S(1)} %add.168, pred[512,512]{0,1:T(8,128)(4,1)} %fusion.63), kind=kOutput, calls=%fused_computation.19 | convolution fusion | flops 545259520 | bytes 11812864 | tf_op jit(solution)/shard_map/bhij,bjhd->bihd/dot_general | solution.py:40
  179.5 3.9 %fusion.37 = bf16[512,1024]{1,0:T(8,128)(2,1)} fusion(bf16[512,1024]{0,1:T(8,128)(2,1)S(1)} %bitcast.160, s32[]{:T(128)S(6)} %select_n.111, bf16[1,1024,1024]{2,1,0:T(8,128)(2,1)S(1)} %bitcast.159, bf16[1,1024,1024]{2,1,0:T(8,128)(2,1)} %bitcast.48), kind=kOutput, calls=%fused_computation.55 | convolution fusion | flops 1075314688 | bytes 6291460 | tf_op jit(solution)/shard_map/dot_general | solution.py:204
  183.5 3.4 %fusion.23 = f32[512,1024]{1,0:T(8,128)S(1)} fusion(bf16[512,1024]{0,1:T(8,128)(2,1)} %bitcast.161, s32[]{:T(128)S(6)} %select_n.108, bf16[1,1024,1024]{2,1,0:T(8,128)(2,1)} %bitcast.158, bf16[1,1024,1024]{2,1,0:T(8,128)(2,1)} %bitcast.48), kind=kOutput, calls=%fused_computation.35 | convolution fusion | flops 1074790400 | bytes 7340036 | tf_op jit(solution)/shard_map/dot_general | solution.py:204
  (109 shorter events, 32.3 us)
Async XLA Ops:
  0.0 34.5 %copy-start = (bf16[1024,1024]{1,0:T(8,128)(2,1)S(1)}, bf16[1024,1024]{1,0:T(8,128)(2,1)}, u32[]{:S(2)}) copy-start(bf16[1024,1024]{1,0:T(8,128)(2,1)} %param.9) | copy-start | bytes 6291460
  0.0 2.3 %copy-start.18 = (f32[2048]{0:T(1024)S(1)}, f32[2048]{0:T(1024)}, u32[]{:S(2)}) copy-start(f32[2048]{0:T(1024)} %param.8) | copy-start | bytes 24580
  2.3 7.6 %copy-start.17 = (f32[1,8,512]{2,1,0:T(8,128)S(1)}, f32[1,8,512]{2,1,0:T(8,128)}, u32[]{:S(2)}) copy-start(f32[1,8,512]{2,1,0:T(8,128)} %param.12) | copy-start | bytes 49156
  6.1 15.0 %collective-permute-start = (bf16[256,1024]{1,0:T(8,128)(2,1)S(1)}, bf16[256,1024]{1,0:T(8,128)(2,1)S(1)}, u32[]{:S(2)}, u32[]{:S(2)}) collective-permute-start(bf16[256,1024]{1,0:T(8,128)(2,1)S(1)} %dynamic-slice_bitcast_fusion.4), channel_id=1, source_target_pairs={{0,2},{2,0},{1,3},{3,1},{4,6},{6,4},{5,7},{7,5},{8,10},{10,8},{9,1... | collective-permute-start | bytes 1572872 | tf_op jit(solution)/shard_map/ppermute | solution.py:77
  12.8 139.6 %copy-start.13 = (pred[512,512]{0,1:T(8,128)(4,1)}, pred[512,512]{0,1:T(8,128)(4,1)S(1)}, u32[]{:S(2)}) copy-start(pred[512,512]{0,1:T(8,128)(4,1)S(1)} %iota_compare_fusion.1) | copy-start | bytes 786436
  21.0 1.9 %collective-permute-start.1 = (bf16[256,1024]{1,0:T(8,128)(2,1)S(1)}, bf16[256,1024]{1,0:T(8,128)(2,1)S(1)}, u32[]{:S(2)}, u32[]{:S(2)}) collective-permute-start(bf16[256,1024]{1,0:T(8,128)(2,1)S(1)} %collective-permute-done), channel_id=1, source_target_pairs={{0,1},{1,0},{2,3},{3,2},{4,5},{5,4},{6,7},{7,6},{8,9},{9,8},{10,11... | collective-permute-start | bytes 1572872 | tf_op jit(solution)/shard_map/ppermute | solution.py:67
  26.0 3.9 %copy-start.20 = (bf16[1024,2,1024]{2,1,0:T(2,128)(2,1)S(1)}, bf16[1024,2,1024]{2,1,0:T(2,128)(2,1)}, u32[]{:S(2)}) copy-start(bf16[1024,2,1024]{2,1,0:T(2,128)(2,1)} %param.10) | copy-start | bytes 12582916
  30.0 4.5 %copy-start.11 = (bf16[1,512,2048]{2,1,0:T(8,128)(2,1)S(1)}, bf16[1,512,2048]{2,1,0:T(8,128)(2,1)}, u32[]{:S(2)}) copy-start(bf16[1,512,2048]{2,1,0:T(8,128)(2,1)} %copy-done.10) | copy-start | bytes 6291460
  31.6 26.1 %collective-permute-start.2 = (bf16[2,256,1024]{2,1,0:T(8,128)(2,1)S(1)}, bf16[2,256,1024]{2,1,0:T(8,128)(2,1)S(1)}, u32[]{:S(2)}, u32[]{:S(2)}) collective-permute-start(bf16[2,256,1024]{2,1,0:T(8,128)(2,1)S(1)} %fusion.50), channel_id=1, source_target_pairs={{0,2},{2,0},{1,3},{3,1},{4,6},{6,4},{5,7},{7,5},{8,10},{10,8},{9,1... | collective-permute-start | bytes 3145736 | tf_op jit(solution)/shard_map/ppermute | solution.py:93
  33.4 45.9 %collective-permute-start.3 = (bf16[2,256,1024]{2,1,0:T(8,128)(2,1)S(1)}, bf16[2,256,1024]{2,1,0:T(8,128)(2,1)S(1)}, u32[]{:S(2)}, u32[]{:S(2)}) collective-permute-start(bf16[2,256,1024]{2,1,0:T(8,128)(2,1)S(1)} %fusion.47), channel_id=1, source_target_pairs={{0,2},{2,0},{1,3},{3,1},{4,6},{6,4},{5,7},{7,5},{8,10},{10,8},{9,1... | collective-permute-start | bytes 3145736 | tf_op jit(solution)/shard_map/ppermute | solution.py:93
  79.3 35.6 %collective-permute-start.4 = (bf16[512,1024]{1,0:T(8,128)(2,1)}, bf16[512,1024]{1,0:T(8,128)(2,1)}, u32[]{:S(2)}, u32[]{:S(2)}) collective-permute-start(bf16[512,1024]{1,0:T(8,128)(2,1)} %convolution_convert_fusion), channel_id=1, source_target_pairs={{0,2},{2,0},{1,3},{3,1},{4,6},{6,4},{5,7},{7,5},{8,10},{10,8},{9,1... | collective-permute-start | bytes 3145736 | tf_op jit(solution)/shard_map/ppermute | solution.py:93
  94.6 7.5 %copy-start.6 = (f32[2,256,1024]{2,1,0:T(8,128)S(1)}, f32[2,256,1024]{2,1,0:T(8,128)}, u32[]{:S(2)}) copy-start(f32[2,256,1024]{2,1,0:T(8,128)} %copy-done.5) | copy-start | bytes 6291460
  94.6 7.5 %copy-start.8 = (f32[2,256,1024]{2,1,0:T(8,128)S(1)}, f32[2,256,1024]{2,1,0:T(8,128)}, u32[]{:S(2)}) copy-start(f32[2,256,1024]{2,1,0:T(8,128)} %copy-done.7) | copy-start | bytes 6291460
  97.6 27.3 %collective-permute-start.5 = (bf16[1,512,1024]{2,1,0:T(8,128)(2,1)}, bf16[1,512,1024]{2,1,0:T(8,128)(2,1)}, u32[]{:S(2)}, u32[]{:S(2)}) collective-permute-start(bf16[1,512,1024]{2,1,0:T(8,128)(2,1)} %multiply_convert_fusion), channel_id=1, source_target_pairs={{0,4},{4,8},{8,12},{1,5},{5,9},{9,13},{2,6},{6,10},{10,14},{3,7},{... | collective-permute-start | bytes 3145736 | tf_op jit(solution)/shard_map/ppermute | solution.py:14
  102.3 43.1 %collective-permute-start.6 = (bf16[1,512,1024]{2,1,0:T(8,128)(2,1)S(1)}, bf16[1,512,1024]{2,1,0:T(8,128)(2,1)}, u32[]{:S(2)}, u32[]{:S(2)}) collective-permute-start(bf16[1,512,1024]{2,1,0:T(8,128)(2,1)S(1)} %fusion.16), channel_id=1, source_target_pairs={{0,4},{4,8},{8,12},{1,5},{5,9},{9,13},{2,6},{6,10},{10,14},{3,7},{... | collective-permute-start | bytes 3145736 | tf_op jit(solution)/shard_map/ppermute | solution.py:14
  111.1 67.5 %collective-permute-start.10 = (bf16[1024,1024]{1,0:T(8,128)(2,1)}, bf16[1024,1024]{1,0:T(8,128)(2,1)}, u32[]{:S(2)}, u32[]{:S(2)}) collective-permute-start(bf16[1024,1024]{1,0:T(8,128)(2,1)} %param.11), channel_id=1, source_target_pairs={{0,2},{2,0},{1,3},{3,1},{4,6},{6,4},{5,7},{7,5},{8,10},{10,8},{9,1... | collective-permute-start | bytes 6291464 | tf_op jit(solution)/shard_map/ppermute | solution.py:189
  111.6 3.3 %copy-start.12 = (f32[512,1024]{1,0:T(8,128)S(1)}, f32[512,1024]{1,0:T(8,128)}, u32[]{:S(2)}) copy-start(f32[512,1024]{1,0:T(8,128)} %fusion.57) | copy-start | bytes 6291460
  119.7 27.1 %copy-start.19 = (f32[9]{0:T(128)S(1)}, f32[9]{0:T(128)}, u32[]{:S(2)}) copy-start(f32[9]{0:T(128)} %pad.11.clone) | copy-start | bytes 112
  122.0 29.6 %copy-start.3 = (f32[64,8,8,128]{3,2,1,0:T(8,128)S(1)}, f32[64,8,8,128]{3,2,1,0:T(8,128)}, u32[]{:S(2)}) copy-start(f32[64,8,8,128]{3,2,1,0:T(8,128)} %get-tuple-element.22) | copy-start | bytes 6291460
  146.8 5.5 %copy-start.4 = (f32[1,512,1024]{1,2,0:T(8,128)S(1)}, f32[1,512,1024]{1,2,0:T(8,128)}, u32[]{:S(2)}) copy-start(f32[1,512,1024]{1,2,0:T(8,128)} %copy.93) | copy-start | bytes 6291460
  147.0 13.3 %collective-permute-start.7 = (bf16[1,9,128,128]{3,2,1,0:T(8,128)(2,1)S(1)}, bf16[1,9,128,128]{3,2,1,0:T(8,128)(2,1)S(1)}, u32[]{:S(2)}, u32[]{:S(2)}) collective-permute-start(bf16[1,9,128,128]{3,2,1,0:T(8,128)(2,1)S(1)} %fusion.68), channel_id=1, source_target_pairs={{0,4},{4,8},{8,12},{1,5},{5,9},{9,13},{2,6},{6,10},{10,14},{3,7},{... | collective-permute-start | bytes 884744 | tf_op jit(solution)/shard_map/ppermute | solution.py:14
  152.4 2.6 %copy-start.15 = (pred[512,512]{0,1:T(8,128)(4,1)S(1)}, pred[512,512]{0,1:T(8,128)(4,1)}, u32[]{:S(2)}) copy-start(pred[512,512]{0,1:T(8,128)(4,1)} %fusion.63) | copy-start | bytes 786436
  155.0 9.0 %copy-start.9 = (bf16[1,512,1024]{1,2,0:T(8,128)(2,1)S(1)}, bf16[1,512,1024]{1,2,0:T(8,128)(2,1)}, u32[]{:S(2)}) copy-start(bf16[1,512,1024]{1,2,0:T(8,128)(2,1)} %copy.96) | copy-start | bytes 3145732
  155.0 9.0 %copy-start.14 = (pred[512,512]{0,1:T(8,128)(4,1)S(1)}, pred[512,512]{0,1:T(8,128)(4,1)}, u32[]{:S(2)}) copy-start(pred[512,512]{0,1:T(8,128)(4,1)} %copy-done.13) | copy-start | bytes 786436
  160.4 8.4 %collective-permute-start.8 = (bf16[1,9,128,128]{3,2,1,0:T(8,128)(2,1)S(1)}, bf16[1,9,128,128]{3,2,1,0:T(8,128)(2,1)S(1)}, u32[]{:S(2)}, u32[]{:S(2)}) collective-permute-start(bf16[1,9,128,128]{3,2,1,0:T(8,128)(2,1)S(1)} %fusion.70), channel_id=1, source_target_pairs={{0,4},{4,8},{8,12},{1,5},{5,9},{9,13},{2,6},{6,10},{10,14},{3,7},{... | collective-permute-start | bytes 884744 | tf_op jit(solution)/shard_map/ppermute | solution.py:14
  169.0 8.9 %collective-permute-start.9 = (bf16[1,9,128,128]{3,2,1,0:T(8,128)(2,1)S(1)}, bf16[1,9,128,128]{3,2,1,0:T(8,128)(2,1)S(1)}, u32[]{:S(2)}, u32[]{:S(2)}) collective-permute-start(bf16[1,9,128,128]{3,2,1,0:T(8,128)(2,1)S(1)} %fusion.72), channel_id=1, source_target_pairs={{0,4},{4,8},{8,12},{1,5},{5,9},{9,13},{2,6},{6,10},{10,14},{3,7},{... | collective-permute-start | bytes 884744 | tf_op jit(solution)/shard_map/ppermute | solution.py:14
  172.8 5.2 %copy-start.16 = (f32[512,8]{0,1:T(8,128)S(1)}, f32[512,8]{0,1:T(8,128)}, u32[]{:S(2)}) copy-start(f32[512,8]{0,1:T(8,128)} %get-tuple-element.17) | copy-start | bytes 49156
  172.8 5.2 %copy-start.23 = (f32[8,128,512]{2,1,0:T(8,128)S(1)}, f32[8,128,512]{2,1,0:T(8,128)}, u32[]{:S(2)}) copy-start(f32[8,128,512]{2,1,0:T(8,128)} %fusion.5) | copy-start | bytes 6291460
  178.6 4.9 %copy-start.22 = (bf16[1,512,8,128]{1,3,2,0:T(8,128)(2,1)}, bf16[1,512,8,128]{1,3,2,0:T(8,128)(2,1)S(1)}, u32[]{:S(2)}) copy-start(bf16[1,512,8,128]{1,3,2,0:T(8,128)(2,1)S(1)} %fusion.28) | copy-start | bytes 3145732
  183.4 3.4 %collective-permute-start.11 = (bf16[512,1024]{1,0:T(8,128)(2,1)}, bf16[512,1024]{1,0:T(8,128)(2,1)S(1)}, u32[]{:S(2)}, u32[]{:S(2)}) collective-permute-start(bf16[512,1024]{1,0:T(8,128)(2,1)} %fusion.37), channel_id=1, source_target_pairs={{0,1},{1,0},{2,3},{3,2},{4,5},{5,4},{6,7},{7,6},{8,9},{9,8},{10,11... | collective-permute-start | bytes 3145736 | tf_op jit(solution)/shard_map/ppermute | solution.py:213
  183.4 3.4 %copy-start.2 = (bf16[1,512,2048]{2,1,0:T(8,128)(2,1)S(1)}, bf16[1,512,2048]{2,1,0:T(8,128)(2,1)}, u32[]{:S(2)}) copy-start(bf16[1,512,2048]{2,1,0:T(8,128)(2,1)} %param.7) | copy-start | bytes 6291460
  183.4 5.0 %copy-start.1 = (bf16[1024,1024]{1,0:T(8,128)(2,1)S(1)}, bf16[1024,1024]{1,0:T(8,128)(2,1)}, u32[]{:S(2)}) copy-start(bf16[1024,1024]{1,0:T(8,128)(2,1)} %param.9) | copy-start | bytes 6291460
  (4 other events, 6.0 us)

commit v21 on v17

--- a/solution.py
+++ b/solution.py
@@ -129,13 +129,12 @@
     whole = climb[:, :, -1]
     factor = jnp.exp(whole) * keep[:, None]
     weight = jnp.exp(whole[:, :, None] - climb)
+    weighted = weight.transpose(0, 2, 1)[..., None] * lookup_vectors.astype(jnp.float32)
+    weighted_hi = weighted.astype(jnp.bfloat16)
+    weighted_lo = (weighted - weighted_hi.astype(jnp.float32)).astype(jnp.bfloat16)
     local_state = jnp.einsum(
-        "bht,bthd,bthe->bhde",
-        weight,
-        lookup_vectors.astype(jnp.float32),
-        values.astype(jnp.float32),
-        precision=lax.Precision.HIGHEST,
-    )
+        "bthd,bthe->bhde", weighted_hi, values, preferred_element_type=jnp.float32
+    ) + jnp.einsum("bthd,bthe->bhde", weighted_lo, values, preferred_element_type=jnp.float32)
     local_mass = jnp.sum(weight * weight, axis=-1)
 
     def as_block(per_head):

time: 173 us -> 194 us (1.12)
  waiting for transfers between devices: 60 us -> 78.1 us
  other arithmetic: 21.1 us -> 23.6 us
    ppermute x5, waiting for transfers between devices: 8.03 us -> 28.6 us  [shifted(): lax.ppermute(value, axis, [(source, source + steps) for source in range(i...]
    ppermute x3, waiting for transfers between devices: 43.8 us -> 40 us  [gathered_sum(): lax.ppermute(outgoing, 'wloop', [(source, (source - step) % ways) for sou...]
    convert_element_type x1 -> x2, other arithmetic: 3.52 us -> 5.41 us  [shards(): rms_rows(pair_raw[0].reshape(trajs, span, heads_here, head_dim), 1e-06)]
    unnamed x53 -> x43, local copies, waits for them, and re-layouts: 6.28 us -> 7.24 us
  transfers between devices with their start and end apart: 12 -> 12, of which waited for: 6 -> 6; matrix products, arithmetic and copies ran while one was open for 35% -> 27% of each run, Pallas kernels for 0% -> 0%
where the time goes in v21:
time: 194 us; the launch traced here: 193 us
  waiting for transfers between devices  78.1 us (40%)
  matrix products  41.2 us (21%)
  starting transfers between devices  27.6 us (14%)
  other arithmetic  23.6 us (12%)
  local copies, waits for them, and re-layouts  21.5 us (11%)
    ppermute x3, waiting for transfers between devices, gathered_sum(): lax.ppermute(outgoing, 'wloop', [(source, (source - step) % ways) for sou...  40 us
    ppermute x5, waiting for transfers between devices, shifted(): lax.ppermute(value, axis, [(source, source + steps) for source in range(i...  28.6 us
    ppermute x5, starting transfers between devices, shifted(): lax.ppermute(value, axis, [(source, source + steps) for source in range(i...  20.4 us
    ppermute x1, waiting for transfers between devices, shards(): lax.ppermute(part, 'wloop', [(source, (source + step) % ways) for source...  9.36 us
    dot_general x4, matrix products, shards(): jnp.einsum('td,dje->jte', rows[lo:hi], w_keyvalue, preferred_element_type...  8.95 us
    dot_general x2, matrix products, output_share(): jnp.dot(attended, lax.dynamic_index_in_dim(from_ranks, (me - rank) % ways...  7.28 us
    unnamed x43, local copies, waits for them, and re-layouts  7.24 us
    dot_general x2, matrix products, shards(): jnp.dot(rows, w_query, preferred_element_type=jnp.float32)  6.08 us
  transfers between devices with their start and end apart: 12, of which 6 were waited for; matrix products, arithmetic and copies ran while one was open for 27% of the time, Pallas kernels for 0%

profile of v21, /device:TPU:0, one launch (start us, length us, event | category | flops | bytes accessed | tf_op | source)
XLA Modules:
  0.0 193.2 jit_solution(13212494937108252760)
XLA Ops:
  0.0 2.2 %fusion.2 = f32[512]{0:T(512)S(1)} fusion(bf16[1,512,2048]{2,1,0:T(8,128)(2,1)} %param.7), kind=kLoop, calls=%fused_computation.18 | loop fusion | flops 3145216 | bytes 2099200 | tf_op jit(solution)/shard_map/reduce_sum | solution.py:18
  4.6 3.0 %collective-permute-start = (bf16[256,1024]{1,0:T(8,128)(2,1)S(1)}, bf16[256,1024]{1,0:T(8,128)(2,1)S(1)}, u32[]{:S(2)}, u32[]{:S(2)}) collective-permute-start(bf16[256,1024]{1,0:T(8,128)(2,1)S(1)} %dynamic-slice_bitcast_fusion.4), channel_id=1, source_target_pairs={{0,2},{2,0},{1,3},{3,1},{4,6},{6,4},{5,7},{7,5},{8,10},{10,8},{9,1... | collective-permute-start | bytes 1572872 | tf_op jit(solution)/shard_map/ppermute | solution.py:77
  10.2 9.4 %collective-permute-done = bf16[256,1024]{1,0:T(8,128)(2,1)S(1)} collective-permute-done((bf16[256,1024]{1,0:T(8,128)(2,1)S(1)}, bf16[256,1024]{1,0:T(8,128)(2,1)S(1)}, u32[]{:S(2)}, u32[]{:S(2)}) %collective-permute-start) | collective-permute-done | bytes 524320 | tf_op jit(solution)/shard_map/ppermute | solution.py:77
  22.5 1.8 gather_fusion
  24.5 3.9 %fusion.51 = bf16[2,256,1024]{2,1,0:T(8,128)(2,1)S(1)} fusion(bf16[1024,2,1024]{2,1,0:T(2,128)(2,1)} %param.10, bf16[2,256,1024]{2,1,0:T(8,128)(2,1)S(1)} %broadcast_select_fusion), kind=kOutput, calls=%fused_computation.65 | convolution fusion | flops 1074266112 | bytes 5767168 | tf_op jit(solution)/shard_map/td,dje->jte/dot_general | solution.py:103
  28.5 1.8 collective-permute-start.2
  32.4 2.2 %convolution_convert_fusion = bf16[512,1024]{1,0:T(8,128)(2,1)} fusion(bf16[512,1024]{1,0:T(8,128)(2,1)S(1)} %bitcast_select_fusion, bf16[1024,1024]{1,0:T(8,128)(2,1)S(1)} %copy-done), kind=kOutput, calls=%fused_computation.61 | convolution fusion | flops 1074266112 | bytes 4194304 | tf_op jit(solution)/shard_map/dot_general | solution.py:112
  34.7 19.9 %collective-permute-done.2 = bf16[2,256,1024]{2,1,0:T(8,128)(2,1)S(1)} collective-permute-done((bf16[2,256,1024]{2,1,0:T(8,128)(2,1)S(1)}, bf16[2,256,1024]{2,1,0:T(8,128)(2,1)S(1)}, u32[]{:S(2)}, u32[]{:S(2)}) %collective-permute-start.2) | collective-permute-done | bytes 1048608 | tf_op jit(solution)/shard_map/ppermute | solution.py:91
  56.3 20.1 %collective-permute-done.3 = bf16[2,256,1024]{2,1,0:T(8,128)(2,1)S(1)} collective-permute-done((bf16[2,256,1024]{2,1,0:T(8,128)(2,1)S(1)}, bf16[2,256,1024]{2,1,0:T(8,128)(2,1)S(1)}, u32[]{:S(2)}, u32[]{:S(2)}) %collective-permute-start.3) | collective-permute-done | bytes 1048608 | tf_op jit(solution)/shard_map/ppermute | solution.py:91
  81.0 1.8 copy.104
  82.8 2.2 %reduce_sum.58 = f32[512,8]{1,0:T(8,128)S(1)} reduce(f32[512,8,128]{2,1,0:T(8,128)} %bitcast.135, f32[]{:T(128)} %constant.107.clone.1), dimensions={2}, to_apply=%region_2.3 | reduce | flops 520192 | bytes 2113540 | tf_op jit(solution)/shard_map/reduce_sum | solution.py:18
  86.7 2.9 %copy.99 = f32[1,512,1024]{2,1,0:T(8,128)} copy(f32[1,512,1024]{1,2,0:T(8,128)} %bitcast.137) | data formatting | bytes 4194304 | tf_op jit(solution)/shard_map/mul | solution.py:18
  89.6 3.5 %multiply_convert_fusion = bf16[1,512,1024]{2,1,0:T(8,128)(2,1)} fusion(f32[1,512,1024]{2,1,0:T(8,128)} %get-tuple-element.20, f32[1,512,1024]{2,1,0:T(8,128)} %copy.99), kind=kLoop, calls=%fused_computation.50 | loop fusion | flops 1048576 | bytes 5242880 | tf_op jit(solution)/shard_map/convert_element_type | solution.py:115
  93.2 4.7 %collective-permute-start.5 = (bf16[1,512,1024]{2,1,0:T(8,128)(2,1)}, bf16[1,512,1024]{2,1,0:T(8,128)(2,1)}, u32[]{:S(2)}, u32[]{:S(2)}) collective-permute-start(bf16[1,512,1024]{2,1,0:T(8,128)(2,1)} %multiply_convert_fusion), channel_id=1, source_target_pairs={{0,4},{4,8},{8,12},{1,5},{5,9},{9,13},{2,6},{6,10},{10,14},{3,7},{... | collective-permute-start | bytes 3145736 | tf_op jit(solution)/shard_map/ppermute | solution.py:14
  97.9 3.5 %collective-permute-start.6 = (bf16[1,512,1024]{2,1,0:T(8,128)(2,1)}, bf16[1,512,1024]{2,1,0:T(8,128)(2,1)}, u32[]{:S(2)}, u32[]{:S(2)}) collective-permute-start(bf16[1,512,1024]{2,1,0:T(8,128)(2,1)} %fusion.24), channel_id=1, source_target_pairs={{0,4},{4,8},{8,12},{1,5},{5,9},{9,13},{2,6},{6,10},{10,14},{3,7},{... | collective-permute-start | bytes 3145736 | tf_op jit(solution)/shard_map/ppermute | solution.py:14
  101.4 2.9 %copy.98 = f32[1,512,1024]{1,2,0:T(8,128)} copy(f32[1,512,1024]{2,1,0:T(8,128)} %get-tuple-element.20) | data formatting | bytes 4194304 | tf_op jit(solution)/shard_map/reshape;squeeze | solution.py:115
  105.8 1.9 multiply_convert_fusion.1
  107.7 2.7 %copy.101 = bf16[1,512,1024]{1,2,0:T(8,128)(2,1)} copy(bf16[1,512,1024]{2,1,0:T(8,128)(2,1)} %fusion.24) | data formatting | bytes 2097152 | tf_op jit(solution)/shard_map/convert_element_type | solution.py:118
  113.1 7.6 %collective-permute-done.5 = bf16[1,512,1024]{2,1,0:T(8,128)(2,1)} collective-permute-done((bf16[1,512,1024]{2,1,0:T(8,128)(2,1)}, bf16[1,512,1024]{2,1,0:T(8,128)(2,1)}, u32[]{:S(2)}, u32[]{:S(2)}) %collective-permute-start.5) | collective-permute-done | bytes 1048608 | tf_op jit(solution)/shard_map/ppermute | solution.py:14
  120.7 21.0 %collective-permute-done.6 = bf16[1,512,1024]{2,1,0:T(8,128)(2,1)} collective-permute-done((bf16[1,512,1024]{2,1,0:T(8,128)(2,1)}, bf16[1,512,1024]{2,1,0:T(8,128)(2,1)}, u32[]{:S(2)}, u32[]{:S(2)}) %collective-permute-start.6) | collective-permute-done | bytes 1048608 | tf_op jit(solution)/shard_map/ppermute | solution.py:14
  141.8 5.1 %collective-permute-start.7 = (bf16[1,9,128,128]{3,2,1,0:T(8,128)(2,1)S(1)}, bf16[1,9,128,128]{3,2,1,0:T(8,128)(2,1)}, u32[]{:S(2)}, u32[]{:S(2)}) collective-permute-start(bf16[1,9,128,128]{3,2,1,0:T(8,128)(2,1)S(1)} %fusion.68), channel_id=1, source_target_pairs={{0,4},{4,8},{8,12},{1,5},{5,9},{9,13},{2,6},{6,10},{10,14},{3,7},{... | collective-permute-start | bytes 884744 | tf_op jit(solution)/shard_map/ppermute | solution.py:14
  147.0 2.5 %copy.105 = bf16[64,8,8,128]{3,2,1,0:T(8,128)(2,1)} copy(bf16[64,8,8,128]{3,1,2,0:T(8,128)(2,1)} %bitcast.67) | data formatting | bytes 2097152
  149.4 3.8 %multiply_bitcast_fusion.1 = (f32[64,8,8,128]{3,1,2,0:T(8,128)S(1)}, f32[64,8,8,128]{3,2,1,0:T(8,128)}) fusion(bf16[512,1024]{1,0:T(8,128)(2,1)} %collective-permute-done.4, bf16[1024,1024]{1,0:T(8,128)(2,1)S(1)} %copy-done, bf16[1,512,2048]{2,1,0:T(8,128)(2,1)S(1)} %copy-done.10, s32[]{:T(128)S(6)} %select_n.93), kind=kOutput, calls=%fused_computation.56 | convolution fusion | flops 1075314688 | bytes 8388612 | tf_op jit(solution)/shard_map/dot_general | solution.py:112
  154.5 2.0 %fusion.26 = bf16[512,8,128]{2,0,1:T(8,128)(2,1)S(1)} fusion(f32[64,8,8,128]{3,2,1,0:T(8,128)} %get-tuple-element.22, f32[512,8]{0,1:T(8,128)S(1)} %add_rsqrt_fusion.1), kind=kLoop, calls=%fused_computation.41 | loop fusion | flops 1048576 | bytes 3162112 | tf_op jit(solution)/shard_map/convert_element_type | solution.py:124
  156.6 2.5 %fusion = (f32[8,512]{1,0:T(8,128)S(1)}, f32[8,512,512]{1,2,0:T(8,128)S(1)}) fusion(pred[512,512]{0,1:T(8,128)(4,1)S(1)} %copy-done.13, bf16[512,8,128]{2,0,1:T(8,128)(2,1)S(1)} %fusion.26, bf16[512,8,128]{0,2,1:T(8,128)(2,1)S(1)} %copy-done.5), kind=kOutput, calls=%fused_computation.5 | convolution fusion | flops 543158272 | bytes 10764288 | tf_op jit(solution)/shard_map/bihd,bjhd->bhij/dot_general | solution.py:23
  159.1 5.3 %fusion.1 = (f32[8,512]{1,0:T(8,128)S(1)}, f32[8,512,512]{1,2,0:T(8,128)}) fusion(pred[512,512]{0,1:T(8,128)(4,1)S(1)} %copy-done.12, bf16[512,8,128]{2,0,1:T(8,128)(2,1)S(1)} %fusion.26, bf16[512,8,128]{2,1,0:T(8,128)(2,1)S(1)} %bitcast.144), kind=kOutput, calls=%fused_computation.6 | convolution fusion | flops 543158272 | bytes 10764288 | tf_op jit(solution)/shard_map/bihd,bjhd->bhij/dot_general | solution.py:27
  165.5 2.8 %collective-permute-start.8 = (bf16[1,9,128,128]{3,2,1,0:T(8,128)(2,1)S(1)}, bf16[1,9,128,128]{3,2,1,0:T(8,128)(2,1)S(1)}, u32[]{:S(2)}, u32[]{:S(2)}) collective-permute-start(bf16[1,9,128,128]{3,2,1,0:T(8,128)(2,1)S(1)} %fusion.70), channel_id=1, source_target_pairs={{0,4},{4,8},{8,12},{1,5},{5,9},{9,13},{2,6},{6,10},{10,14},{3,7},{... | collective-permute-start | bytes 884744 | tf_op jit(solution)/shard_map/ppermute | solution.py:14
  168.3 3.3 %fusion.5 = f32[8,128,512]{2,1,0:T(8,128)} fusion(bf16[512,8,128]{0,2,1:T(8,128)(2,1)S(1)} %bitcast.140, f32[8,512,512]{1,2,0:T(8,128)S(1)} %get-tuple-element.26, f32[8,512]{1,0:T(8,128)S(1)} %add.176, pred[512,512]{0,1:T(8,128)(4,1)S(1)} %copy-done.13), kind=kOutput, calls=%fused_computation.21 | convolution fusion | flops 545259520 | bytes 11812864 | tf_op jit(solution)/shard_map/bhij,bjhd->bihd/dot_general | solution.py:38
  173.3 4.3 %collective-permute-start.9 = (bf16[1,9,128,128]{3,2,1,0:T(8,128)(2,1)S(1)}, bf16[1,9,128,128]{3,2,1,0:T(8,128)(2,1)S(1)}, u32[]{:S(2)}, u32[]{:S(2)}) collective-permute-start(bf16[1,9,128,128]{3,2,1,0:T(8,128)(2,1)S(1)} %fusion.72), channel_id=1, source_target_pairs={{0,4},{4,8},{8,12},{1,5},{5,9},{9,13},{2,6},{6,10},{10,14},{3,7},{... | collective-permute-start | bytes 884744 | tf_op jit(solution)/shard_map/ppermute | solution.py:14
  177.6 5.0 %fusion.6 = f32[8,128,512]{2,1,0:T(8,128)S(1)} fusion(bf16[512,8,128]{0,2,1:T(8,128)(2,1)S(1)} %bitcast.145, f32[8,512,512]{1,2,0:T(8,128)} %get-tuple-element.28, f32[8,512]{1,0:T(8,128)S(1)} %add.176, pred[512,512]{0,1:T(8,128)(4,1)} %fusion.63), kind=kOutput, calls=%fused_computation.22 | convolution fusion | flops 545259520 | bytes 11812864 | tf_op jit(solution)/shard_map/bhij,bjhd->bihd/dot_general | solution.py:40
  184.3 3.9 %fusion.36 = bf16[512,1024]{1,0:T(8,128)(2,1)} fusion(bf16[512,1024]{0,1:T(8,128)(2,1)S(1)} %bitcast.156, s32[]{:T(128)S(6)} %select_n.111, bf16[1,1024,1024]{2,1,0:T(8,128)(2,1)S(1)} %bitcast.155, bf16[1,1024,1024]{2,1,0:T(8,128)(2,1)} %bitcast.47), kind=kOutput, calls=%fused_computation.58 | convolution fusion | flops 1075314688 | bytes 6291460 | tf_op jit(solution)/shard_map/dot_general | solution.py:199
  188.2 3.4 %fusion.21 = f32[512,1024]{1,0:T(8,128)S(1)} fusion(bf16[512,1024]{0,1:T(8,128)(2,1)} %bitcast.157, s32[]{:T(128)S(6)} %select_n.108, bf16[1,1024,1024]{2,1,0:T(8,128)(2,1)} %bitcast.154, bf16[1,1024,1024]{2,1,0:T(8,128)(2,1)} %bitcast.47), kind=kOutput, calls=%fused_computation.36 | convolution fusion | flops 1074790400 | bytes 7340036 | tf_op jit(solution)/shard_map/dot_general | solution.py:199
  (101 shorter events, 29.0 us)
Async XLA Ops:
  0.0 32.4 %copy-start = (bf16[1024,1024]{1,0:T(8,128)(2,1)S(1)}, bf16[1024,1024]{1,0:T(8,128)(2,1)}, u32[]{:S(2)}) copy-start(bf16[1024,1024]{1,0:T(8,128)(2,1)} %param.9) | copy-start | bytes 6291460
  0.0 2.2 %copy-start.15 = (f32[2048]{0:T(1024)S(1)}, f32[2048]{0:T(1024)}, u32[]{:S(2)}) copy-start(f32[2048]{0:T(1024)} %param.8) | copy-start | bytes 24580
  0.0 2.4 %copy-start.2 = (bf16[1,512,2048]{2,1,0:T(8,128)(2,1)S(1)}, bf16[1,512,2048]{2,1,0:T(8,128)(2,1)}, u32[]{:S(2)}) copy-start(bf16[1,512,2048]{2,1,0:T(8,128)(2,1)} %param.7) | copy-start | bytes 6291460
  2.4 5.2 %copy-start.14 = (f32[1,8,512]{2,1,0:T(8,128)S(1)}, f32[1,8,512]{2,1,0:T(8,128)}, u32[]{:S(2)}) copy-start(f32[1,8,512]{2,1,0:T(8,128)} %param.12) | copy-start | bytes 49156
  2.9 1.4 copy-start.8
  4.6 15.0 %collective-permute-start = (bf16[256,1024]{1,0:T(8,128)(2,1)S(1)}, bf16[256,1024]{1,0:T(8,128)(2,1)S(1)}, u32[]{:S(2)}, u32[]{:S(2)}) collective-permute-start(bf16[256,1024]{1,0:T(8,128)(2,1)S(1)} %dynamic-slice_bitcast_fusion.4), channel_id=1, source_target_pairs={{0,2},{2,0},{1,3},{3,1},{4,6},{6,4},{5,7},{7,5},{8,10},{10,8},{9,1... | collective-permute-start | bytes 1572872 | tf_op jit(solution)/shard_map/ppermute | solution.py:77
  19.5 1.9 collective-permute-start.1
  24.5 5.7 %copy-start.16 = (bf16[1024,2,1024]{2,1,0:T(2,128)(2,1)S(1)}, bf16[1024,2,1024]{2,1,0:T(2,128)(2,1)}, u32[]{:S(2)}) copy-start(bf16[1024,2,1024]{2,1,0:T(2,128)(2,1)} %param.10) | copy-start | bytes 12582916
  28.5 26.1 %collective-permute-start.2 = (bf16[2,256,1024]{2,1,0:T(8,128)(2,1)S(1)}, bf16[2,256,1024]{2,1,0:T(8,128)(2,1)S(1)}, u32[]{:S(2)}, u32[]{:S(2)}) collective-permute-start(bf16[2,256,1024]{2,1,0:T(8,128)(2,1)S(1)} %fusion.51), channel_id=1, source_target_pairs={{0,2},{2,0},{1,3},{3,1},{4,6},{6,4},{5,7},{7,5},{8,10},{10,8},{9,1... | collective-permute-start | bytes 3145736 | tf_op jit(solution)/shard_map/ppermute | solution.py:91
  31.9 44.5 %collective-permute-start.3 = (bf16[2,256,1024]{2,1,0:T(8,128)(2,1)S(1)}, bf16[2,256,1024]{2,1,0:T(8,128)(2,1)S(1)}, u32[]{:S(2)}, u32[]{:S(2)}) collective-permute-start(bf16[2,256,1024]{2,1,0:T(8,128)(2,1)S(1)} %fusion.48), channel_id=1, source_target_pairs={{0,2},{2,0},{1,3},{3,1},{4,6},{6,4},{5,7},{7,5},{8,10},{10,8},{9,1... | collective-permute-start | bytes 3145736 | tf_op jit(solution)/shard_map/ppermute | solution.py:91
  32.4 22.1 %copy-start.9 = (bf16[1,512,2048]{2,1,0:T(8,128)(2,1)S(1)}, bf16[1,512,2048]{2,1,0:T(8,128)(2,1)}, u32[]{:S(2)}) copy-start(bf16[1,512,2048]{2,1,0:T(8,128)(2,1)} %copy-done.8) | copy-start | bytes 6291460
  93.2 27.6 %collective-permute-start.5 = (bf16[1,512,1024]{2,1,0:T(8,128)(2,1)}, bf16[1,512,1024]{2,1,0:T(8,128)(2,1)}, u32[]{:S(2)}, u32[]{:S(2)}) collective-permute-start(bf16[1,512,1024]{2,1,0:T(8,128)(2,1)} %multiply_convert_fusion), channel_id=1, source_target_pairs={{0,4},{4,8},{8,12},{1,5},{5,9},{9,13},{2,6},{6,10},{10,14},{3,7},{... | collective-permute-start | bytes 3145736 | tf_op jit(solution)/shard_map/ppermute | solution.py:14
  97.9 43.8 %collective-permute-start.6 = (bf16[1,512,1024]{2,1,0:T(8,128)(2,1)}, bf16[1,512,1024]{2,1,0:T(8,128)(2,1)}, u32[]{:S(2)}, u32[]{:S(2)}) collective-permute-start(bf16[1,512,1024]{2,1,0:T(8,128)(2,1)} %fusion.24), channel_id=1, source_target_pairs={{0,4},{4,8},{8,12},{1,5},{5,9},{9,13},{2,6},{6,10},{10,14},{3,7},{... | collective-permute-start | bytes 3145736 | tf_op jit(solution)/shard_map/ppermute | solution.py:14
  104.3 45.1 %collective-permute-start.4 = (bf16[512,1024]{1,0:T(8,128)(2,1)}, bf16[512,1024]{1,0:T(8,128)(2,1)}, u32[]{:S(2)}, u32[]{:S(2)}) collective-permute-start(bf16[512,1024]{1,0:T(8,128)(2,1)} %convolution_convert_fusion), channel_id=1, source_target_pairs={{0,2},{2,0},{1,3},{3,1},{4,6},{6,4},{5,7},{7,5},{8,10},{10,8},{9,1... | collective-permute-start | bytes 3145736 | tf_op jit(solution)/shard_map/ppermute | solution.py:91
  107.7 4.9 %copy-start.4 = (bf16[512,8,128]{0,2,1:T(8,128)(2,1)}, bf16[512,8,128]{0,2,1:T(8,128)(2,1)S(1)}, u32[]{:S(2)}) copy-start(bf16[512,8,128]{0,2,1:T(8,128)(2,1)S(1)} %multiply_convert_fusion.1) | copy-start | bytes 3145732
  110.4 2.2 %copy-start.6 = (bf16[1,512,1024]{1,2,0:T(8,128)(2,1)S(1)}, bf16[1,512,1024]{1,2,0:T(8,128)(2,1)}, u32[]{:S(2)}) copy-start(bf16[1,512,1024]{1,2,0:T(8,128)(2,1)} %copy.101) | copy-start | bytes 3145732
  110.4 72.9 %collective-permute-start.10 = (bf16[1024,1024]{1,0:T(8,128)(2,1)}, bf16[1024,1024]{1,0:T(8,128)(2,1)}, u32[]{:S(2)}, u32[]{:S(2)}) collective-permute-start(bf16[1024,1024]{1,0:T(8,128)(2,1)} %param.11), channel_id=1, source_target_pairs={{0,2},{2,0},{1,3},{3,1},{4,6},{6,4},{5,7},{7,5},{8,10},{10,8},{9,1... | collective-permute-start | bytes 6291464 | tf_op jit(solution)/shard_map/ppermute | solution.py:184
  113.1 36.3 %copy-start.10 = (bf16[1,512,2048]{2,1,0:T(8,128)(2,1)S(1)}, bf16[1,512,2048]{2,1,0:T(8,128)(2,1)}, u32[]{:S(2)}) copy-start(bf16[1,512,2048]{2,1,0:T(8,128)(2,1)} %copy-done.8) | copy-start | bytes 6291460
  141.8 22.5 %collective-permute-start.7 = (bf16[1,9,128,128]{3,2,1,0:T(8,128)(2,1)S(1)}, bf16[1,9,128,128]{3,2,1,0:T(8,128)(2,1)}, u32[]{:S(2)}, u32[]{:S(2)}) collective-permute-start(bf16[1,9,128,128]{3,2,1,0:T(8,128)(2,1)S(1)} %fusion.68), channel_id=1, source_target_pairs={{0,4},{4,8},{8,12},{1,5},{5,9},{9,13},{2,6},{6,10},{10,14},{3,7},{... | collective-permute-start | bytes 884744 | tf_op jit(solution)/shard_map/ppermute | solution.py:14
  154.4 2.2 %copy-start.5 = (bf16[512,8,128]{0,2,1:T(8,128)(2,1)S(1)}, bf16[512,8,128]{0,2,1:T(8,128)(2,1)}, u32[]{:S(2)}) copy-start(bf16[512,8,128]{0,2,1:T(8,128)(2,1)} %copy-done.4) | copy-start | bytes 3145732
  154.5 2.1 %copy-start.13 = (pred[512,512]{0,1:T(8,128)(4,1)S(1)}, pred[512,512]{0,1:T(8,128)(4,1)}, u32[]{:S(2)}) copy-start(pred[512,512]{0,1:T(8,128)(4,1)} %iota_compare_fusion.1) | copy-start | bytes 786436
  156.5 2.5 %copy-start.11 = (bf16[64,8,8,128]{3,2,1,0:T(8,128)(2,1)S(1)}, bf16[64,8,8,128]{3,2,1,0:T(8,128)(2,1)}, u32[]{:S(2)}) copy-start(bf16[64,8,8,128]{3,2,1,0:T(8,128)(2,1)} %copy.105) | copy-start | bytes 3145732
  156.5 2.5 %copy-start.12 = (pred[512,512]{0,1:T(8,128)(4,1)S(1)}, pred[512,512]{0,1:T(8,128)(4,1)}, u32[]{:S(2)}) copy-start(pred[512,512]{0,1:T(8,128)(4,1)} %fusion.63) | copy-start | bytes 786436
  159.1 9.2 %copy-start.7 = (bf16[1,512,1024]{1,2,0:T(8,128)(2,1)S(1)}, bf16[1,512,1024]{1,2,0:T(8,128)(2,1)}, u32[]{:S(2)}) copy-start(bf16[1,512,1024]{1,2,0:T(8,128)(2,1)} %copy.101) | copy-start | bytes 3145732
  165.5 7.6 %collective-permute-start.8 = (bf16[1,9,128,128]{3,2,1,0:T(8,128)(2,1)S(1)}, bf16[1,9,128,128]{3,2,1,0:T(8,128)(2,1)S(1)}, u32[]{:S(2)}, u32[]{:S(2)}) collective-permute-start(bf16[1,9,128,128]{3,2,1,0:T(8,128)(2,1)S(1)} %fusion.70), channel_id=1, source_target_pairs={{0,4},{4,8},{8,12},{1,5},{5,9},{9,13},{2,6},{6,10},{10,14},{3,7},{... | collective-permute-start | bytes 884744 | tf_op jit(solution)/shard_map/ppermute | solution.py:14
  173.3 9.3 %collective-permute-start.9 = (bf16[1,9,128,128]{3,2,1,0:T(8,128)(2,1)S(1)}, bf16[1,9,128,128]{3,2,1,0:T(8,128)(2,1)S(1)}, u32[]{:S(2)}, u32[]{:S(2)}) collective-permute-start(bf16[1,9,128,128]{3,2,1,0:T(8,128)(2,1)S(1)} %fusion.72), channel_id=1, source_target_pairs={{0,4},{4,8},{8,12},{1,5},{5,9},{9,13},{2,6},{6,10},{10,14},{3,7},{... | collective-permute-start | bytes 884744 | tf_op jit(solution)/shard_map/ppermute | solution.py:14
  177.5 5.1 %copy-start.19 = (f32[8,128,512]{2,1,0:T(8,128)S(1)}, f32[8,128,512]{2,1,0:T(8,128)}, u32[]{:S(2)}) copy-start(f32[8,128,512]{2,1,0:T(8,128)} %fusion.5) | copy-start | bytes 6291460
  182.7 1.6 copy-start.17
  183.3 4.9 %copy-start.18 = (bf16[1,512,8,128]{1,3,2,0:T(8,128)(2,1)}, bf16[1,512,8,128]{1,3,2,0:T(8,128)(2,1)S(1)}, u32[]{:S(2)}) copy-start(bf16[1,512,8,128]{1,3,2,0:T(8,128)(2,1)S(1)} %fusion.29) | copy-start | bytes 3145732
  188.2 3.4 %collective-permute-start.11 = (bf16[512,1024]{1,0:T(8,128)(2,1)}, bf16[512,1024]{1,0:T(8,128)(2,1)S(1)}, u32[]{:S(2)}, u32[]{:S(2)}) collective-permute-start(bf16[512,1024]{1,0:T(8,128)(2,1)} %fusion.36), channel_id=1, source_target_pairs={{0,1},{1,0},{2,3},{3,2},{4,5},{5,4},{6,7},{7,6},{8,9},{9,8},{10,11... | collective-permute-start | bytes 3145736 | tf_op jit(solution)/shard_map/ppermute | solution.py:208
  188.2 3.4 %copy-start.3 = (bf16[1,512,2048]{2,1,0:T(8,128)(2,1)S(1)}, bf16[1,512,2048]{2,1,0:T(8,128)(2,1)}, u32[]{:S(2)}) copy-start(bf16[1,512,2048]{2,1,0:T(8,128)(2,1)} %param.7) | copy-start | bytes 6291460
  188.2 5.0 %copy-start.1 = (bf16[1024,1024]{1,0:T(8,128)(2,1)S(1)}, bf16[1024,1024]{1,0:T(8,128)(2,1)}, u32[]{:S(2)}) copy-start(bf16[1024,1024]{1,0:T(8,128)(2,1)} %param.9) | copy-start | bytes 6291460
